TPU v7x, 768 devices: a whole 4x8x12 slice. The times are simulated.
768 devices in a mesh: ctx: 64 (over x, y, core), head: 12 (over z).
Axes of the slice: x: 4, y: 8, z: 12, core: 2. Of those that a mesh axis runs over, the one named last changes fastest.
Arguments:
- queries: bfloat16 [24576, 3072], P('ctx', 'head'), may hold values from -6 to 6, as said below
- keys: bfloat16 [24576, 3072], P('ctx', 'head'), may hold values from -6 to 6, as said below
- values: bfloat16 [24576, 3072], P('ctx', 'head'), may hold values from -6 to 6
- out_weight: bfloat16 [3072, 4096], P('head'), may hold values from -0.109375 to 0.109375
Outputs:
- mixed: bfloat16 [24576, 4096], P(('ctx', 'head'))
Inputs may be any that keep to these rules, and one draw needn't show every extreme that they name: `queries`: entries of order one. `keys`: entries of order one.
All inputs are finite; a program needn't handle non-finite values.
Results may differ from a plain program's by a relative error of at most 0.012.
Values may be sent and summed in bfloat16 or wider, within the bound.
No kernel may reach another device: no remote copies, remote signals or barrier semaphores. Data moves between devices by JAX's collectives and lax.ppermute only.
A program may use at most 32 MiB of HBM per device.

v0:
```python
import math

import jax
import jax.numpy as jnp
from jax import lax
from jax.sharding import PartitionSpec as P

HEAD_DIM = 128
BAND = 256
SUMMARY = 128


LOW_SCORE = -1e30


def shifted(value, axis, steps):
    count = lax.axis_size(axis)
    leading, last = (max(0, -steps), min(count, count - steps))
    return lax.ppermute(value, axis, [(source, source + steps) for source in range(leading, last)])


def block_terms(query_rows, key_rows, value_rows, allowed):
    scale = 1.0 / math.sqrt(HEAD_DIM)
    head_count = query_rows.shape[1] // HEAD_DIM
    tops = []
    totals = []
    weighted = []
    for head_idx in range(head_count):
        low_col = head_idx * HEAD_DIM
        q_part = query_rows[:, low_col : low_col + HEAD_DIM]
        k_part = key_rows[:, low_col : low_col + HEAD_DIM]
        v_part = value_rows[:, low_col : low_col + HEAD_DIM]
        scores = (
            lax.dot_general(
                q_part, k_part, (((1,), (1,)), ((), ())), preferred_element_type=jnp.float32
            )
            * scale
        )
        scores = jnp.where(allowed, scores, LOW_SCORE)
        top_score = jnp.max(scores, axis=1)
        weights = jnp.where(allowed, jnp.exp(scores - top_score[:, None]), 0.0)
        tops.append(top_score)
        totals.append(jnp.sum(weights, axis=1))
        weighted.append(
            jnp.dot(weights.astype(jnp.bfloat16), v_part, preferred_element_type=jnp.float32)
        )
    return (jnp.stack(tops), jnp.stack(totals), jnp.stack(weighted))


def combine_terms(first, second):
    top_score = jnp.maximum(first[0], second[0])
    first_factor = jnp.exp(first[0] - top_score)
    second_factor = jnp.exp(second[0] - top_score)
    totals = first[1] * first_factor + second[1] * second_factor
    weighted = first[2] * first_factor[:, :, None] + second[2] * second_factor[:, :, None]
    return (top_score, totals, weighted)


def on_device(queries, keys, values, out_weight):
    tok_rows, width = queries.shape
    head_count = width // HEAD_DIM
    half_sum = SUMMARY // 2
    my_index = lax.axis_index("ctx")
    rim_keys, rim_values = shifted((keys[tok_rows - BAND :], values[tok_rows - BAND :]), "ctx", 1)
    band_keys = jnp.concatenate([rim_keys, keys], axis=0)
    band_values = jnp.concatenate([rim_values, values], axis=0)
    own_pos = my_index * tok_rows + jnp.arange(tok_rows, dtype=jnp.int32)
    band_pos = my_index * tok_rows - BAND + jnp.arange(tok_rows + BAND, dtype=jnp.int32)
    band_gap = own_pos[:, None] - band_pos[None, :]
    band_mask = (band_gap >= 0) & (band_gap < BAND) & (band_pos[None, :] >= 0)
    band_part = block_terms(queries, band_keys, band_values, band_mask)
    sum_start = jnp.where(my_index % 2 == 0, tok_rows - half_sum, 0).astype(jnp.int32)
    own_keys = lax.dynamic_slice_in_dim(keys, sum_start, half_sum, 0)
    own_values = lax.dynamic_slice_in_dim(values, sum_start, half_sum, 0)
    all_sum_keys, all_sum_values = (
        lax.all_gather(own_keys, "ctx", axis=0, tiled=True),
        lax.all_gather(own_values, "ctx", axis=0, tiled=True),
    )
    sum_rows = all_sum_keys.shape[0]
    step_rows = math.gcd(sum_rows, 512)
    step_count = sum_rows // step_rows
    row_count = queries.shape[0]
    newest = jnp.max(own_pos)
    initial = (
        jnp.full((head_count, row_count), LOW_SCORE, jnp.float32),
        jnp.zeros((head_count, row_count), jnp.float32),
        jnp.zeros((head_count, row_count, HEAD_DIM), jnp.float32),
    )

    def fold_block(block_idx, carry):
        start = (block_idx * step_rows).astype(jnp.int32)
        index = start + jnp.arange(step_rows, dtype=jnp.int32)
        owner = index // half_sum
        key_pos = (
            owner * tok_rows + jnp.where(owner % 2 == 0, tok_rows - half_sum, 0) + index % half_sum
        )

        def compute(carry_in):
            key_piece = lax.dynamic_slice_in_dim(all_sum_keys, start, step_rows, 0)
            value_piece = lax.dynamic_slice_in_dim(all_sum_values, start, step_rows, 0)
            gap = own_pos[:, None] - key_pos[None, :]
            return combine_terms(
                carry_in, block_terms(queries, key_piece, value_piece, gap >= BAND)
            )

        def keep_carry(carry_in):
            return carry_in

        return lax.cond(jnp.min(key_pos) + BAND <= newest, compute, keep_carry, carry)

    far_part = lax.fori_loop(0, step_count, fold_block, initial)
    merged = combine_terms(band_part, far_part)
    heads_out = merged[2] / merged[1][:, :, None]
    attn = jnp.transpose(heads_out, (1, 0, 2)).reshape(tok_rows, width).astype(jnp.bfloat16)
    mixed = lax.psum_scatter(
        jnp.dot(attn, out_weight, preferred_element_type=jnp.float32),
        "head",
        scatter_dimension=0,
        tiled=True,
    )
    return mixed.astype(jnp.bfloat16)


def solution(mesh):
    placed = (P("ctx", "head"), P("ctx", "head"), P("ctx", "head"), P("head", None))
    return jax.shard_map(
        on_device, mesh=mesh, in_specs=placed, out_specs=P(("ctx", "head"), None), check_vma=False
    )
```

profile of v0, /device:TPU:1, one launch (start us, length us, event | category | flops | bytes accessed | tf_op | source)
XLA Modules:
  0.0 357.0 jit_solution(793646058836477439)
XLA Ops:
  6.5 0.0 copy-start
  6.5 0.0 all-gather.3.cloned.1.call-start
  6.5 1.5 constant_dynamic-slice_fusion.1
  8.1 0.0 all-gather.3.cloned.1.call-update
  8.1 0.0 all-gather.5.cloned.1.call-start
  8.1 1.4 constant_dynamic-slice_fusion
  9.5 0.0 all-gather.5.cloned.1.call-update
  9.5 0.0 reduce-scatter.2.cloned.1.call-start
  9.6 0.9 slice.42
  10.5 4.6 %collective-permute-start = (bf16[256,256]{1,0:T(8,128)(2,1)S(1)}, bf16[256,256]{1,0:T(8,128)(2,1)S(1)}, u32[]{:S(2)}, u32[]{:S(2)}) collective-permute-start(bf16[256,256]{1,0:T(8,128)(2,1)S(1)} %slice.42), channel_id=1, source_target_pairs={{0,12},{12,24},{24,36},{36,48},{48,60},{60,72},{72,84},{84,96},{96... | collective-permute-start | bytes 393224 | tf_op jit(solution)/shard_map/ppermute | solution.py:19
  15.1 0.9 slice.45
  16.0 1.9 collective-permute-start.1
  18.0 0.7 fusion.71
  18.7 4.4 %collective-permute-done = bf16[256,256]{1,0:T(8,128)(2,1)S(1)} collective-permute-done((bf16[256,256]{1,0:T(8,128)(2,1)S(1)}, bf16[256,256]{1,0:T(8,128)(2,1)S(1)}, u32[]{:S(2)}, u32[]{:S(2)}) %collective-permute-start) | collective-permute-done | bytes 131104 | tf_op jit(solution)/shard_map/ppermute | solution.py:19
  23.1 0.9 constant_dynamic-update-slice_fusion
  24.1 1.4 fusion.81
  25.5 0.0 copy-done.2
  25.5 0.0 copy-start.1
  25.5 0.5 fusion.82
  26.0 0.6 fusion.49
  26.6 0.0 collective-permute-done.1
  26.6 0.0 copy-done.1
  26.7 0.6 convolution_bitcast_fusion.2
  27.3 1.3 convolution_bitcast_fusion.3
  28.6 78.9 %all-gather.3.cloned.1.call-done = bf16[4096,256]{1,0:T(8,128)(2,1)} async-done(((bf16[64,256]{1,0:T(8,128)(2,1)}), bf16[4096,256]{1,0:T(8,128)(2,1)}) %all-gather.3.cloned.1.call-update) | async-done | bytes 2097168 | tf_op jit(solution)/shard_map/all_gather | solution.py:76
  107.5 90.1 %all-gather.5.cloned.1.call-done = bf16[4096,256]{1,0:T(8,128)(2,1)} async-done(((bf16[64,256]{1,0:T(8,128)(2,1)}), bf16[4096,256]{1,0:T(8,128)(2,1)}) %all-gather.5.cloned.1.call-update) | async-done | bytes 2097168 | tf_op jit(solution)/shard_map/all_gather | solution.py:77
  197.6 22.2 %while.21 = (s32[]{:T(128)}, f32[2,384]{1,0:T(2,128)S(1)}, f32[2,384]{1,0:T(2,128)S(1)}, f32[2,384,128]{2,1,0:T(8,128)S(1)}, s32[]{:T(128)}, /*index=5*/bf16[409...) while((s32[]{:T(128)}, f32[2,384]{1,0:T(2,128)S(1)}, ...), condition=%wide.region_11.12_spmd.clone, body=%wide.region_3.11_spmd.clone.sunk | while | flops 207248768 | bytes 7092605 | solution.py:111
  197.6 0.7 fusion.87
  199.6 6.0 %conditional.3 = ((f32[2,384]{1,0:T(2,128)S(1)}, f32[2,384]{1,0:T(2,128)S(1)}, f32[2,384,128]{2,1,0:T(8,128)S(1)})) conditional(s32[]{:T(128)} %convert_element_type.52, (f32[2,384]{1,0:T(2,128)S(1)}, f32[2,384]{1,0:T(2,128)S(1)}, f32[2,384,128]{2,1,0:T(8,128)S(1)}) %tuple.67, (s32[]{:T(128)}, s32[512]{0:T(512)S(1)}, s32[]{:T(128)}, ...), branch_computations={%region_5.5_spmd, %region_6.10_spmd} | conditional | flops 207229824 | bytes 7088746 | solution.py:109
  199.6 1.3 fusion.79
  200.9 1.3 fusion.80
  202.2 0.3 fusion.7
  202.6 1.3 convolution_bitcast_fusion
  203.9 1.3 convolution_bitcast_fusion.1
  205.2 0.4 fusion.12
  205.6 0.7 fusion.87
  207.6 0.7 fusion.87
  209.7 0.7 fusion.87
  211.7 0.7 fusion.87
  213.7 0.7 fusion.87
  215.7 0.7 fusion.87
  217.8 0.7 fusion.87
  219.8 0.2 copy.5
  220.0 1.0 fusion.61
  221.0 3.7 %fusion.83 = f32[384,4096]{1,0:T(8,128)} fusion(bf16[384,256]{0,1:T(8,128)(2,1)S(1)} %bitcast.29, bf16[256,4096]{1,0:T(8,128)(2,1)S(1)} %copy-done), kind=kOutput, calls=%fused_computation.118 | convolution fusion | flops 805306368 | bytes 8585216 | tf_op jit(solution)/shard_map/dot_general | solution.py:116
  224.7 0.0 reduce-scatter.2.cloned.1.call-update
  224.7 123.9 %reduce-scatter.2.cloned.1.call-done = f32[32,4096]{1,0:T(8,128)} async-done(((f32[384,4096]{1,0:T(8,128)}), f32[32,4096]{1,0:T(8,128)}) %reduce-scatter.2.cloned.1.call-update) | async-done | bytes 524304 | tf_op jit(solution)/shard_map/reduce_scatter | solution.py:115
  348.7 1.8 convert_element_type.40
  (37 shorter events, 0.3 us)
Async XLA Ops:
  6.5 214.5 %copy-start = (bf16[256,4096]{1,0:T(8,128)(2,1)S(1)}, bf16[256,4096]{1,0:T(8,128)(2,1)}, u32[]{:S(2)}) copy-start(bf16[256,4096]{1,0:T(8,128)(2,1)} %param.11) | copy-start | bytes 6291460
  6.5 18.9 %copy-start.2 = (bf16[384,256]{1,0:T(8,128)(2,1)S(1)}, bf16[384,256]{1,0:T(8,128)(2,1)}, u32[]{:S(2)}) copy-start(bf16[384,256]{1,0:T(8,128)(2,1)} %param.8) | copy-start | bytes 589828
  6.5 100.9 %all-gather.3.cloned.1.call-start = ((), (), s32[]{:S(2)}) async-start(), calls=%async_computation.1 | async-start | bytes 2129920 | tf_op jit(solution)/shard_map/all_gather | solution.py:76
  8.1 189.5 %all-gather.5.cloned.1.call-start = ((), (), s32[]{:S(2)}) async-start(), calls=%async_computation.2 | async-start | bytes 2129920 | tf_op jit(solution)/shard_map/all_gather | solution.py:77
  9.5 339.1 %reduce-scatter.2.cloned.1.call-start = ((), (), s32[]{:S(2)}) async-start(), calls=%async_computation.3 | async-start | bytes 6815744 | tf_op jit(solution)/shard_map/reduce_scatter | solution.py:115
  10.5 12.6 %collective-permute-start = (bf16[256,256]{1,0:T(8,128)(2,1)S(1)}, bf16[256,256]{1,0:T(8,128)(2,1)S(1)}, u32[]{:S(2)}, u32[]{:S(2)}) collective-permute-start(bf16[256,256]{1,0:T(8,128)(2,1)S(1)} %slice.42), channel_id=1, source_target_pairs={{0,12},{12,24},{24,36},{36,48},{48,60},{60,72},{72,84},{84,96},{96... | collective-permute-start | bytes 393224 | tf_op jit(solution)/shard_map/ppermute | solution.py:19
  16.0 10.6 %collective-permute-start.1 = (bf16[256,256]{1,0:T(8,128)(2,1)S(1)}, bf16[256,256]{1,0:T(8,128)(2,1)S(1)}, u32[]{:S(2)}, u32[]{:S(2)}) collective-permute-start(bf16[256,256]{1,0:T(8,128)(2,1)S(1)} %slice.45), channel_id=1, source_target_pairs={{0,12},{12,24},{24,36},{36,48},{48,60},{60,72},{72,84},{84,96},{96... | collective-permute-start | bytes 393224 | tf_op jit(solution)/shard_map/ppermute | solution.py:19
  25.5 1.2 copy-start.1
Sparse Core Ops, SparseCore 0:
  11.3 96.1 all-gather.2
  111.4 86.0 all-gather.4
  224.8 123.7 reduce-scatter.1
where the time goes:
time: 358 us; the launch traced here: 357 us
  waiting for transfers between devices  297 us (83%)
  between operations  13.3 us (4%)
  matrix products  12.6 us (4%)
  loops' own time  10.8 us (3%)
  other arithmetic  10.3 us (3%)
  starting transfers between devices  6.59 us (2%)
  local copies, waits for them, and re-layouts  5.97 us (2%)
    reduce_scatter x1, waiting for transfers between devices, on_device(): lax.psum_scatter(jnp.dot(attn, out_weight, preferred_element_type=jnp.flo...  124 us
    all_gather x1, waiting for transfers between devices, on_device(): lax.all_gather(own_values, 'ctx', axis=0, tiled=True)  90.1 us
    all_gather x1, waiting for transfers between devices, on_device(): lax.all_gather(own_keys, 'ctx', axis=0, tiled=True)  78.9 us
    another operation x1, loops' own time, on_device(): far_part = lax.fori_loop(0, step_count, fold_block, initial)  10.6 us
  transfers between devices with their start and end apart: 5, of which 4 were waited for; matrix products, arithmetic and copies ran while one was open for 3% of the time, Pallas kernels for 0%

commit v1 on v0

--- a/solution.py
+++ b/solution.py
@@ -3,11 +3,14 @@
 import jax
 import jax.numpy as jnp
 from jax import lax
-from jax.sharding import PartitionSpec as P
+from jax.sharding import Mesh, PartitionSpec as P
 
 HEAD_DIM = 128
 BAND = 256
 SUMMARY = 128
+CTX = ("cx", "cy", "cc")
+CHIPS = ("cx", "cy")
+CORE = "cc"
 
 
 LOW_SCORE = -1e30
@@ -60,8 +63,8 @@
     tok_rows, width = queries.shape
     head_count = width // HEAD_DIM
     half_sum = SUMMARY // 2
-    my_index = lax.axis_index("ctx")
-    rim_keys, rim_values = shifted((keys[tok_rows - BAND :], values[tok_rows - BAND :]), "ctx", 1)
+    my_index = lax.axis_index(CTX)
+    rim_keys, rim_values = shifted((keys[tok_rows - BAND :], values[tok_rows - BAND :]), CTX, 1)
     band_keys = jnp.concatenate([rim_keys, keys], axis=0)
     band_values = jnp.concatenate([rim_values, values], axis=0)
     own_pos = my_index * tok_rows + jnp.arange(tok_rows, dtype=jnp.int32)
@@ -69,13 +72,17 @@
     band_gap = own_pos[:, None] - band_pos[None, :]
     band_mask = (band_gap >= 0) & (band_gap < BAND) & (band_pos[None, :] >= 0)
     band_part = block_terms(queries, band_keys, band_values, band_mask)
+    core = lax.axis_index(CORE)
     sum_start = jnp.where(my_index % 2 == 0, tok_rows - half_sum, 0).astype(jnp.int32)
     own_keys = lax.dynamic_slice_in_dim(keys, sum_start, half_sum, 0)
     own_values = lax.dynamic_slice_in_dim(values, sum_start, half_sum, 0)
-    all_sum_keys, all_sum_values = (
-        lax.all_gather(own_keys, "ctx", axis=0, tiled=True),
-        lax.all_gather(own_values, "ctx", axis=0, tiled=True),
+    chip_rows = lax.all_gather(
+        jnp.concatenate([own_keys, own_values], axis=1), CORE, axis=0, tiled=True
     )
+    my_half = lax.dynamic_slice_in_dim(chip_rows, core * width, width, 1)
+    gathered = lax.all_gather(my_half, CHIPS, axis=0, tiled=True)
+    both = lax.all_gather(gathered, CORE, axis=0, tiled=False)
+    all_sum_keys, all_sum_values = both[0], both[1]
     sum_rows = all_sum_keys.shape[0]
     step_rows = math.gcd(sum_rows, 512)
     step_count = sum_rows // step_rows
@@ -112,17 +119,17 @@
     merged = combine_terms(band_part, far_part)
     heads_out = merged[2] / merged[1][:, :, None]
     attn = jnp.transpose(heads_out, (1, 0, 2)).reshape(tok_rows, width).astype(jnp.bfloat16)
-    mixed = lax.psum_scatter(
-        jnp.dot(attn, out_weight, preferred_element_type=jnp.float32),
-        "head",
-        scatter_dimension=0,
-        tiled=True,
+    partial = jnp.dot(attn, out_weight, preferred_element_type=jnp.float32)
+    return lax.psum_scatter(
+        partial.astype(jnp.bfloat16), "head", scatter_dimension=0, tiled=True
     )
-    return mixed.astype(jnp.bfloat16)
 
 
 def solution(mesh):
-    placed = (P("ctx", "head"), P("ctx", "head"), P("ctx", "head"), P("head", None))
+    ctx_size, head_size = mesh.devices.shape
+    split = mesh.devices.reshape(ctx_size // 16, 8, 2, head_size)
+    fine = Mesh(split, ("cx", "cy", "cc", "head"))
+    placed = (P(CTX, "head"), P(CTX, "head"), P(CTX, "head"), P("head", None))
     return jax.shard_map(
-        on_device, mesh=mesh, in_specs=placed, out_specs=P(("ctx", "head"), None), check_vma=False
+        on_device, mesh=fine, in_specs=placed, out_specs=P(CTX + ("head",), None), check_vma=False
     )

time: 358 us -> 274 us (0.77)
  the two profiles are of different devices: /device:TPU:1 before, /device:TPU:14 now
where the time goes in v1:
time: 274 us
  waiting for transfers between devices  184 us (67%)
  matrix products  40.4 us (15%)
  between operations  13.3 us (5%)
  other arithmetic  11.6 us (4%)
  loops' own time  9.92 us (4%)
  local copies, waits for them, and re-layouts  7.2 us (3%)
  starting transfers between devices  4.8 us (2%)
    all_gather x1, waiting for transfers between devices, on_device(): gathered = lax.all_gather(my_half, CHIPS, axis=0, tiled=True)  93.7 us
    reduce_scatter x1, waiting for transfers between devices, on_device(): lax.psum_scatter(partial.astype(jnp.bfloat16), 'head', scatter_dimension=...  72.9 us
    dot_general x16, matrix products, block_terms(): jnp.dot(weights.astype(jnp.bfloat16), v_part, preferred_element_type=jnp....  19.7 us
    dot_general x16, matrix products, block_terms(): lax.dot_general(q_part, k_part, (((1,), (1,)), ((), ())), preferred_eleme...  18 us
    all_gather x1, waiting for transfers between devices, on_device(): both = lax.all_gather(gathered, CORE, axis=0, tiled=False)  14.9 us
    another operation x1, loops' own time, on_device(): far_part = lax.fori_loop(0, step_count, fold_block, initial)  9.35 us
  transfers between devices with their start and end apart: 5, of which 4 were waited for; matrix products, arithmetic and copies ran while one was open for 1% of the time, Pallas kernels for 0%

profile of v1, /device:TPU:14, one launch (start us, length us, event | category | flops | bytes accessed | tf_op | source)
XLA Modules:
  0.0 273.5 jit_solution(1177690275635424638)
XLA Ops:
  6.6 0.9 constant_dynamic-slice_fusion.2
  7.6 0.8 constant_dynamic-slice_fusion.1
  8.3 1.9 all_gather.12
  10.9 93.7 %all-gather.4.cloned.1.call-done = bf16[4096,256]{1,0:T(8,128)(2,1)} async-done(((bf16[128,256]{1,0:T(8,128)(2,1)}), bf16[4096,256]{1,0:T(8,128)(2,1)}) %all-gather.4.cloned.1.call-update) | async-done | bytes 2097168 | tf_op jit(solution)/shard_map/all_gather | solution.py:83
  104.7 1.9 collective-permute-start.1
  106.7 2.8 %collective-permute-start = (bf16[256,256]{1,0:T(8,128)(2,1)S(1)}, bf16[256,256]{1,0:T(8,128)(2,1)S(1)}, u32[]{:S(2)}, u32[]{:S(2)}) collective-permute-start(bf16[256,256]{1,0:T(8,128)(2,1)S(1)} %slice.48), channel_id=1, source_target_pairs={{0,12},{12,24},{24,36},{36,48},{48,60},{60,72},{72,84},{84,96},{96... | collective-permute-start | bytes 393224 | tf_op jit(solution)/shard_map/ppermute | solution.py:22
  110.1 2.9 %collective-permute-done = bf16[256,256]{1,0:T(8,128)(2,1)S(1)} collective-permute-done((bf16[256,256]{1,0:T(8,128)(2,1)S(1)}, bf16[256,256]{1,0:T(8,128)(2,1)S(1)}, u32[]{:S(2)}, u32[]{:S(2)}) %collective-permute-start) | collective-permute-done | bytes 131104 | tf_op jit(solution)/shard_map/ppermute | solution.py:22
  115.9 14.9 %all-gather.6.cloned.1.call-done = bf16[8192,256]{1,0:T(8,128)(2,1)} async-done(((bf16[4096,256]{1,0:T(8,128)(2,1)}), bf16[8192,256]{1,0:T(8,128)(2,1)}) %all-gather.6.cloned.1.call-update) | async-done | bytes 4194320 | tf_op jit(solution)/shard_map/all_gather | solution.py:84
  130.8 4.5 %fusion.81 = (bf16[4096,256]{1,0:T(8,128)(2,1)}, bf16[4096,256]{1,0:T(8,128)(2,1)}) fusion(bf16[8192,256]{1,0:T(8,128)(2,1)} %all-gather.6.cloned.1.call-done), kind=kLoop, calls=%fused_computation.119 | loop fusion | bytes 8388608 | tf_op jit(solution)/shard_map/slice | solution.py:85
  135.3 55.8 %while.21 = (s32[]{:T(128)}, f32[2,384]{1,0:T(2,128)S(1)}, f32[2,384]{1,0:T(2,128)S(1)}, f32[2,384,128]{2,1,0:T(8,128)S(1)}, s32[]{:T(128)}, /*index=5*/bf16[409...) while((s32[]{:T(128)}, f32[2,384]{1,0:T(2,128)S(1)}, ...), condition=%wide.region_11.12_spmd.clone, body=%wide.region_3.11_spmd.clone.sunk | while | flops 207248768 | bytes 7093621 | solution.py:118
  135.3 0.6 fusion.87
  137.1 5.9 %conditional.3 = ((f32[2,384]{1,0:T(2,128)S(1)}, f32[2,384]{1,0:T(2,128)S(1)}, f32[2,384,128]{2,1,0:T(8,128)S(1)})) conditional(s32[]{:T(128)} %convert_element_type.53, (f32[2,384]{1,0:T(2,128)S(1)}, f32[2,384]{1,0:T(2,128)S(1)}, f32[2,384,128]{2,1,0:T(8,128)S(1)}) %tuple.68, (s32[]{:T(128)}, s32[512]{0:T(512)S(1)}, s32[]{:T(128)}, ...), branch_computations={%region_5.5_spmd, %region_6.10_spmd} | conditional | flops 207229824 | bytes 7089770 | solution.py:116
  137.1 1.2 fusion.80
  138.3 1.2 fusion.79
  139.9 1.3 convolution_bitcast_fusion
  141.3 1.3 convolution_bitcast_fusion.1
  144.8 5.9 %conditional.3 = ((f32[2,384]{1,0:T(2,128)S(1)}, f32[2,384]{1,0:T(2,128)S(1)}, f32[2,384,128]{2,1,0:T(8,128)S(1)})) conditional(s32[]{:T(128)} %convert_element_type.53, (f32[2,384]{1,0:T(2,128)S(1)}, f32[2,384]{1,0:T(2,128)S(1)}, f32[2,384,128]{2,1,0:T(8,128)S(1)}) %tuple.68, (s32[]{:T(128)}, s32[512]{0:T(512)S(1)}, s32[]{:T(128)}, ...), branch_computations={%region_5.5_spmd, %region_6.10_spmd} | conditional | flops 207229824 | bytes 7089770 | solution.py:116
  144.8 1.2 fusion.80
  146.1 1.2 fusion.79
  147.6 1.3 convolution_bitcast_fusion
  149.0 1.3 convolution_bitcast_fusion.1
  152.5 5.9 %conditional.3 = ((f32[2,384]{1,0:T(2,128)S(1)}, f32[2,384]{1,0:T(2,128)S(1)}, f32[2,384,128]{2,1,0:T(8,128)S(1)})) conditional(s32[]{:T(128)} %convert_element_type.53, (f32[2,384]{1,0:T(2,128)S(1)}, f32[2,384]{1,0:T(2,128)S(1)}, f32[2,384,128]{2,1,0:T(8,128)S(1)}) %tuple.68, (s32[]{:T(128)}, s32[512]{0:T(512)S(1)}, s32[]{:T(128)}, ...), branch_computations={%region_5.5_spmd, %region_6.10_spmd} | conditional | flops 207229824 | bytes 7089770 | solution.py:116
  152.6 1.2 fusion.80
  153.8 1.2 fusion.79
  155.4 1.3 convolution_bitcast_fusion
  156.7 1.3 convolution_bitcast_fusion.1
  160.2 5.9 %conditional.3 = ((f32[2,384]{1,0:T(2,128)S(1)}, f32[2,384]{1,0:T(2,128)S(1)}, f32[2,384,128]{2,1,0:T(8,128)S(1)})) conditional(s32[]{:T(128)} %convert_element_type.53, (f32[2,384]{1,0:T(2,128)S(1)}, f32[2,384]{1,0:T(2,128)S(1)}, f32[2,384,128]{2,1,0:T(8,128)S(1)}) %tuple.68, (s32[]{:T(128)}, s32[512]{0:T(512)S(1)}, s32[]{:T(128)}, ...), branch_computations={%region_5.5_spmd, %region_6.10_spmd} | conditional | flops 207229824 | bytes 7089770 | solution.py:116
  160.3 1.2 fusion.80
  161.5 1.2 fusion.79
  163.1 1.3 convolution_bitcast_fusion
  164.4 1.3 convolution_bitcast_fusion.1
  167.9 5.9 %conditional.3 = ((f32[2,384]{1,0:T(2,128)S(1)}, f32[2,384]{1,0:T(2,128)S(1)}, f32[2,384,128]{2,1,0:T(8,128)S(1)})) conditional(s32[]{:T(128)} %convert_element_type.53, (f32[2,384]{1,0:T(2,128)S(1)}, f32[2,384]{1,0:T(2,128)S(1)}, f32[2,384,128]{2,1,0:T(8,128)S(1)}) %tuple.68, (s32[]{:T(128)}, s32[512]{0:T(512)S(1)}, s32[]{:T(128)}, ...), branch_computations={%region_5.5_spmd, %region_6.10_spmd} | conditional | flops 207229824 | bytes 7089770 | solution.py:116
  168.0 1.2 fusion.80
  169.2 1.2 fusion.79
  170.8 1.3 convolution_bitcast_fusion
  172.1 1.3 convolution_bitcast_fusion.1
  175.7 5.9 %conditional.3 = ((f32[2,384]{1,0:T(2,128)S(1)}, f32[2,384]{1,0:T(2,128)S(1)}, f32[2,384,128]{2,1,0:T(8,128)S(1)})) conditional(s32[]{:T(128)} %convert_element_type.53, (f32[2,384]{1,0:T(2,128)S(1)}, f32[2,384]{1,0:T(2,128)S(1)}, f32[2,384,128]{2,1,0:T(8,128)S(1)}) %tuple.68, (s32[]{:T(128)}, s32[512]{0:T(512)S(1)}, s32[]{:T(128)}, ...), branch_computations={%region_5.5_spmd, %region_6.10_spmd} | conditional | flops 207229824 | bytes 7089770 | solution.py:116
  175.7 1.2 fusion.80
  176.9 1.2 fusion.79
  178.5 1.3 convolution_bitcast_fusion
  179.8 1.3 convolution_bitcast_fusion.1
  183.4 5.9 %conditional.3 = ((f32[2,384]{1,0:T(2,128)S(1)}, f32[2,384]{1,0:T(2,128)S(1)}, f32[2,384,128]{2,1,0:T(8,128)S(1)})) conditional(s32[]{:T(128)} %convert_element_type.53, (f32[2,384]{1,0:T(2,128)S(1)}, f32[2,384]{1,0:T(2,128)S(1)}, f32[2,384,128]{2,1,0:T(8,128)S(1)}) %tuple.68, (s32[]{:T(128)}, s32[512]{0:T(512)S(1)}, s32[]{:T(128)}, ...), branch_computations={%region_5.5_spmd, %region_6.10_spmd} | conditional | flops 207229824 | bytes 7089770 | solution.py:116
  183.4 1.2 fusion.80
  184.6 1.2 fusion.79
  186.2 1.3 convolution_bitcast_fusion
  187.5 1.3 convolution_bitcast_fusion.1
  191.4 2.7 convolution_convert_fusion
  194.1 72.9 %reduce-scatter.2.cloned.1.call-done = bf16[32,4096]{1,0:T(8,128)(2,1)} async-done(((bf16[384,4096]{1,0:T(8,128)(2,1)}), bf16[32,4096]{1,0:T(8,128)(2,1)}) %reduce-scatter.2.cloned.1.call-update) | async-done | bytes 262160 | tf_op jit(solution)/shard_map/reduce_scatter | solution.py:123
  (114 shorter events, 14.3 us)
Async XLA Ops:
  6.5 184.9 %copy-start = (bf16[256,4096]{1,0:T(8,128)(2,1)S(1)}, bf16[256,4096]{1,0:T(8,128)(2,1)}, u32[]{:S(2)}) copy-start(bf16[256,4096]{1,0:T(8,128)(2,1)} %param.11) | copy-start | bytes 6291460
  6.5 100.1 %copy-start.1 = (bf16[384,256]{1,0:T(8,128)(2,1)S(1)}, bf16[384,256]{1,0:T(8,128)(2,1)}, u32[]{:S(2)}) copy-start(bf16[384,256]{1,0:T(8,128)(2,1)} %param.9) | copy-start | bytes 589828
  6.5 98.2 %copy-start.2 = (bf16[384,256]{1,0:T(8,128)(2,1)S(1)}, bf16[384,256]{1,0:T(8,128)(2,1)}, u32[]{:S(2)}) copy-start(bf16[384,256]{1,0:T(8,128)(2,1)} %param.10) | copy-start | bytes 589828
  6.5 106.5 %copy-start.3 = (bf16[384,256]{1,0:T(8,128)(2,1)S(1)}, bf16[384,256]{1,0:T(8,128)(2,1)}, u32[]{:S(2)}) copy-start(bf16[384,256]{1,0:T(8,128)(2,1)} %param.8) | copy-start | bytes 589828
  6.5 98.1 %all-gather.4.cloned.1.call-start = ((), (), s32[]{:S(2)}) async-start(), calls=%async_computation.1 | async-start | bytes 2162688 | tf_op jit(solution)/shard_map/all_gather | solution.py:83
  10.9 119.9 %all-gather.6.cloned.1.call-start = ((), (), s32[]{:S(2)}) async-start(), calls=%async_computation.3 | async-start | bytes 6291456 | tf_op jit(solution)/shard_map/all_gather | solution.py:84
  104.7 162.3 %reduce-scatter.2.cloned.1.call-start = ((), (), s32[]{:S(2)}) async-start(), calls=%async_computation.2 | async-start | bytes 3407872 | tf_op jit(solution)/shard_map/reduce_scatter | solution.py:123
  104.7 9.9 %collective-permute-start.1 = (bf16[256,256]{1,0:T(8,128)(2,1)S(1)}, bf16[256,256]{1,0:T(8,128)(2,1)S(1)}, u32[]{:S(2)}, u32[]{:S(2)}) collective-permute-start(bf16[256,256]{1,0:T(8,128)(2,1)S(1)} %slice.51), channel_id=1, source_target_pairs={{0,12},{12,24},{24,36},{36,48},{48,60},{60,72},{72,84},{84,96},{96... | collective-permute-start | bytes 393224 | tf_op jit(solution)/shard_map/ppermute | solution.py:22
  106.7 6.3 %collective-permute-start = (bf16[256,256]{1,0:T(8,128)(2,1)S(1)}, bf16[256,256]{1,0:T(8,128)(2,1)S(1)}, u32[]{:S(2)}, u32[]{:S(2)}) collective-permute-start(bf16[256,256]{1,0:T(8,128)(2,1)S(1)} %slice.48), channel_id=1, source_target_pairs={{0,12},{12,24},{24,36},{36,48},{48,60},{60,72},{72,84},{84,96},{96... | collective-permute-start | bytes 393224 | tf_op jit(solution)/shard_map/ppermute | solution.py:22
Sparse Core Ops, SparseCore 0:
  11.1 93.4 all-gather.3
  107.0 23.7 all-gather.5
  194.2 72.7 reduce-scatter.1

commit v2 on v1

--- a/solution.py
+++ b/solution.py
@@ -59,6 +59,30 @@
     return (top_score, totals, weighted)
 
 
+def ring_reduce_scatter(partial, axis):
+    count = lax.axis_size(axis)
+    me = lax.axis_index(axis)
+    rows = partial.shape[0] // count
+    half = partial.shape[1] // 2
+    ahead = [(source, (source + 1) % count) for source in range(count)]
+    behind = [(source, (source - 1) % count) for source in range(count)]
+
+    def piece(block, low):
+        start = (block % count) * rows
+        return lax.dynamic_slice(partial, (start, low), (rows, half))
+
+    up = piece(me - 1, 0).astype(jnp.bfloat16)
+    down = piece(me + 1, half).astype(jnp.bfloat16)
+    for step in range(count - 1):
+        up_sum = lax.ppermute(up, axis, ahead).astype(jnp.float32) + piece(me - 2 - step, 0)
+        down_sum = lax.ppermute(down, axis, behind).astype(jnp.float32) + piece(
+            me + 2 + step, half
+        )
+        up = up_sum.astype(jnp.bfloat16)
+        down = down_sum.astype(jnp.bfloat16)
+    return jnp.concatenate([up, down], axis=1)
+
+
 def on_device(queries, keys, values, out_weight):
     tok_rows, width = queries.shape
     head_count = width // HEAD_DIM
@@ -80,9 +104,12 @@
         jnp.concatenate([own_keys, own_values], axis=1), CORE, axis=0, tiled=True
     )
     my_half = lax.dynamic_slice_in_dim(chip_rows, core * width, width, 1)
-    gathered = lax.all_gather(my_half, CHIPS, axis=0, tiled=True)
-    both = lax.all_gather(gathered, CORE, axis=0, tiled=False)
-    all_sum_keys, all_sum_values = both[0], both[1]
+    gathered = lax.all_gather(my_half, "cy", axis=0, tiled=True)
+    gathered = lax.all_gather(gathered, "cx", axis=0, tiled=True)
+    other = lax.ppermute(gathered, CORE, [(0, 1), (1, 0)])
+    both = jnp.stack([gathered, other])
+    all_sum_keys = both[core]
+    all_sum_values = both[1 - core]
     sum_rows = all_sum_keys.shape[0]
     step_rows = math.gcd(sum_rows, 512)
     step_count = sum_rows // step_rows
@@ -120,9 +147,7 @@
     heads_out = merged[2] / merged[1][:, :, None]
     attn = jnp.transpose(heads_out, (1, 0, 2)).reshape(tok_rows, width).astype(jnp.bfloat16)
     partial = jnp.dot(attn, out_weight, preferred_element_type=jnp.float32)
-    return lax.psum_scatter(
-        partial.astype(jnp.bfloat16), "head", scatter_dimension=0, tiled=True
-    )
+    return ring_reduce_scatter(partial, "head")
 
 
 def solution(mesh):

time: 274 us -> 305 us (1.11)
  the two profiles are of different devices: /device:TPU:14 before, /device:TPU:62 now
where the time goes in v2:
time: 305 us; the launch traced here: 303 us
  waiting for transfers between devices  90.9 us (30%)
  starting transfers between devices  79.3 us (26%)
  matrix products  43.8 us (14%)
  blocking collectives  29.3 us (10%)
  other arithmetic  28.9 us (9%)
  between operations  14.4 us (5%)
  loops' own time  10.8 us (4%)
  local copies, waits for them, and re-layouts  6.02 us (2%)
    all_gather x1, waiting for transfers between devices, on_device(): gathered = lax.all_gather(gathered, 'cx', axis=0, tiled=True)  43.2 us
    ppermute x11, starting transfers between devices, ring_reduce_scatter(): lax.ppermute(down, axis, behind).astype(jnp.float32)  38.4 us
    ppermute x11, starting transfers between devices, ring_reduce_scatter(): lax.ppermute(up, axis, ahead).astype(jnp.float32) + piece(me - 2 - step, 0)  34.7 us
    ppermute x11, waiting for transfers between devices, ring_reduce_scatter(): lax.ppermute(up, axis, ahead).astype(jnp.float32) + piece(me - 2 - step, 0)  30.6 us
    all_gather x1, blocking collectives, on_device(): gathered = lax.all_gather(my_half, 'cy', axis=0, tiled=True)  27.4 us
    dot_general x18, matrix products, block_terms(): jnp.dot(weights.astype(jnp.bfloat16), v_part, preferred_element_type=jnp....  22.3 us
    dot_general x18, matrix products, block_terms(): lax.dot_general(q_part, k_part, (((1,), (1,)), ((), ())), preferred_eleme...  20.4 us
    ppermute x11, waiting for transfers between devices, ring_reduce_scatter(): lax.ppermute(down, axis, behind).astype(jnp.float32)  15.1 us
  transfers between devices with their start and end apart: 26, of which 25 were waited for; matrix products, arithmetic and copies ran while one was open for 1% of the time, Pallas kernels for 0%

profile of v2, /device:TPU:62, one launch (start us, length us, event | category | flops | bytes accessed | tf_op | source)
XLA Modules:
  0.0 303.3 jit_solution(7515110416415885046)
XLA Ops:
  8.3 1.9 all_gather.9
  10.2 27.4 %all_gather.10 = bf16[1024,256]{1,0:T(8,128)(2,1)} all-gather(bf16[128,256]{1,0:T(8,128)(2,1)S(1)} %constant_dynamic-slice_fusion), channel_id=1, replica_groups=mesh['cx'=4,'cy'=8,'cc'=2,'head'=12] {'cy'}, dimensions={0}, use_global_device_ids=true | all-gather | bytes 589824 | tf_op jit(solution)/shard_map/all_gather | solution.py:107
  37.7 43.2 %all-gather.2.cloned.1.call-done = bf16[4096,256]{1,0:T(8,128)(2,1)} async-done(((bf16[1024,256]{1,0:T(8,128)(2,1)}), bf16[4096,256]{1,0:T(8,128)(2,1)}) %all-gather.2.cloned.1.call-update) | async-done | bytes 2097168 | tf_op jit(solution)/shard_map/all_gather | solution.py:108
  80.9 1.9 collective-permute-start.2
  83.7 2.4 collective-permute-start
  86.2 1.9 collective-permute-start.1
  94.1 4.1 %fusion.44 = (bf16[4096,256]{1,0:T(8,128)(2,1)}, bf16[4096,256]{1,0:T(8,128)(2,1)}) fusion(s32[]{:T(128)S(6)} %select_n.291, bf16[1,4096,256]{2,1,0:T(8,128)(2,1)S(1)} %bitcast.35, bf16[1,4096,256]{2,1,0:T(8,128)(2,1)} %bitcast.9, s32[]{:T(128)S(6)} %select_n.290), kind=kLoop, calls=%fused_computation.68 | loop fusion | flops 2097152 | bytes 8388616 | tf_op jit(solution)/shard_map/squeeze | solution.py:112
  98.2 62.3 %while.21 = (s32[]{:T(128)}, f32[2,384]{1,0:T(2,128)S(1)}, f32[2,384]{1,0:T(2,128)S(1)}, f32[2,384,128]{2,1,0:T(8,128)S(1)}, s32[]{:T(128)}, /*index=5*/bf16[409...) while((s32[]{:T(128)}, f32[2,384]{1,0:T(2,128)S(1)}, ...), condition=%wide.region_11.12_spmd.clone, body=%wide.region_3.11_spmd.clone.sunk | while | flops 207248768 | bytes 7093621 | solution.py:145
  100.1 5.9 %conditional.3 = ((f32[2,384]{1,0:T(2,128)S(1)}, f32[2,384]{1,0:T(2,128)S(1)}, f32[2,384,128]{2,1,0:T(8,128)S(1)})) conditional(s32[]{:T(128)} %convert_element_type.278, (f32[2,384]{1,0:T(2,128)S(1)}, f32[2,384]{1,0:T(2,128)S(1)}, f32[2,384,128]{2,1,0:T(8,128)S(1)}) %tuple.80, (s32[]{:T(128)}, s32[512]{0:T(512)S(1)}, s32[]{:T(128)}, ...), branch_computations={%region_5.5_spmd, %region_6.10_spmd} | conditional | flops 207229824 | bytes 7089770 | solution.py:143
  107.9 5.9 %conditional.3 = ((f32[2,384]{1,0:T(2,128)S(1)}, f32[2,384]{1,0:T(2,128)S(1)}, f32[2,384,128]{2,1,0:T(8,128)S(1)})) conditional(s32[]{:T(128)} %convert_element_type.278, (f32[2,384]{1,0:T(2,128)S(1)}, f32[2,384]{1,0:T(2,128)S(1)}, f32[2,384,128]{2,1,0:T(8,128)S(1)}) %tuple.80, (s32[]{:T(128)}, s32[512]{0:T(512)S(1)}, s32[]{:T(128)}, ...), branch_computations={%region_5.5_spmd, %region_6.10_spmd} | conditional | flops 207229824 | bytes 7089770 | solution.py:143
  115.7 5.9 %conditional.3 = ((f32[2,384]{1,0:T(2,128)S(1)}, f32[2,384]{1,0:T(2,128)S(1)}, f32[2,384,128]{2,1,0:T(8,128)S(1)})) conditional(s32[]{:T(128)} %convert_element_type.278, (f32[2,384]{1,0:T(2,128)S(1)}, f32[2,384]{1,0:T(2,128)S(1)}, f32[2,384,128]{2,1,0:T(8,128)S(1)}) %tuple.80, (s32[]{:T(128)}, s32[512]{0:T(512)S(1)}, s32[]{:T(128)}, ...), branch_computations={%region_5.5_spmd, %region_6.10_spmd} | conditional | flops 207229824 | bytes 7089770 | solution.py:143
  123.5 5.9 %conditional.3 = ((f32[2,384]{1,0:T(2,128)S(1)}, f32[2,384]{1,0:T(2,128)S(1)}, f32[2,384,128]{2,1,0:T(8,128)S(1)})) conditional(s32[]{:T(128)} %convert_element_type.278, (f32[2,384]{1,0:T(2,128)S(1)}, f32[2,384]{1,0:T(2,128)S(1)}, f32[2,384,128]{2,1,0:T(8,128)S(1)}) %tuple.80, (s32[]{:T(128)}, s32[512]{0:T(512)S(1)}, s32[]{:T(128)}, ...), branch_computations={%region_5.5_spmd, %region_6.10_spmd} | conditional | flops 207229824 | bytes 7089770 | solution.py:143
  131.3 5.9 %conditional.3 = ((f32[2,384]{1,0:T(2,128)S(1)}, f32[2,384]{1,0:T(2,128)S(1)}, f32[2,384,128]{2,1,0:T(8,128)S(1)})) conditional(s32[]{:T(128)} %convert_element_type.278, (f32[2,384]{1,0:T(2,128)S(1)}, f32[2,384]{1,0:T(2,128)S(1)}, f32[2,384,128]{2,1,0:T(8,128)S(1)}) %tuple.80, (s32[]{:T(128)}, s32[512]{0:T(512)S(1)}, s32[]{:T(128)}, ...), branch_computations={%region_5.5_spmd, %region_6.10_spmd} | conditional | flops 207229824 | bytes 7089770 | solution.py:143
  139.0 5.9 %conditional.3 = ((f32[2,384]{1,0:T(2,128)S(1)}, f32[2,384]{1,0:T(2,128)S(1)}, f32[2,384,128]{2,1,0:T(8,128)S(1)})) conditional(s32[]{:T(128)} %convert_element_type.278, (f32[2,384]{1,0:T(2,128)S(1)}, f32[2,384]{1,0:T(2,128)S(1)}, f32[2,384,128]{2,1,0:T(8,128)S(1)}) %tuple.80, (s32[]{:T(128)}, s32[512]{0:T(512)S(1)}, s32[]{:T(128)}, ...), branch_computations={%region_5.5_spmd, %region_6.10_spmd} | conditional | flops 207229824 | bytes 7089770 | solution.py:143
  146.8 5.9 %conditional.3 = ((f32[2,384]{1,0:T(2,128)S(1)}, f32[2,384]{1,0:T(2,128)S(1)}, f32[2,384,128]{2,1,0:T(8,128)S(1)})) conditional(s32[]{:T(128)} %convert_element_type.278, (f32[2,384]{1,0:T(2,128)S(1)}, f32[2,384]{1,0:T(2,128)S(1)}, f32[2,384,128]{2,1,0:T(8,128)S(1)}) %tuple.80, (s32[]{:T(128)}, s32[512]{0:T(512)S(1)}, s32[]{:T(128)}, ...), branch_computations={%region_5.5_spmd, %region_6.10_spmd} | conditional | flops 207229824 | bytes 7089770 | solution.py:143
  154.6 5.9 %conditional.3 = ((f32[2,384]{1,0:T(2,128)S(1)}, f32[2,384]{1,0:T(2,128)S(1)}, f32[2,384,128]{2,1,0:T(8,128)S(1)})) conditional(s32[]{:T(128)} %convert_element_type.278, (f32[2,384]{1,0:T(2,128)S(1)}, f32[2,384]{1,0:T(2,128)S(1)}, f32[2,384,128]{2,1,0:T(8,128)S(1)}) %tuple.80, (s32[]{:T(128)}, s32[512]{0:T(512)S(1)}, s32[]{:T(128)}, ...), branch_computations={%region_5.5_spmd, %region_6.10_spmd} | conditional | flops 207229824 | bytes 7089770 | solution.py:143
  161.8 2.6 copy-done.1
  164.5 6.6 %collective-permute-start.14 = (bf16[32,2048]{1,0:T(8,128)(2,1)S(1)}, bf16[32,2048]{1,0:T(8,128)(2,1)S(1)}, u32[]{:S(2)}, u32[]{:S(2)}) collective-permute-start(bf16[32,2048]{1,0:T(8,128)(2,1)S(1)} %get-tuple-element.405), channel_id=1, source_target_pairs={{0,11},{1,0},{2,1},{3,2},{4,3},{5,4},{6,5},{7,6},{8,7},{9,8},{10,9... | collective-permute-start | bytes 393224 | tf_op jit(solution)/shard_map/ppermute | solution.py:78
  171.1 1.9 collective-permute-start.3
  173.6 5.6 %collective-permute-done.3 = bf16[32,2048]{1,0:T(8,128)(2,1)S(1)} collective-permute-done((bf16[32,2048]{1,0:T(8,128)(2,1)S(1)}, bf16[32,2048]{1,0:T(8,128)(2,1)S(1)}, u32[]{:S(2)}, u32[]{:S(2)}) %collective-permute-start.3) | collective-permute-done | bytes 131104 | tf_op jit(solution)/shard_map/ppermute | solution.py:77
  180.3 2.0 collective-permute-start.15
  182.2 3.9 %collective-permute-start.4 = (bf16[32,2048]{1,0:T(8,128)(2,1)S(1)}, bf16[32,2048]{1,0:T(8,128)(2,1)S(1)}, u32[]{:S(2)}, u32[]{:S(2)}) collective-permute-start(bf16[32,2048]{1,0:T(8,128)(2,1)S(1)} %get-tuple-element.402), channel_id=1, source_target_pairs={{0,1},{1,2},{2,3},{3,4},{4,5},{5,6},{6,7},{7,8},{8,9},{9,10},{10,1... | collective-permute-start | bytes 393224 | tf_op jit(solution)/shard_map/ppermute | solution.py:77
  187.1 3.2 %collective-permute-done.4 = bf16[32,2048]{1,0:T(8,128)(2,1)S(1)} collective-permute-done((bf16[32,2048]{1,0:T(8,128)(2,1)S(1)}, bf16[32,2048]{1,0:T(8,128)(2,1)S(1)}, u32[]{:S(2)}, u32[]{:S(2)}) %collective-permute-start.4) | collective-permute-done | bytes 131104 | tf_op jit(solution)/shard_map/ppermute | solution.py:77
  191.4 2.0 collective-permute-start.16
  193.4 3.9 %collective-permute-start.5 = (bf16[32,2048]{1,0:T(8,128)(2,1)S(1)}, bf16[32,2048]{1,0:T(8,128)(2,1)S(1)}, u32[]{:S(2)}, u32[]{:S(2)}) collective-permute-start(bf16[32,2048]{1,0:T(8,128)(2,1)S(1)} %get-tuple-element.400), channel_id=1, source_target_pairs={{0,1},{1,2},{2,3},{3,4},{4,5},{5,6},{6,7},{7,8},{8,9},{9,10},{10,1... | collective-permute-start | bytes 393224 | tf_op jit(solution)/shard_map/ppermute | solution.py:77
  198.3 3.2 %collective-permute-done.5 = bf16[32,2048]{1,0:T(8,128)(2,1)S(1)} collective-permute-done((bf16[32,2048]{1,0:T(8,128)(2,1)S(1)}, bf16[32,2048]{1,0:T(8,128)(2,1)S(1)}, u32[]{:S(2)}, u32[]{:S(2)}) %collective-permute-start.5) | collective-permute-done | bytes 131104 | tf_op jit(solution)/shard_map/ppermute | solution.py:77
  202.5 3.7 %collective-permute-start.17 = (bf16[32,2048]{1,0:T(8,128)(2,1)S(1)}, bf16[32,2048]{1,0:T(8,128)(2,1)S(1)}, u32[]{:S(2)}, u32[]{:S(2)}) collective-permute-start(bf16[32,2048]{1,0:T(8,128)(2,1)S(1)} %get-tuple-element.399), channel_id=1, source_target_pairs={{0,11},{1,0},{2,1},{3,2},{4,3},{5,4},{6,5},{7,6},{8,7},{9,8},{10,9... | collective-permute-start | bytes 393224 | tf_op jit(solution)/shard_map/ppermute | solution.py:78
  206.2 2.2 collective-permute-start.6
  209.4 4.9 %collective-permute-done.6 = bf16[32,2048]{1,0:T(8,128)(2,1)S(1)} collective-permute-done((bf16[32,2048]{1,0:T(8,128)(2,1)S(1)}, bf16[32,2048]{1,0:T(8,128)(2,1)S(1)}, u32[]{:S(2)}, u32[]{:S(2)}) %collective-permute-start.6) | collective-permute-done | bytes 131104 | tf_op jit(solution)/shard_map/ppermute | solution.py:77
  215.4 2.8 collective-permute-start.18
  218.1 3.1 %collective-permute-start.7 = (bf16[32,2048]{1,0:T(8,128)(2,1)S(1)}, bf16[32,2048]{1,0:T(8,128)(2,1)S(1)}, u32[]{:S(2)}, u32[]{:S(2)}) collective-permute-start(bf16[32,2048]{1,0:T(8,128)(2,1)S(1)} %get-tuple-element.396), channel_id=1, source_target_pairs={{0,1},{1,2},{2,3},{3,4},{4,5},{5,6},{6,7},{7,8},{8,9},{9,10},{10,1... | collective-permute-start | bytes 393224 | tf_op jit(solution)/shard_map/ppermute | solution.py:77
  222.6 4.8 %collective-permute-done.7 = bf16[32,2048]{1,0:T(8,128)(2,1)S(1)} collective-permute-done((bf16[32,2048]{1,0:T(8,128)(2,1)S(1)}, bf16[32,2048]{1,0:T(8,128)(2,1)S(1)}, u32[]{:S(2)}, u32[]{:S(2)}) %collective-permute-start.7) | collective-permute-done | bytes 131104 | tf_op jit(solution)/shard_map/ppermute | solution.py:77
  228.5 1.9 collective-permute-start.19
  230.4 3.9 %collective-permute-start.8 = (bf16[32,2048]{1,0:T(8,128)(2,1)S(1)}, bf16[32,2048]{1,0:T(8,128)(2,1)S(1)}, u32[]{:S(2)}, u32[]{:S(2)}) collective-permute-start(bf16[32,2048]{1,0:T(8,128)(2,1)S(1)} %get-tuple-element.394), channel_id=1, source_target_pairs={{0,1},{1,2},{2,3},{3,4},{4,5},{5,6},{6,7},{7,8},{8,9},{9,10},{10,1... | collective-permute-start | bytes 393224 | tf_op jit(solution)/shard_map/ppermute | solution.py:77
  235.9 3.1 %collective-permute-done.8 = bf16[32,2048]{1,0:T(8,128)(2,1)S(1)} collective-permute-done((bf16[32,2048]{1,0:T(8,128)(2,1)S(1)}, bf16[32,2048]{1,0:T(8,128)(2,1)S(1)}, u32[]{:S(2)}, u32[]{:S(2)}) %collective-permute-start.8) | collective-permute-done | bytes 131104 | tf_op jit(solution)/shard_map/ppermute | solution.py:77
  240.1 1.9 collective-permute-start.20
  242.1 3.9 %collective-permute-start.9 = (bf16[32,2048]{1,0:T(8,128)(2,1)S(1)}, bf16[32,2048]{1,0:T(8,128)(2,1)S(1)}, u32[]{:S(2)}, u32[]{:S(2)}) collective-permute-start(bf16[32,2048]{1,0:T(8,128)(2,1)S(1)} %get-tuple-element.392), channel_id=1, source_target_pairs={{0,1},{1,2},{2,3},{3,4},{4,5},{5,6},{6,7},{7,8},{8,9},{9,10},{10,1... | collective-permute-start | bytes 393224 | tf_op jit(solution)/shard_map/ppermute | solution.py:77
  246.0 2.1 collective-permute-done.20
  248.2 2.0 collective-permute-done.9
  251.2 2.7 collective-permute-start.10
  253.9 4.3 %collective-permute-start.21 = (bf16[32,2048]{1,0:T(8,128)(2,1)S(1)}, bf16[32,2048]{1,0:T(8,128)(2,1)S(1)}, u32[]{:S(2)}, u32[]{:S(2)}) collective-permute-start(bf16[32,2048]{1,0:T(8,128)(2,1)S(1)} %get-tuple-element.391), channel_id=1, source_target_pairs={{0,11},{1,0},{2,1},{3,2},{4,3},{5,4},{6,5},{7,6},{8,7},{9,8},{10,9... | collective-permute-start | bytes 393224 | tf_op jit(solution)/shard_map/ppermute | solution.py:78
  261.9 2.4 collective-permute-start.11
  264.3 5.0 %collective-permute-start.22 = (bf16[32,2048]{1,0:T(8,128)(2,1)S(1)}, bf16[32,2048]{1,0:T(8,128)(2,1)S(1)}, u32[]{:S(2)}, u32[]{:S(2)}) collective-permute-start(bf16[32,2048]{1,0:T(8,128)(2,1)S(1)} %get-tuple-element.389), channel_id=1, source_target_pairs={{0,11},{1,0},{2,1},{3,2},{4,3},{5,4},{6,5},{7,6},{8,7},{9,8},{10,9... | collective-permute-start | bytes 393224 | tf_op jit(solution)/shard_map/ppermute | solution.py:78
  272.9 3.0 collective-permute-start.12
  275.9 4.5 %collective-permute-start.23 = (bf16[32,2048]{1,0:T(8,128)(2,1)S(1)}, bf16[32,2048]{1,0:T(8,128)(2,1)S(1)}, u32[]{:S(2)}, u32[]{:S(2)}) collective-permute-start(bf16[32,2048]{1,0:T(8,128)(2,1)S(1)} %get-tuple-element.387), channel_id=1, source_target_pairs={{0,11},{1,0},{2,1},{3,2},{4,3},{5,4},{6,5},{7,6},{8,7},{9,8},{10,9... | collective-permute-start | bytes 393224 | tf_op jit(solution)/shard_map/ppermute | solution.py:78
  284.0 3.8 %collective-permute-start.13 = (bf16[32,2048]{1,0:T(8,128)(2,1)S(1)}, bf16[32,2048]{1,0:T(8,128)(2,1)S(1)}, u32[]{:S(2)}, u32[]{:S(2)}) collective-permute-start(bf16[32,2048]{1,0:T(8,128)(2,1)S(1)} %get-tuple-element.384), channel_id=1, source_target_pairs={{0,1},{1,2},{2,3},{3,4},{4,5},{5,6},{6,7},{7,8},{8,9},{9,10},{10,1... | collective-permute-start | bytes 393224 | tf_op jit(solution)/shard_map/ppermute | solution.py:77
  287.8 3.7 %collective-permute-start.24 = (bf16[32,2048]{1,0:T(8,128)(2,1)S(1)}, bf16[32,2048]{1,0:T(8,128)(2,1)S(1)}, u32[]{:S(2)}, u32[]{:S(2)}) collective-permute-start(bf16[32,2048]{1,0:T(8,128)(2,1)S(1)} %get-tuple-element.385), channel_id=1, source_target_pairs={{0,11},{1,0},{2,1},{3,2},{4,3},{5,4},{6,5},{7,6},{8,7},{9,8},{10,9... | collective-permute-start | bytes 393224 | tf_op jit(solution)/shard_map/ppermute | solution.py:78
  292.5 2.1 collective-permute-done.24
  (184 shorter events, 88.6 us)
Async XLA Ops:
  6.5 154.3 %copy-start = (bf16[256,4096]{1,0:T(8,128)(2,1)S(1)}, bf16[256,4096]{1,0:T(8,128)(2,1)}, u32[]{:S(2)}) copy-start(bf16[256,4096]{1,0:T(8,128)(2,1)} %param.11) | copy-start | bytes 6291460
  6.5 79.6 %copy-start.4 = (bf16[384,256]{1,0:T(8,128)(2,1)S(1)}, bf16[384,256]{1,0:T(8,128)(2,1)}, u32[]{:S(2)}) copy-start(bf16[384,256]{1,0:T(8,128)(2,1)} %param.10) | copy-start | bytes 589828
  6.5 83.5 %copy-start.3 = (bf16[384,256]{1,0:T(8,128)(2,1)S(1)}, bf16[384,256]{1,0:T(8,128)(2,1)}, u32[]{:S(2)}) copy-start(bf16[384,256]{1,0:T(8,128)(2,1)} %param.9) | copy-start | bytes 589828
  6.5 83.5 %copy-start.5 = (bf16[384,256]{1,0:T(8,128)(2,1)S(1)}, bf16[384,256]{1,0:T(8,128)(2,1)}, u32[]{:S(2)}) copy-start(bf16[384,256]{1,0:T(8,128)(2,1)} %param.8) | copy-start | bytes 589828
  6.5 74.4 %all-gather.2.cloned.1.call-start = ((), (), s32[]{:S(2)}) async-start(), calls=%async_computation | async-start | bytes 2621440 | tf_op jit(solution)/shard_map/all_gather | solution.py:108
  80.9 12.8 %collective-permute-start.2 = (bf16[4096,256]{1,0:T(8,128)(2,1)}, bf16[4096,256]{1,0:T(8,128)(2,1)}, u32[]{:S(2)}, u32[]{:S(2)}) collective-permute-start(bf16[4096,256]{1,0:T(8,128)(2,1)} %all-gather.2.cloned.1.call-done), channel_id=1, source_target_pairs={{0,12},{12,0},{1,13},{13,1},{2,14},{14,2},{3,15},{15,3},{4,16},{16... | collective-permute-start | bytes 6291464 | tf_op jit(solution)/shard_map/ppermute | solution.py:109
  83.7 6.3 %collective-permute-start = (bf16[256,256]{1,0:T(8,128)(2,1)S(1)}, bf16[256,256]{1,0:T(8,128)(2,1)S(1)}, u32[]{:S(2)}, u32[]{:S(2)}) collective-permute-start(bf16[256,256]{1,0:T(8,128)(2,1)S(1)} %slice.42), channel_id=1, source_target_pairs={{0,12},{12,24},{24,36},{36,48},{48,60},{60,72},{72,84},{84,96},{96... | collective-permute-start | bytes 393224 | tf_op jit(solution)/shard_map/ppermute | solution.py:22
  86.2 6.3 %collective-permute-start.1 = (bf16[256,256]{1,0:T(8,128)(2,1)S(1)}, bf16[256,256]{1,0:T(8,128)(2,1)S(1)}, u32[]{:S(2)}, u32[]{:S(2)}) collective-permute-start(bf16[256,256]{1,0:T(8,128)(2,1)S(1)} %slice.45), channel_id=1, source_target_pairs={{0,12},{12,24},{24,36},{36,48},{48,60},{60,72},{72,84},{84,96},{96... | collective-permute-start | bytes 393224 | tf_op jit(solution)/shard_map/ppermute | solution.py:22
  92.5 1.6 copy-start.2
  161.8 2.6 copy-start.1
  164.5 9.1 %collective-permute-start.14 = (bf16[32,2048]{1,0:T(8,128)(2,1)S(1)}, bf16[32,2048]{1,0:T(8,128)(2,1)S(1)}, u32[]{:S(2)}, u32[]{:S(2)}) collective-permute-start(bf16[32,2048]{1,0:T(8,128)(2,1)S(1)} %get-tuple-element.405), channel_id=1, source_target_pairs={{0,11},{1,0},{2,1},{3,2},{4,3},{5,4},{6,5},{7,6},{8,7},{9,8},{10,9... | collective-permute-start | bytes 393224 | tf_op jit(solution)/shard_map/ppermute | solution.py:78
  171.1 8.1 %collective-permute-start.3 = (bf16[32,2048]{1,0:T(8,128)(2,1)S(1)}, bf16[32,2048]{1,0:T(8,128)(2,1)S(1)}, u32[]{:S(2)}, u32[]{:S(2)}) collective-permute-start(bf16[32,2048]{1,0:T(8,128)(2,1)S(1)} %get-tuple-element.404), channel_id=1, source_target_pairs={{0,1},{1,2},{2,3},{3,4},{4,5},{5,6},{6,7},{7,8},{8,9},{9,10},{10,1... | collective-permute-start | bytes 393224 | tf_op jit(solution)/shard_map/ppermute | solution.py:77
  180.3 6.9 %collective-permute-start.15 = (bf16[32,2048]{1,0:T(8,128)(2,1)S(1)}, bf16[32,2048]{1,0:T(8,128)(2,1)S(1)}, u32[]{:S(2)}, u32[]{:S(2)}) collective-permute-start(bf16[32,2048]{1,0:T(8,128)(2,1)S(1)} %get-tuple-element.403), channel_id=1, source_target_pairs={{0,11},{1,0},{2,1},{3,2},{4,3},{5,4},{6,5},{7,6},{8,7},{9,8},{10,9... | collective-permute-start | bytes 393224 | tf_op jit(solution)/shard_map/ppermute | solution.py:78
  182.2 8.1 %collective-permute-start.4 = (bf16[32,2048]{1,0:T(8,128)(2,1)S(1)}, bf16[32,2048]{1,0:T(8,128)(2,1)S(1)}, u32[]{:S(2)}, u32[]{:S(2)}) collective-permute-start(bf16[32,2048]{1,0:T(8,128)(2,1)S(1)} %get-tuple-element.402), channel_id=1, source_target_pairs={{0,1},{1,2},{2,3},{3,4},{4,5},{5,6},{6,7},{7,8},{8,9},{9,10},{10,1... | collective-permute-start | bytes 393224 | tf_op jit(solution)/shard_map/ppermute | solution.py:77
  191.4 6.9 %collective-permute-start.16 = (bf16[32,2048]{1,0:T(8,128)(2,1)S(1)}, bf16[32,2048]{1,0:T(8,128)(2,1)S(1)}, u32[]{:S(2)}, u32[]{:S(2)}) collective-permute-start(bf16[32,2048]{1,0:T(8,128)(2,1)S(1)} %get-tuple-element.401), channel_id=1, source_target_pairs={{0,11},{1,0},{2,1},{3,2},{4,3},{5,4},{6,5},{7,6},{8,7},{9,8},{10,9... | collective-permute-start | bytes 393224 | tf_op jit(solution)/shard_map/ppermute | solution.py:78
  193.4 8.1 %collective-permute-start.5 = (bf16[32,2048]{1,0:T(8,128)(2,1)S(1)}, bf16[32,2048]{1,0:T(8,128)(2,1)S(1)}, u32[]{:S(2)}, u32[]{:S(2)}) collective-permute-start(bf16[32,2048]{1,0:T(8,128)(2,1)S(1)} %get-tuple-element.400), channel_id=1, source_target_pairs={{0,1},{1,2},{2,3},{3,4},{4,5},{5,6},{6,7},{7,8},{8,9},{9,10},{10,1... | collective-permute-start | bytes 393224 | tf_op jit(solution)/shard_map/ppermute | solution.py:77
  202.5 6.9 %collective-permute-start.17 = (bf16[32,2048]{1,0:T(8,128)(2,1)S(1)}, bf16[32,2048]{1,0:T(8,128)(2,1)S(1)}, u32[]{:S(2)}, u32[]{:S(2)}) collective-permute-start(bf16[32,2048]{1,0:T(8,128)(2,1)S(1)} %get-tuple-element.399), channel_id=1, source_target_pairs={{0,11},{1,0},{2,1},{3,2},{4,3},{5,4},{6,5},{7,6},{8,7},{9,8},{10,9... | collective-permute-start | bytes 393224 | tf_op jit(solution)/shard_map/ppermute | solution.py:78
  206.2 8.1 %collective-permute-start.6 = (bf16[32,2048]{1,0:T(8,128)(2,1)S(1)}, bf16[32,2048]{1,0:T(8,128)(2,1)S(1)}, u32[]{:S(2)}, u32[]{:S(2)}) collective-permute-start(bf16[32,2048]{1,0:T(8,128)(2,1)S(1)} %get-tuple-element.398), channel_id=1, source_target_pairs={{0,1},{1,2},{2,3},{3,4},{4,5},{5,6},{6,7},{7,8},{8,9},{9,10},{10,1... | collective-permute-start | bytes 393224 | tf_op jit(solution)/shard_map/ppermute | solution.py:77
  215.4 7.3 %collective-permute-start.18 = (bf16[32,2048]{1,0:T(8,128)(2,1)S(1)}, bf16[32,2048]{1,0:T(8,128)(2,1)S(1)}, u32[]{:S(2)}, u32[]{:S(2)}) collective-permute-start(bf16[32,2048]{1,0:T(8,128)(2,1)S(1)} %get-tuple-element.397), channel_id=1, source_target_pairs={{0,11},{1,0},{2,1},{3,2},{4,3},{5,4},{6,5},{7,6},{8,7},{9,8},{10,9... | collective-permute-start | bytes 393224 | tf_op jit(solution)/shard_map/ppermute | solution.py:78
  218.1 9.3 %collective-permute-start.7 = (bf16[32,2048]{1,0:T(8,128)(2,1)S(1)}, bf16[32,2048]{1,0:T(8,128)(2,1)S(1)}, u32[]{:S(2)}, u32[]{:S(2)}) collective-permute-start(bf16[32,2048]{1,0:T(8,128)(2,1)S(1)} %get-tuple-element.396), channel_id=1, source_target_pairs={{0,1},{1,2},{2,3},{3,4},{4,5},{5,6},{6,7},{7,8},{8,9},{9,10},{10,1... | collective-permute-start | bytes 393224 | tf_op jit(solution)/shard_map/ppermute | solution.py:77
  228.5 7.4 %collective-permute-start.19 = (bf16[32,2048]{1,0:T(8,128)(2,1)S(1)}, bf16[32,2048]{1,0:T(8,128)(2,1)S(1)}, u32[]{:S(2)}, u32[]{:S(2)}) collective-permute-start(bf16[32,2048]{1,0:T(8,128)(2,1)S(1)} %get-tuple-element.395), channel_id=1, source_target_pairs={{0,11},{1,0},{2,1},{3,2},{4,3},{5,4},{6,5},{7,6},{8,7},{9,8},{10,9... | collective-permute-start | bytes 393224 | tf_op jit(solution)/shard_map/ppermute | solution.py:78
  230.4 8.6 %collective-permute-start.8 = (bf16[32,2048]{1,0:T(8,128)(2,1)S(1)}, bf16[32,2048]{1,0:T(8,128)(2,1)S(1)}, u32[]{:S(2)}, u32[]{:S(2)}) collective-permute-start(bf16[32,2048]{1,0:T(8,128)(2,1)S(1)} %get-tuple-element.394), channel_id=1, source_target_pairs={{0,1},{1,2},{2,3},{3,4},{4,5},{5,6},{6,7},{7,8},{8,9},{9,10},{10,1... | collective-permute-start | bytes 393224 | tf_op jit(solution)/shard_map/ppermute | solution.py:77
  240.1 8.0 %collective-permute-start.20 = (bf16[32,2048]{1,0:T(8,128)(2,1)S(1)}, bf16[32,2048]{1,0:T(8,128)(2,1)S(1)}, u32[]{:S(2)}, u32[]{:S(2)}) collective-permute-start(bf16[32,2048]{1,0:T(8,128)(2,1)S(1)} %get-tuple-element.393), channel_id=1, source_target_pairs={{0,11},{1,0},{2,1},{3,2},{4,3},{5,4},{6,5},{7,6},{8,7},{9,8},{10,9... | collective-permute-start | bytes 393224 | tf_op jit(solution)/shard_map/ppermute | solution.py:78
  242.1 8.1 %collective-permute-start.9 = (bf16[32,2048]{1,0:T(8,128)(2,1)S(1)}, bf16[32,2048]{1,0:T(8,128)(2,1)S(1)}, u32[]{:S(2)}, u32[]{:S(2)}) collective-permute-start(bf16[32,2048]{1,0:T(8,128)(2,1)S(1)} %get-tuple-element.392), channel_id=1, source_target_pairs={{0,1},{1,2},{2,3},{3,4},{4,5},{5,6},{6,7},{7,8},{8,9},{9,10},{10,1... | collective-permute-start | bytes 393224 | tf_op jit(solution)/shard_map/ppermute | solution.py:77
  251.2 8.1 %collective-permute-start.10 = (bf16[32,2048]{1,0:T(8,128)(2,1)S(1)}, bf16[32,2048]{1,0:T(8,128)(2,1)S(1)}, u32[]{:S(2)}, u32[]{:S(2)}) collective-permute-start(bf16[32,2048]{1,0:T(8,128)(2,1)S(1)} %get-tuple-element.390), channel_id=1, source_target_pairs={{0,1},{1,2},{2,3},{3,4},{4,5},{5,6},{6,7},{7,8},{8,9},{9,10},{10,1... | collective-permute-start | bytes 393224 | tf_op jit(solution)/shard_map/ppermute | solution.py:77
  253.9 6.9 %collective-permute-start.21 = (bf16[32,2048]{1,0:T(8,128)(2,1)S(1)}, bf16[32,2048]{1,0:T(8,128)(2,1)S(1)}, u32[]{:S(2)}, u32[]{:S(2)}) collective-permute-start(bf16[32,2048]{1,0:T(8,128)(2,1)S(1)} %get-tuple-element.391), channel_id=1, source_target_pairs={{0,11},{1,0},{2,1},{3,2},{4,3},{5,4},{6,5},{7,6},{8,7},{9,8},{10,9... | collective-permute-start | bytes 393224 | tf_op jit(solution)/shard_map/ppermute | solution.py:78
  261.9 8.5 %collective-permute-start.11 = (bf16[32,2048]{1,0:T(8,128)(2,1)S(1)}, bf16[32,2048]{1,0:T(8,128)(2,1)S(1)}, u32[]{:S(2)}, u32[]{:S(2)}) collective-permute-start(bf16[32,2048]{1,0:T(8,128)(2,1)S(1)} %get-tuple-element.388), channel_id=1, source_target_pairs={{0,1},{1,2},{2,3},{3,4},{4,5},{5,6},{6,7},{7,8},{8,9},{9,10},{10,1... | collective-permute-start | bytes 393224 | tf_op jit(solution)/shard_map/ppermute | solution.py:77
  264.3 7.5 %collective-permute-start.22 = (bf16[32,2048]{1,0:T(8,128)(2,1)S(1)}, bf16[32,2048]{1,0:T(8,128)(2,1)S(1)}, u32[]{:S(2)}, u32[]{:S(2)}) collective-permute-start(bf16[32,2048]{1,0:T(8,128)(2,1)S(1)} %get-tuple-element.389), channel_id=1, source_target_pairs={{0,11},{1,0},{2,1},{3,2},{4,3},{5,4},{6,5},{7,6},{8,7},{9,8},{10,9... | collective-permute-start | bytes 393224 | tf_op jit(solution)/shard_map/ppermute | solution.py:78
  272.9 8.5 %collective-permute-start.12 = (bf16[32,2048]{1,0:T(8,128)(2,1)S(1)}, bf16[32,2048]{1,0:T(8,128)(2,1)S(1)}, u32[]{:S(2)}, u32[]{:S(2)}) collective-permute-start(bf16[32,2048]{1,0:T(8,128)(2,1)S(1)} %get-tuple-element.386), channel_id=1, source_target_pairs={{0,1},{1,2},{2,3},{3,4},{4,5},{5,6},{6,7},{7,8},{8,9},{9,10},{10,1... | collective-permute-start | bytes 393224 | tf_op jit(solution)/shard_map/ppermute | solution.py:77
  275.9 7.0 %collective-permute-start.23 = (bf16[32,2048]{1,0:T(8,128)(2,1)S(1)}, bf16[32,2048]{1,0:T(8,128)(2,1)S(1)}, u32[]{:S(2)}, u32[]{:S(2)}) collective-permute-start(bf16[32,2048]{1,0:T(8,128)(2,1)S(1)} %get-tuple-element.387), channel_id=1, source_target_pairs={{0,11},{1,0},{2,1},{3,2},{4,3},{5,4},{6,5},{7,6},{8,7},{9,8},{10,9... | collective-permute-start | bytes 393224 | tf_op jit(solution)/shard_map/ppermute | solution.py:78
  284.0 8.5 %collective-permute-start.13 = (bf16[32,2048]{1,0:T(8,128)(2,1)S(1)}, bf16[32,2048]{1,0:T(8,128)(2,1)S(1)}, u32[]{:S(2)}, u32[]{:S(2)}) collective-permute-start(bf16[32,2048]{1,0:T(8,128)(2,1)S(1)} %get-tuple-element.384), channel_id=1, source_target_pairs={{0,1},{1,2},{2,3},{3,4},{4,5},{5,6},{6,7},{7,8},{8,9},{9,10},{10,1... | collective-permute-start | bytes 393224 | tf_op jit(solution)/shard_map/ppermute | solution.py:77
  287.8 6.9 %collective-permute-start.24 = (bf16[32,2048]{1,0:T(8,128)(2,1)S(1)}, bf16[32,2048]{1,0:T(8,128)(2,1)S(1)}, u32[]{:S(2)}, u32[]{:S(2)}) collective-permute-start(bf16[32,2048]{1,0:T(8,128)(2,1)S(1)} %get-tuple-element.385), channel_id=1, source_target_pairs={{0,11},{1,0},{2,1},{3,2},{4,3},{5,4},{6,5},{7,6},{8,7},{9,8},{10,9... | collective-permute-start | bytes 393224 | tf_op jit(solution)/shard_map/ppermute | solution.py:78
Sparse Core Ops, SparseCore 0:
  37.8 43.0 all-gather.1

commit v3 on v2

--- a/solution.py
+++ b/solution.py
@@ -63,24 +63,28 @@
     count = lax.axis_size(axis)
     me = lax.axis_index(axis)
     rows = partial.shape[0] // count
-    half = partial.shape[1] // 2
+    left_hops = count // 2
+    right_hops = count - 1 - left_hops
     ahead = [(source, (source + 1) % count) for source in range(count)]
     behind = [(source, (source - 1) % count) for source in range(count)]
 
-    def piece(block, low):
-        start = (block % count) * rows
-        return lax.dynamic_slice(partial, (start, low), (rows, half))
+    def piece(block):
+        return lax.dynamic_slice_in_dim(partial, (block % count) * rows, rows, 0)
 
-    up = piece(me - 1, 0).astype(jnp.bfloat16)
-    down = piece(me + 1, half).astype(jnp.bfloat16)
-    for step in range(count - 1):
-        up_sum = lax.ppermute(up, axis, ahead).astype(jnp.float32) + piece(me - 2 - step, 0)
-        down_sum = lax.ppermute(down, axis, behind).astype(jnp.float32) + piece(
-            me + 2 + step, half
+    up = piece(me + left_hops).astype(jnp.bfloat16)
+    down = piece(me - right_hops).astype(jnp.bfloat16)
+    up_sum = down_sum = None
+    for step in range(left_hops):
+        up_sum = lax.ppermute(up, axis, ahead).astype(jnp.float32) + piece(
+            me + left_hops - 1 - step
         )
         up = up_sum.astype(jnp.bfloat16)
-        down = down_sum.astype(jnp.bfloat16)
-    return jnp.concatenate([up, down], axis=1)
+        if step < right_hops:
+            down_sum = lax.ppermute(down, axis, behind).astype(jnp.float32)
+            if step < right_hops - 1:
+                down_sum = down_sum + piece(me - right_hops + 1 + step)
+                down = down_sum.astype(jnp.bfloat16)
+    return (up_sum + down_sum).astype(jnp.bfloat16)
 
 
 def on_device(queries, keys, values, out_weight):

time: 305 us -> 254 us (0.83)
  the two profiles are of different devices: /device:TPU:62 before, /device:TPU:38 now
where the time goes in v3:
time: 254 us; the launch traced here: 253 us
  waiting for transfers between devices  88.2 us (35%)
  starting transfers between devices  40.3 us (16%)
  matrix products  38.7 us (15%)
  blocking collectives  29.4 us (12%)
  other arithmetic  24.4 us (10%)
  between operations  14 us (6%)
  loops' own time  11.8 us (5%)
  local copies, waits for them, and re-layouts  6.05 us (2%)
    all_gather x1, waiting for transfers between devices, on_device(): gathered = lax.all_gather(gathered, 'cx', axis=0, tiled=True)  43.4 us
    all_gather x1, blocking collectives, on_device(): gathered = lax.all_gather(my_half, 'cy', axis=0, tiled=True)  27.5 us
    ppermute x6, waiting for transfers between devices, ring_reduce_scatter(): lax.ppermute(up, axis, ahead).astype(jnp.float32)  26.9 us
    dot_general x16, matrix products, block_terms(): jnp.dot(weights.astype(jnp.bfloat16), v_part, preferred_element_type=jnp....  19.7 us
    dot_general x16, matrix products, block_terms(): lax.dot_general(q_part, k_part, (((1,), (1,)), ((), ())), preferred_eleme...  18 us
    ppermute x6, starting transfers between devices, ring_reduce_scatter(): lax.ppermute(up, axis, ahead).astype(jnp.float32)  18 us
    ppermute x5, starting transfers between devices, ring_reduce_scatter(): down_sum = lax.ppermute(down, axis, behind).astype(jnp.float32)  15.8 us
    ppermute x5, waiting for transfers between devices, ring_reduce_scatter(): down_sum = lax.ppermute(down, axis, behind).astype(jnp.float32)  14.9 us
  transfers between devices with their start and end apart: 15, of which 13 were waited for; matrix products, arithmetic and copies ran while one was open for 2% of the time, Pallas kernels for 0%

profile of v3, /device:TPU:38, one launch (start us, length us, event | category | flops | bytes accessed | tf_op | source)
XLA Modules:
  0.0 252.8 jit_solution(2352324644342583251)
XLA Ops:
  8.3 1.9 all_gather.9
  10.2 27.5 %all_gather.10 = bf16[1024,256]{1,0:T(8,128)(2,1)} all-gather(bf16[128,256]{1,0:T(8,128)(2,1)S(1)} %constant_dynamic-slice_fusion), channel_id=1, replica_groups=mesh['cx'=4,'cy'=8,'cc'=2,'head'=12] {'cy'}, dimensions={0}, use_global_device_ids=true | all-gather | bytes 589824 | tf_op jit(solution)/shard_map/all_gather | solution.py:111
  37.7 43.4 %all-gather.2.cloned.1.call-done = bf16[4096,256]{1,0:T(8,128)(2,1)} async-done(((bf16[1024,256]{1,0:T(8,128)(2,1)}), bf16[4096,256]{1,0:T(8,128)(2,1)}) %all-gather.2.cloned.1.call-update) | async-done | bytes 2097168 | tf_op jit(solution)/shard_map/all_gather | solution.py:112
  81.2 1.9 collective-permute-start.2
  84.0 2.4 collective-permute-start
  86.4 2.1 collective-permute-start.1
  89.3 2.2 collective-permute-done
  95.6 4.1 %fusion.44 = (bf16[4096,256]{1,0:T(8,128)(2,1)}, bf16[4096,256]{1,0:T(8,128)(2,1)}) fusion(s32[]{:T(128)S(6)} %select_n.207, bf16[1,4096,256]{2,1,0:T(8,128)(2,1)S(1)} %bitcast.35, bf16[1,4096,256]{2,1,0:T(8,128)(2,1)} %bitcast.9, s32[]{:T(128)S(6)} %select_n.206), kind=kLoop, calls=%fused_computation.68 | loop fusion | flops 2097152 | bytes 8388616 | tf_op jit(solution)/shard_map/squeeze | solution.py:116
  99.7 58.3 %while.21 = (s32[]{:T(128)}, f32[2,384]{1,0:T(2,128)S(1)}, f32[2,384]{1,0:T(2,128)S(1)}, f32[2,384,128]{2,1,0:T(8,128)S(1)}, s32[]{:T(128)}, /*index=5*/bf16[409...) while((s32[]{:T(128)}, f32[2,384]{1,0:T(2,128)S(1)}, ...), condition=%wide.region_11.12_spmd.clone, body=%wide.region_3.11_spmd.clone.sunk | while | flops 207248768 | bytes 7093621 | solution.py:149
  101.8 5.9 %conditional.3 = ((f32[2,384]{1,0:T(2,128)S(1)}, f32[2,384]{1,0:T(2,128)S(1)}, f32[2,384,128]{2,1,0:T(8,128)S(1)})) conditional(s32[]{:T(128)} %convert_element_type.163, (f32[2,384]{1,0:T(2,128)S(1)}, f32[2,384]{1,0:T(2,128)S(1)}, f32[2,384,128]{2,1,0:T(8,128)S(1)}) %tuple.73, (s32[]{:T(128)}, s32[512]{0:T(512)S(1)}, s32[]{:T(128)}, ...), branch_computations={%region_5.5_spmd, %region_6.10_spmd} | conditional | flops 207229824 | bytes 7089770 | solution.py:147
  105.6 1.3 convolution_bitcast_fusion.1
  109.8 5.9 %conditional.3 = ((f32[2,384]{1,0:T(2,128)S(1)}, f32[2,384]{1,0:T(2,128)S(1)}, f32[2,384,128]{2,1,0:T(8,128)S(1)})) conditional(s32[]{:T(128)} %convert_element_type.163, (f32[2,384]{1,0:T(2,128)S(1)}, f32[2,384]{1,0:T(2,128)S(1)}, f32[2,384,128]{2,1,0:T(8,128)S(1)}) %tuple.73, (s32[]{:T(128)}, s32[512]{0:T(512)S(1)}, s32[]{:T(128)}, ...), branch_computations={%region_5.5_spmd, %region_6.10_spmd} | conditional | flops 207229824 | bytes 7089770 | solution.py:147
  113.6 1.3 convolution_bitcast_fusion.1
  117.8 5.9 %conditional.3 = ((f32[2,384]{1,0:T(2,128)S(1)}, f32[2,384]{1,0:T(2,128)S(1)}, f32[2,384,128]{2,1,0:T(8,128)S(1)})) conditional(s32[]{:T(128)} %convert_element_type.163, (f32[2,384]{1,0:T(2,128)S(1)}, f32[2,384]{1,0:T(2,128)S(1)}, f32[2,384,128]{2,1,0:T(8,128)S(1)}) %tuple.73, (s32[]{:T(128)}, s32[512]{0:T(512)S(1)}, s32[]{:T(128)}, ...), branch_computations={%region_5.5_spmd, %region_6.10_spmd} | conditional | flops 207229824 | bytes 7089770 | solution.py:147
  121.6 1.3 convolution_bitcast_fusion.1
  125.9 5.9 %conditional.3 = ((f32[2,384]{1,0:T(2,128)S(1)}, f32[2,384]{1,0:T(2,128)S(1)}, f32[2,384,128]{2,1,0:T(8,128)S(1)})) conditional(s32[]{:T(128)} %convert_element_type.163, (f32[2,384]{1,0:T(2,128)S(1)}, f32[2,384]{1,0:T(2,128)S(1)}, f32[2,384,128]{2,1,0:T(8,128)S(1)}) %tuple.73, (s32[]{:T(128)}, s32[512]{0:T(512)S(1)}, s32[]{:T(128)}, ...), branch_computations={%region_5.5_spmd, %region_6.10_spmd} | conditional | flops 207229824 | bytes 7089770 | solution.py:147
  127.1 1.3 convolution_bitcast_fusion
  129.6 1.3 convolution_bitcast_fusion.1
  133.9 5.9 %conditional.3 = ((f32[2,384]{1,0:T(2,128)S(1)}, f32[2,384]{1,0:T(2,128)S(1)}, f32[2,384,128]{2,1,0:T(8,128)S(1)})) conditional(s32[]{:T(128)} %convert_element_type.163, (f32[2,384]{1,0:T(2,128)S(1)}, f32[2,384]{1,0:T(2,128)S(1)}, f32[2,384,128]{2,1,0:T(8,128)S(1)}) %tuple.73, (s32[]{:T(128)}, s32[512]{0:T(512)S(1)}, s32[]{:T(128)}, ...), branch_computations={%region_5.5_spmd, %region_6.10_spmd} | conditional | flops 207229824 | bytes 7089770 | solution.py:147
  135.1 1.3 convolution_bitcast_fusion
  137.7 1.3 convolution_bitcast_fusion.1
  141.9 5.9 %conditional.3 = ((f32[2,384]{1,0:T(2,128)S(1)}, f32[2,384]{1,0:T(2,128)S(1)}, f32[2,384,128]{2,1,0:T(8,128)S(1)})) conditional(s32[]{:T(128)} %convert_element_type.163, (f32[2,384]{1,0:T(2,128)S(1)}, f32[2,384]{1,0:T(2,128)S(1)}, f32[2,384,128]{2,1,0:T(8,128)S(1)}) %tuple.73, (s32[]{:T(128)}, s32[512]{0:T(512)S(1)}, s32[]{:T(128)}, ...), branch_computations={%region_5.5_spmd, %region_6.10_spmd} | conditional | flops 207229824 | bytes 7089770 | solution.py:147
  145.7 1.3 convolution_bitcast_fusion.1
  149.9 5.9 %conditional.3 = ((f32[2,384]{1,0:T(2,128)S(1)}, f32[2,384]{1,0:T(2,128)S(1)}, f32[2,384,128]{2,1,0:T(8,128)S(1)})) conditional(s32[]{:T(128)} %convert_element_type.163, (f32[2,384]{1,0:T(2,128)S(1)}, f32[2,384]{1,0:T(2,128)S(1)}, f32[2,384,128]{2,1,0:T(8,128)S(1)}) %tuple.73, (s32[]{:T(128)}, s32[512]{0:T(512)S(1)}, s32[]{:T(128)}, ...), branch_computations={%region_5.5_spmd, %region_6.10_spmd} | conditional | flops 207229824 | bytes 7089770 | solution.py:147
  153.7 1.3 convolution_bitcast_fusion.1
  159.3 2.6 %copy-done.1 = f32[384,4096]{1,0:T(8,128)} copy-done((f32[384,4096]{1,0:T(8,128)}, f32[384,4096]{1,0:T(8,128)S(1)}, u32[]{:S(2)}) %copy-start.1) | copy-done | bytes 6291480
  162.0 3.6 %collective-permute-start.3 = (bf16[32,4096]{1,0:T(8,128)(2,1)S(1)}, bf16[32,4096]{1,0:T(8,128)(2,1)S(1)}, u32[]{:S(2)}, u32[]{:S(2)}) collective-permute-start(bf16[32,4096]{1,0:T(8,128)(2,1)S(1)} %get-tuple-element.390), channel_id=1, source_target_pairs={{0,1},{1,2},{2,3},{3,4},{4,5},{5,6},{6,7},{7,8},{8,9},{9,10},{10,1... | collective-permute-start | bytes 786440 | tf_op jit(solution)/shard_map/ppermute | solution.py:78
  165.6 5.0 %collective-permute-start.9 = (bf16[32,4096]{1,0:T(8,128)(2,1)S(1)}, bf16[32,4096]{1,0:T(8,128)(2,1)S(1)}, u32[]{:S(2)}, u32[]{:S(2)}) collective-permute-start(bf16[32,4096]{1,0:T(8,128)(2,1)S(1)} %get-tuple-element.391), channel_id=1, source_target_pairs={{0,11},{1,0},{2,1},{3,2},{4,3},{5,4},{6,5},{7,6},{8,7},{9,8},{10,9... | collective-permute-start | bytes 786440 | tf_op jit(solution)/shard_map/ppermute | solution.py:83
  170.5 2.5 collective-permute-done.3
  174.1 1.9 collective-permute-start.4
  176.1 8.7 %collective-permute-done.4 = bf16[32,4096]{1,0:T(8,128)(2,1)S(1)} collective-permute-done((bf16[32,4096]{1,0:T(8,128)(2,1)S(1)}, bf16[32,4096]{1,0:T(8,128)(2,1)S(1)}, u32[]{:S(2)}, u32[]{:S(2)}) %collective-permute-start.4) | collective-permute-done | bytes 262176 | tf_op jit(solution)/shard_map/ppermute | solution.py:78
  186.1 3.0 %collective-permute-start.10 = (bf16[32,4096]{1,0:T(8,128)(2,1)S(1)}, bf16[32,4096]{1,0:T(8,128)(2,1)S(1)}, u32[]{:S(2)}, u32[]{:S(2)}) collective-permute-start(bf16[32,4096]{1,0:T(8,128)(2,1)S(1)} %get-tuple-element.389), channel_id=1, source_target_pairs={{0,11},{1,0},{2,1},{3,2},{4,3},{5,4},{6,5},{7,6},{8,7},{9,8},{10,9... | collective-permute-start | bytes 786440 | tf_op jit(solution)/shard_map/ppermute | solution.py:83
  189.1 2.9 %collective-permute-start.5 = (bf16[32,4096]{1,0:T(8,128)(2,1)S(1)}, bf16[32,4096]{1,0:T(8,128)(2,1)S(1)}, u32[]{:S(2)}, u32[]{:S(2)}) collective-permute-start(bf16[32,4096]{1,0:T(8,128)(2,1)S(1)} %get-tuple-element.388), channel_id=1, source_target_pairs={{0,1},{1,2},{2,3},{3,4},{4,5},{5,6},{6,7},{7,8},{8,9},{9,10},{10,1... | collective-permute-start | bytes 786440 | tf_op jit(solution)/shard_map/ppermute | solution.py:78
  192.0 4.7 %collective-permute-done.10 = bf16[32,4096]{1,0:T(8,128)(2,1)S(1)} collective-permute-done((bf16[32,4096]{1,0:T(8,128)(2,1)S(1)}, bf16[32,4096]{1,0:T(8,128)(2,1)S(1)}, u32[]{:S(2)}, u32[]{:S(2)}) %collective-permute-start.10) | collective-permute-done | bytes 262176 | tf_op jit(solution)/shard_map/ppermute | solution.py:83
  196.7 4.5 %collective-permute-done.5 = bf16[32,4096]{1,0:T(8,128)(2,1)S(1)} collective-permute-done((bf16[32,4096]{1,0:T(8,128)(2,1)S(1)}, bf16[32,4096]{1,0:T(8,128)(2,1)S(1)}, u32[]{:S(2)}, u32[]{:S(2)}) %collective-permute-start.5) | collective-permute-done | bytes 262176 | tf_op jit(solution)/shard_map/ppermute | solution.py:78
  202.5 1.9 collective-permute-start.11
  204.4 3.9 %collective-permute-start.6 = (bf16[32,4096]{1,0:T(8,128)(2,1)S(1)}, bf16[32,4096]{1,0:T(8,128)(2,1)S(1)}, u32[]{:S(2)}, u32[]{:S(2)}) collective-permute-start(bf16[32,4096]{1,0:T(8,128)(2,1)S(1)} %get-tuple-element.386), channel_id=1, source_target_pairs={{0,1},{1,2},{2,3},{3,4},{4,5},{5,6},{6,7},{7,8},{8,9},{9,10},{10,1... | collective-permute-start | bytes 786440 | tf_op jit(solution)/shard_map/ppermute | solution.py:78
  208.4 4.3 %collective-permute-done.11 = bf16[32,4096]{1,0:T(8,128)(2,1)S(1)} collective-permute-done((bf16[32,4096]{1,0:T(8,128)(2,1)S(1)}, bf16[32,4096]{1,0:T(8,128)(2,1)S(1)}, u32[]{:S(2)}, u32[]{:S(2)}) %collective-permute-start.11) | collective-permute-done | bytes 262176 | tf_op jit(solution)/shard_map/ppermute | solution.py:83
  212.7 3.2 %collective-permute-done.6 = bf16[32,4096]{1,0:T(8,128)(2,1)S(1)} collective-permute-done((bf16[32,4096]{1,0:T(8,128)(2,1)S(1)}, bf16[32,4096]{1,0:T(8,128)(2,1)S(1)}, u32[]{:S(2)}, u32[]{:S(2)}) %collective-permute-start.6) | collective-permute-done | bytes 262176 | tf_op jit(solution)/shard_map/ppermute | solution.py:78
  217.3 3.8 %collective-permute-start.12 = (bf16[32,4096]{1,0:T(8,128)(2,1)S(1)}, bf16[32,4096]{1,0:T(8,128)(2,1)S(1)}, u32[]{:S(2)}, u32[]{:S(2)}) collective-permute-start(bf16[32,4096]{1,0:T(8,128)(2,1)S(1)} %get-tuple-element.385), channel_id=1, source_target_pairs={{0,11},{1,0},{2,1},{3,2},{4,3},{5,4},{6,5},{7,6},{8,7},{9,8},{10,9... | collective-permute-start | bytes 786440 | tf_op jit(solution)/shard_map/ppermute | solution.py:83
  221.1 2.0 collective-permute-start.7
  223.2 3.5 %collective-permute-done.12 = bf16[32,4096]{1,0:T(8,128)(2,1)S(1)} collective-permute-done((bf16[32,4096]{1,0:T(8,128)(2,1)S(1)}, bf16[32,4096]{1,0:T(8,128)(2,1)S(1)}, u32[]{:S(2)}, u32[]{:S(2)}) %collective-permute-start.12) | collective-permute-done | bytes 262176 | tf_op jit(solution)/shard_map/ppermute | solution.py:83
  226.6 4.6 %collective-permute-done.7 = bf16[32,4096]{1,0:T(8,128)(2,1)S(1)} collective-permute-done((bf16[32,4096]{1,0:T(8,128)(2,1)S(1)}, bf16[32,4096]{1,0:T(8,128)(2,1)S(1)}, u32[]{:S(2)}, u32[]{:S(2)}) %collective-permute-start.7) | collective-permute-done | bytes 262176 | tf_op jit(solution)/shard_map/ppermute | solution.py:78
  232.5 2.2 collective-permute-start.13
  234.7 3.7 %collective-permute-start.8 = (bf16[32,4096]{1,0:T(8,128)(2,1)S(1)}, bf16[32,4096]{1,0:T(8,128)(2,1)S(1)}, u32[]{:S(2)}, u32[]{:S(2)}) collective-permute-start(bf16[32,4096]{1,0:T(8,128)(2,1)S(1)} %get-tuple-element.382), channel_id=1, source_target_pairs={{0,1},{1,2},{2,3},{3,4},{4,5},{5,6},{6,7},{7,8},{8,9},{9,10},{10,1... | collective-permute-start | bytes 786440 | tf_op jit(solution)/shard_map/ppermute | solution.py:78
  238.4 2.4 collective-permute-done.13
  240.8 3.4 %collective-permute-done.8 = bf16[32,4096]{1,0:T(8,128)(2,1)S(1)} collective-permute-done((bf16[32,4096]{1,0:T(8,128)(2,1)S(1)}, bf16[32,4096]{1,0:T(8,128)(2,1)S(1)}, u32[]{:S(2)}, u32[]{:S(2)}) %collective-permute-start.8) | collective-permute-done | bytes 262176 | tf_op jit(solution)/shard_map/ppermute | solution.py:78
  244.1 1.8 add_convert_fusion
  (144 shorter events, 49.6 us)
Async XLA Ops:
  6.5 151.7 %copy-start = (bf16[256,4096]{1,0:T(8,128)(2,1)S(1)}, bf16[256,4096]{1,0:T(8,128)(2,1)}, u32[]{:S(2)}) copy-start(bf16[256,4096]{1,0:T(8,128)(2,1)} %param.11) | copy-start | bytes 6291460
  6.5 79.9 %copy-start.4 = (bf16[384,256]{1,0:T(8,128)(2,1)S(1)}, bf16[384,256]{1,0:T(8,128)(2,1)}, u32[]{:S(2)}) copy-start(bf16[384,256]{1,0:T(8,128)(2,1)} %param.10) | copy-start | bytes 589828
  6.5 85.0 %copy-start.3 = (bf16[384,256]{1,0:T(8,128)(2,1)S(1)}, bf16[384,256]{1,0:T(8,128)(2,1)}, u32[]{:S(2)}) copy-start(bf16[384,256]{1,0:T(8,128)(2,1)} %param.9) | copy-start | bytes 589828
  6.5 85.0 %copy-start.5 = (bf16[384,256]{1,0:T(8,128)(2,1)S(1)}, bf16[384,256]{1,0:T(8,128)(2,1)}, u32[]{:S(2)}) copy-start(bf16[384,256]{1,0:T(8,128)(2,1)} %param.8) | copy-start | bytes 589828
  6.5 74.6 %all-gather.2.cloned.1.call-start = ((), (), s32[]{:S(2)}) async-start(), calls=%async_computation | async-start | bytes 2621440 | tf_op jit(solution)/shard_map/all_gather | solution.py:112
  81.2 14.1 %collective-permute-start.2 = (bf16[4096,256]{1,0:T(8,128)(2,1)}, bf16[4096,256]{1,0:T(8,128)(2,1)}, u32[]{:S(2)}, u32[]{:S(2)}) collective-permute-start(bf16[4096,256]{1,0:T(8,128)(2,1)} %all-gather.2.cloned.1.call-done), channel_id=1, source_target_pairs={{0,12},{12,0},{1,13},{13,1},{2,14},{14,2},{3,15},{15,3},{4,16},{16... | collective-permute-start | bytes 6291464 | tf_op jit(solution)/shard_map/ppermute | solution.py:113
  84.0 7.5 %collective-permute-start = (bf16[256,256]{1,0:T(8,128)(2,1)S(1)}, bf16[256,256]{1,0:T(8,128)(2,1)S(1)}, u32[]{:S(2)}, u32[]{:S(2)}) collective-permute-start(bf16[256,256]{1,0:T(8,128)(2,1)S(1)} %slice.42), channel_id=1, source_target_pairs={{0,12},{12,24},{24,36},{36,48},{48,60},{60,72},{72,84},{84,96},{96... | collective-permute-start | bytes 393224 | tf_op jit(solution)/shard_map/ppermute | solution.py:22
  86.4 7.5 %collective-permute-start.1 = (bf16[256,256]{1,0:T(8,128)(2,1)S(1)}, bf16[256,256]{1,0:T(8,128)(2,1)S(1)}, u32[]{:S(2)}, u32[]{:S(2)}) collective-permute-start(bf16[256,256]{1,0:T(8,128)(2,1)S(1)} %slice.45), channel_id=1, source_target_pairs={{0,12},{12,24},{24,36},{36,48},{48,60},{60,72},{72,84},{84,96},{96... | collective-permute-start | bytes 393224 | tf_op jit(solution)/shard_map/ppermute | solution.py:22
  94.0 1.6 copy-start.2
  159.3 2.7 %copy-start.1 = (f32[384,4096]{1,0:T(8,128)}, f32[384,4096]{1,0:T(8,128)S(1)}, u32[]{:S(2)}) copy-start(f32[384,4096]{1,0:T(8,128)S(1)} %fusion.87) | copy-start | bytes 18874372
  162.0 11.0 %collective-permute-start.3 = (bf16[32,4096]{1,0:T(8,128)(2,1)S(1)}, bf16[32,4096]{1,0:T(8,128)(2,1)S(1)}, u32[]{:S(2)}, u32[]{:S(2)}) collective-permute-start(bf16[32,4096]{1,0:T(8,128)(2,1)S(1)} %get-tuple-element.390), channel_id=1, source_target_pairs={{0,1},{1,2},{2,3},{3,4},{4,5},{5,6},{6,7},{7,8},{8,9},{9,10},{10,1... | collective-permute-start | bytes 786440 | tf_op jit(solution)/shard_map/ppermute | solution.py:78
  165.6 10.5 %collective-permute-start.9 = (bf16[32,4096]{1,0:T(8,128)(2,1)S(1)}, bf16[32,4096]{1,0:T(8,128)(2,1)S(1)}, u32[]{:S(2)}, u32[]{:S(2)}) collective-permute-start(bf16[32,4096]{1,0:T(8,128)(2,1)S(1)} %get-tuple-element.391), channel_id=1, source_target_pairs={{0,11},{1,0},{2,1},{3,2},{4,3},{5,4},{6,5},{7,6},{8,7},{9,8},{10,9... | collective-permute-start | bytes 786440 | tf_op jit(solution)/shard_map/ppermute | solution.py:83
  174.1 10.7 %collective-permute-start.4 = (bf16[32,4096]{1,0:T(8,128)(2,1)S(1)}, bf16[32,4096]{1,0:T(8,128)(2,1)S(1)}, u32[]{:S(2)}, u32[]{:S(2)}) collective-permute-start(bf16[32,4096]{1,0:T(8,128)(2,1)S(1)} %add_convert_fusion.9), channel_id=1, source_target_pairs={{0,1},{1,2},{2,3},{3,4},{4,5},{5,6},{6,7},{7,8},{8,9},{9,10},{10,1... | collective-permute-start | bytes 786440 | tf_op jit(solution)/shard_map/ppermute | solution.py:78
  186.1 10.6 %collective-permute-start.10 = (bf16[32,4096]{1,0:T(8,128)(2,1)S(1)}, bf16[32,4096]{1,0:T(8,128)(2,1)S(1)}, u32[]{:S(2)}, u32[]{:S(2)}) collective-permute-start(bf16[32,4096]{1,0:T(8,128)(2,1)S(1)} %get-tuple-element.389), channel_id=1, source_target_pairs={{0,11},{1,0},{2,1},{3,2},{4,3},{5,4},{6,5},{7,6},{8,7},{9,8},{10,9... | collective-permute-start | bytes 786440 | tf_op jit(solution)/shard_map/ppermute | solution.py:83
  189.1 12.1 %collective-permute-start.5 = (bf16[32,4096]{1,0:T(8,128)(2,1)S(1)}, bf16[32,4096]{1,0:T(8,128)(2,1)S(1)}, u32[]{:S(2)}, u32[]{:S(2)}) collective-permute-start(bf16[32,4096]{1,0:T(8,128)(2,1)S(1)} %get-tuple-element.388), channel_id=1, source_target_pairs={{0,1},{1,2},{2,3},{3,4},{4,5},{5,6},{6,7},{7,8},{8,9},{9,10},{10,1... | collective-permute-start | bytes 786440 | tf_op jit(solution)/shard_map/ppermute | solution.py:78
  202.5 10.2 %collective-permute-start.11 = (bf16[32,4096]{1,0:T(8,128)(2,1)S(1)}, bf16[32,4096]{1,0:T(8,128)(2,1)S(1)}, u32[]{:S(2)}, u32[]{:S(2)}) collective-permute-start(bf16[32,4096]{1,0:T(8,128)(2,1)S(1)} %get-tuple-element.387), channel_id=1, source_target_pairs={{0,11},{1,0},{2,1},{3,2},{4,3},{5,4},{6,5},{7,6},{8,7},{9,8},{10,9... | collective-permute-start | bytes 786440 | tf_op jit(solution)/shard_map/ppermute | solution.py:83
  204.4 11.5 %collective-permute-start.6 = (bf16[32,4096]{1,0:T(8,128)(2,1)S(1)}, bf16[32,4096]{1,0:T(8,128)(2,1)S(1)}, u32[]{:S(2)}, u32[]{:S(2)}) collective-permute-start(bf16[32,4096]{1,0:T(8,128)(2,1)S(1)} %get-tuple-element.386), channel_id=1, source_target_pairs={{0,1},{1,2},{2,3},{3,4},{4,5},{5,6},{6,7},{7,8},{8,9},{9,10},{10,1... | collective-permute-start | bytes 786440 | tf_op jit(solution)/shard_map/ppermute | solution.py:78
  217.3 9.4 %collective-permute-start.12 = (bf16[32,4096]{1,0:T(8,128)(2,1)S(1)}, bf16[32,4096]{1,0:T(8,128)(2,1)S(1)}, u32[]{:S(2)}, u32[]{:S(2)}) collective-permute-start(bf16[32,4096]{1,0:T(8,128)(2,1)S(1)} %get-tuple-element.385), channel_id=1, source_target_pairs={{0,11},{1,0},{2,1},{3,2},{4,3},{5,4},{6,5},{7,6},{8,7},{9,8},{10,9... | collective-permute-start | bytes 786440 | tf_op jit(solution)/shard_map/ppermute | solution.py:83
  221.1 10.2 %collective-permute-start.7 = (bf16[32,4096]{1,0:T(8,128)(2,1)S(1)}, bf16[32,4096]{1,0:T(8,128)(2,1)S(1)}, u32[]{:S(2)}, u32[]{:S(2)}) collective-permute-start(bf16[32,4096]{1,0:T(8,128)(2,1)S(1)} %get-tuple-element.384), channel_id=1, source_target_pairs={{0,1},{1,2},{2,3},{3,4},{4,5},{5,6},{6,7},{7,8},{8,9},{9,10},{10,1... | collective-permute-start | bytes 786440 | tf_op jit(solution)/shard_map/ppermute | solution.py:78
  232.5 8.3 %collective-permute-start.13 = (bf16[32,4096]{1,0:T(8,128)(2,1)S(1)}, bf16[32,4096]{1,0:T(8,128)(2,1)S(1)}, u32[]{:S(2)}, u32[]{:S(2)}) collective-permute-start(bf16[32,4096]{1,0:T(8,128)(2,1)S(1)} %get-tuple-element.383), channel_id=1, source_target_pairs={{0,11},{1,0},{2,1},{3,2},{4,3},{5,4},{6,5},{7,6},{8,7},{9,8},{10,9... | collective-permute-start | bytes 786440 | tf_op jit(solution)/shard_map/ppermute | solution.py:83
  234.7 9.5 %collective-permute-start.8 = (bf16[32,4096]{1,0:T(8,128)(2,1)S(1)}, bf16[32,4096]{1,0:T(8,128)(2,1)S(1)}, u32[]{:S(2)}, u32[]{:S(2)}) collective-permute-start(bf16[32,4096]{1,0:T(8,128)(2,1)S(1)} %get-tuple-element.382), channel_id=1, source_target_pairs={{0,1},{1,2},{2,3},{3,4},{4,5},{5,6},{6,7},{7,8},{8,9},{9,10},{10,1... | collective-permute-start | bytes 786440 | tf_op jit(solution)/shard_map/ppermute | solution.py:78
Sparse Core Ops, SparseCore 0:
  37.8 43.2 all-gather.1

commit v4 on v3

--- a/solution.py
+++ b/solution.py
@@ -11,6 +11,7 @@
 CTX = ("cx", "cy", "cc")
 CHIPS = ("cx", "cy")
 CORE = "cc"
+QUERY_CHUNKS = 2
 
 
 LOW_SCORE = -1e30
@@ -59,6 +60,31 @@
     return (top_score, totals, weighted)
 
 
+def attend(query_rows, *parts):
+    scale = 1.0 / math.sqrt(HEAD_DIM)
+    rows, width = query_rows.shape
+    heads = width // HEAD_DIM
+    q = query_rows.reshape(rows, heads, HEAD_DIM)
+    scores = []
+    for keys, _, allowed in parts:
+        k = keys.reshape(keys.shape[0], heads, HEAD_DIM)
+        s = jnp.einsum("qhd,khd->hqk", q, k, preferred_element_type=jnp.float32) * scale
+        scores.append(jnp.where(allowed[None], s, LOW_SCORE))
+    top = scores[0].max(axis=2)
+    for s in scores[1:]:
+        top = jnp.maximum(top, s.max(axis=2))
+    total = 0.0
+    summed = 0.0
+    for s, (_, values, allowed) in zip(scores, parts):
+        w = jnp.where(allowed[None], jnp.exp(s - top[:, :, None]), 0.0)
+        total = total + w.sum(axis=2)
+        v = values.reshape(values.shape[0], heads, HEAD_DIM)
+        summed = summed + jnp.einsum(
+            "hqk,khd->hqd", w.astype(jnp.bfloat16), v, preferred_element_type=jnp.float32
+        )
+    return summed / total[:, :, None]
+
+
 def ring_reduce_scatter(partial, axis):
     count = lax.axis_size(axis)
     me = lax.axis_index(axis)
@@ -99,7 +125,6 @@
     band_pos = my_index * tok_rows - BAND + jnp.arange(tok_rows + BAND, dtype=jnp.int32)
     band_gap = own_pos[:, None] - band_pos[None, :]
     band_mask = (band_gap >= 0) & (band_gap < BAND) & (band_pos[None, :] >= 0)
-    band_part = block_terms(queries, band_keys, band_values, band_mask)
     core = lax.axis_index(CORE)
     sum_start = jnp.where(my_index % 2 == 0, tok_rows - half_sum, 0).astype(jnp.int32)
     own_keys = lax.dynamic_slice_in_dim(keys, sum_start, half_sum, 0)
@@ -114,41 +139,21 @@
     both = jnp.stack([gathered, other])
     all_sum_keys = both[core]
     all_sum_values = both[1 - core]
-    sum_rows = all_sum_keys.shape[0]
-    step_rows = math.gcd(sum_rows, 512)
-    step_count = sum_rows // step_rows
-    row_count = queries.shape[0]
-    newest = jnp.max(own_pos)
-    initial = (
-        jnp.full((head_count, row_count), LOW_SCORE, jnp.float32),
-        jnp.zeros((head_count, row_count), jnp.float32),
-        jnp.zeros((head_count, row_count, HEAD_DIM), jnp.float32),
-    )
-
-    def fold_block(block_idx, carry):
-        start = (block_idx * step_rows).astype(jnp.int32)
-        index = start + jnp.arange(step_rows, dtype=jnp.int32)
-        owner = index // half_sum
-        key_pos = (
-            owner * tok_rows + jnp.where(owner % 2 == 0, tok_rows - half_sum, 0) + index % half_sum
+    index = jnp.arange(all_sum_keys.shape[0], dtype=jnp.int32)
+    owner = index // half_sum
+    key_pos = owner * tok_rows + jnp.where(owner % 2 == 0, tok_rows - half_sum, 0) + index % half_sum
+    sum_mask = own_pos[:, None] - key_pos[None, :] >= BAND
+    pieces = []
+    chunk = tok_rows // QUERY_CHUNKS
+    for low in range(0, tok_rows, chunk):
+        pieces.append(
+            attend(
+                queries[low : low + chunk],
+                (band_keys, band_values, band_mask[low : low + chunk]),
+                (all_sum_keys, all_sum_values, sum_mask[low : low + chunk]),
+            )
         )
-
-        def compute(carry_in):
-            key_piece = lax.dynamic_slice_in_dim(all_sum_keys, start, step_rows, 0)
-            value_piece = lax.dynamic_slice_in_dim(all_sum_values, start, step_rows, 0)
-            gap = own_pos[:, None] - key_pos[None, :]
-            return combine_terms(
-                carry_in, block_terms(queries, key_piece, value_piece, gap >= BAND)
-            )
-
-        def keep_carry(carry_in):
-            return carry_in
-
-        return lax.cond(jnp.min(key_pos) + BAND <= newest, compute, keep_carry, carry)
-
-    far_part = lax.fori_loop(0, step_count, fold_block, initial)
-    merged = combine_terms(band_part, far_part)
-    heads_out = merged[2] / merged[1][:, :, None]
+    heads_out = jnp.concatenate(pieces, axis=1)
     attn = jnp.transpose(heads_out, (1, 0, 2)).reshape(tok_rows, width).astype(jnp.bfloat16)
     partial = jnp.dot(attn, out_weight, preferred_element_type=jnp.float32)
     return ring_reduce_scatter(partial, "head")

time: 254 us -> 199 us (0.78)
  the two profiles are of different devices: /device:TPU:38 before, /device:TPU:8 now
where the time goes in v4:
time: 199 us; the launch traced here: 198 us
  waiting for transfers between devices  67.1 us (34%)
  starting transfers between devices  42.2 us (21%)
  blocking collectives  32.4 us (16%)
  other arithmetic  19.7 us (10%)
  between operations  14 us (7%)
  local copies, waits for them, and re-layouts  12.3 us (6%)
  matrix products  10.5 us (5%)
    all_gather x1, blocking collectives, on_device(): gathered = lax.all_gather(my_half, 'cy', axis=0, tiled=True)  30.6 us
    ppermute x6, waiting for transfers between devices, ring_reduce_scatter(): lax.ppermute(up, axis, ahead).astype(jnp.float32)  29.1 us
    all_gather x1, waiting for transfers between devices, on_device(): gathered = lax.all_gather(gathered, 'cx', axis=0, tiled=True)  27.6 us
    ppermute x6, starting transfers between devices, ring_reduce_scatter(): lax.ppermute(up, axis, ahead).astype(jnp.float32)  18.6 us
    ppermute x5, starting transfers between devices, ring_reduce_scatter(): down_sum = lax.ppermute(down, axis, behind).astype(jnp.float32)  15.2 us
    ppermute x5, waiting for transfers between devices, ring_reduce_scatter(): down_sum = lax.ppermute(down, axis, behind).astype(jnp.float32)  10.4 us
    unnamed x14, local copies, waits for them, and re-layouts  6.58 us
    ppermute x2, starting transfers between devices, shifted(): lax.ppermute(value, axis, [(source, source + steps) for source in range(l...  6.31 us
  transfers between devices with their start and end apart: 15, of which 11 were waited for; matrix products, arithmetic and copies ran while one was open for 8% of the time, Pallas kernels for 0%

profile of v4, /device:TPU:8, one launch (start us, length us, event | category | flops | bytes accessed | tf_op | source)
XLA Modules:
  0.0 198.2 jit_solution(8122129068660465183)
XLA Ops:
  8.2 1.9 all_gather.9
  10.2 30.6 %all_gather.10 = bf16[1024,256]{0,1:T(8,128)(2,1)} all-gather(bf16[128,256]{0,1:T(8,128)(2,1)S(1)} %copy.50), channel_id=1, replica_groups=mesh['cx'=4,'cy'=8,'cc'=2,'head'=12] {'cy'}, dimensions={0}, use_global_device_ids=true | all-gather | bytes 589824 | tf_op jit(solution)/shard_map/all_gather | solution.py:136
  40.8 1.1 copy.24
  42.6 1.9 collective-permute-start
  44.5 1.1 copy.31
  46.3 4.4 %collective-permute-start.2 = (bf16[256,256]{0,1:T(8,128)(2,1)}, bf16[256,256]{0,1:T(8,128)(2,1)}, u32[]{:S(2)}, u32[]{:S(2)}) collective-permute-start(bf16[256,256]{0,1:T(8,128)(2,1)} %slice.35), channel_id=1, source_target_pairs={{0,12},{12,24},{24,36},{36,48},{48,60},{60,72},{72,84},{84,96},{96... | collective-permute-start | bytes 393224 | tf_op jit(solution)/shard_map/ppermute | solution.py:23
  51.1 2.3 %subtract_compare_fusion = pred[384,4096]{1,0:T(8,128)(4,1)} fusion(s32[4096]{0:T(1024)S(1)} %fusion.54, s32[384]{0:T(512)S(1)} %iota_add_fusion.1), kind=kLoop, calls=%fused_computation.4 | loop fusion | flops 3145728 | bytes 1590784 | tf_op jit(solution)/shard_map/ge | solution.py:145
  53.3 27.6 %all-gather.2.cloned.1.call-done = bf16[4096,256]{0,1:T(8,128)(2,1)} async-done(((bf16[1024,256]{0,1:T(8,128)(2,1)}), bf16[4096,256]{0,1:T(8,128)(2,1)}) %all-gather.2.cloned.1.call-update) | async-done | bytes 2097168 | tf_op jit(solution)/shard_map/all_gather | solution.py:137
  80.9 2.1 %collective-permute-start.1 = (bf16[4096,256]{0,1:T(8,128)(2,1)}, bf16[4096,256]{0,1:T(8,128)(2,1)}, u32[]{:S(2)}, u32[]{:S(2)}) collective-permute-start(bf16[4096,256]{0,1:T(8,128)(2,1)} %all-gather.2.cloned.1.call-done), channel_id=1, source_target_pairs={{0,12},{12,0},{1,13},{13,1},{2,14},{14,2},{3,15},{15,3},{4,16},{16... | collective-permute-start | bytes 6291464 | tf_op jit(solution)/shard_map/ppermute | solution.py:138
  83.0 2.4 %fusion.62 = (pred[192,4096]{1,0:T(8,128)(4,1)}, pred[192,4096]{1,0:T(8,128)(4,1)S(1)}) fusion(pred[384,4096]{1,0:T(8,128)(4,1)} %subtract_compare_fusion), kind=kLoop, calls=%fused_computation.106 | loop fusion | bytes 3145728 | tf_op jit(solution)/shard_map/slice | solution.py:153
  85.5 1.6 slice_bitcast_fusion.1
  87.1 1.0 pad_maximum_fusion
  89.1 1.3 fusion.66
  90.4 1.3 fusion.64
  91.7 3.1 %fusion.15 = (bf16[1,4096,256]{1,2,0:T(8,128)(2,1)S(1)}, bf16[1,4096,256]{1,2,0:T(8,128)(2,1)S(1)}) fusion(s32[]{:T(128)S(6)} %select_n.175, bf16[1,4096,256]{1,2,0:T(8,128)(2,1)} %bitcast.57, bf16[1,4096,256]{1,2,0:T(8,128)(2,1)} %bitcast.3, s32[]{:T(128)S(6)} %select_n.179), kind=kLoop, calls=%fused_computation.22 | loop fusion | flops 2097152 | bytes 8388616 | tf_op jit(solution)/shard_map/stack | solution.py:139
  94.9 1.8 fusion.67
  96.6 1.8 fusion.65
  98.4 1.2 fusion.6
  99.7 3.3 %fusion = (f32[2,192]{1,0:T(2,128)S(1)}, f32[2,192]{1,0:T(2,128)S(1)}) fusion(f32[2,192,4096]{2,1,0:T(8,128)S(1)} %get-tuple-element.30, f32[2,192]{1,0:T(2,128)S(1)} %max.14, pred[192,4096]{1,0:T(8,128)(4,1)S(1)} %copy-done.2, f32[2,192,4096]{2,1,0:T(8,128)S(1)} %get-tuple-element.26, f32[2,192]{1,0:T(2,128)S(1)} %max.15, ...), kind=kLoop, calls=%fused_computation.5 | loop fusion | flops 9436416 | bytes 14161920 | tf_op jit(solution)/shard_map/reduce_sum | solution.py:80
  102.9 1.3 fusion.4
  107.0 2.6 %copy-done.1 = f32[384,4096]{1,0:T(8,128)} copy-done((f32[384,4096]{1,0:T(8,128)}, f32[384,4096]{1,0:T(8,128)S(1)}, u32[]{:S(2)}) %copy-start.1) | copy-done | bytes 6291480
  109.7 3.6 %collective-permute-start.3 = (bf16[32,4096]{1,0:T(8,128)(2,1)S(1)}, bf16[32,4096]{1,0:T(8,128)(2,1)S(1)}, u32[]{:S(2)}, u32[]{:S(2)}) collective-permute-start(bf16[32,4096]{1,0:T(8,128)(2,1)S(1)} %get-tuple-element.13), channel_id=1, source_target_pairs={{0,1},{1,2},{2,3},{3,4},{4,5},{5,6},{6,7},{7,8},{8,9},{9,10},{10,1... | collective-permute-start | bytes 786440 | tf_op jit(solution)/shard_map/ppermute | solution.py:104
  113.3 5.0 %collective-permute-start.9 = (bf16[32,4096]{1,0:T(8,128)(2,1)S(1)}, bf16[32,4096]{1,0:T(8,128)(2,1)S(1)}, u32[]{:S(2)}, u32[]{:S(2)}) collective-permute-start(bf16[32,4096]{1,0:T(8,128)(2,1)S(1)} %get-tuple-element.14), channel_id=1, source_target_pairs={{0,11},{1,0},{2,1},{3,2},{4,3},{5,4},{6,5},{7,6},{8,7},{9,8},{10,9... | collective-permute-start | bytes 786440 | tf_op jit(solution)/shard_map/ppermute | solution.py:109
  118.2 5.0 %collective-permute-done.3 = bf16[32,4096]{1,0:T(8,128)(2,1)S(1)} collective-permute-done((bf16[32,4096]{1,0:T(8,128)(2,1)S(1)}, bf16[32,4096]{1,0:T(8,128)(2,1)S(1)}, u32[]{:S(2)}, u32[]{:S(2)}) %collective-permute-start.3) | collective-permute-done | bytes 262176 | tf_op jit(solution)/shard_map/ppermute | solution.py:104
  123.2 1.1 add_convert_fusion.9
  124.3 1.9 collective-permute-start.4
  126.3 9.3 %collective-permute-done.4 = bf16[32,4096]{1,0:T(8,128)(2,1)S(1)} collective-permute-done((bf16[32,4096]{1,0:T(8,128)(2,1)S(1)}, bf16[32,4096]{1,0:T(8,128)(2,1)S(1)}, u32[]{:S(2)}, u32[]{:S(2)}) %collective-permute-start.4) | collective-permute-done | bytes 262176 | tf_op jit(solution)/shard_map/ppermute | solution.py:104
  135.6 1.3 add_convert_fusion.8
  136.9 2.2 %collective-permute-start.10 = (bf16[32,4096]{1,0:T(8,128)(2,1)S(1)}, bf16[32,4096]{1,0:T(8,128)(2,1)S(1)}, u32[]{:S(2)}, u32[]{:S(2)}) collective-permute-start(bf16[32,4096]{1,0:T(8,128)(2,1)S(1)} %get-tuple-element.12), channel_id=1, source_target_pairs={{0,11},{1,0},{2,1},{3,2},{4,3},{5,4},{6,5},{7,6},{8,7},{9,8},{10,9... | collective-permute-start | bytes 786440 | tf_op jit(solution)/shard_map/ppermute | solution.py:109
  139.0 3.7 %collective-permute-start.5 = (bf16[32,4096]{1,0:T(8,128)(2,1)S(1)}, bf16[32,4096]{1,0:T(8,128)(2,1)S(1)}, u32[]{:S(2)}, u32[]{:S(2)}) collective-permute-start(bf16[32,4096]{1,0:T(8,128)(2,1)S(1)} %get-tuple-element.11), channel_id=1, source_target_pairs={{0,1},{1,2},{2,3},{3,4},{4,5},{5,6},{6,7},{7,8},{8,9},{9,10},{10,1... | collective-permute-start | bytes 786440 | tf_op jit(solution)/shard_map/ppermute | solution.py:104
  142.8 3.3 %collective-permute-done.10 = bf16[32,4096]{1,0:T(8,128)(2,1)S(1)} collective-permute-done((bf16[32,4096]{1,0:T(8,128)(2,1)S(1)}, bf16[32,4096]{1,0:T(8,128)(2,1)S(1)}, u32[]{:S(2)}, u32[]{:S(2)}) %collective-permute-start.10) | collective-permute-done | bytes 262176 | tf_op jit(solution)/shard_map/ppermute | solution.py:109
  146.0 3.1 %collective-permute-done.5 = bf16[32,4096]{1,0:T(8,128)(2,1)S(1)} collective-permute-done((bf16[32,4096]{1,0:T(8,128)(2,1)S(1)}, bf16[32,4096]{1,0:T(8,128)(2,1)S(1)}, u32[]{:S(2)}, u32[]{:S(2)}) %collective-permute-start.5) | collective-permute-done | bytes 262176 | tf_op jit(solution)/shard_map/ppermute | solution.py:104
  149.2 1.3 add_convert_fusion.7
  150.5 2.2 %collective-permute-start.11 = (bf16[32,4096]{1,0:T(8,128)(2,1)S(1)}, bf16[32,4096]{1,0:T(8,128)(2,1)S(1)}, u32[]{:S(2)}, u32[]{:S(2)}) collective-permute-start(bf16[32,4096]{1,0:T(8,128)(2,1)S(1)} %get-tuple-element.10), channel_id=1, source_target_pairs={{0,11},{1,0},{2,1},{3,2},{4,3},{5,4},{6,5},{7,6},{8,7},{9,8},{10,9... | collective-permute-start | bytes 786440 | tf_op jit(solution)/shard_map/ppermute | solution.py:109
  152.7 3.6 %collective-permute-start.6 = (bf16[32,4096]{1,0:T(8,128)(2,1)S(1)}, bf16[32,4096]{1,0:T(8,128)(2,1)S(1)}, u32[]{:S(2)}, u32[]{:S(2)}) collective-permute-start(bf16[32,4096]{1,0:T(8,128)(2,1)S(1)} %get-tuple-element.9), channel_id=1, source_target_pairs={{0,1},{1,2},{2,3},{3,4},{4,5},{5,6},{6,7},{7,8},{8,9},{9,10},{10,1... | collective-permute-start | bytes 786440 | tf_op jit(solution)/shard_map/ppermute | solution.py:104
  156.4 2.4 %collective-permute-done.11 = bf16[32,4096]{1,0:T(8,128)(2,1)S(1)} collective-permute-done((bf16[32,4096]{1,0:T(8,128)(2,1)S(1)}, bf16[32,4096]{1,0:T(8,128)(2,1)S(1)}, u32[]{:S(2)}, u32[]{:S(2)}) %collective-permute-start.11) | collective-permute-done | bytes 262176 | tf_op jit(solution)/shard_map/ppermute | solution.py:109
  158.7 3.5 %collective-permute-done.6 = bf16[32,4096]{1,0:T(8,128)(2,1)S(1)} collective-permute-done((bf16[32,4096]{1,0:T(8,128)(2,1)S(1)}, bf16[32,4096]{1,0:T(8,128)(2,1)S(1)}, u32[]{:S(2)}, u32[]{:S(2)}) %collective-permute-start.6) | collective-permute-done | bytes 262176 | tf_op jit(solution)/shard_map/ppermute | solution.py:104
  162.2 1.3 add_convert_fusion.6
  163.5 3.4 %collective-permute-start.12 = (bf16[32,4096]{1,0:T(8,128)(2,1)S(1)}, bf16[32,4096]{1,0:T(8,128)(2,1)S(1)}, u32[]{:S(2)}, u32[]{:S(2)}) collective-permute-start(bf16[32,4096]{1,0:T(8,128)(2,1)S(1)} %get-tuple-element.8), channel_id=1, source_target_pairs={{0,11},{1,0},{2,1},{3,2},{4,3},{5,4},{6,5},{7,6},{8,7},{9,8},{10,9... | collective-permute-start | bytes 786440 | tf_op jit(solution)/shard_map/ppermute | solution.py:109
  166.9 2.5 %collective-permute-start.7 = (bf16[32,4096]{1,0:T(8,128)(2,1)S(1)}, bf16[32,4096]{1,0:T(8,128)(2,1)S(1)}, u32[]{:S(2)}, u32[]{:S(2)}) collective-permute-start(bf16[32,4096]{1,0:T(8,128)(2,1)S(1)} %get-tuple-element.7), channel_id=1, source_target_pairs={{0,1},{1,2},{2,3},{3,4},{4,5},{5,6},{6,7},{7,8},{8,9},{9,10},{10,1... | collective-permute-start | bytes 786440 | tf_op jit(solution)/shard_map/ppermute | solution.py:104
  169.4 2.4 %collective-permute-done.12 = bf16[32,4096]{1,0:T(8,128)(2,1)S(1)} collective-permute-done((bf16[32,4096]{1,0:T(8,128)(2,1)S(1)}, bf16[32,4096]{1,0:T(8,128)(2,1)S(1)}, u32[]{:S(2)}, u32[]{:S(2)}) %collective-permute-start.12) | collective-permute-done | bytes 262176 | tf_op jit(solution)/shard_map/ppermute | solution.py:109
  171.8 4.6 %collective-permute-done.7 = bf16[32,4096]{1,0:T(8,128)(2,1)S(1)} collective-permute-done((bf16[32,4096]{1,0:T(8,128)(2,1)S(1)}, bf16[32,4096]{1,0:T(8,128)(2,1)S(1)}, u32[]{:S(2)}, u32[]{:S(2)}) %collective-permute-start.7) | collective-permute-done | bytes 262176 | tf_op jit(solution)/shard_map/ppermute | solution.py:104
  176.4 1.3 add_convert_fusion.5
  177.6 2.4 %collective-permute-start.13 = (bf16[32,4096]{1,0:T(8,128)(2,1)S(1)}, bf16[32,4096]{1,0:T(8,128)(2,1)S(1)}, u32[]{:S(2)}, u32[]{:S(2)}) collective-permute-start(bf16[32,4096]{1,0:T(8,128)(2,1)S(1)} %get-tuple-element.6), channel_id=1, source_target_pairs={{0,11},{1,0},{2,1},{3,2},{4,3},{5,4},{6,5},{7,6},{8,7},{9,8},{10,9... | collective-permute-start | bytes 786440 | tf_op jit(solution)/shard_map/ppermute | solution.py:109
  180.1 3.4 %collective-permute-start.8 = (bf16[32,4096]{1,0:T(8,128)(2,1)S(1)}, bf16[32,4096]{1,0:T(8,128)(2,1)S(1)}, u32[]{:S(2)}, u32[]{:S(2)}) collective-permute-start(bf16[32,4096]{1,0:T(8,128)(2,1)S(1)} %get-tuple-element.5), channel_id=1, source_target_pairs={{0,1},{1,2},{2,3},{3,4},{4,5},{5,6},{6,7},{7,8},{8,9},{9,10},{10,1... | collective-permute-start | bytes 786440 | tf_op jit(solution)/shard_map/ppermute | solution.py:104
  183.5 2.4 %collective-permute-done.13 = bf16[32,4096]{1,0:T(8,128)(2,1)S(1)} collective-permute-done((bf16[32,4096]{1,0:T(8,128)(2,1)S(1)}, bf16[32,4096]{1,0:T(8,128)(2,1)S(1)}, u32[]{:S(2)}, u32[]{:S(2)}) %collective-permute-start.13) | collective-permute-done | bytes 262176 | tf_op jit(solution)/shard_map/ppermute | solution.py:109
  185.9 3.6 %collective-permute-done.8 = bf16[32,4096]{1,0:T(8,128)(2,1)S(1)} collective-permute-done((bf16[32,4096]{1,0:T(8,128)(2,1)S(1)}, bf16[32,4096]{1,0:T(8,128)(2,1)S(1)}, u32[]{:S(2)}, u32[]{:S(2)}) %collective-permute-start.8) | collective-permute-done | bytes 262176 | tf_op jit(solution)/shard_map/ppermute | solution.py:104
  189.6 1.8 add_convert_fusion
  (40 shorter events, 7.3 us)
Async XLA Ops:
  6.5 99.4 %copy-start = (bf16[256,4096]{1,0:T(8,128)(2,1)S(1)}, bf16[256,4096]{1,0:T(8,128)(2,1)}, u32[]{:S(2)}) copy-start(bf16[256,4096]{1,0:T(8,128)(2,1)} %param.7) | copy-start | bytes 6291460
  6.5 74.4 %all-gather.2.cloned.1.call-start = ((), (), s32[]{:S(2)}) async-start(), calls=%async_computation | async-start | bytes 2621440 | tf_op jit(solution)/shard_map/all_gather | solution.py:137
  42.6 44.5 %collective-permute-start = (bf16[256,256]{0,1:T(8,128)(2,1)}, bf16[256,256]{0,1:T(8,128)(2,1)}, u32[]{:S(2)}, u32[]{:S(2)}) collective-permute-start(bf16[256,256]{0,1:T(8,128)(2,1)} %slice.33), channel_id=1, source_target_pairs={{0,12},{12,24},{24,36},{36,48},{48,60},{60,72},{72,84},{84,96},{96... | collective-permute-start | bytes 393224 | tf_op jit(solution)/shard_map/ppermute | solution.py:23
  46.3 41.9 %collective-permute-start.2 = (bf16[256,256]{0,1:T(8,128)(2,1)}, bf16[256,256]{0,1:T(8,128)(2,1)}, u32[]{:S(2)}, u32[]{:S(2)}) collective-permute-start(bf16[256,256]{0,1:T(8,128)(2,1)} %slice.35), channel_id=1, source_target_pairs={{0,12},{12,24},{24,36},{36,48},{48,60},{60,72},{72,84},{84,96},{96... | collective-permute-start | bytes 393224 | tf_op jit(solution)/shard_map/ppermute | solution.py:23
  80.9 10.8 %collective-permute-start.1 = (bf16[4096,256]{0,1:T(8,128)(2,1)}, bf16[4096,256]{0,1:T(8,128)(2,1)}, u32[]{:S(2)}, u32[]{:S(2)}) collective-permute-start(bf16[4096,256]{0,1:T(8,128)(2,1)} %all-gather.2.cloned.1.call-done), channel_id=1, source_target_pairs={{0,12},{12,0},{1,13},{13,1},{2,14},{14,2},{3,15},{15,3},{4,16},{16... | collective-permute-start | bytes 6291464 | tf_op jit(solution)/shard_map/ppermute | solution.py:138
  87.1 7.7 %copy-start.2 = (pred[192,4096]{1,0:T(8,128)(4,1)S(1)}, pred[192,4096]{1,0:T(8,128)(4,1)}, u32[]{:S(2)}) copy-start(pred[192,4096]{1,0:T(8,128)(4,1)} %get-tuple-element.17) | copy-start | bytes 2359300
  87.1 7.7 %copy-start.4 = (bf16[24,2,8,128]{3,2,1,0:T(8,128)(2,1)S(1)}, bf16[24,2,8,128]{3,2,1,0:T(8,128)(2,1)}, u32[]{:S(2)}) copy-start(bf16[24,2,8,128]{3,2,1,0:T(8,128)(2,1)} %get-tuple-element.21) | copy-start | bytes 294916
  94.8 1.8 copy-start.3
  107.0 2.6 %copy-start.1 = (f32[384,4096]{1,0:T(8,128)}, f32[384,4096]{1,0:T(8,128)S(1)}, u32[]{:S(2)}) copy-start(f32[384,4096]{1,0:T(8,128)S(1)} %fusion.68) | copy-start | bytes 18874372
  109.7 13.6 %collective-permute-start.3 = (bf16[32,4096]{1,0:T(8,128)(2,1)S(1)}, bf16[32,4096]{1,0:T(8,128)(2,1)S(1)}, u32[]{:S(2)}, u32[]{:S(2)}) collective-permute-start(bf16[32,4096]{1,0:T(8,128)(2,1)S(1)} %get-tuple-element.13), channel_id=1, source_target_pairs={{0,1},{1,2},{2,3},{3,4},{4,5},{5,6},{6,7},{7,8},{8,9},{9,10},{10,1... | collective-permute-start | bytes 786440 | tf_op jit(solution)/shard_map/ppermute | solution.py:104
  113.3 13.0 %collective-permute-start.9 = (bf16[32,4096]{1,0:T(8,128)(2,1)S(1)}, bf16[32,4096]{1,0:T(8,128)(2,1)S(1)}, u32[]{:S(2)}, u32[]{:S(2)}) collective-permute-start(bf16[32,4096]{1,0:T(8,128)(2,1)S(1)} %get-tuple-element.14), channel_id=1, source_target_pairs={{0,11},{1,0},{2,1},{3,2},{4,3},{5,4},{6,5},{7,6},{8,7},{9,8},{10,9... | collective-permute-start | bytes 786440 | tf_op jit(solution)/shard_map/ppermute | solution.py:109
  124.3 11.2 %collective-permute-start.4 = (bf16[32,4096]{1,0:T(8,128)(2,1)S(1)}, bf16[32,4096]{1,0:T(8,128)(2,1)S(1)}, u32[]{:S(2)}, u32[]{:S(2)}) collective-permute-start(bf16[32,4096]{1,0:T(8,128)(2,1)S(1)} %add_convert_fusion.9), channel_id=1, source_target_pairs={{0,1},{1,2},{2,3},{3,4},{4,5},{5,6},{6,7},{7,8},{8,9},{9,10},{10,1... | collective-permute-start | bytes 786440 | tf_op jit(solution)/shard_map/ppermute | solution.py:104
  136.9 9.2 %collective-permute-start.10 = (bf16[32,4096]{1,0:T(8,128)(2,1)S(1)}, bf16[32,4096]{1,0:T(8,128)(2,1)S(1)}, u32[]{:S(2)}, u32[]{:S(2)}) collective-permute-start(bf16[32,4096]{1,0:T(8,128)(2,1)S(1)} %get-tuple-element.12), channel_id=1, source_target_pairs={{0,11},{1,0},{2,1},{3,2},{4,3},{5,4},{6,5},{7,6},{8,7},{9,8},{10,9... | collective-permute-start | bytes 786440 | tf_op jit(solution)/shard_map/ppermute | solution.py:109
  139.0 10.2 %collective-permute-start.5 = (bf16[32,4096]{1,0:T(8,128)(2,1)S(1)}, bf16[32,4096]{1,0:T(8,128)(2,1)S(1)}, u32[]{:S(2)}, u32[]{:S(2)}) collective-permute-start(bf16[32,4096]{1,0:T(8,128)(2,1)S(1)} %get-tuple-element.11), channel_id=1, source_target_pairs={{0,1},{1,2},{2,3},{3,4},{4,5},{5,6},{6,7},{7,8},{8,9},{9,10},{10,1... | collective-permute-start | bytes 786440 | tf_op jit(solution)/shard_map/ppermute | solution.py:104
  150.5 8.3 %collective-permute-start.11 = (bf16[32,4096]{1,0:T(8,128)(2,1)S(1)}, bf16[32,4096]{1,0:T(8,128)(2,1)S(1)}, u32[]{:S(2)}, u32[]{:S(2)}) collective-permute-start(bf16[32,4096]{1,0:T(8,128)(2,1)S(1)} %get-tuple-element.10), channel_id=1, source_target_pairs={{0,11},{1,0},{2,1},{3,2},{4,3},{5,4},{6,5},{7,6},{8,7},{9,8},{10,9... | collective-permute-start | bytes 786440 | tf_op jit(solution)/shard_map/ppermute | solution.py:109
  152.7 9.5 %collective-permute-start.6 = (bf16[32,4096]{1,0:T(8,128)(2,1)S(1)}, bf16[32,4096]{1,0:T(8,128)(2,1)S(1)}, u32[]{:S(2)}, u32[]{:S(2)}) collective-permute-start(bf16[32,4096]{1,0:T(8,128)(2,1)S(1)} %get-tuple-element.9), channel_id=1, source_target_pairs={{0,1},{1,2},{2,3},{3,4},{4,5},{5,6},{6,7},{7,8},{8,9},{9,10},{10,1... | collective-permute-start | bytes 786440 | tf_op jit(solution)/shard_map/ppermute | solution.py:104
  163.5 8.3 %collective-permute-start.12 = (bf16[32,4096]{1,0:T(8,128)(2,1)S(1)}, bf16[32,4096]{1,0:T(8,128)(2,1)S(1)}, u32[]{:S(2)}, u32[]{:S(2)}) collective-permute-start(bf16[32,4096]{1,0:T(8,128)(2,1)S(1)} %get-tuple-element.8), channel_id=1, source_target_pairs={{0,11},{1,0},{2,1},{3,2},{4,3},{5,4},{6,5},{7,6},{8,7},{9,8},{10,9... | collective-permute-start | bytes 786440 | tf_op jit(solution)/shard_map/ppermute | solution.py:109
  166.9 9.5 %collective-permute-start.7 = (bf16[32,4096]{1,0:T(8,128)(2,1)S(1)}, bf16[32,4096]{1,0:T(8,128)(2,1)S(1)}, u32[]{:S(2)}, u32[]{:S(2)}) collective-permute-start(bf16[32,4096]{1,0:T(8,128)(2,1)S(1)} %get-tuple-element.7), channel_id=1, source_target_pairs={{0,1},{1,2},{2,3},{3,4},{4,5},{5,6},{6,7},{7,8},{8,9},{9,10},{10,1... | collective-permute-start | bytes 786440 | tf_op jit(solution)/shard_map/ppermute | solution.py:104
  177.6 8.3 %collective-permute-start.13 = (bf16[32,4096]{1,0:T(8,128)(2,1)S(1)}, bf16[32,4096]{1,0:T(8,128)(2,1)S(1)}, u32[]{:S(2)}, u32[]{:S(2)}) collective-permute-start(bf16[32,4096]{1,0:T(8,128)(2,1)S(1)} %get-tuple-element.6), channel_id=1, source_target_pairs={{0,11},{1,0},{2,1},{3,2},{4,3},{5,4},{6,5},{7,6},{8,7},{9,8},{10,9... | collective-permute-start | bytes 786440 | tf_op jit(solution)/shard_map/ppermute | solution.py:109
  180.1 9.5 %collective-permute-start.8 = (bf16[32,4096]{1,0:T(8,128)(2,1)S(1)}, bf16[32,4096]{1,0:T(8,128)(2,1)S(1)}, u32[]{:S(2)}, u32[]{:S(2)}) collective-permute-start(bf16[32,4096]{1,0:T(8,128)(2,1)S(1)} %get-tuple-element.5), channel_id=1, source_target_pairs={{0,1},{1,2},{2,3},{3,4},{4,5},{5,6},{6,7},{7,8},{8,9},{9,10},{10,1... | collective-permute-start | bytes 786440 | tf_op jit(solution)/shard_map/ppermute | solution.py:104
Sparse Core Ops, SparseCore 0:
  40.9 39.9 all-gather.1

commit v5 on v4

v5 whole, which is shorter than its diff:
```python
import math

import jax
import jax.numpy as jnp
from jax import lax
from jax.sharding import Mesh, PartitionSpec as P

HEAD_DIM = 128
BAND = 256
SUMMARY = 128
CTX = ("cx", "cy", "cc")
CORE = "cc"
QUERY_CHUNKS = 2


LOW_SCORE = -1e30


def shifted(value, axis, steps):
    count = lax.axis_size(axis)
    leading, last = (max(0, -steps), min(count, count - steps))
    return lax.ppermute(value, axis, [(source, source + steps) for source in range(leading, last)])


def combine_terms(first, second):
    top_score = jnp.maximum(first[0], second[0])
    first_factor = jnp.exp(first[0] - top_score)
    second_factor = jnp.exp(second[0] - top_score)
    totals = first[1] * first_factor + second[1] * second_factor
    weighted = first[2] * first_factor[:, :, None] + second[2] * second_factor[:, :, None]
    return (top_score, totals, weighted)


def attend(query_rows, keys, values, allowed):
    scale = 1.0 / math.sqrt(HEAD_DIM)
    rows, width = query_rows.shape
    heads = width // HEAD_DIM
    q = query_rows.reshape(rows, heads, HEAD_DIM)
    k = keys.reshape(keys.shape[0], heads, HEAD_DIM)
    s = jnp.einsum("qhd,khd->hqk", q, k, preferred_element_type=jnp.float32) * scale
    s = jnp.where(allowed[None], s, LOW_SCORE)
    top = s.max(axis=2)
    w = jnp.where(allowed[None], jnp.exp(s - top[:, :, None]), 0.0)
    v = values.reshape(values.shape[0], heads, HEAD_DIM)
    summed = jnp.einsum(
        "hqk,khd->hqd", w.astype(jnp.bfloat16), v, preferred_element_type=jnp.float32
    )
    return top, w.sum(axis=2), summed


def ring_reduce_scatter(partial, axis):
    count = lax.axis_size(axis)
    me = lax.axis_index(axis)
    rows = partial.shape[0] // count
    left_hops = count // 2
    right_hops = count - 1 - left_hops
    ahead = [(source, (source + 1) % count) for source in range(count)]
    behind = [(source, (source - 1) % count) for source in range(count)]

    def piece(block):
        return lax.dynamic_slice_in_dim(partial, (block % count) * rows, rows, 0)

    up = piece(me + left_hops).astype(jnp.bfloat16)
    down = piece(me - right_hops).astype(jnp.bfloat16)
    up_sum = down_sum = None
    for step in range(left_hops):
        up_sum = lax.ppermute(up, axis, ahead).astype(jnp.float32) + piece(
            me + left_hops - 1 - step
        )
        up = up_sum.astype(jnp.bfloat16)
        if step < right_hops:
            down_sum = lax.ppermute(down, axis, behind).astype(jnp.float32)
            if step < right_hops - 1:
                down_sum = down_sum + piece(me - right_hops + 1 + step)
                down = down_sum.astype(jnp.bfloat16)
    return (up_sum + down_sum).astype(jnp.bfloat16)


def layer(queries, keys, values, out_weight):
    tok_rows, width = queries.shape
    half_sum = SUMMARY // 2
    my_index = lax.axis_index(CTX)
    rim_keys, rim_values = shifted((keys[tok_rows - BAND :], values[tok_rows - BAND :]), CTX, 1)
    band_keys = jnp.concatenate([rim_keys, keys], axis=0)
    band_values = jnp.concatenate([rim_values, values], axis=0)
    own_pos = my_index * tok_rows + jnp.arange(tok_rows, dtype=jnp.int32)
    band_pos = my_index * tok_rows - BAND + jnp.arange(tok_rows + BAND, dtype=jnp.int32)
    band_gap = own_pos[:, None] - band_pos[None, :]
    band_mask = (band_gap >= 0) & (band_gap < BAND) & (band_pos[None, :] >= 0)
    chunk = tok_rows // QUERY_CHUNKS
    near = [
        attend(queries[low : low + chunk], band_keys, band_values, band_mask[low : low + chunk])
        for low in range(0, tok_rows, chunk)
    ]
    core = lax.axis_index(CORE)
    sum_start = jnp.where(my_index % 2 == 0, tok_rows - half_sum, 0).astype(jnp.int32)
    own_keys = lax.dynamic_slice_in_dim(keys, sum_start, half_sum, 0)
    own_values = lax.dynamic_slice_in_dim(values, sum_start, half_sum, 0)
    chip_rows = lax.all_gather(
        jnp.concatenate([own_keys, own_values], axis=1), CORE, axis=0, tiled=True
    )
    my_half = lax.dynamic_slice_in_dim(chip_rows, core * width, width, 1)
    ring = lax.axis_size("cy")
    gathered = my_half
    shift = 1
    while shift < ring:
        moved = lax.ppermute(gathered, "cy", [(j, (j + shift) % ring) for j in range(ring)])
        gathered = jnp.concatenate([gathered, moved], axis=0)
        shift *= 2
    gathered = lax.all_gather(gathered, "cx", axis=0, tiled=True)
    other = lax.ppermute(gathered, CORE, [(0, 1), (1, 0)])
    both = jnp.stack([gathered, other])
    all_sum_keys = both[core]
    all_sum_values = both[1 - core]
    index = jnp.arange(all_sum_keys.shape[0], dtype=jnp.int32)
    across = index // (SUMMARY * ring)
    back = (index // SUMMARY) % ring
    chip = across * ring + (lax.axis_index("cy") - back) % ring
    key_pos = chip * 2 * tok_rows + tok_rows - half_sum + index % SUMMARY
    sum_mask = own_pos[:, None] - key_pos[None, :] >= BAND
    pieces = []
    for low in range(0, tok_rows, chunk):
        rows = slice(low, low + chunk)
        far = attend(queries[rows], all_sum_keys, all_sum_values, sum_mask[rows])
        merged = combine_terms(near[low // chunk], far)
        pieces.append(merged[2] / merged[1][:, :, None])
    heads_out = jnp.concatenate(pieces, axis=1)
    attn = jnp.transpose(heads_out, (1, 0, 2)).reshape(tok_rows, width).astype(jnp.bfloat16)
    partial = jnp.dot(attn, out_weight, preferred_element_type=jnp.float32)
    return ring_reduce_scatter(partial, "head")


def solution(mesh):
    ctx_size, head_size = mesh.devices.shape
    split = mesh.devices.reshape(ctx_size // 16, 8, 2, head_size)
    fine = Mesh(split, ("cx", "cy", "cc", "head"))
    placed = (P(CTX, "head"), P(CTX, "head"), P(CTX, "head"), P("head", None))
    return jax.shard_map(
        layer, mesh=fine, in_specs=placed, out_specs=P(CTX + ("head",), None), check_vma=False
    )
```

time: 199 us -> 210 us (1.055)
  blocking collectives: 32.4 us -> 1.89 us
  waiting for transfers between devices: 67.1 us -> 97.5 us
  starting transfers between devices: 42.2 us -> 52.5 us
    ppermute x1 -> x4, waiting for transfers between devices: 0.01 us -> 32.7 us  [the longest x3 32.7 us: layer(): lax.ppermute(gathered, 'cy', [(j, (j + shift) % ring) for j in range(ring)])]
    all_gather x2 -> x1, blocking collectives: 32.4 us -> 1.89 us  [layer(): lax.all_gather(jnp.concatenate([own_keys, own_values], axis=1), CORE, axi...]
    ppermute x5, starting transfers between devices: 15.2 us -> 22.7 us  [ring_reduce_scatter(): down_sum = lax.ppermute(down, axis, behind).astype(jnp.float32)]
    ppermute x1 -> x4, starting transfers between devices: 2.09 us -> 9.44 us  [the longest x3 7.35 us: layer(): lax.ppermute(gathered, 'cy', [(j, (j + shift) % ring) for j in range(ring)])]
    ppermute x6, starting transfers between devices: 18.6 us -> 15.9 us  [ring_reduce_scatter(): lax.ppermute(up, axis, ahead).astype(jnp.float32)]
    ppermute x5, waiting for transfers between devices: 10.4 us -> 7.76 us  [ring_reduce_scatter(): down_sum = lax.ppermute(down, axis, behind).astype(jnp.float32)]
    unnamed x14 -> x16, local copies, waits for them, and re-layouts: 6.58 us -> 6.61 us
  transfers between devices with their start and end apart: 15 -> 18, of which waited for: 11 -> 14; matrix products, arithmetic and copies ran while one was open for 8% -> 8% of each run, Pallas kernels for 0% -> 0%
where the time goes in v5:
time: 210 us; the launch traced here: 209 us
  waiting for transfers between devices  97.5 us (46%)
  starting transfers between devices  52.5 us (25%)
  other arithmetic  20.4 us (10%)
  between operations  14 us (7%)
  local copies, waits for them, and re-layouts  12.3 us (6%)
  matrix products  10.6 us (5%)
    ppermute x3, waiting for transfers between devices, layer(): lax.ppermute(gathered, 'cy', [(j, (j + shift) % ring) for j in range(ring)])  32.7 us
    all_gather x1, waiting for transfers between devices, layer(): gathered = lax.all_gather(gathered, 'cx', axis=0, tiled=True)  29.4 us
    ppermute x6, waiting for transfers between devices, ring_reduce_scatter(): lax.ppermute(up, axis, ahead).astype(jnp.float32)  27.6 us
    ppermute x5, starting transfers between devices, ring_reduce_scatter(): down_sum = lax.ppermute(down, axis, behind).astype(jnp.float32)  22.7 us
    ppermute x6, starting transfers between devices, ring_reduce_scatter(): lax.ppermute(up, axis, ahead).astype(jnp.float32)  15.9 us
    ppermute x5, waiting for transfers between devices, ring_reduce_scatter(): down_sum = lax.ppermute(down, axis, behind).astype(jnp.float32)  7.76 us
    ppermute x3, starting transfers between devices, layer(): lax.ppermute(gathered, 'cy', [(j, (j + shift) % ring) for j in range(ring)])  7.35 us
    unnamed x16, local copies, waits for them, and re-layouts  6.61 us
  transfers between devices with their start and end apart: 18, of which 14 were waited for; matrix products, arithmetic and copies ran while one was open for 8% of the time, Pallas kernels for 0%

profile of v5, /device:TPU:8, one launch (start us, length us, event | category | flops | bytes accessed | tf_op | source)
XLA Modules:
  0.0 209.2 jit_solution(11703091901659825004)
XLA Ops:
  8.2 1.9 all_gather.6
  10.2 3.5 %collective-permute-start.2 = (bf16[128,256]{0,1:T(8,128)(2,1)S(1)}, bf16[128,256]{0,1:T(8,128)(2,1)S(1)}, u32[]{:S(2)}, u32[]{:S(2)}) collective-permute-start(bf16[128,256]{0,1:T(8,128)(2,1)S(1)} %copy.50), channel_id=1, source_target_pairs={{0,24},{24,48},{48,72},{72,96},{96,120},{120,144},{144,168},{168,0... | collective-permute-start | bytes 196616 | tf_op jit(solution)/shard_map/ppermute | solution.py:107
  13.7 10.3 %collective-permute-done.2 = bf16[128,256]{0,1:T(8,128)(2,1)S(1)} collective-permute-done((bf16[128,256]{0,1:T(8,128)(2,1)S(1)}, bf16[128,256]{0,1:T(8,128)(2,1)S(1)}, u32[]{:S(2)}, u32[]{:S(2)}) %collective-permute-start.2) | collective-permute-done | bytes 65568 | tf_op jit(solution)/shard_map/ppermute | solution.py:107
  24.0 1.9 collective-permute-start.3
  25.9 7.2 %collective-permute-done.3 = bf16[256,256]{0,1:T(8,128)(2,1)S(1)} collective-permute-done((bf16[256,256]{0,1:T(8,128)(2,1)S(1)}, bf16[256,256]{0,1:T(8,128)(2,1)S(1)}, u32[]{:S(2)}, u32[]{:S(2)}) %collective-permute-start.3) | collective-permute-done | bytes 131104 | tf_op jit(solution)/shard_map/ppermute | solution.py:107
  33.1 1.9 collective-permute-start.4
  35.1 15.3 %collective-permute-done.4 = bf16[512,256]{0,1:T(8,128)(2,1)S(1)} collective-permute-done((bf16[512,256]{0,1:T(8,128)(2,1)S(1)}, bf16[512,256]{0,1:T(8,128)(2,1)S(1)}, u32[]{:S(2)}, u32[]{:S(2)}) %collective-permute-start.4) | collective-permute-done | bytes 262176 | tf_op jit(solution)/shard_map/ppermute | solution.py:107
  53.0 1.9 collective-permute-start
  56.6 2.6 %collective-permute-start.1 = (bf16[256,256]{0,1:T(8,128)(2,1)}, bf16[256,256]{0,1:T(8,128)(2,1)}, u32[]{:S(2)}, u32[]{:S(2)}) collective-permute-start(bf16[256,256]{0,1:T(8,128)(2,1)} %slice.36), channel_id=1, source_target_pairs={{0,12},{12,24},{24,36},{36,48},{48,60},{60,72},{72,84},{84,96},{96... | collective-permute-start | bytes 393224 | tf_op jit(solution)/shard_map/ppermute | solution.py:22
  59.7 2.3 %subtract_compare_fusion = pred[384,4096]{1,0:T(8,128)(4,1)} fusion(s32[4096]{0:T(1024)S(1)} %fusion.62, s32[384]{0:T(512)S(1)} %iota_add_fusion.1), kind=kLoop, calls=%fused_computation.4 | loop fusion | flops 3145728 | bytes 1590784 | tf_op jit(solution)/shard_map/ge | solution.py:120
  62.0 29.4 %all-gather.2.cloned.1.call-done = bf16[4096,256]{0,1:T(8,128)(2,1)} async-done(((bf16[1024,256]{0,1:T(8,128)(2,1)}), bf16[4096,256]{0,1:T(8,128)(2,1)}) %all-gather.2.cloned.1.call-update) | async-done | bytes 2097168 | tf_op jit(solution)/shard_map/all_gather | solution.py:110
  91.4 2.1 collective-permute-start.5
  93.5 2.4 %fusion.81 = (pred[192,4096]{1,0:T(8,128)(4,1)S(1)}, pred[192,4096]{1,0:T(8,128)(4,1)}) fusion(pred[384,4096]{1,0:T(8,128)(4,1)} %subtract_compare_fusion), kind=kLoop, calls=%fused_computation.133 | loop fusion | bytes 3145728 | tf_op jit(solution)/shard_map/slice | solution.py:124
  96.0 1.6 slice_bitcast_fusion.1
  99.6 1.3 fusion.86
  101.0 1.4 fusion.84
  103.0 2.8 %fusion.15 = (bf16[1,4096,256]{1,2,0:T(8,128)(2,1)S(1)}, bf16[1,4096,256]{1,2,0:T(8,128)(2,1)S(1)}) fusion(s32[]{:T(128)S(6)} %select_n.184, bf16[1,4096,256]{1,2,0:T(8,128)(2,1)S(1)} %bitcast.57, bf16[1,4096,256]{1,2,0:T(8,128)(2,1)} %bitcast.4, s32[]{:T(128)S(6)} %select_n.187), kind=kLoop, calls=%fused_computation.22 | loop fusion | flops 2097152 | bytes 8388616 | tf_op jit(solution)/shard_map/stack | solution.py:112
  105.9 1.8 fusion.83
  107.6 1.8 fusion.85
  109.4 3.3 %fusion = (f32[2,192]{1,0:T(2,128)S(1)}, f32[2,192]{1,0:T(2,128)S(1)}) fusion(f32[2,192,4096]{2,1,0:T(8,128)S(1)} %get-tuple-element.34, f32[2,192]{1,0:T(2,128)S(1)} %get-tuple-element.33, pred[192,4096]{1,0:T(8,128)(4,1)S(1)} %get-tuple-element.23, f32[2,192,4096]{2,1,0:T(8,128)S(1)} %get-tuple-element.30, f32[2,192]{1,0:T(2,128)S(1)} %get-tuple-element.29, ...), kind=kLoop, calls=%fused_computation.5 | loop fusion | flops 9436416 | bytes 14161920 | tf_op jit(solution)/shard_map/reduce_sum | solution.py:48
  112.7 1.2 fusion.27
  114.0 1.3 fusion.24
  117.3 2.7 %copy-done.1 = f32[384,4096]{1,0:T(8,128)} copy-done((f32[384,4096]{1,0:T(8,128)}, f32[384,4096]{1,0:T(8,128)S(1)}, u32[]{:S(2)}) %copy-start.1) | copy-done | bytes 6291480
  120.0 3.6 %collective-permute-start.6 = (bf16[32,4096]{1,0:T(8,128)(2,1)S(1)}, bf16[32,4096]{1,0:T(8,128)(2,1)S(1)}, u32[]{:S(2)}, u32[]{:S(2)}) collective-permute-start(bf16[32,4096]{1,0:T(8,128)(2,1)S(1)} %get-tuple-element.19), channel_id=1, source_target_pairs={{0,1},{1,2},{2,3},{3,4},{4,5},{5,6},{6,7},{7,8},{8,9},{9,10},{10,1... | collective-permute-start | bytes 786440 | tf_op jit(solution)/shard_map/ppermute | solution.py:67
  123.6 5.0 %collective-permute-start.12 = (bf16[32,4096]{1,0:T(8,128)(2,1)S(1)}, bf16[32,4096]{1,0:T(8,128)(2,1)S(1)}, u32[]{:S(2)}, u32[]{:S(2)}) collective-permute-start(bf16[32,4096]{1,0:T(8,128)(2,1)S(1)} %get-tuple-element.20), channel_id=1, source_target_pairs={{0,11},{1,0},{2,1},{3,2},{4,3},{5,4},{6,5},{7,6},{8,7},{9,8},{10,9... | collective-permute-start | bytes 786440 | tf_op jit(solution)/shard_map/ppermute | solution.py:72
  128.6 5.0 %collective-permute-done.6 = bf16[32,4096]{1,0:T(8,128)(2,1)S(1)} collective-permute-done((bf16[32,4096]{1,0:T(8,128)(2,1)S(1)}, bf16[32,4096]{1,0:T(8,128)(2,1)S(1)}, u32[]{:S(2)}, u32[]{:S(2)}) %collective-permute-start.6) | collective-permute-done | bytes 262176 | tf_op jit(solution)/shard_map/ppermute | solution.py:67
  134.7 1.9 collective-permute-start.7
  136.7 9.3 %collective-permute-done.7 = bf16[32,4096]{1,0:T(8,128)(2,1)S(1)} collective-permute-done((bf16[32,4096]{1,0:T(8,128)(2,1)S(1)}, bf16[32,4096]{1,0:T(8,128)(2,1)S(1)}, u32[]{:S(2)}, u32[]{:S(2)}) %collective-permute-start.7) | collective-permute-done | bytes 262176 | tf_op jit(solution)/shard_map/ppermute | solution.py:67
  145.9 1.3 add_convert_fusion.8
  147.2 1.9 collective-permute-start.8
  149.1 5.1 %collective-permute-start.13 = (bf16[32,4096]{1,0:T(8,128)(2,1)S(1)}, bf16[32,4096]{1,0:T(8,128)(2,1)S(1)}, u32[]{:S(2)}, u32[]{:S(2)}) collective-permute-start(bf16[32,4096]{1,0:T(8,128)(2,1)S(1)} %get-tuple-element.18), channel_id=1, source_target_pairs={{0,11},{1,0},{2,1},{3,2},{4,3},{5,4},{6,5},{7,6},{8,7},{9,8},{10,9... | collective-permute-start | bytes 786440 | tf_op jit(solution)/shard_map/ppermute | solution.py:72
  154.3 3.3 %collective-permute-done.8 = bf16[32,4096]{1,0:T(8,128)(2,1)S(1)} collective-permute-done((bf16[32,4096]{1,0:T(8,128)(2,1)S(1)}, bf16[32,4096]{1,0:T(8,128)(2,1)S(1)}, u32[]{:S(2)}, u32[]{:S(2)}) %collective-permute-start.8) | collective-permute-done | bytes 262176 | tf_op jit(solution)/shard_map/ppermute | solution.py:67
  158.8 1.3 add_convert_fusion.7
  160.1 1.9 collective-permute-start.9
  162.0 5.6 %collective-permute-start.14 = (bf16[32,4096]{1,0:T(8,128)(2,1)S(1)}, bf16[32,4096]{1,0:T(8,128)(2,1)S(1)}, u32[]{:S(2)}, u32[]{:S(2)}) collective-permute-start(bf16[32,4096]{1,0:T(8,128)(2,1)S(1)} %get-tuple-element.16), channel_id=1, source_target_pairs={{0,11},{1,0},{2,1},{3,2},{4,3},{5,4},{6,5},{7,6},{8,7},{9,8},{10,9... | collective-permute-start | bytes 786440 | tf_op jit(solution)/shard_map/ppermute | solution.py:72
  167.6 2.4 %collective-permute-done.9 = bf16[32,4096]{1,0:T(8,128)(2,1)S(1)} collective-permute-done((bf16[32,4096]{1,0:T(8,128)(2,1)S(1)}, bf16[32,4096]{1,0:T(8,128)(2,1)S(1)}, u32[]{:S(2)}, u32[]{:S(2)}) %collective-permute-start.9) | collective-permute-done | bytes 262176 | tf_op jit(solution)/shard_map/ppermute | solution.py:67
  170.0 1.4 collective-permute-done.14
  171.5 1.3 add_convert_fusion.6
  172.8 4.6 %collective-permute-start.10 = (bf16[32,4096]{1,0:T(8,128)(2,1)S(1)}, bf16[32,4096]{1,0:T(8,128)(2,1)S(1)}, u32[]{:S(2)}, u32[]{:S(2)}) collective-permute-start(bf16[32,4096]{1,0:T(8,128)(2,1)S(1)} %get-tuple-element.13), channel_id=1, source_target_pairs={{0,1},{1,2},{2,3},{3,4},{4,5},{5,6},{6,7},{7,8},{8,9},{9,10},{10,1... | collective-permute-start | bytes 786440 | tf_op jit(solution)/shard_map/ppermute | solution.py:67
  177.4 2.9 %collective-permute-start.15 = (bf16[32,4096]{1,0:T(8,128)(2,1)S(1)}, bf16[32,4096]{1,0:T(8,128)(2,1)S(1)}, u32[]{:S(2)}, u32[]{:S(2)}) collective-permute-start(bf16[32,4096]{1,0:T(8,128)(2,1)S(1)} %get-tuple-element.14), channel_id=1, source_target_pairs={{0,11},{1,0},{2,1},{3,2},{4,3},{5,4},{6,5},{7,6},{8,7},{9,8},{10,9... | collective-permute-start | bytes 786440 | tf_op jit(solution)/shard_map/ppermute | solution.py:72
  180.3 2.4 %collective-permute-done.10 = bf16[32,4096]{1,0:T(8,128)(2,1)S(1)} collective-permute-done((bf16[32,4096]{1,0:T(8,128)(2,1)S(1)}, bf16[32,4096]{1,0:T(8,128)(2,1)S(1)}, u32[]{:S(2)}, u32[]{:S(2)}) %collective-permute-start.10) | collective-permute-done | bytes 262176 | tf_op jit(solution)/shard_map/ppermute | solution.py:67
  182.7 3.0 %collective-permute-done.15 = bf16[32,4096]{1,0:T(8,128)(2,1)S(1)} collective-permute-done((bf16[32,4096]{1,0:T(8,128)(2,1)S(1)}, bf16[32,4096]{1,0:T(8,128)(2,1)S(1)}, u32[]{:S(2)}, u32[]{:S(2)}) %collective-permute-start.15) | collective-permute-done | bytes 262176 | tf_op jit(solution)/shard_map/ppermute | solution.py:72
  185.7 1.3 add_convert_fusion.5
  186.9 4.1 %collective-permute-start.16 = (bf16[32,4096]{1,0:T(8,128)(2,1)S(1)}, bf16[32,4096]{1,0:T(8,128)(2,1)S(1)}, u32[]{:S(2)}, u32[]{:S(2)}) collective-permute-start(bf16[32,4096]{1,0:T(8,128)(2,1)S(1)} %get-tuple-element.12), channel_id=1, source_target_pairs={{0,11},{1,0},{2,1},{3,2},{4,3},{5,4},{6,5},{7,6},{8,7},{9,8},{10,9... | collective-permute-start | bytes 786440 | tf_op jit(solution)/shard_map/ppermute | solution.py:72
  191.1 1.9 collective-permute-start.11
  193.0 2.2 %collective-permute-done.16 = bf16[32,4096]{1,0:T(8,128)(2,1)S(1)} collective-permute-done((bf16[32,4096]{1,0:T(8,128)(2,1)S(1)}, bf16[32,4096]{1,0:T(8,128)(2,1)S(1)}, u32[]{:S(2)}, u32[]{:S(2)}) %collective-permute-start.16) | collective-permute-done | bytes 262176 | tf_op jit(solution)/shard_map/ppermute | solution.py:72
  195.2 5.3 %collective-permute-done.11 = bf16[32,4096]{1,0:T(8,128)(2,1)S(1)} collective-permute-done((bf16[32,4096]{1,0:T(8,128)(2,1)S(1)}, bf16[32,4096]{1,0:T(8,128)(2,1)S(1)}, u32[]{:S(2)}, u32[]{:S(2)}) %collective-permute-start.11) | collective-permute-done | bytes 262176 | tf_op jit(solution)/shard_map/ppermute | solution.py:67
  200.5 1.8 add_convert_fusion
  (48 shorter events, 13.7 us)
Async XLA Ops:
  6.5 109.8 %copy-start = (bf16[256,4096]{1,0:T(8,128)(2,1)S(1)}, bf16[256,4096]{1,0:T(8,128)(2,1)}, u32[]{:S(2)}) copy-start(bf16[256,4096]{1,0:T(8,128)(2,1)} %param.7) | copy-start | bytes 6291460
  6.5 84.9 %all-gather.2.cloned.1.call-start = ((), (), s32[]{:S(2)}) async-start(), calls=%async_computation | async-start | bytes 2621440 | tf_op jit(solution)/shard_map/all_gather | solution.py:110
  10.2 13.7 %collective-permute-start.2 = (bf16[128,256]{0,1:T(8,128)(2,1)S(1)}, bf16[128,256]{0,1:T(8,128)(2,1)S(1)}, u32[]{:S(2)}, u32[]{:S(2)}) collective-permute-start(bf16[128,256]{0,1:T(8,128)(2,1)S(1)} %copy.50), channel_id=1, source_target_pairs={{0,24},{24,48},{48,72},{72,96},{96,120},{120,144},{144,168},{168,0... | collective-permute-start | bytes 196616 | tf_op jit(solution)/shard_map/ppermute | solution.py:107
  24.0 9.1 %collective-permute-start.3 = (bf16[256,256]{0,1:T(8,128)(2,1)S(1)}, bf16[256,256]{0,1:T(8,128)(2,1)S(1)}, u32[]{:S(2)}, u32[]{:S(2)}) collective-permute-start(bf16[256,256]{0,1:T(8,128)(2,1)S(1)} %pad_maximum_fusion.4), channel_id=1, source_target_pairs={{0,48},{24,72},{48,96},{72,120},{96,144},{120,168},{144,0},{168,24... | collective-permute-start | bytes 393224 | tf_op jit(solution)/shard_map/ppermute | solution.py:107
  33.1 17.2 %collective-permute-start.4 = (bf16[512,256]{0,1:T(8,128)(2,1)S(1)}, bf16[512,256]{0,1:T(8,128)(2,1)S(1)}, u32[]{:S(2)}, u32[]{:S(2)}) collective-permute-start(bf16[512,256]{0,1:T(8,128)(2,1)S(1)} %pad_maximum_fusion.3), channel_id=1, source_target_pairs={{0,96},{24,120},{48,144},{72,168},{96,0},{120,24},{144,48},{168,72... | collective-permute-start | bytes 786440 | tf_op jit(solution)/shard_map/ppermute | solution.py:107
  53.0 44.6 %collective-permute-start = (bf16[256,256]{0,1:T(8,128)(2,1)}, bf16[256,256]{0,1:T(8,128)(2,1)}, u32[]{:S(2)}, u32[]{:S(2)}) collective-permute-start(bf16[256,256]{0,1:T(8,128)(2,1)} %slice.35), channel_id=1, source_target_pairs={{0,12},{12,24},{24,36},{36,48},{48,60},{60,72},{72,84},{84,96},{96... | collective-permute-start | bytes 393224 | tf_op jit(solution)/shard_map/ppermute | solution.py:22
  56.6 42.0 %collective-permute-start.1 = (bf16[256,256]{0,1:T(8,128)(2,1)}, bf16[256,256]{0,1:T(8,128)(2,1)}, u32[]{:S(2)}, u32[]{:S(2)}) collective-permute-start(bf16[256,256]{0,1:T(8,128)(2,1)} %slice.36), channel_id=1, source_target_pairs={{0,12},{12,24},{24,36},{36,48},{48,60},{60,72},{72,84},{84,96},{96... | collective-permute-start | bytes 393224 | tf_op jit(solution)/shard_map/ppermute | solution.py:22
  91.4 11.6 %collective-permute-start.5 = (bf16[4096,256]{0,1:T(8,128)(2,1)}, bf16[4096,256]{0,1:T(8,128)(2,1)}, u32[]{:S(2)}, u32[]{:S(2)}) collective-permute-start(bf16[4096,256]{0,1:T(8,128)(2,1)} %all-gather.2.cloned.1.call-done), channel_id=1, source_target_pairs={{0,12},{12,0},{1,13},{13,1},{2,14},{14,2},{3,15},{15,3},{4,16},{16... | collective-permute-start | bytes 6291464 | tf_op jit(solution)/shard_map/ppermute | solution.py:111
  97.6 5.4 %copy-start.3 = (bf16[4096,256]{0,1:T(8,128)(2,1)S(1)}, bf16[4096,256]{0,1:T(8,128)(2,1)}, u32[]{:S(2)}) copy-start(bf16[4096,256]{0,1:T(8,128)(2,1)} %all-gather.2.cloned.1.call-done) | copy-start | bytes 6291460
  101.0 4.9 %copy-start.2 = (pred[192,4096]{1,0:T(8,128)(4,1)S(1)}, pred[192,4096]{1,0:T(8,128)(4,1)}, u32[]{:S(2)}) copy-start(pred[192,4096]{1,0:T(8,128)(4,1)} %get-tuple-element.24) | copy-start | bytes 2359300
  101.0 4.9 %copy-start.5 = (bf16[24,2,8,128]{3,2,1,0:T(8,128)(2,1)S(1)}, bf16[24,2,8,128]{3,2,1,0:T(8,128)(2,1)}, u32[]{:S(2)}) copy-start(bf16[24,2,8,128]{3,2,1,0:T(8,128)(2,1)} %get-tuple-element.28) | copy-start | bytes 294916
  105.8 1.8 copy-start.4
  117.3 2.7 %copy-start.1 = (f32[384,4096]{1,0:T(8,128)}, f32[384,4096]{1,0:T(8,128)S(1)}, u32[]{:S(2)}) copy-start(f32[384,4096]{1,0:T(8,128)S(1)} %fusion.87) | copy-start | bytes 18874372
  120.0 13.5 %collective-permute-start.6 = (bf16[32,4096]{1,0:T(8,128)(2,1)S(1)}, bf16[32,4096]{1,0:T(8,128)(2,1)S(1)}, u32[]{:S(2)}, u32[]{:S(2)}) collective-permute-start(bf16[32,4096]{1,0:T(8,128)(2,1)S(1)} %get-tuple-element.19), channel_id=1, source_target_pairs={{0,1},{1,2},{2,3},{3,4},{4,5},{5,6},{6,7},{7,8},{8,9},{9,10},{10,1... | collective-permute-start | bytes 786440 | tf_op jit(solution)/shard_map/ppermute | solution.py:67
  123.6 13.0 %collective-permute-start.12 = (bf16[32,4096]{1,0:T(8,128)(2,1)S(1)}, bf16[32,4096]{1,0:T(8,128)(2,1)S(1)}, u32[]{:S(2)}, u32[]{:S(2)}) collective-permute-start(bf16[32,4096]{1,0:T(8,128)(2,1)S(1)} %get-tuple-element.20), channel_id=1, source_target_pairs={{0,11},{1,0},{2,1},{3,2},{4,3},{5,4},{6,5},{7,6},{8,7},{9,8},{10,9... | collective-permute-start | bytes 786440 | tf_op jit(solution)/shard_map/ppermute | solution.py:72
  134.7 11.2 %collective-permute-start.7 = (bf16[32,4096]{1,0:T(8,128)(2,1)S(1)}, bf16[32,4096]{1,0:T(8,128)(2,1)S(1)}, u32[]{:S(2)}, u32[]{:S(2)}) collective-permute-start(bf16[32,4096]{1,0:T(8,128)(2,1)S(1)} %add_convert_fusion.9), channel_id=1, source_target_pairs={{0,1},{1,2},{2,3},{3,4},{4,5},{5,6},{6,7},{7,8},{8,9},{9,10},{10,1... | collective-permute-start | bytes 786440 | tf_op jit(solution)/shard_map/ppermute | solution.py:67
  147.2 10.4 %collective-permute-start.8 = (bf16[32,4096]{1,0:T(8,128)(2,1)S(1)}, bf16[32,4096]{1,0:T(8,128)(2,1)S(1)}, u32[]{:S(2)}, u32[]{:S(2)}) collective-permute-start(bf16[32,4096]{1,0:T(8,128)(2,1)S(1)} %get-tuple-element.17), channel_id=1, source_target_pairs={{0,1},{1,2},{2,3},{3,4},{4,5},{5,6},{6,7},{7,8},{8,9},{9,10},{10,1... | collective-permute-start | bytes 786440 | tf_op jit(solution)/shard_map/ppermute | solution.py:67
  149.1 9.6 %collective-permute-start.13 = (bf16[32,4096]{1,0:T(8,128)(2,1)S(1)}, bf16[32,4096]{1,0:T(8,128)(2,1)S(1)}, u32[]{:S(2)}, u32[]{:S(2)}) collective-permute-start(bf16[32,4096]{1,0:T(8,128)(2,1)S(1)} %get-tuple-element.18), channel_id=1, source_target_pairs={{0,11},{1,0},{2,1},{3,2},{4,3},{5,4},{6,5},{7,6},{8,7},{9,8},{10,9... | collective-permute-start | bytes 786440 | tf_op jit(solution)/shard_map/ppermute | solution.py:72
  160.1 10.0 %collective-permute-start.9 = (bf16[32,4096]{1,0:T(8,128)(2,1)S(1)}, bf16[32,4096]{1,0:T(8,128)(2,1)S(1)}, u32[]{:S(2)}, u32[]{:S(2)}) collective-permute-start(bf16[32,4096]{1,0:T(8,128)(2,1)S(1)} %get-tuple-element.15), channel_id=1, source_target_pairs={{0,1},{1,2},{2,3},{3,4},{4,5},{5,6},{6,7},{7,8},{8,9},{9,10},{10,1... | collective-permute-start | bytes 786440 | tf_op jit(solution)/shard_map/ppermute | solution.py:67
  162.0 9.5 %collective-permute-start.14 = (bf16[32,4096]{1,0:T(8,128)(2,1)S(1)}, bf16[32,4096]{1,0:T(8,128)(2,1)S(1)}, u32[]{:S(2)}, u32[]{:S(2)}) collective-permute-start(bf16[32,4096]{1,0:T(8,128)(2,1)S(1)} %get-tuple-element.16), channel_id=1, source_target_pairs={{0,11},{1,0},{2,1},{3,2},{4,3},{5,4},{6,5},{7,6},{8,7},{9,8},{10,9... | collective-permute-start | bytes 786440 | tf_op jit(solution)/shard_map/ppermute | solution.py:72
  172.8 9.9 %collective-permute-start.10 = (bf16[32,4096]{1,0:T(8,128)(2,1)S(1)}, bf16[32,4096]{1,0:T(8,128)(2,1)S(1)}, u32[]{:S(2)}, u32[]{:S(2)}) collective-permute-start(bf16[32,4096]{1,0:T(8,128)(2,1)S(1)} %get-tuple-element.13), channel_id=1, source_target_pairs={{0,1},{1,2},{2,3},{3,4},{4,5},{5,6},{6,7},{7,8},{8,9},{9,10},{10,1... | collective-permute-start | bytes 786440 | tf_op jit(solution)/shard_map/ppermute | solution.py:67
  177.4 8.3 %collective-permute-start.15 = (bf16[32,4096]{1,0:T(8,128)(2,1)S(1)}, bf16[32,4096]{1,0:T(8,128)(2,1)S(1)}, u32[]{:S(2)}, u32[]{:S(2)}) collective-permute-start(bf16[32,4096]{1,0:T(8,128)(2,1)S(1)} %get-tuple-element.14), channel_id=1, source_target_pairs={{0,11},{1,0},{2,1},{3,2},{4,3},{5,4},{6,5},{7,6},{8,7},{9,8},{10,9... | collective-permute-start | bytes 786440 | tf_op jit(solution)/shard_map/ppermute | solution.py:72
  186.9 8.3 %collective-permute-start.16 = (bf16[32,4096]{1,0:T(8,128)(2,1)S(1)}, bf16[32,4096]{1,0:T(8,128)(2,1)S(1)}, u32[]{:S(2)}, u32[]{:S(2)}) collective-permute-start(bf16[32,4096]{1,0:T(8,128)(2,1)S(1)} %get-tuple-element.12), channel_id=1, source_target_pairs={{0,11},{1,0},{2,1},{3,2},{4,3},{5,4},{6,5},{7,6},{8,7},{9,8},{10,9... | collective-permute-start | bytes 786440 | tf_op jit(solution)/shard_map/ppermute | solution.py:72
  191.1 9.5 %collective-permute-start.11 = (bf16[32,4096]{1,0:T(8,128)(2,1)S(1)}, bf16[32,4096]{1,0:T(8,128)(2,1)S(1)}, u32[]{:S(2)}, u32[]{:S(2)}) collective-permute-start(bf16[32,4096]{1,0:T(8,128)(2,1)S(1)} %get-tuple-element.11), channel_id=1, source_target_pairs={{0,1},{1,2},{2,3},{3,4},{4,5},{5,6},{6,7},{7,8},{8,9},{9,10},{10,1... | collective-permute-start | bytes 786440 | tf_op jit(solution)/shard_map/ppermute | solution.py:67
Sparse Core Ops, SparseCore 0:
  51.3 40.0 all-gather.1

commit v6 on v5

--- a/solution.py
+++ b/solution.py
@@ -100,23 +100,15 @@
         jnp.concatenate([own_keys, own_values], axis=1), CORE, axis=0, tiled=True
     )
     my_half = lax.dynamic_slice_in_dim(chip_rows, core * width, width, 1)
-    ring = lax.axis_size("cy")
-    gathered = my_half
-    shift = 1
-    while shift < ring:
-        moved = lax.ppermute(gathered, "cy", [(j, (j + shift) % ring) for j in range(ring)])
-        gathered = jnp.concatenate([gathered, moved], axis=0)
-        shift *= 2
+    gathered = lax.all_gather(my_half, "cy", axis=0, tiled=True)
     gathered = lax.all_gather(gathered, "cx", axis=0, tiled=True)
     other = lax.ppermute(gathered, CORE, [(0, 1), (1, 0)])
     both = jnp.stack([gathered, other])
     all_sum_keys = both[core]
     all_sum_values = both[1 - core]
     index = jnp.arange(all_sum_keys.shape[0], dtype=jnp.int32)
-    across = index // (SUMMARY * ring)
-    back = (index // SUMMARY) % ring
-    chip = across * ring + (lax.axis_index("cy") - back) % ring
-    key_pos = chip * 2 * tok_rows + tok_rows - half_sum + index % SUMMARY
+    owner = index // half_sum
+    key_pos = owner * tok_rows + jnp.where(owner % 2 == 0, tok_rows - half_sum, 0) + index % half_sum
     sum_mask = own_pos[:, None] - key_pos[None, :] >= BAND
     pieces = []
     for low in range(0, tok_rows, chunk):

time: 210 us -> 200 us (0.952)
  waiting for transfers between devices: 97.5 us -> 62.9 us
  blocking collectives: 1.89 us -> 32.4 us
  starting transfers between devices: 52.5 us -> 47 us
    ppermute x3 -> x0, waiting for transfers between devices: 32.7 us -> none  [layer(): lax.ppermute(gathered, 'cy', [(j, (j + shift) % ring) for j in range(ring)])]
    all_gather x0 -> x1, blocking collectives: none -> 30.6 us  [layer(): gathered = lax.all_gather(my_half, 'cy', axis=0, tiled=True)]
    ppermute x3 -> x0, starting transfers between devices: 7.35 us -> none  [layer(): lax.ppermute(gathered, 'cy', [(j, (j + shift) % ring) for j in range(ring)])]
  transfers between devices with their start and end apart: 18 -> 15, of which waited for: 14 -> 11; matrix products, arithmetic and copies ran while one was open for 8% -> 8% of each run, Pallas kernels for 0% -> 0%
where the time goes in v6:
time: 200 us; the launch traced here: 199 us
  waiting for transfers between devices  62.9 us (31%)
  starting transfers between devices  47 us (24%)
  blocking collectives  32.4 us (16%)
  other arithmetic  19.5 us (10%)
  between operations  14 us (7%)
  local copies, waits for them, and re-layouts  12.3 us (6%)
  matrix products  10.6 us (5%)
    all_gather x1, blocking collectives, layer(): gathered = lax.all_gather(my_half, 'cy', axis=0, tiled=True)  30.6 us
    ppermute x6, waiting for transfers between devices, ring_reduce_scatter(): lax.ppermute(up, axis, ahead).astype(jnp.float32)  27.6 us
    all_gather x1, waiting for transfers between devices, layer(): gathered = lax.all_gather(gathered, 'cx', axis=0, tiled=True)  27.5 us
    ppermute x5, starting transfers between devices, ring_reduce_scatter(): down_sum = lax.ppermute(down, axis, behind).astype(jnp.float32)  22.7 us
    ppermute x6, starting transfers between devices, ring_reduce_scatter(): lax.ppermute(up, axis, ahead).astype(jnp.float32)  15.8 us
    ppermute x5, waiting for transfers between devices, ring_reduce_scatter(): down_sum = lax.ppermute(down, axis, behind).astype(jnp.float32)  7.72 us
    unnamed x16, local copies, waits for them, and re-layouts  6.6 us
    ppermute x2, starting transfers between devices, shifted(): lax.ppermute(value, axis, [(source, source + steps) for source in range(l...  6.31 us
  transfers between devices with their start and end apart: 15, of which 11 were waited for; matrix products, arithmetic and copies ran while one was open for 8% of the time, Pallas kernels for 0%

profile of v6, /device:TPU:8, one launch (start us, length us, event | category | flops | bytes accessed | tf_op | source)
XLA Modules:
  0.0 198.7 jit_solution(18243592754057755060)
XLA Ops:
  8.2 1.9 all_gather.9
  10.2 30.6 %all_gather.10 = bf16[1024,256]{0,1:T(8,128)(2,1)} all-gather(bf16[128,256]{0,1:T(8,128)(2,1)S(1)} %copy.50), channel_id=1, replica_groups=mesh['cx'=4,'cy'=8,'cc'=2,'head'=12] {'cy'}, dimensions={0}, use_global_device_ids=true | all-gather | bytes 589824 | tf_op jit(solution)/shard_map/all_gather | solution.py:103
  40.8 1.1 copy.24
  42.6 1.9 collective-permute-start
  44.5 1.1 copy.28
  46.3 4.4 %collective-permute-start.1 = (bf16[256,256]{0,1:T(8,128)(2,1)}, bf16[256,256]{0,1:T(8,128)(2,1)}, u32[]{:S(2)}, u32[]{:S(2)}) collective-permute-start(bf16[256,256]{0,1:T(8,128)(2,1)} %slice.36), channel_id=1, source_target_pairs={{0,12},{12,24},{24,36},{36,48},{48,60},{60,72},{72,84},{84,96},{96... | collective-permute-start | bytes 393224 | tf_op jit(solution)/shard_map/ppermute | solution.py:22
  51.1 2.3 %subtract_compare_fusion = pred[384,4096]{1,0:T(8,128)(4,1)} fusion(s32[4096]{0:T(1024)S(1)} %fusion.62, s32[384]{0:T(512)S(1)} %iota_add_fusion.1), kind=kLoop, calls=%fused_computation.4 | loop fusion | flops 3145728 | bytes 1590784 | tf_op jit(solution)/shard_map/ge | solution.py:112
  53.4 27.5 %all-gather.2.cloned.1.call-done = bf16[4096,256]{0,1:T(8,128)(2,1)} async-done(((bf16[1024,256]{0,1:T(8,128)(2,1)}), bf16[4096,256]{0,1:T(8,128)(2,1)}) %all-gather.2.cloned.1.call-update) | async-done | bytes 2097168 | tf_op jit(solution)/shard_map/all_gather | solution.py:104
  80.9 2.1 %collective-permute-start.2 = (bf16[4096,256]{0,1:T(8,128)(2,1)}, bf16[4096,256]{0,1:T(8,128)(2,1)}, u32[]{:S(2)}, u32[]{:S(2)}) collective-permute-start(bf16[4096,256]{0,1:T(8,128)(2,1)} %all-gather.2.cloned.1.call-done), channel_id=1, source_target_pairs={{0,12},{12,0},{1,13},{13,1},{2,14},{14,2},{3,15},{15,3},{4,16},{16... | collective-permute-start | bytes 6291464 | tf_op jit(solution)/shard_map/ppermute | solution.py:105
  83.0 2.4 %fusion.78 = (pred[192,4096]{1,0:T(8,128)(4,1)S(1)}, pred[192,4096]{1,0:T(8,128)(4,1)}) fusion(pred[384,4096]{1,0:T(8,128)(4,1)} %subtract_compare_fusion), kind=kLoop, calls=%fused_computation.120 | loop fusion | bytes 3145728 | tf_op jit(solution)/shard_map/slice | solution.py:116
  85.4 1.6 slice_bitcast_fusion.1
  87.1 1.1 pad_maximum_fusion
  89.1 1.3 fusion.83
  90.5 1.4 fusion.81
  92.5 2.8 %fusion.15 = (bf16[1,4096,256]{1,2,0:T(8,128)(2,1)S(1)}, bf16[1,4096,256]{1,2,0:T(8,128)(2,1)S(1)}) fusion(s32[]{:T(128)S(6)} %select_n.176, bf16[1,4096,256]{1,2,0:T(8,128)(2,1)S(1)} %bitcast.57, bf16[1,4096,256]{1,2,0:T(8,128)(2,1)} %bitcast.4, s32[]{:T(128)S(6)} %select_n.179), kind=kLoop, calls=%fused_computation.22 | loop fusion | flops 2097152 | bytes 8388616 | tf_op jit(solution)/shard_map/stack | solution.py:106
  95.3 1.8 fusion.80
  97.1 1.8 fusion.82
  98.9 3.3 %fusion = (f32[2,192]{1,0:T(2,128)S(1)}, f32[2,192]{1,0:T(2,128)S(1)}) fusion(f32[2,192,4096]{2,1,0:T(8,128)S(1)} %get-tuple-element.34, f32[2,192]{1,0:T(2,128)S(1)} %get-tuple-element.33, pred[192,4096]{1,0:T(8,128)(4,1)S(1)} %get-tuple-element.23, f32[2,192,4096]{2,1,0:T(8,128)S(1)} %get-tuple-element.30, f32[2,192]{1,0:T(2,128)S(1)} %get-tuple-element.29, ...), kind=kLoop, calls=%fused_computation.5 | loop fusion | flops 9436416 | bytes 14161920 | tf_op jit(solution)/shard_map/reduce_sum | solution.py:48
  102.2 1.2 fusion.27
  103.5 1.3 fusion.24
  106.8 2.7 %copy-done.1 = f32[384,4096]{1,0:T(8,128)} copy-done((f32[384,4096]{1,0:T(8,128)}, f32[384,4096]{1,0:T(8,128)S(1)}, u32[]{:S(2)}) %copy-start.1) | copy-done | bytes 6291480
  109.5 3.6 %collective-permute-start.3 = (bf16[32,4096]{1,0:T(8,128)(2,1)S(1)}, bf16[32,4096]{1,0:T(8,128)(2,1)S(1)}, u32[]{:S(2)}, u32[]{:S(2)}) collective-permute-start(bf16[32,4096]{1,0:T(8,128)(2,1)S(1)} %get-tuple-element.19), channel_id=1, source_target_pairs={{0,1},{1,2},{2,3},{3,4},{4,5},{5,6},{6,7},{7,8},{8,9},{9,10},{10,1... | collective-permute-start | bytes 786440 | tf_op jit(solution)/shard_map/ppermute | solution.py:67
  113.1 5.0 %collective-permute-start.9 = (bf16[32,4096]{1,0:T(8,128)(2,1)S(1)}, bf16[32,4096]{1,0:T(8,128)(2,1)S(1)}, u32[]{:S(2)}, u32[]{:S(2)}) collective-permute-start(bf16[32,4096]{1,0:T(8,128)(2,1)S(1)} %get-tuple-element.20), channel_id=1, source_target_pairs={{0,11},{1,0},{2,1},{3,2},{4,3},{5,4},{6,5},{7,6},{8,7},{9,8},{10,9... | collective-permute-start | bytes 786440 | tf_op jit(solution)/shard_map/ppermute | solution.py:72
  118.1 5.0 %collective-permute-done.3 = bf16[32,4096]{1,0:T(8,128)(2,1)S(1)} collective-permute-done((bf16[32,4096]{1,0:T(8,128)(2,1)S(1)}, bf16[32,4096]{1,0:T(8,128)(2,1)S(1)}, u32[]{:S(2)}, u32[]{:S(2)}) %collective-permute-start.3) | collective-permute-done | bytes 262176 | tf_op jit(solution)/shard_map/ppermute | solution.py:67
  123.1 1.1 add_convert_fusion.9
  124.2 1.9 collective-permute-start.4
  126.2 9.3 %collective-permute-done.4 = bf16[32,4096]{1,0:T(8,128)(2,1)S(1)} collective-permute-done((bf16[32,4096]{1,0:T(8,128)(2,1)S(1)}, bf16[32,4096]{1,0:T(8,128)(2,1)S(1)}, u32[]{:S(2)}, u32[]{:S(2)}) %collective-permute-start.4) | collective-permute-done | bytes 262176 | tf_op jit(solution)/shard_map/ppermute | solution.py:67
  135.4 1.3 add_convert_fusion.8
  136.7 1.9 collective-permute-start.5
  138.6 5.1 %collective-permute-start.10 = (bf16[32,4096]{1,0:T(8,128)(2,1)S(1)}, bf16[32,4096]{1,0:T(8,128)(2,1)S(1)}, u32[]{:S(2)}, u32[]{:S(2)}) collective-permute-start(bf16[32,4096]{1,0:T(8,128)(2,1)S(1)} %get-tuple-element.18), channel_id=1, source_target_pairs={{0,11},{1,0},{2,1},{3,2},{4,3},{5,4},{6,5},{7,6},{8,7},{9,8},{10,9... | collective-permute-start | bytes 786440 | tf_op jit(solution)/shard_map/ppermute | solution.py:72
  143.8 3.3 %collective-permute-done.5 = bf16[32,4096]{1,0:T(8,128)(2,1)S(1)} collective-permute-done((bf16[32,4096]{1,0:T(8,128)(2,1)S(1)}, bf16[32,4096]{1,0:T(8,128)(2,1)S(1)}, u32[]{:S(2)}, u32[]{:S(2)}) %collective-permute-start.5) | collective-permute-done | bytes 262176 | tf_op jit(solution)/shard_map/ppermute | solution.py:67
  147.1 1.2 collective-permute-done.10
  148.3 1.3 add_convert_fusion.7
  149.6 1.9 collective-permute-start.6
  151.5 5.6 %collective-permute-start.11 = (bf16[32,4096]{1,0:T(8,128)(2,1)S(1)}, bf16[32,4096]{1,0:T(8,128)(2,1)S(1)}, u32[]{:S(2)}, u32[]{:S(2)}) collective-permute-start(bf16[32,4096]{1,0:T(8,128)(2,1)S(1)} %get-tuple-element.16), channel_id=1, source_target_pairs={{0,11},{1,0},{2,1},{3,2},{4,3},{5,4},{6,5},{7,6},{8,7},{9,8},{10,9... | collective-permute-start | bytes 786440 | tf_op jit(solution)/shard_map/ppermute | solution.py:72
  157.1 2.4 %collective-permute-done.6 = bf16[32,4096]{1,0:T(8,128)(2,1)S(1)} collective-permute-done((bf16[32,4096]{1,0:T(8,128)(2,1)S(1)}, bf16[32,4096]{1,0:T(8,128)(2,1)S(1)}, u32[]{:S(2)}, u32[]{:S(2)}) %collective-permute-start.6) | collective-permute-done | bytes 262176 | tf_op jit(solution)/shard_map/ppermute | solution.py:67
  159.6 1.4 collective-permute-done.11
  161.0 1.3 add_convert_fusion.6
  162.3 4.6 %collective-permute-start.7 = (bf16[32,4096]{1,0:T(8,128)(2,1)S(1)}, bf16[32,4096]{1,0:T(8,128)(2,1)S(1)}, u32[]{:S(2)}, u32[]{:S(2)}) collective-permute-start(bf16[32,4096]{1,0:T(8,128)(2,1)S(1)} %get-tuple-element.13), channel_id=1, source_target_pairs={{0,1},{1,2},{2,3},{3,4},{4,5},{5,6},{6,7},{7,8},{8,9},{9,10},{10,1... | collective-permute-start | bytes 786440 | tf_op jit(solution)/shard_map/ppermute | solution.py:67
  166.9 2.9 %collective-permute-start.12 = (bf16[32,4096]{1,0:T(8,128)(2,1)S(1)}, bf16[32,4096]{1,0:T(8,128)(2,1)S(1)}, u32[]{:S(2)}, u32[]{:S(2)}) collective-permute-start(bf16[32,4096]{1,0:T(8,128)(2,1)S(1)} %get-tuple-element.14), channel_id=1, source_target_pairs={{0,11},{1,0},{2,1},{3,2},{4,3},{5,4},{6,5},{7,6},{8,7},{9,8},{10,9... | collective-permute-start | bytes 786440 | tf_op jit(solution)/shard_map/ppermute | solution.py:72
  169.8 2.4 %collective-permute-done.7 = bf16[32,4096]{1,0:T(8,128)(2,1)S(1)} collective-permute-done((bf16[32,4096]{1,0:T(8,128)(2,1)S(1)}, bf16[32,4096]{1,0:T(8,128)(2,1)S(1)}, u32[]{:S(2)}, u32[]{:S(2)}) %collective-permute-start.7) | collective-permute-done | bytes 262176 | tf_op jit(solution)/shard_map/ppermute | solution.py:67
  172.2 2.9 %collective-permute-done.12 = bf16[32,4096]{1,0:T(8,128)(2,1)S(1)} collective-permute-done((bf16[32,4096]{1,0:T(8,128)(2,1)S(1)}, bf16[32,4096]{1,0:T(8,128)(2,1)S(1)}, u32[]{:S(2)}, u32[]{:S(2)}) %collective-permute-start.12) | collective-permute-done | bytes 262176 | tf_op jit(solution)/shard_map/ppermute | solution.py:72
  175.1 1.3 add_convert_fusion.5
  176.4 4.1 %collective-permute-start.13 = (bf16[32,4096]{1,0:T(8,128)(2,1)S(1)}, bf16[32,4096]{1,0:T(8,128)(2,1)S(1)}, u32[]{:S(2)}, u32[]{:S(2)}) collective-permute-start(bf16[32,4096]{1,0:T(8,128)(2,1)S(1)} %get-tuple-element.12), channel_id=1, source_target_pairs={{0,11},{1,0},{2,1},{3,2},{4,3},{5,4},{6,5},{7,6},{8,7},{9,8},{10,9... | collective-permute-start | bytes 786440 | tf_op jit(solution)/shard_map/ppermute | solution.py:72
  180.6 1.9 collective-permute-start.8
  182.5 2.2 %collective-permute-done.13 = bf16[32,4096]{1,0:T(8,128)(2,1)S(1)} collective-permute-done((bf16[32,4096]{1,0:T(8,128)(2,1)S(1)}, bf16[32,4096]{1,0:T(8,128)(2,1)S(1)}, u32[]{:S(2)}, u32[]{:S(2)}) %collective-permute-start.13) | collective-permute-done | bytes 262176 | tf_op jit(solution)/shard_map/ppermute | solution.py:72
  184.7 5.3 %collective-permute-done.8 = bf16[32,4096]{1,0:T(8,128)(2,1)S(1)} collective-permute-done((bf16[32,4096]{1,0:T(8,128)(2,1)S(1)}, bf16[32,4096]{1,0:T(8,128)(2,1)S(1)}, u32[]{:S(2)}, u32[]{:S(2)}) %collective-permute-start.8) | collective-permute-done | bytes 262176 | tf_op jit(solution)/shard_map/ppermute | solution.py:67
  190.0 1.8 add_convert_fusion
  (40 shorter events, 7.3 us)
Async XLA Ops:
  6.5 99.2 %copy-start = (bf16[256,4096]{1,0:T(8,128)(2,1)S(1)}, bf16[256,4096]{1,0:T(8,128)(2,1)}, u32[]{:S(2)}) copy-start(bf16[256,4096]{1,0:T(8,128)(2,1)} %param.7) | copy-start | bytes 6291460
  6.5 74.4 %all-gather.2.cloned.1.call-start = ((), (), s32[]{:S(2)}) async-start(), calls=%async_computation | async-start | bytes 2621440 | tf_op jit(solution)/shard_map/all_gather | solution.py:104
  42.6 44.5 %collective-permute-start = (bf16[256,256]{0,1:T(8,128)(2,1)}, bf16[256,256]{0,1:T(8,128)(2,1)}, u32[]{:S(2)}, u32[]{:S(2)}) collective-permute-start(bf16[256,256]{0,1:T(8,128)(2,1)} %slice.35), channel_id=1, source_target_pairs={{0,12},{12,24},{24,36},{36,48},{48,60},{60,72},{72,84},{84,96},{96... | collective-permute-start | bytes 393224 | tf_op jit(solution)/shard_map/ppermute | solution.py:22
  46.3 41.9 %collective-permute-start.1 = (bf16[256,256]{0,1:T(8,128)(2,1)}, bf16[256,256]{0,1:T(8,128)(2,1)}, u32[]{:S(2)}, u32[]{:S(2)}) collective-permute-start(bf16[256,256]{0,1:T(8,128)(2,1)} %slice.36), channel_id=1, source_target_pairs={{0,12},{12,24},{24,36},{36,48},{48,60},{60,72},{72,84},{84,96},{96... | collective-permute-start | bytes 393224 | tf_op jit(solution)/shard_map/ppermute | solution.py:22
  80.9 11.6 %collective-permute-start.2 = (bf16[4096,256]{0,1:T(8,128)(2,1)}, bf16[4096,256]{0,1:T(8,128)(2,1)}, u32[]{:S(2)}, u32[]{:S(2)}) collective-permute-start(bf16[4096,256]{0,1:T(8,128)(2,1)} %all-gather.2.cloned.1.call-done), channel_id=1, source_target_pairs={{0,12},{12,0},{1,13},{13,1},{2,14},{14,2},{3,15},{15,3},{4,16},{16... | collective-permute-start | bytes 6291464 | tf_op jit(solution)/shard_map/ppermute | solution.py:105
  87.1 5.4 %copy-start.3 = (bf16[4096,256]{0,1:T(8,128)(2,1)S(1)}, bf16[4096,256]{0,1:T(8,128)(2,1)}, u32[]{:S(2)}) copy-start(bf16[4096,256]{0,1:T(8,128)(2,1)} %all-gather.2.cloned.1.call-done) | copy-start | bytes 6291460
  90.4 4.9 %copy-start.2 = (pred[192,4096]{1,0:T(8,128)(4,1)S(1)}, pred[192,4096]{1,0:T(8,128)(4,1)}, u32[]{:S(2)}) copy-start(pred[192,4096]{1,0:T(8,128)(4,1)} %get-tuple-element.24) | copy-start | bytes 2359300
  90.4 4.9 %copy-start.5 = (bf16[24,2,8,128]{3,2,1,0:T(8,128)(2,1)S(1)}, bf16[24,2,8,128]{3,2,1,0:T(8,128)(2,1)}, u32[]{:S(2)}) copy-start(bf16[24,2,8,128]{3,2,1,0:T(8,128)(2,1)} %get-tuple-element.28) | copy-start | bytes 294916
  95.3 1.8 copy-start.4
  106.8 2.7 %copy-start.1 = (f32[384,4096]{1,0:T(8,128)}, f32[384,4096]{1,0:T(8,128)S(1)}, u32[]{:S(2)}) copy-start(f32[384,4096]{1,0:T(8,128)S(1)} %fusion.84) | copy-start | bytes 18874372
  109.5 13.6 %collective-permute-start.3 = (bf16[32,4096]{1,0:T(8,128)(2,1)S(1)}, bf16[32,4096]{1,0:T(8,128)(2,1)S(1)}, u32[]{:S(2)}, u32[]{:S(2)}) collective-permute-start(bf16[32,4096]{1,0:T(8,128)(2,1)S(1)} %get-tuple-element.19), channel_id=1, source_target_pairs={{0,1},{1,2},{2,3},{3,4},{4,5},{5,6},{6,7},{7,8},{8,9},{9,10},{10,1... | collective-permute-start | bytes 786440 | tf_op jit(solution)/shard_map/ppermute | solution.py:67
  113.1 13.0 %collective-permute-start.9 = (bf16[32,4096]{1,0:T(8,128)(2,1)S(1)}, bf16[32,4096]{1,0:T(8,128)(2,1)S(1)}, u32[]{:S(2)}, u32[]{:S(2)}) collective-permute-start(bf16[32,4096]{1,0:T(8,128)(2,1)S(1)} %get-tuple-element.20), channel_id=1, source_target_pairs={{0,11},{1,0},{2,1},{3,2},{4,3},{5,4},{6,5},{7,6},{8,7},{9,8},{10,9... | collective-permute-start | bytes 786440 | tf_op jit(solution)/shard_map/ppermute | solution.py:72
  124.2 11.2 %collective-permute-start.4 = (bf16[32,4096]{1,0:T(8,128)(2,1)S(1)}, bf16[32,4096]{1,0:T(8,128)(2,1)S(1)}, u32[]{:S(2)}, u32[]{:S(2)}) collective-permute-start(bf16[32,4096]{1,0:T(8,128)(2,1)S(1)} %add_convert_fusion.9), channel_id=1, source_target_pairs={{0,1},{1,2},{2,3},{3,4},{4,5},{5,6},{6,7},{7,8},{8,9},{9,10},{10,1... | collective-permute-start | bytes 786440 | tf_op jit(solution)/shard_map/ppermute | solution.py:67
  136.7 10.4 %collective-permute-start.5 = (bf16[32,4096]{1,0:T(8,128)(2,1)S(1)}, bf16[32,4096]{1,0:T(8,128)(2,1)S(1)}, u32[]{:S(2)}, u32[]{:S(2)}) collective-permute-start(bf16[32,4096]{1,0:T(8,128)(2,1)S(1)} %get-tuple-element.17), channel_id=1, source_target_pairs={{0,1},{1,2},{2,3},{3,4},{4,5},{5,6},{6,7},{7,8},{8,9},{9,10},{10,1... | collective-permute-start | bytes 786440 | tf_op jit(solution)/shard_map/ppermute | solution.py:67
  138.6 9.6 %collective-permute-start.10 = (bf16[32,4096]{1,0:T(8,128)(2,1)S(1)}, bf16[32,4096]{1,0:T(8,128)(2,1)S(1)}, u32[]{:S(2)}, u32[]{:S(2)}) collective-permute-start(bf16[32,4096]{1,0:T(8,128)(2,1)S(1)} %get-tuple-element.18), channel_id=1, source_target_pairs={{0,11},{1,0},{2,1},{3,2},{4,3},{5,4},{6,5},{7,6},{8,7},{9,8},{10,9... | collective-permute-start | bytes 786440 | tf_op jit(solution)/shard_map/ppermute | solution.py:72
  149.6 10.0 %collective-permute-start.6 = (bf16[32,4096]{1,0:T(8,128)(2,1)S(1)}, bf16[32,4096]{1,0:T(8,128)(2,1)S(1)}, u32[]{:S(2)}, u32[]{:S(2)}) collective-permute-start(bf16[32,4096]{1,0:T(8,128)(2,1)S(1)} %get-tuple-element.15), channel_id=1, source_target_pairs={{0,1},{1,2},{2,3},{3,4},{4,5},{5,6},{6,7},{7,8},{8,9},{9,10},{10,1... | collective-permute-start | bytes 786440 | tf_op jit(solution)/shard_map/ppermute | solution.py:67
  151.5 9.5 %collective-permute-start.11 = (bf16[32,4096]{1,0:T(8,128)(2,1)S(1)}, bf16[32,4096]{1,0:T(8,128)(2,1)S(1)}, u32[]{:S(2)}, u32[]{:S(2)}) collective-permute-start(bf16[32,4096]{1,0:T(8,128)(2,1)S(1)} %get-tuple-element.16), channel_id=1, source_target_pairs={{0,11},{1,0},{2,1},{3,2},{4,3},{5,4},{6,5},{7,6},{8,7},{9,8},{10,9... | collective-permute-start | bytes 786440 | tf_op jit(solution)/shard_map/ppermute | solution.py:72
  162.3 9.9 %collective-permute-start.7 = (bf16[32,4096]{1,0:T(8,128)(2,1)S(1)}, bf16[32,4096]{1,0:T(8,128)(2,1)S(1)}, u32[]{:S(2)}, u32[]{:S(2)}) collective-permute-start(bf16[32,4096]{1,0:T(8,128)(2,1)S(1)} %get-tuple-element.13), channel_id=1, source_target_pairs={{0,1},{1,2},{2,3},{3,4},{4,5},{5,6},{6,7},{7,8},{8,9},{9,10},{10,1... | collective-permute-start | bytes 786440 | tf_op jit(solution)/shard_map/ppermute | solution.py:67
  166.9 8.3 %collective-permute-start.12 = (bf16[32,4096]{1,0:T(8,128)(2,1)S(1)}, bf16[32,4096]{1,0:T(8,128)(2,1)S(1)}, u32[]{:S(2)}, u32[]{:S(2)}) collective-permute-start(bf16[32,4096]{1,0:T(8,128)(2,1)S(1)} %get-tuple-element.14), channel_id=1, source_target_pairs={{0,11},{1,0},{2,1},{3,2},{4,3},{5,4},{6,5},{7,6},{8,7},{9,8},{10,9... | collective-permute-start | bytes 786440 | tf_op jit(solution)/shard_map/ppermute | solution.py:72
  176.4 8.3 %collective-permute-start.13 = (bf16[32,4096]{1,0:T(8,128)(2,1)S(1)}, bf16[32,4096]{1,0:T(8,128)(2,1)S(1)}, u32[]{:S(2)}, u32[]{:S(2)}) collective-permute-start(bf16[32,4096]{1,0:T(8,128)(2,1)S(1)} %get-tuple-element.12), channel_id=1, source_target_pairs={{0,11},{1,0},{2,1},{3,2},{4,3},{5,4},{6,5},{7,6},{8,7},{9,8},{10,9... | collective-permute-start | bytes 786440 | tf_op jit(solution)/shard_map/ppermute | solution.py:72
  180.6 9.5 %collective-permute-start.8 = (bf16[32,4096]{1,0:T(8,128)(2,1)S(1)}, bf16[32,4096]{1,0:T(8,128)(2,1)S(1)}, u32[]{:S(2)}, u32[]{:S(2)}) collective-permute-start(bf16[32,4096]{1,0:T(8,128)(2,1)S(1)} %get-tuple-element.11), channel_id=1, source_target_pairs={{0,1},{1,2},{2,3},{3,4},{4,5},{5,6},{6,7},{7,8},{8,9},{9,10},{10,1... | collective-permute-start | bytes 786440 | tf_op jit(solution)/shard_map/ppermute | solution.py:67
Sparse Core Ops, SparseCore 0:
  40.9 39.9 all-gather.1

commit v7 on v6

--- a/solution.py
+++ b/solution.py
@@ -46,6 +46,27 @@
         "hqk,khd->hqd", w.astype(jnp.bfloat16), v, preferred_element_type=jnp.float32
     )
     return top, w.sum(axis=2), summed
+
+
+def gather_row_blocks(block, axis):
+    count = lax.axis_size(axis)
+    if count != 4:
+        gathered = lax.all_gather(block, axis, axis=0, tiled=True)
+        me = lax.axis_index(axis)
+        return gathered, [(j - me) for j in range(count)]
+    ahead = [(j, (j + 1) % count) for j in range(count)]
+    behind = [(j, (j - 1) % count) for j in range(count)]
+    from_left = lax.ppermute(block, axis, ahead)
+    from_right = lax.ppermute(block, axis, behind)
+    half = block.shape[0] // 2
+    far = jnp.concatenate(
+        [
+            lax.ppermute(from_left[:half], axis, ahead),
+            lax.ppermute(from_right[half:], axis, behind),
+        ],
+        axis=0,
+    )
+    return jnp.concatenate([block, from_left, far, from_right], axis=0), [0, -1, -2, 1]
 
 
 def ring_reduce_scatter(partial, axis):
@@ -101,13 +122,17 @@
     )
     my_half = lax.dynamic_slice_in_dim(chip_rows, core * width, width, 1)
     gathered = lax.all_gather(my_half, "cy", axis=0, tiled=True)
-    gathered = lax.all_gather(gathered, "cx", axis=0, tiled=True)
+    gathered, offsets = gather_row_blocks(gathered, "cx")
     other = lax.ppermute(gathered, CORE, [(0, 1), (1, 0)])
     both = jnp.stack([gathered, other])
     all_sum_keys = both[core]
     all_sum_values = both[1 - core]
     index = jnp.arange(all_sum_keys.shape[0], dtype=jnp.int32)
-    owner = index // half_sum
+    row_len = index.shape[0] // len(offsets)
+    x_count = lax.axis_size("cx")
+    moved = jnp.asarray(offsets, jnp.int32)[index // row_len]
+    source_x = (lax.axis_index("cx") + moved) % x_count
+    owner = source_x * (row_len // half_sum) + (index % row_len) // half_sum
     key_pos = owner * tok_rows + jnp.where(owner % 2 == 0, tok_rows - half_sum, 0) + index % half_sum
     sum_mask = own_pos[:, None] - key_pos[None, :] >= BAND
     pieces = []

time: 200 us -> 184 us (0.920)
  the two profiles are of different devices: /device:TPU:8 before, /device:TPU:14 now
where the time goes in v7:
time: 184 us; the launch traced here: 183 us
  starting transfers between devices  67.7 us (37%)
  waiting for transfers between devices  39.5 us (21%)
  blocking collectives  26.8 us (15%)
  other arithmetic  19.7 us (11%)
  local copies, waits for them, and re-layouts  18.2 us (10%)
  matrix products  10.5 us (6%)
    ppermute x5, starting transfers between devices, ring_reduce_scatter(): down_sum = lax.ppermute(down, axis, behind).astype(jnp.float32)  31.9 us
    ppermute x6, waiting for transfers between devices, ring_reduce_scatter(): lax.ppermute(up, axis, ahead).astype(jnp.float32)  28 us
    all_gather x1, blocking collectives, layer(): gathered = lax.all_gather(my_half, 'cy', axis=0, tiled=True)  24.9 us
    ppermute x6, starting transfers between devices, ring_reduce_scatter(): lax.ppermute(up, axis, ahead).astype(jnp.float32)  11.5 us
    unnamed x22, local copies, waits for them, and re-layouts  9.97 us
    ppermute x1, starting transfers between devices, gather_row_blocks(): from_left = lax.ppermute(block, axis, ahead)  6.96 us
    convert_element_type x5, other arithmetic, ring_reduce_scatter(): up = up_sum.astype(jnp.bfloat16)  6.24 us
    ppermute x2, starting transfers between devices, shifted(): lax.ppermute(value, axis, [(source, source + steps) for source in range(l...  6.21 us
  transfers between devices with their start and end apart: 18, of which 11 were waited for; matrix products, arithmetic and copies ran while one was open for 12% of the time, Pallas kernels for 0%

profile of v7, /device:TPU:14, one launch (start us, length us, event | category | flops | bytes accessed | tf_op | source)
XLA Modules:
  0.0 183.0 jit_solution(13670390595600678710)
XLA Ops:
  1.7 1.9 %all_gather.6 = bf16[128,512]{1,0:T(8,128)(2,1)S(1)} all-gather(bf16[64,512]{1,0:T(8,128)(2,1)S(1)} %pad_maximum_fusion.2), channel_id=1, replica_groups=mesh['cx'=4,'cy'=8,'cc'=2,'head'=12] {'cc'}, dimensions={0}, use_global_device_ids=true | all-gather | bytes 196608 | tf_op jit(solution)/shard_map/all_gather | solution.py:120
  3.7 24.9 %all_gather.7 = bf16[1024,256]{0,1:T(8,128)(2,1)S(1)} all-gather(bf16[128,256]{0,1:T(8,128)(2,1)S(1)} %copy.51), channel_id=1, replica_groups=mesh['cx'=4,'cy'=8,'cc'=2,'head'=12] {'cy'}, dimensions={0}, use_global_device_ids=true | all-gather | bytes 589824 | tf_op jit(solution)/shard_map/all_gather | solution.py:124
  28.6 7.0 %collective-permute-start.2 = (bf16[1024,256]{0,1:T(8,128)(2,1)S(1)}, bf16[1024,256]{0,1:T(8,128)(2,1)}, u32[]{:S(2)}, u32[]{:S(2)}) collective-permute-start(bf16[1024,256]{0,1:T(8,128)(2,1)S(1)} %all_gather.7), channel_id=1, source_target_pairs={{0,192},{192,384},{384,576},{576,0},{1,193},{193,385},{385,577},{5... | collective-permute-start | bytes 1572872 | tf_op jit(solution)/shard_map/ppermute | solution.py:59
  35.5 1.9 %collective-permute-start.4 = (bf16[1024,256]{0,1:T(8,128)(2,1)S(1)}, bf16[1024,256]{0,1:T(8,128)(2,1)}, u32[]{:S(2)}, u32[]{:S(2)}) collective-permute-start(bf16[1024,256]{0,1:T(8,128)(2,1)S(1)} %all_gather.7), channel_id=1, source_target_pairs={{0,576},{192,0},{384,192},{576,384},{1,577},{193,1},{385,193},{577... | collective-permute-start | bytes 1572872 | tf_op jit(solution)/shard_map/ppermute | solution.py:60
  39.2 1.9 %collective-permute-start = (bf16[256,256]{0,1:T(8,128)(2,1)}, bf16[256,256]{0,1:T(8,128)(2,1)}, u32[]{:S(2)}, u32[]{:S(2)}) collective-permute-start(bf16[256,256]{0,1:T(8,128)(2,1)} %slice.48), channel_id=1, source_target_pairs={{0,12},{12,24},{24,36},{36,48},{48,60},{60,72},{72,84},{84,96},{96... | collective-permute-start | bytes 393224 | tf_op jit(solution)/shard_map/ppermute | solution.py:22
  42.9 4.3 %collective-permute-start.1 = (bf16[256,256]{0,1:T(8,128)(2,1)}, bf16[256,256]{0,1:T(8,128)(2,1)}, u32[]{:S(2)}, u32[]{:S(2)}) collective-permute-start(bf16[256,256]{0,1:T(8,128)(2,1)} %slice.49), channel_id=1, source_target_pairs={{0,12},{12,24},{24,36},{36,48},{48,60},{60,72},{72,84},{84,96},{96... | collective-permute-start | bytes 393224 | tf_op jit(solution)/shard_map/ppermute | solution.py:22
  47.3 2.3 %subtract_compare_fusion = pred[384,4096]{1,0:T(8,128)(4,1)} fusion(s32[4096]{0:T(1024)S(1)} %fusion.60, s32[384]{0:T(512)S(1)} %iota_add_fusion.1), kind=kLoop, calls=%fused_computation.4 | loop fusion | flops 3145728 | bytes 1590784 | tf_op jit(solution)/shard_map/ge | solution.py:137
  51.0 5.1 %collective-permute-start.3 = (bf16[512,256]{0,1:T(8,128)(2,1)S(1)}, bf16[512,256]{0,1:T(8,128)(2,1)S(1)}, u32[]{:S(2)}, u32[]{:S(2)}) collective-permute-start(bf16[512,256]{0,1:T(8,128)(2,1)S(1)} %slice.51), channel_id=1, source_target_pairs={{0,192},{192,384},{384,576},{576,0},{1,193},{193,385},{385,577},{5... | collective-permute-start | bytes 786440 | tf_op jit(solution)/shard_map/ppermute | solution.py:64
  57.2 1.9 %collective-permute-start.5 = (bf16[512,256]{0,1:T(8,128)(2,1)S(1)}, bf16[512,256]{0,1:T(8,128)(2,1)S(1)}, u32[]{:S(2)}, u32[]{:S(2)}) collective-permute-start(bf16[512,256]{0,1:T(8,128)(2,1)S(1)} %slice.52), channel_id=1, source_target_pairs={{0,576},{192,0},{384,192},{576,384},{1,577},{193,1},{385,193},{577... | collective-permute-start | bytes 786440 | tf_op jit(solution)/shard_map/ppermute | solution.py:65
  60.0 2.0 %constant_dynamic-update-slice_fusion.3 = bf16[4096,256]{0,1:T(8,128)(2,1)} fusion(bf16[4096,256]{0,1:T(8,128)(2,1)} %constant_dynamic-update-slice_fusion.4, bf16[1024,256]{0,1:T(8,128)(2,1)} %collective-permute-done.2), kind=kLoop, calls=%fused_computation.124 | loop fusion | bytes 1048576
  62.7 5.6 %collective-permute-done.5 = bf16[512,256]{0,1:T(8,128)(2,1)S(1)} collective-permute-done((bf16[512,256]{0,1:T(8,128)(2,1)S(1)}, bf16[512,256]{0,1:T(8,128)(2,1)S(1)}, u32[]{:S(2)}, u32[]{:S(2)}) %collective-permute-start.5) | collective-permute-done | bytes 262176 | tf_op jit(solution)/shard_map/ppermute | solution.py:65
  69.0 1.9 %constant_dynamic-update-slice_fusion = bf16[4096,256]{0,1:T(8,128)(2,1)} fusion(bf16[4096,256]{0,1:T(8,128)(2,1)} %constant_dynamic-update-slice_fusion.1, bf16[1024,256]{0,1:T(8,128)(2,1)} %collective-permute-done.4), kind=kLoop, calls=%fused_computation.121 | loop fusion | bytes 1048576 | tf_op jit(solution)/shard_map/concatenate | solution.py:69
  70.9 2.1 %collective-permute-start.6 = (bf16[4096,256]{0,1:T(8,128)(2,1)}, bf16[4096,256]{0,1:T(8,128)(2,1)}, u32[]{:S(2)}, u32[]{:S(2)}) collective-permute-start(bf16[4096,256]{0,1:T(8,128)(2,1)} %constant_dynamic-update-slice_fusion), channel_id=1, source_target_pairs={{0,12},{12,0},{1,13},{13,1},{2,14},{14,2},{3,15},{15,3},{4,16},{16... | collective-permute-start | bytes 6291464 | tf_op jit(solution)/shard_map/ppermute | solution.py:126
  76.5 1.3 fusion.88
  77.9 1.3 fusion.86
  79.9 3.2 %fusion.15 = (bf16[1,4096,256]{1,2,0:T(8,128)(2,1)S(1)}, bf16[1,4096,256]{1,2,0:T(8,128)(2,1)S(1)}) fusion(s32[]{:T(128)S(6)} %select_n.216, bf16[1,4096,256]{1,2,0:T(8,128)(2,1)} %bitcast.4, bf16[1,4096,256]{1,2,0:T(8,128)(2,1)} %bitcast.5, s32[]{:T(128)S(6)} %select_n.219), kind=kLoop, calls=%fused_computation.22 | loop fusion | flops 2097152 | bytes 8388616 | tf_op jit(solution)/shard_map/stack | solution.py:127
  83.1 1.8 fusion.85
  84.8 1.8 fusion.87
  86.6 3.3 %fusion = (f32[2,192]{1,0:T(2,128)S(1)}, f32[2,192]{1,0:T(2,128)S(1)}) fusion(f32[2,192,4096]{2,1,0:T(8,128)S(1)} %get-tuple-element.34, f32[2,192]{1,0:T(2,128)S(1)} %get-tuple-element.33, pred[192,4096]{1,0:T(8,128)(4,1)S(1)} %get-tuple-element.23, f32[2,192,4096]{2,1,0:T(8,128)S(1)} %get-tuple-element.30, f32[2,192]{1,0:T(2,128)S(1)} %get-tuple-element.29, ...), kind=kLoop, calls=%fused_computation.5 | loop fusion | flops 9436416 | bytes 14161920 | tf_op jit(solution)/shard_map/reduce_sum | solution.py:48
  89.9 1.2 fusion.27
  91.2 1.3 fusion.24
  94.5 2.7 %copy-done.1 = f32[384,4096]{1,0:T(8,128)} copy-done((f32[384,4096]{1,0:T(8,128)}, f32[384,4096]{1,0:T(8,128)S(1)}, u32[]{:S(2)}) %copy-start.1) | copy-done | bytes 6291480
  97.2 1.9 %collective-permute-start.7 = (bf16[32,4096]{1,0:T(8,128)(2,1)S(1)}, bf16[32,4096]{1,0:T(8,128)(2,1)S(1)}, u32[]{:S(2)}, u32[]{:S(2)}) collective-permute-start(bf16[32,4096]{1,0:T(8,128)(2,1)S(1)} %get-tuple-element.19), channel_id=1, source_target_pairs={{0,1},{1,2},{2,3},{3,4},{4,5},{5,6},{6,7},{7,8},{8,9},{9,10},{10,1... | collective-permute-start | bytes 786440 | tf_op jit(solution)/shard_map/ppermute | solution.py:88
  99.2 10.0 %collective-permute-start.13 = (bf16[32,4096]{1,0:T(8,128)(2,1)S(1)}, bf16[32,4096]{1,0:T(8,128)(2,1)S(1)}, u32[]{:S(2)}, u32[]{:S(2)}) collective-permute-start(bf16[32,4096]{1,0:T(8,128)(2,1)S(1)} %get-tuple-element.20), channel_id=1, source_target_pairs={{0,11},{1,0},{2,1},{3,2},{4,3},{5,4},{6,5},{7,6},{8,7},{9,8},{10,9... | collective-permute-start | bytes 786440 | tf_op jit(solution)/shard_map/ppermute | solution.py:93
  109.2 5.0 %collective-permute-done.7 = bf16[32,4096]{1,0:T(8,128)(2,1)S(1)} collective-permute-done((bf16[32,4096]{1,0:T(8,128)(2,1)S(1)}, bf16[32,4096]{1,0:T(8,128)(2,1)S(1)}, u32[]{:S(2)}, u32[]{:S(2)}) %collective-permute-start.7) | collective-permute-done | bytes 262176 | tf_op jit(solution)/shard_map/ppermute | solution.py:88
  115.3 1.9 %collective-permute-start.8 = (bf16[32,4096]{1,0:T(8,128)(2,1)S(1)}, bf16[32,4096]{1,0:T(8,128)(2,1)S(1)}, u32[]{:S(2)}, u32[]{:S(2)}) collective-permute-start(bf16[32,4096]{1,0:T(8,128)(2,1)S(1)} %add_convert_fusion.9), channel_id=1, source_target_pairs={{0,1},{1,2},{2,3},{3,4},{4,5},{5,6},{6,7},{7,8},{8,9},{9,10},{10,1... | collective-permute-start | bytes 786440 | tf_op jit(solution)/shard_map/ppermute | solution.py:88
  117.3 9.3 %collective-permute-done.8 = bf16[32,4096]{1,0:T(8,128)(2,1)S(1)} collective-permute-done((bf16[32,4096]{1,0:T(8,128)(2,1)S(1)}, bf16[32,4096]{1,0:T(8,128)(2,1)S(1)}, u32[]{:S(2)}, u32[]{:S(2)}) %collective-permute-start.8) | collective-permute-done | bytes 262176 | tf_op jit(solution)/shard_map/ppermute | solution.py:88
  126.6 1.3 add_convert_fusion.8
  127.9 1.9 %collective-permute-start.9 = (bf16[32,4096]{1,0:T(8,128)(2,1)S(1)}, bf16[32,4096]{1,0:T(8,128)(2,1)S(1)}, u32[]{:S(2)}, u32[]{:S(2)}) collective-permute-start(bf16[32,4096]{1,0:T(8,128)(2,1)S(1)} %get-tuple-element.17), channel_id=1, source_target_pairs={{0,1},{1,2},{2,3},{3,4},{4,5},{5,6},{6,7},{7,8},{8,9},{9,10},{10,1... | collective-permute-start | bytes 786440 | tf_op jit(solution)/shard_map/ppermute | solution.py:88
  129.8 5.1 %collective-permute-start.14 = (bf16[32,4096]{1,0:T(8,128)(2,1)S(1)}, bf16[32,4096]{1,0:T(8,128)(2,1)S(1)}, u32[]{:S(2)}, u32[]{:S(2)}) collective-permute-start(bf16[32,4096]{1,0:T(8,128)(2,1)S(1)} %get-tuple-element.18), channel_id=1, source_target_pairs={{0,11},{1,0},{2,1},{3,2},{4,3},{5,4},{6,5},{7,6},{8,7},{9,8},{10,9... | collective-permute-start | bytes 786440 | tf_op jit(solution)/shard_map/ppermute | solution.py:93
  135.0 3.3 %collective-permute-done.9 = bf16[32,4096]{1,0:T(8,128)(2,1)S(1)} collective-permute-done((bf16[32,4096]{1,0:T(8,128)(2,1)S(1)}, bf16[32,4096]{1,0:T(8,128)(2,1)S(1)}, u32[]{:S(2)}, u32[]{:S(2)}) %collective-permute-start.9) | collective-permute-done | bytes 262176 | tf_op jit(solution)/shard_map/ppermute | solution.py:88
  138.3 1.2 collective-permute-done.14
  139.4 1.3 add_convert_fusion.7
  140.7 1.9 %collective-permute-start.10 = (bf16[32,4096]{1,0:T(8,128)(2,1)S(1)}, bf16[32,4096]{1,0:T(8,128)(2,1)S(1)}, u32[]{:S(2)}, u32[]{:S(2)}) collective-permute-start(bf16[32,4096]{1,0:T(8,128)(2,1)S(1)} %get-tuple-element.15), channel_id=1, source_target_pairs={{0,1},{1,2},{2,3},{3,4},{4,5},{5,6},{6,7},{7,8},{8,9},{9,10},{10,1... | collective-permute-start | bytes 786440 | tf_op jit(solution)/shard_map/ppermute | solution.py:88
  142.7 5.6 %collective-permute-start.15 = (bf16[32,4096]{1,0:T(8,128)(2,1)S(1)}, bf16[32,4096]{1,0:T(8,128)(2,1)S(1)}, u32[]{:S(2)}, u32[]{:S(2)}) collective-permute-start(bf16[32,4096]{1,0:T(8,128)(2,1)S(1)} %get-tuple-element.16), channel_id=1, source_target_pairs={{0,11},{1,0},{2,1},{3,2},{4,3},{5,4},{6,5},{7,6},{8,7},{9,8},{10,9... | collective-permute-start | bytes 786440 | tf_op jit(solution)/shard_map/ppermute | solution.py:93
  148.3 2.4 %collective-permute-done.10 = bf16[32,4096]{1,0:T(8,128)(2,1)S(1)} collective-permute-done((bf16[32,4096]{1,0:T(8,128)(2,1)S(1)}, bf16[32,4096]{1,0:T(8,128)(2,1)S(1)}, u32[]{:S(2)}, u32[]{:S(2)}) %collective-permute-start.10) | collective-permute-done | bytes 262176 | tf_op jit(solution)/shard_map/ppermute | solution.py:88
  150.7 1.4 collective-permute-done.15
  152.1 1.3 add_convert_fusion.6
  153.4 1.9 %collective-permute-start.11 = (bf16[32,4096]{1,0:T(8,128)(2,1)S(1)}, bf16[32,4096]{1,0:T(8,128)(2,1)S(1)}, u32[]{:S(2)}, u32[]{:S(2)}) collective-permute-start(bf16[32,4096]{1,0:T(8,128)(2,1)S(1)} %get-tuple-element.13), channel_id=1, source_target_pairs={{0,1},{1,2},{2,3},{3,4},{4,5},{5,6},{6,7},{7,8},{8,9},{9,10},{10,1... | collective-permute-start | bytes 786440 | tf_op jit(solution)/shard_map/ppermute | solution.py:88
  155.4 5.6 %collective-permute-start.16 = (bf16[32,4096]{1,0:T(8,128)(2,1)S(1)}, bf16[32,4096]{1,0:T(8,128)(2,1)S(1)}, u32[]{:S(2)}, u32[]{:S(2)}) collective-permute-start(bf16[32,4096]{1,0:T(8,128)(2,1)S(1)} %get-tuple-element.14), channel_id=1, source_target_pairs={{0,11},{1,0},{2,1},{3,2},{4,3},{5,4},{6,5},{7,6},{8,7},{9,8},{10,9... | collective-permute-start | bytes 786440 | tf_op jit(solution)/shard_map/ppermute | solution.py:93
  161.0 2.4 %collective-permute-done.11 = bf16[32,4096]{1,0:T(8,128)(2,1)S(1)} collective-permute-done((bf16[32,4096]{1,0:T(8,128)(2,1)S(1)}, bf16[32,4096]{1,0:T(8,128)(2,1)S(1)}, u32[]{:S(2)}, u32[]{:S(2)}) %collective-permute-start.11) | collective-permute-done | bytes 262176 | tf_op jit(solution)/shard_map/ppermute | solution.py:88
  163.4 1.5 collective-permute-done.16
  164.8 1.3 add_convert_fusion.5
  166.1 5.6 %collective-permute-start.17 = (bf16[32,4096]{1,0:T(8,128)(2,1)S(1)}, bf16[32,4096]{1,0:T(8,128)(2,1)S(1)}, u32[]{:S(2)}, u32[]{:S(2)}) collective-permute-start(bf16[32,4096]{1,0:T(8,128)(2,1)S(1)} %get-tuple-element.12), channel_id=1, source_target_pairs={{0,11},{1,0},{2,1},{3,2},{4,3},{5,4},{6,5},{7,6},{8,7},{9,8},{10,9... | collective-permute-start | bytes 786440 | tf_op jit(solution)/shard_map/ppermute | solution.py:93
  171.7 1.9 %collective-permute-start.12 = (bf16[32,4096]{1,0:T(8,128)(2,1)S(1)}, bf16[32,4096]{1,0:T(8,128)(2,1)S(1)}, u32[]{:S(2)}, u32[]{:S(2)}) collective-permute-start(bf16[32,4096]{1,0:T(8,128)(2,1)S(1)} %get-tuple-element.11), channel_id=1, source_target_pairs={{0,1},{1,2},{2,3},{3,4},{4,5},{5,6},{6,7},{7,8},{8,9},{9,10},{10,1... | collective-permute-start | bytes 786440 | tf_op jit(solution)/shard_map/ppermute | solution.py:88
  173.7 1.9 %collective-permute-done.17 = bf16[32,4096]{1,0:T(8,128)(2,1)S(1)} collective-permute-done((bf16[32,4096]{1,0:T(8,128)(2,1)S(1)}, bf16[32,4096]{1,0:T(8,128)(2,1)S(1)}, u32[]{:S(2)}, u32[]{:S(2)}) %collective-permute-start.17) | collective-permute-done | bytes 262176 | tf_op jit(solution)/shard_map/ppermute | solution.py:93
  175.6 5.6 %collective-permute-done.12 = bf16[32,4096]{1,0:T(8,128)(2,1)S(1)} collective-permute-done((bf16[32,4096]{1,0:T(8,128)(2,1)S(1)}, bf16[32,4096]{1,0:T(8,128)(2,1)S(1)}, u32[]{:S(2)}, u32[]{:S(2)}) %collective-permute-start.12) | collective-permute-done | bytes 262176 | tf_op jit(solution)/shard_map/ppermute | solution.py:88
  181.2 1.8 add_convert_fusion
  (55 shorter events, 17.6 us)
Async XLA Ops:
  0.0 93.5 %copy-start = (bf16[256,4096]{1,0:T(8,128)(2,1)S(1)}, bf16[256,4096]{1,0:T(8,128)(2,1)}, u32[]{:S(2)}) copy-start(bf16[256,4096]{1,0:T(8,128)(2,1)} %param.8) | copy-start | bytes 6291460
  28.6 21.3 %collective-permute-start.2 = (bf16[1024,256]{0,1:T(8,128)(2,1)S(1)}, bf16[1024,256]{0,1:T(8,128)(2,1)}, u32[]{:S(2)}, u32[]{:S(2)}) collective-permute-start(bf16[1024,256]{0,1:T(8,128)(2,1)S(1)} %all_gather.7), channel_id=1, source_target_pairs={{0,192},{192,384},{384,576},{576,0},{1,193},{193,385},{385,577},{5... | collective-permute-start | bytes 1572872 | tf_op jit(solution)/shard_map/ppermute | solution.py:59
  35.5 20.6 %collective-permute-start.4 = (bf16[1024,256]{0,1:T(8,128)(2,1)S(1)}, bf16[1024,256]{0,1:T(8,128)(2,1)}, u32[]{:S(2)}, u32[]{:S(2)}) collective-permute-start(bf16[1024,256]{0,1:T(8,128)(2,1)S(1)} %all_gather.7), channel_id=1, source_target_pairs={{0,576},{192,0},{384,192},{576,384},{1,577},{193,1},{385,193},{577... | collective-permute-start | bytes 1572872 | tf_op jit(solution)/shard_map/ppermute | solution.py:60
  39.2 35.4 %collective-permute-start = (bf16[256,256]{0,1:T(8,128)(2,1)}, bf16[256,256]{0,1:T(8,128)(2,1)}, u32[]{:S(2)}, u32[]{:S(2)}) collective-permute-start(bf16[256,256]{0,1:T(8,128)(2,1)} %slice.48), channel_id=1, source_target_pairs={{0,12},{12,24},{24,36},{36,48},{48,60},{60,72},{72,84},{84,96},{96... | collective-permute-start | bytes 393224 | tf_op jit(solution)/shard_map/ppermute | solution.py:22
  42.9 32.7 %collective-permute-start.1 = (bf16[256,256]{0,1:T(8,128)(2,1)}, bf16[256,256]{0,1:T(8,128)(2,1)}, u32[]{:S(2)}, u32[]{:S(2)}) collective-permute-start(bf16[256,256]{0,1:T(8,128)(2,1)} %slice.49), channel_id=1, source_target_pairs={{0,12},{12,24},{24,36},{36,48},{48,60},{60,72},{72,84},{84,96},{96... | collective-permute-start | bytes 393224 | tf_op jit(solution)/shard_map/ppermute | solution.py:22
  49.6 23.4 %copy-start.3 = (pred[384,4096]{1,0:T(8,128)(4,1)S(1)}, pred[384,4096]{1,0:T(8,128)(4,1)}, u32[]{:S(2)}) copy-start(pred[384,4096]{1,0:T(8,128)(4,1)} %subtract_compare_fusion) | copy-start | bytes 4718596
  51.0 10.9 %collective-permute-start.3 = (bf16[512,256]{0,1:T(8,128)(2,1)S(1)}, bf16[512,256]{0,1:T(8,128)(2,1)S(1)}, u32[]{:S(2)}, u32[]{:S(2)}) collective-permute-start(bf16[512,256]{0,1:T(8,128)(2,1)S(1)} %slice.51), channel_id=1, source_target_pairs={{0,192},{192,384},{384,576},{576,0},{1,193},{193,385},{385,577},{5... | collective-permute-start | bytes 786440 | tf_op jit(solution)/shard_map/ppermute | solution.py:64
  57.2 11.0 %collective-permute-start.5 = (bf16[512,256]{0,1:T(8,128)(2,1)S(1)}, bf16[512,256]{0,1:T(8,128)(2,1)S(1)}, u32[]{:S(2)}, u32[]{:S(2)}) collective-permute-start(bf16[512,256]{0,1:T(8,128)(2,1)S(1)} %slice.52), channel_id=1, source_target_pairs={{0,576},{192,0},{384,192},{576,384},{1,577},{193,1},{385,193},{577... | collective-permute-start | bytes 786440 | tf_op jit(solution)/shard_map/ppermute | solution.py:65
  60.0 14.0 %copy-start.6 = (bf16[384,256]{1,0:T(8,128)(2,1)S(1)}, bf16[384,256]{1,0:T(8,128)(2,1)}, u32[]{:S(2)}) copy-start(bf16[384,256]{1,0:T(8,128)(2,1)} %param.5) | copy-start | bytes 589828
  70.9 9.0 %collective-permute-start.6 = (bf16[4096,256]{0,1:T(8,128)(2,1)}, bf16[4096,256]{0,1:T(8,128)(2,1)}, u32[]{:S(2)}, u32[]{:S(2)}) collective-permute-start(bf16[4096,256]{0,1:T(8,128)(2,1)} %constant_dynamic-update-slice_fusion), channel_id=1, source_target_pairs={{0,12},{12,0},{1,13},{13,1},{2,14},{14,2},{3,15},{15,3},{4,16},{16... | collective-permute-start | bytes 6291464 | tf_op jit(solution)/shard_map/ppermute | solution.py:126
  79.9 3.2 %copy-start.2 = (pred[192,4096]{1,0:T(8,128)(4,1)S(1)}, pred[192,4096]{1,0:T(8,128)(4,1)}, u32[]{:S(2)}) copy-start(pred[192,4096]{1,0:T(8,128)(4,1)} %get-tuple-element.24) | copy-start | bytes 2359300
  79.9 3.2 %copy-start.5 = (bf16[24,2,8,128]{3,2,1,0:T(8,128)(2,1)S(1)}, bf16[24,2,8,128]{3,2,1,0:T(8,128)(2,1)}, u32[]{:S(2)}) copy-start(bf16[24,2,8,128]{3,2,1,0:T(8,128)(2,1)} %get-tuple-element.28) | copy-start | bytes 294916
  83.1 1.8 copy-start.4
  94.5 2.7 %copy-start.1 = (f32[384,4096]{1,0:T(8,128)}, f32[384,4096]{1,0:T(8,128)S(1)}, u32[]{:S(2)}) copy-start(f32[384,4096]{1,0:T(8,128)S(1)} %fusion.89) | copy-start | bytes 18874372
  97.2 17.0 %collective-permute-start.7 = (bf16[32,4096]{1,0:T(8,128)(2,1)S(1)}, bf16[32,4096]{1,0:T(8,128)(2,1)S(1)}, u32[]{:S(2)}, u32[]{:S(2)}) collective-permute-start(bf16[32,4096]{1,0:T(8,128)(2,1)S(1)} %get-tuple-element.19), channel_id=1, source_target_pairs={{0,1},{1,2},{2,3},{3,4},{4,5},{5,6},{6,7},{7,8},{8,9},{9,10},{10,1... | collective-permute-start | bytes 786440 | tf_op jit(solution)/shard_map/ppermute | solution.py:88
  99.2 18.1 %collective-permute-start.13 = (bf16[32,4096]{1,0:T(8,128)(2,1)S(1)}, bf16[32,4096]{1,0:T(8,128)(2,1)S(1)}, u32[]{:S(2)}, u32[]{:S(2)}) collective-permute-start(bf16[32,4096]{1,0:T(8,128)(2,1)S(1)} %get-tuple-element.20), channel_id=1, source_target_pairs={{0,11},{1,0},{2,1},{3,2},{4,3},{5,4},{6,5},{7,6},{8,7},{9,8},{10,9... | collective-permute-start | bytes 786440 | tf_op jit(solution)/shard_map/ppermute | solution.py:93
  115.3 11.3 %collective-permute-start.8 = (bf16[32,4096]{1,0:T(8,128)(2,1)S(1)}, bf16[32,4096]{1,0:T(8,128)(2,1)S(1)}, u32[]{:S(2)}, u32[]{:S(2)}) collective-permute-start(bf16[32,4096]{1,0:T(8,128)(2,1)S(1)} %add_convert_fusion.9), channel_id=1, source_target_pairs={{0,1},{1,2},{2,3},{3,4},{4,5},{5,6},{6,7},{7,8},{8,9},{9,10},{10,1... | collective-permute-start | bytes 786440 | tf_op jit(solution)/shard_map/ppermute | solution.py:88
  127.9 10.4 %collective-permute-start.9 = (bf16[32,4096]{1,0:T(8,128)(2,1)S(1)}, bf16[32,4096]{1,0:T(8,128)(2,1)S(1)}, u32[]{:S(2)}, u32[]{:S(2)}) collective-permute-start(bf16[32,4096]{1,0:T(8,128)(2,1)S(1)} %get-tuple-element.17), channel_id=1, source_target_pairs={{0,1},{1,2},{2,3},{3,4},{4,5},{5,6},{6,7},{7,8},{8,9},{9,10},{10,1... | collective-permute-start | bytes 786440 | tf_op jit(solution)/shard_map/ppermute | solution.py:88
  129.8 9.7 %collective-permute-start.14 = (bf16[32,4096]{1,0:T(8,128)(2,1)S(1)}, bf16[32,4096]{1,0:T(8,128)(2,1)S(1)}, u32[]{:S(2)}, u32[]{:S(2)}) collective-permute-start(bf16[32,4096]{1,0:T(8,128)(2,1)S(1)} %get-tuple-element.18), channel_id=1, source_target_pairs={{0,11},{1,0},{2,1},{3,2},{4,3},{5,4},{6,5},{7,6},{8,7},{9,8},{10,9... | collective-permute-start | bytes 786440 | tf_op jit(solution)/shard_map/ppermute | solution.py:93
  140.7 10.0 %collective-permute-start.10 = (bf16[32,4096]{1,0:T(8,128)(2,1)S(1)}, bf16[32,4096]{1,0:T(8,128)(2,1)S(1)}, u32[]{:S(2)}, u32[]{:S(2)}) collective-permute-start(bf16[32,4096]{1,0:T(8,128)(2,1)S(1)} %get-tuple-element.15), channel_id=1, source_target_pairs={{0,1},{1,2},{2,3},{3,4},{4,5},{5,6},{6,7},{7,8},{8,9},{9,10},{10,1... | collective-permute-start | bytes 786440 | tf_op jit(solution)/shard_map/ppermute | solution.py:88
  142.7 9.5 %collective-permute-start.15 = (bf16[32,4096]{1,0:T(8,128)(2,1)S(1)}, bf16[32,4096]{1,0:T(8,128)(2,1)S(1)}, u32[]{:S(2)}, u32[]{:S(2)}) collective-permute-start(bf16[32,4096]{1,0:T(8,128)(2,1)S(1)} %get-tuple-element.16), channel_id=1, source_target_pairs={{0,11},{1,0},{2,1},{3,2},{4,3},{5,4},{6,5},{7,6},{8,7},{9,8},{10,9... | collective-permute-start | bytes 786440 | tf_op jit(solution)/shard_map/ppermute | solution.py:93
  153.4 9.9 %collective-permute-start.11 = (bf16[32,4096]{1,0:T(8,128)(2,1)S(1)}, bf16[32,4096]{1,0:T(8,128)(2,1)S(1)}, u32[]{:S(2)}, u32[]{:S(2)}) collective-permute-start(bf16[32,4096]{1,0:T(8,128)(2,1)S(1)} %get-tuple-element.13), channel_id=1, source_target_pairs={{0,1},{1,2},{2,3},{3,4},{4,5},{5,6},{6,7},{7,8},{8,9},{9,10},{10,1... | collective-permute-start | bytes 786440 | tf_op jit(solution)/shard_map/ppermute | solution.py:88
  155.4 9.5 %collective-permute-start.16 = (bf16[32,4096]{1,0:T(8,128)(2,1)S(1)}, bf16[32,4096]{1,0:T(8,128)(2,1)S(1)}, u32[]{:S(2)}, u32[]{:S(2)}) collective-permute-start(bf16[32,4096]{1,0:T(8,128)(2,1)S(1)} %get-tuple-element.14), channel_id=1, source_target_pairs={{0,11},{1,0},{2,1},{3,2},{4,3},{5,4},{6,5},{7,6},{8,7},{9,8},{10,9... | collective-permute-start | bytes 786440 | tf_op jit(solution)/shard_map/ppermute | solution.py:93
  166.1 9.5 %collective-permute-start.17 = (bf16[32,4096]{1,0:T(8,128)(2,1)S(1)}, bf16[32,4096]{1,0:T(8,128)(2,1)S(1)}, u32[]{:S(2)}, u32[]{:S(2)}) collective-permute-start(bf16[32,4096]{1,0:T(8,128)(2,1)S(1)} %get-tuple-element.12), channel_id=1, source_target_pairs={{0,11},{1,0},{2,1},{3,2},{4,3},{5,4},{6,5},{7,6},{8,7},{9,8},{10,9... | collective-permute-start | bytes 786440 | tf_op jit(solution)/shard_map/ppermute | solution.py:93
  171.7 9.5 %collective-permute-start.12 = (bf16[32,4096]{1,0:T(8,128)(2,1)S(1)}, bf16[32,4096]{1,0:T(8,128)(2,1)S(1)}, u32[]{:S(2)}, u32[]{:S(2)}) collective-permute-start(bf16[32,4096]{1,0:T(8,128)(2,1)S(1)} %get-tuple-element.11), channel_id=1, source_target_pairs={{0,1},{1,2},{2,3},{3,4},{4,5},{5,6},{6,7},{7,8},{8,9},{9,10},{10,1... | collective-permute-start | bytes 786440 | tf_op jit(solution)/shard_map/ppermute | solution.py:88

commit v8 on v7

--- a/solution.py
+++ b/solution.py
@@ -31,21 +31,29 @@
     return (top_score, totals, weighted)
 
 
-def attend(query_rows, keys, values, allowed):
+def attend(query_rows, parts):
     scale = 1.0 / math.sqrt(HEAD_DIM)
     rows, width = query_rows.shape
     heads = width // HEAD_DIM
     q = query_rows.reshape(rows, heads, HEAD_DIM)
-    k = keys.reshape(keys.shape[0], heads, HEAD_DIM)
-    s = jnp.einsum("qhd,khd->hqk", q, k, preferred_element_type=jnp.float32) * scale
-    s = jnp.where(allowed[None], s, LOW_SCORE)
-    top = s.max(axis=2)
-    w = jnp.where(allowed[None], jnp.exp(s - top[:, :, None]), 0.0)
-    v = values.reshape(values.shape[0], heads, HEAD_DIM)
-    summed = jnp.einsum(
-        "hqk,khd->hqd", w.astype(jnp.bfloat16), v, preferred_element_type=jnp.float32
-    )
-    return top, w.sum(axis=2), summed
+    scores = []
+    for keys, _, allowed in parts:
+        k = keys.reshape(keys.shape[0], heads, HEAD_DIM)
+        s = jnp.einsum("qhd,khd->hqk", q, k, preferred_element_type=jnp.float32) * scale
+        scores.append(jnp.where(allowed[None], s, LOW_SCORE))
+    top = scores[0].max(axis=2)
+    for s in scores[1:]:
+        top = jnp.maximum(top, s.max(axis=2))
+    total = 0.0
+    summed = 0.0
+    for s, (_, values, allowed) in zip(scores, parts):
+        w = jnp.where(allowed[None], jnp.exp(s - top[:, :, None]), 0.0)
+        total = total + w.sum(axis=2)
+        v = values.reshape(values.shape[0], heads, HEAD_DIM)
+        summed = summed + jnp.einsum(
+            "hqk,khd->hqd", w.astype(jnp.bfloat16), v, preferred_element_type=jnp.float32
+        )
+    return top, total, summed
 
 
 def gather_row_blocks(block, axis):
@@ -53,7 +61,10 @@
     if count != 4:
         gathered = lax.all_gather(block, axis, axis=0, tiled=True)
         me = lax.axis_index(axis)
-        return gathered, [(j - me) for j in range(count)]
+        rows = block.shape[0]
+        return [gathered[j * rows : (j + 1) * rows] for j in range(count)], [
+            j - me for j in range(count)
+        ]
     ahead = [(j, (j + 1) % count) for j in range(count)]
     behind = [(j, (j - 1) % count) for j in range(count)]
     from_left = lax.ppermute(block, axis, ahead)
@@ -66,7 +77,7 @@
         ],
         axis=0,
     )
-    return jnp.concatenate([block, from_left, far, from_right], axis=0), [0, -1, -2, 1]
+    return [block, from_left, far, from_right], [0, -1, -2, 1]
 
 
 def ring_reduce_scatter(partial, axis):
@@ -110,7 +121,7 @@
     band_mask = (band_gap >= 0) & (band_gap < BAND) & (band_pos[None, :] >= 0)
     chunk = tok_rows // QUERY_CHUNKS
     near = [
-        attend(queries[low : low + chunk], band_keys, band_values, band_mask[low : low + chunk])
+        attend(queries[low : low + chunk], [(band_keys, band_values, band_mask[low : low + chunk])])
         for low in range(0, tok_rows, chunk)
     ]
     core = lax.axis_index(CORE)
@@ -122,23 +133,22 @@
     )
     my_half = lax.dynamic_slice_in_dim(chip_rows, core * width, width, 1)
     gathered = lax.all_gather(my_half, "cy", axis=0, tiled=True)
-    gathered, offsets = gather_row_blocks(gathered, "cx")
-    other = lax.ppermute(gathered, CORE, [(0, 1), (1, 0)])
-    both = jnp.stack([gathered, other])
-    all_sum_keys = both[core]
-    all_sum_values = both[1 - core]
-    index = jnp.arange(all_sum_keys.shape[0], dtype=jnp.int32)
-    row_len = index.shape[0] // len(offsets)
-    x_count = lax.axis_size("cx")
-    moved = jnp.asarray(offsets, jnp.int32)[index // row_len]
-    source_x = (lax.axis_index("cx") + moved) % x_count
-    owner = source_x * (row_len // half_sum) + (index % row_len) // half_sum
-    key_pos = owner * tok_rows + jnp.where(owner % 2 == 0, tok_rows - half_sum, 0) + index % half_sum
-    sum_mask = own_pos[:, None] - key_pos[None, :] >= BAND
+    blocks, offsets = gather_row_blocks(gathered, "cx")
+    others = lax.ppermute(tuple(blocks), CORE, [(0, 1), (1, 0)])
+    first = core == 0
+    row_len = blocks[0].shape[0]
+    index = jnp.arange(row_len, dtype=jnp.int32)
+    far_parts = []
+    for mine, other, moved in zip(blocks, others, offsets):
+        source_x = (lax.axis_index("cx") + moved) % lax.axis_size("cx")
+        owner = source_x * (row_len // half_sum) + index // half_sum
+        key_pos = owner * tok_rows + jnp.where(owner % 2 == 0, tok_rows - half_sum, 0) + index % half_sum
+        allowed = own_pos[:, None] - key_pos[None, :] >= BAND
+        far_parts.append((jnp.where(first, mine, other), jnp.where(first, other, mine), allowed))
     pieces = []
     for low in range(0, tok_rows, chunk):
         rows = slice(low, low + chunk)
-        far = attend(queries[rows], all_sum_keys, all_sum_values, sum_mask[rows])
+        far = attend(queries[rows], [(k, v, ok[rows]) for k, v, ok in far_parts])
         merged = combine_terms(near[low // chunk], far)
         pieces.append(merged[2] / merged[1][:, :, None])
     heads_out = jnp.concatenate(pieces, axis=1)

time: 184 us -> 186 us (1.011)
  the two profiles are of different devices: /device:TPU:14 before, /device:TPU:24 now
where the time goes in v8:
time: 186 us; the launch traced here: 185 us
  starting transfers between devices  73 us (39%)
  waiting for transfers between devices  33.9 us (18%)
  blocking collectives  31.3 us (17%)
  other arithmetic  17.9 us (10%)
  local copies, waits for them, and re-layouts  15.9 us (9%)
  matrix products  12.4 us (7%)
    ppermute x5, starting transfers between devices, ring_reduce_scatter(): down_sum = lax.ppermute(down, axis, behind).astype(jnp.float32)  32.9 us
    all_gather x1, blocking collectives, layer(): gathered = lax.all_gather(my_half, 'cy', axis=0, tiled=True)  29.4 us
    ppermute x6, waiting for transfers between devices, ring_reduce_scatter(): lax.ppermute(up, axis, ahead).astype(jnp.float32)  27.9 us
    ppermute x6, starting transfers between devices, ring_reduce_scatter(): lax.ppermute(up, axis, ahead).astype(jnp.float32)  11.5 us
    ppermute x4, starting transfers between devices, layer(): others = lax.ppermute(tuple(blocks), CORE, [(0, 1), (1, 0)])  8.47 us
    unnamed x28, local copies, waits for them, and re-layouts  7.84 us
    ppermute x2, starting transfers between devices, shifted(): lax.ppermute(value, axis, [(source, source + steps) for source in range(l...  6.98 us
    convert_element_type x5, other arithmetic, ring_reduce_scatter(): up = up_sum.astype(jnp.bfloat16)  6.24 us
  transfers between devices with their start and end apart: 21, of which 10 were waited for; matrix products, arithmetic and copies ran while one was open for 12% of the time, Pallas kernels for 0%

profile of v8, /device:TPU:24, one launch (start us, length us, event | category | flops | bytes accessed | tf_op | source)
XLA Modules:
  0.0 185.3 jit_solution(15423753850770413864)
XLA Ops:
  1.7 1.9 %all_gather.6 = bf16[128,512]{1,0:T(8,128)(2,1)S(1)} all-gather(bf16[64,512]{1,0:T(8,128)(2,1)S(1)} %pad_maximum_fusion.2), channel_id=1, replica_groups=mesh['cx'=4,'cy'=8,'cc'=2,'head'=12] {'cc'}, dimensions={0}, use_global_device_ids=true | all-gather | bytes 196608 | tf_op jit(solution)/shard_map/all_gather | solution.py:131
  3.6 29.4 %all_gather.7 = bf16[1024,256]{1,0:T(8,128)(2,1)S(1)} all-gather(bf16[128,256]{1,0:T(8,128)(2,1)S(1)} %constant_dynamic-slice_fusion), channel_id=1, replica_groups=mesh['cx'=4,'cy'=8,'cc'=2,'head'=12] {'cy'}, dimensions={0}, use_global_device_ids=true | all-gather | bytes 589824 | tf_op jit(solution)/shard_map/all_gather | solution.py:135
  33.0 1.9 %collective-permute-start.2 = (bf16[1024,256]{1,0:T(8,128)(2,1)S(1)}, bf16[1024,256]{1,0:T(8,128)(2,1)}, u32[]{:S(2)}, u32[]{:S(2)}) collective-permute-start(bf16[1024,256]{1,0:T(8,128)(2,1)S(1)} %all_gather.7), channel_id=1, source_target_pairs={{0,12},{12,0},{1,13},{13,1},{2,14},{14,2},{3,15},{15,3},{4,16},{16... | collective-permute-start | bytes 1572872 | tf_op jit(solution)/shard_map/ppermute | solution.py:137
  34.9 1.9 %collective-permute-start.6 = (bf16[1024,256]{1,0:T(8,128)(2,1)S(1)}, bf16[1024,256]{1,0:T(8,128)(2,1)}, u32[]{:S(2)}, u32[]{:S(2)}) collective-permute-start(bf16[1024,256]{1,0:T(8,128)(2,1)S(1)} %all_gather.7), channel_id=1, source_target_pairs={{0,576},{192,0},{384,192},{576,384},{1,577},{193,1},{385,193},{577... | collective-permute-start | bytes 1572872 | tf_op jit(solution)/shard_map/ppermute | solution.py:71
  36.8 3.9 %collective-permute-start.3 = (bf16[1024,256]{1,0:T(8,128)(2,1)S(1)}, bf16[1024,256]{1,0:T(8,128)(2,1)S(1)}, u32[]{:S(2)}, u32[]{:S(2)}) collective-permute-start(bf16[1024,256]{1,0:T(8,128)(2,1)S(1)} %all_gather.7), channel_id=1, source_target_pairs={{0,192},{192,384},{384,576},{576,0},{1,193},{193,385},{385,577},{5... | collective-permute-start | bytes 1572872 | tf_op jit(solution)/shard_map/ppermute | solution.py:70
  40.7 1.1 copy.21
  42.5 1.9 %collective-permute-start = (bf16[256,256]{0,1:T(8,128)(2,1)}, bf16[256,256]{0,1:T(8,128)(2,1)}, u32[]{:S(2)}, u32[]{:S(2)}) collective-permute-start(bf16[256,256]{0,1:T(8,128)(2,1)} %slice.67), channel_id=1, source_target_pairs={{0,12},{12,24},{24,36},{36,48},{48,60},{60,72},{72,84},{84,96},{96... | collective-permute-start | bytes 393224 | tf_op jit(solution)/shard_map/ppermute | solution.py:22
  44.4 1.1 copy.25
  46.2 5.1 %collective-permute-start.1 = (bf16[256,256]{0,1:T(8,128)(2,1)}, bf16[256,256]{0,1:T(8,128)(2,1)}, u32[]{:S(2)}, u32[]{:S(2)}) collective-permute-start(bf16[256,256]{0,1:T(8,128)(2,1)} %slice.68), channel_id=1, source_target_pairs={{0,12},{12,24},{24,36},{36,48},{48,60},{60,72},{72,84},{84,96},{96... | collective-permute-start | bytes 393224 | tf_op jit(solution)/shard_map/ppermute | solution.py:22
  51.5 1.1 subtract_compare_fusion.2
  58.7 1.4 fusion.191
  62.1 2.1 %collective-permute-start.5 = (bf16[512,256]{1,0:T(8,128)(2,1)S(1)}, bf16[512,256]{1,0:T(8,128)(2,1)S(1)}, u32[]{:S(2)}, u32[]{:S(2)}) collective-permute-start(bf16[512,256]{1,0:T(8,128)(2,1)S(1)} %slice.72), channel_id=1, source_target_pairs={{0,192},{192,384},{384,576},{576,0},{1,193},{193,385},{385,577},{5... | collective-permute-start | bytes 786440 | tf_op jit(solution)/shard_map/ppermute | solution.py:75
  65.2 5.1 %collective-permute-start.7 = (bf16[512,256]{1,0:T(8,128)(2,1)S(1)}, bf16[512,256]{1,0:T(8,128)(2,1)S(1)}, u32[]{:S(2)}, u32[]{:S(2)}) collective-permute-start(bf16[512,256]{1,0:T(8,128)(2,1)S(1)} %slice.73), channel_id=1, source_target_pairs={{0,576},{192,0},{384,192},{576,384},{1,577},{193,1},{385,193},{577... | collective-permute-start | bytes 786440 | tf_op jit(solution)/shard_map/ppermute | solution.py:76
  70.3 1.9 %collective-permute-start.9 = (bf16[1024,256]{1,0:T(8,128)(2,1)}, bf16[1024,256]{1,0:T(8,128)(2,1)S(1)}, u32[]{:S(2)}, u32[]{:S(2)}) collective-permute-start(bf16[1024,256]{1,0:T(8,128)(2,1)} %collective-permute-done.6), channel_id=1, source_target_pairs={{0,12},{12,0},{1,13},{13,1},{2,14},{14,2},{3,15},{15,3},{4,16},{16... | collective-permute-start | bytes 1572872 | tf_op jit(solution)/shard_map/ppermute | solution.py:137
  72.3 1.1 select_bitcast_fusion.3
  74.0 2.4 %collective-permute-start.4 = (bf16[1024,256]{1,0:T(8,128)(2,1)S(1)}, bf16[1024,256]{1,0:T(8,128)(2,1)S(1)}, u32[]{:S(2)}, u32[]{:S(2)}) collective-permute-start(bf16[1024,256]{1,0:T(8,128)(2,1)S(1)} %collective-permute-done.3), channel_id=1, source_target_pairs={{0,12},{12,0},{1,13},{13,1},{2,14},{14,2},{3,15},{15,3},{4,16},{16... | collective-permute-start | bytes 1572872 | tf_op jit(solution)/shard_map/ppermute | solution.py:137
  77.0 2.2 %collective-permute-start.8 = (bf16[1024,256]{1,0:T(8,128)(2,1)S(1)}, bf16[1024,256]{1,0:T(8,128)(2,1)S(1)}, u32[]{:S(2)}, u32[]{:S(2)}) collective-permute-start(bf16[1024,256]{1,0:T(8,128)(2,1)S(1)} %constant_dynamic-update-slice_fusion), channel_id=1, source_target_pairs={{0,12},{12,0},{1,13},{13,1},{2,14},{14,2},{3,15},{15,3},{4,16},{16... | collective-permute-start | bytes 1572872 | tf_op jit(solution)/shard_map/ppermute | solution.py:137
  79.3 1.2 select_bitcast_fusion
  87.1 1.6 fusion.14
  91.0 1.6 fusion.6
  95.8 2.7 %copy-done.1 = f32[384,4096]{1,0:T(8,128)} copy-done((f32[384,4096]{1,0:T(8,128)}, f32[384,4096]{1,0:T(8,128)S(1)}, u32[]{:S(2)}) %copy-start.1) | copy-done | bytes 6291480
  98.5 1.9 %collective-permute-start.10 = (bf16[32,4096]{1,0:T(8,128)(2,1)S(1)}, bf16[32,4096]{1,0:T(8,128)(2,1)S(1)}, u32[]{:S(2)}, u32[]{:S(2)}) collective-permute-start(bf16[32,4096]{1,0:T(8,128)(2,1)S(1)} %get-tuple-element.27), channel_id=1, source_target_pairs={{0,1},{1,2},{2,3},{3,4},{4,5},{5,6},{6,7},{7,8},{8,9},{9,10},{10,1... | collective-permute-start | bytes 786440 | tf_op jit(solution)/shard_map/ppermute | solution.py:99
  100.5 11.0 %collective-permute-start.16 = (bf16[32,4096]{1,0:T(8,128)(2,1)S(1)}, bf16[32,4096]{1,0:T(8,128)(2,1)S(1)}, u32[]{:S(2)}, u32[]{:S(2)}) collective-permute-start(bf16[32,4096]{1,0:T(8,128)(2,1)S(1)} %get-tuple-element.28), channel_id=1, source_target_pairs={{0,11},{1,0},{2,1},{3,2},{4,3},{5,4},{6,5},{7,6},{8,7},{9,8},{10,9... | collective-permute-start | bytes 786440 | tf_op jit(solution)/shard_map/ppermute | solution.py:104
  111.5 5.0 %collective-permute-done.10 = bf16[32,4096]{1,0:T(8,128)(2,1)S(1)} collective-permute-done((bf16[32,4096]{1,0:T(8,128)(2,1)S(1)}, bf16[32,4096]{1,0:T(8,128)(2,1)S(1)}, u32[]{:S(2)}, u32[]{:S(2)}) %collective-permute-start.10) | collective-permute-done | bytes 262176 | tf_op jit(solution)/shard_map/ppermute | solution.py:99
  116.5 1.1 add_convert_fusion.9
  117.6 1.9 %collective-permute-start.11 = (bf16[32,4096]{1,0:T(8,128)(2,1)S(1)}, bf16[32,4096]{1,0:T(8,128)(2,1)S(1)}, u32[]{:S(2)}, u32[]{:S(2)}) collective-permute-start(bf16[32,4096]{1,0:T(8,128)(2,1)S(1)} %add_convert_fusion.9), channel_id=1, source_target_pairs={{0,1},{1,2},{2,3},{3,4},{4,5},{5,6},{6,7},{7,8},{8,9},{9,10},{10,1... | collective-permute-start | bytes 786440 | tf_op jit(solution)/shard_map/ppermute | solution.py:99
  119.6 9.3 %collective-permute-done.11 = bf16[32,4096]{1,0:T(8,128)(2,1)S(1)} collective-permute-done((bf16[32,4096]{1,0:T(8,128)(2,1)S(1)}, bf16[32,4096]{1,0:T(8,128)(2,1)S(1)}, u32[]{:S(2)}, u32[]{:S(2)}) %collective-permute-start.11) | collective-permute-done | bytes 262176 | tf_op jit(solution)/shard_map/ppermute | solution.py:99
  128.8 1.3 add_convert_fusion.8
  130.1 1.9 %collective-permute-start.12 = (bf16[32,4096]{1,0:T(8,128)(2,1)S(1)}, bf16[32,4096]{1,0:T(8,128)(2,1)S(1)}, u32[]{:S(2)}, u32[]{:S(2)}) collective-permute-start(bf16[32,4096]{1,0:T(8,128)(2,1)S(1)} %get-tuple-element.25), channel_id=1, source_target_pairs={{0,1},{1,2},{2,3},{3,4},{4,5},{5,6},{6,7},{7,8},{8,9},{9,10},{10,1... | collective-permute-start | bytes 786440 | tf_op jit(solution)/shard_map/ppermute | solution.py:99
  132.0 5.1 %collective-permute-start.17 = (bf16[32,4096]{1,0:T(8,128)(2,1)S(1)}, bf16[32,4096]{1,0:T(8,128)(2,1)S(1)}, u32[]{:S(2)}, u32[]{:S(2)}) collective-permute-start(bf16[32,4096]{1,0:T(8,128)(2,1)S(1)} %get-tuple-element.26), channel_id=1, source_target_pairs={{0,11},{1,0},{2,1},{3,2},{4,3},{5,4},{6,5},{7,6},{8,7},{9,8},{10,9... | collective-permute-start | bytes 786440 | tf_op jit(solution)/shard_map/ppermute | solution.py:104
  137.2 3.3 %collective-permute-done.12 = bf16[32,4096]{1,0:T(8,128)(2,1)S(1)} collective-permute-done((bf16[32,4096]{1,0:T(8,128)(2,1)S(1)}, bf16[32,4096]{1,0:T(8,128)(2,1)S(1)}, u32[]{:S(2)}, u32[]{:S(2)}) %collective-permute-start.12) | collective-permute-done | bytes 262176 | tf_op jit(solution)/shard_map/ppermute | solution.py:99
  140.5 1.2 collective-permute-done.17
  141.7 1.3 add_convert_fusion.7
  143.0 1.9 %collective-permute-start.13 = (bf16[32,4096]{1,0:T(8,128)(2,1)S(1)}, bf16[32,4096]{1,0:T(8,128)(2,1)S(1)}, u32[]{:S(2)}, u32[]{:S(2)}) collective-permute-start(bf16[32,4096]{1,0:T(8,128)(2,1)S(1)} %get-tuple-element.23), channel_id=1, source_target_pairs={{0,1},{1,2},{2,3},{3,4},{4,5},{5,6},{6,7},{7,8},{8,9},{9,10},{10,1... | collective-permute-start | bytes 786440 | tf_op jit(solution)/shard_map/ppermute | solution.py:99
  144.9 5.6 %collective-permute-start.18 = (bf16[32,4096]{1,0:T(8,128)(2,1)S(1)}, bf16[32,4096]{1,0:T(8,128)(2,1)S(1)}, u32[]{:S(2)}, u32[]{:S(2)}) collective-permute-start(bf16[32,4096]{1,0:T(8,128)(2,1)S(1)} %get-tuple-element.24), channel_id=1, source_target_pairs={{0,11},{1,0},{2,1},{3,2},{4,3},{5,4},{6,5},{7,6},{8,7},{9,8},{10,9... | collective-permute-start | bytes 786440 | tf_op jit(solution)/shard_map/ppermute | solution.py:104
  150.5 2.4 %collective-permute-done.13 = bf16[32,4096]{1,0:T(8,128)(2,1)S(1)} collective-permute-done((bf16[32,4096]{1,0:T(8,128)(2,1)S(1)}, bf16[32,4096]{1,0:T(8,128)(2,1)S(1)}, u32[]{:S(2)}, u32[]{:S(2)}) %collective-permute-start.13) | collective-permute-done | bytes 262176 | tf_op jit(solution)/shard_map/ppermute | solution.py:99
  153.0 1.4 collective-permute-done.18
  154.4 1.3 add_convert_fusion.6
  155.7 1.9 %collective-permute-start.14 = (bf16[32,4096]{1,0:T(8,128)(2,1)S(1)}, bf16[32,4096]{1,0:T(8,128)(2,1)S(1)}, u32[]{:S(2)}, u32[]{:S(2)}) collective-permute-start(bf16[32,4096]{1,0:T(8,128)(2,1)S(1)} %get-tuple-element.21), channel_id=1, source_target_pairs={{0,1},{1,2},{2,3},{3,4},{4,5},{5,6},{6,7},{7,8},{8,9},{9,10},{10,1... | collective-permute-start | bytes 786440 | tf_op jit(solution)/shard_map/ppermute | solution.py:99
  157.6 5.6 %collective-permute-start.19 = (bf16[32,4096]{1,0:T(8,128)(2,1)S(1)}, bf16[32,4096]{1,0:T(8,128)(2,1)S(1)}, u32[]{:S(2)}, u32[]{:S(2)}) collective-permute-start(bf16[32,4096]{1,0:T(8,128)(2,1)S(1)} %get-tuple-element.22), channel_id=1, source_target_pairs={{0,11},{1,0},{2,1},{3,2},{4,3},{5,4},{6,5},{7,6},{8,7},{9,8},{10,9... | collective-permute-start | bytes 786440 | tf_op jit(solution)/shard_map/ppermute | solution.py:104
  163.2 2.4 %collective-permute-done.14 = bf16[32,4096]{1,0:T(8,128)(2,1)S(1)} collective-permute-done((bf16[32,4096]{1,0:T(8,128)(2,1)S(1)}, bf16[32,4096]{1,0:T(8,128)(2,1)S(1)}, u32[]{:S(2)}, u32[]{:S(2)}) %collective-permute-start.14) | collective-permute-done | bytes 262176 | tf_op jit(solution)/shard_map/ppermute | solution.py:99
  165.6 1.5 collective-permute-done.19
  167.1 1.3 add_convert_fusion.5
  168.4 5.6 %collective-permute-start.20 = (bf16[32,4096]{1,0:T(8,128)(2,1)S(1)}, bf16[32,4096]{1,0:T(8,128)(2,1)S(1)}, u32[]{:S(2)}, u32[]{:S(2)}) collective-permute-start(bf16[32,4096]{1,0:T(8,128)(2,1)S(1)} %get-tuple-element.20), channel_id=1, source_target_pairs={{0,11},{1,0},{2,1},{3,2},{4,3},{5,4},{6,5},{7,6},{8,7},{9,8},{10,9... | collective-permute-start | bytes 786440 | tf_op jit(solution)/shard_map/ppermute | solution.py:104
  174.0 1.9 %collective-permute-start.15 = (bf16[32,4096]{1,0:T(8,128)(2,1)S(1)}, bf16[32,4096]{1,0:T(8,128)(2,1)S(1)}, u32[]{:S(2)}, u32[]{:S(2)}) collective-permute-start(bf16[32,4096]{1,0:T(8,128)(2,1)S(1)} %get-tuple-element.19), channel_id=1, source_target_pairs={{0,1},{1,2},{2,3},{3,4},{4,5},{5,6},{6,7},{7,8},{8,9},{9,10},{10,1... | collective-permute-start | bytes 786440 | tf_op jit(solution)/shard_map/ppermute | solution.py:99
  175.9 1.9 %collective-permute-done.20 = bf16[32,4096]{1,0:T(8,128)(2,1)S(1)} collective-permute-done((bf16[32,4096]{1,0:T(8,128)(2,1)S(1)}, bf16[32,4096]{1,0:T(8,128)(2,1)S(1)}, u32[]{:S(2)}, u32[]{:S(2)}) %collective-permute-start.20) | collective-permute-done | bytes 262176 | tf_op jit(solution)/shard_map/ppermute | solution.py:104
  177.8 5.6 %collective-permute-done.15 = bf16[32,4096]{1,0:T(8,128)(2,1)S(1)} collective-permute-done((bf16[32,4096]{1,0:T(8,128)(2,1)S(1)}, bf16[32,4096]{1,0:T(8,128)(2,1)S(1)}, u32[]{:S(2)}, u32[]{:S(2)}) %collective-permute-start.15) | collective-permute-done | bytes 262176 | tf_op jit(solution)/shard_map/ppermute | solution.py:99
  183.4 1.8 add_convert_fusion
  (88 shorter events, 25.3 us)
Async XLA Ops:
  0.0 94.8 %copy-start = (bf16[256,4096]{1,0:T(8,128)(2,1)S(1)}, bf16[256,4096]{1,0:T(8,128)(2,1)}, u32[]{:S(2)}) copy-start(bf16[256,4096]{1,0:T(8,128)(2,1)} %param.7) | copy-start | bytes 6291460
  33.0 39.3 %collective-permute-start.2 = (bf16[1024,256]{1,0:T(8,128)(2,1)S(1)}, bf16[1024,256]{1,0:T(8,128)(2,1)}, u32[]{:S(2)}, u32[]{:S(2)}) collective-permute-start(bf16[1024,256]{1,0:T(8,128)(2,1)S(1)} %all_gather.7), channel_id=1, source_target_pairs={{0,12},{12,0},{1,13},{13,1},{2,14},{14,2},{3,15},{15,3},{4,16},{16... | collective-permute-start | bytes 1572872 | tf_op jit(solution)/shard_map/ppermute | solution.py:137
  34.9 29.3 %collective-permute-start.6 = (bf16[1024,256]{1,0:T(8,128)(2,1)S(1)}, bf16[1024,256]{1,0:T(8,128)(2,1)}, u32[]{:S(2)}, u32[]{:S(2)}) collective-permute-start(bf16[1024,256]{1,0:T(8,128)(2,1)S(1)} %all_gather.7), channel_id=1, source_target_pairs={{0,576},{192,0},{384,192},{576,384},{1,577},{193,1},{385,193},{577... | collective-permute-start | bytes 1572872 | tf_op jit(solution)/shard_map/ppermute | solution.py:71
  36.8 25.3 %collective-permute-start.3 = (bf16[1024,256]{1,0:T(8,128)(2,1)S(1)}, bf16[1024,256]{1,0:T(8,128)(2,1)S(1)}, u32[]{:S(2)}, u32[]{:S(2)}) collective-permute-start(bf16[1024,256]{1,0:T(8,128)(2,1)S(1)} %all_gather.7), channel_id=1, source_target_pairs={{0,192},{192,384},{384,576},{576,0},{1,193},{193,385},{385,577},{5... | collective-permute-start | bytes 1572872 | tf_op jit(solution)/shard_map/ppermute | solution.py:70
  42.5 15.2 %collective-permute-start = (bf16[256,256]{0,1:T(8,128)(2,1)}, bf16[256,256]{0,1:T(8,128)(2,1)}, u32[]{:S(2)}, u32[]{:S(2)}) collective-permute-start(bf16[256,256]{0,1:T(8,128)(2,1)} %slice.67), channel_id=1, source_target_pairs={{0,12},{12,24},{24,36},{36,48},{48,60},{60,72},{72,84},{84,96},{96... | collective-permute-start | bytes 393224 | tf_op jit(solution)/shard_map/ppermute | solution.py:22
  46.2 13.9 %collective-permute-start.1 = (bf16[256,256]{0,1:T(8,128)(2,1)}, bf16[256,256]{0,1:T(8,128)(2,1)}, u32[]{:S(2)}, u32[]{:S(2)}) collective-permute-start(bf16[256,256]{0,1:T(8,128)(2,1)} %slice.68), channel_id=1, source_target_pairs={{0,12},{12,24},{24,36},{36,48},{48,60},{60,72},{72,84},{84,96},{96... | collective-permute-start | bytes 393224 | tf_op jit(solution)/shard_map/ppermute | solution.py:22
  56.7 4.3 %copy-start.3 = (pred[192,640]{1,0:T(8,128)(4,1)S(1)}, pred[192,640]{1,0:T(8,128)(4,1)}, u32[]{:S(2)}) copy-start(pred[192,640]{1,0:T(8,128)(4,1)} %get-tuple-element.46) | copy-start | bytes 368644
  58.7 2.8 %copy-start.2 = (pred[192,640]{1,0:T(8,128)(4,1)S(1)}, pred[192,640]{1,0:T(8,128)(4,1)}, u32[]{:S(2)}) copy-start(pred[192,640]{1,0:T(8,128)(4,1)} %get-tuple-element.45) | copy-start | bytes 368644
  62.1 11.3 %copy-start.9 = (pred[192,1024]{1,0:T(8,128)(4,1)S(1)}, pred[192,1024]{1,0:T(8,128)(4,1)}, u32[]{:S(2)}) copy-start(pred[192,1024]{1,0:T(8,128)(4,1)} %get-tuple-element.44) | copy-start | bytes 589828
  62.1 14.8 %collective-permute-start.5 = (bf16[512,256]{1,0:T(8,128)(2,1)S(1)}, bf16[512,256]{1,0:T(8,128)(2,1)S(1)}, u32[]{:S(2)}, u32[]{:S(2)}) collective-permute-start(bf16[512,256]{1,0:T(8,128)(2,1)S(1)} %slice.72), channel_id=1, source_target_pairs={{0,192},{192,384},{384,576},{576,0},{1,193},{193,385},{385,577},{5... | collective-permute-start | bytes 786440 | tf_op jit(solution)/shard_map/ppermute | solution.py:75
  65.2 11.8 %collective-permute-start.7 = (bf16[512,256]{1,0:T(8,128)(2,1)S(1)}, bf16[512,256]{1,0:T(8,128)(2,1)S(1)}, u32[]{:S(2)}, u32[]{:S(2)}) collective-permute-start(bf16[512,256]{1,0:T(8,128)(2,1)S(1)} %slice.73), channel_id=1, source_target_pairs={{0,576},{192,0},{384,192},{576,384},{1,577},{193,1},{385,193},{577... | collective-permute-start | bytes 786440 | tf_op jit(solution)/shard_map/ppermute | solution.py:76
  70.3 8.9 %collective-permute-start.9 = (bf16[1024,256]{1,0:T(8,128)(2,1)}, bf16[1024,256]{1,0:T(8,128)(2,1)S(1)}, u32[]{:S(2)}, u32[]{:S(2)}) collective-permute-start(bf16[1024,256]{1,0:T(8,128)(2,1)} %collective-permute-done.6), channel_id=1, source_target_pairs={{0,12},{12,0},{1,13},{13,1},{2,14},{14,2},{3,15},{15,3},{4,16},{16... | collective-permute-start | bytes 1572872 | tf_op jit(solution)/shard_map/ppermute | solution.py:137
  73.4 3.0 %copy-start.6 = (pred[192,1024]{1,0:T(8,128)(4,1)S(1)}, pred[192,1024]{1,0:T(8,128)(4,1)}, u32[]{:S(2)}) copy-start(pred[192,1024]{1,0:T(8,128)(4,1)} %get-tuple-element.43) | copy-start | bytes 589828
  74.0 8.0 %collective-permute-start.4 = (bf16[1024,256]{1,0:T(8,128)(2,1)S(1)}, bf16[1024,256]{1,0:T(8,128)(2,1)S(1)}, u32[]{:S(2)}, u32[]{:S(2)}) collective-permute-start(bf16[1024,256]{1,0:T(8,128)(2,1)S(1)} %collective-permute-done.3), channel_id=1, source_target_pairs={{0,12},{12,0},{1,13},{13,1},{2,14},{14,2},{3,15},{15,3},{4,16},{16... | collective-permute-start | bytes 1572872 | tf_op jit(solution)/shard_map/ppermute | solution.py:137
  76.9 3.5 %copy-start.5 = (pred[192,1024]{1,0:T(8,128)(4,1)S(1)}, pred[192,1024]{1,0:T(8,128)(4,1)}, u32[]{:S(2)}) copy-start(pred[192,1024]{1,0:T(8,128)(4,1)} %get-tuple-element.42) | copy-start | bytes 589828
  77.0 7.0 %collective-permute-start.8 = (bf16[1024,256]{1,0:T(8,128)(2,1)S(1)}, bf16[1024,256]{1,0:T(8,128)(2,1)S(1)}, u32[]{:S(2)}, u32[]{:S(2)}) collective-permute-start(bf16[1024,256]{1,0:T(8,128)(2,1)S(1)} %constant_dynamic-update-slice_fusion), channel_id=1, source_target_pairs={{0,12},{12,0},{1,13},{13,1},{2,14},{14,2},{3,15},{15,3},{4,16},{16... | collective-permute-start | bytes 1572872 | tf_op jit(solution)/shard_map/ppermute | solution.py:137
  80.4 0.9 copy-start.4
  81.9 0.9 copy-start.11
  82.1 1.3 copy-start.8
  84.0 0.9 copy-start.10
  84.1 1.4 copy-start.7
  95.8 2.7 %copy-start.1 = (f32[384,4096]{1,0:T(8,128)}, f32[384,4096]{1,0:T(8,128)S(1)}, u32[]{:S(2)}) copy-start(f32[384,4096]{1,0:T(8,128)S(1)} %fusion.192) | copy-start | bytes 18874372
  98.5 18.0 %collective-permute-start.10 = (bf16[32,4096]{1,0:T(8,128)(2,1)S(1)}, bf16[32,4096]{1,0:T(8,128)(2,1)S(1)}, u32[]{:S(2)}, u32[]{:S(2)}) collective-permute-start(bf16[32,4096]{1,0:T(8,128)(2,1)S(1)} %get-tuple-element.27), channel_id=1, source_target_pairs={{0,1},{1,2},{2,3},{3,4},{4,5},{5,6},{6,7},{7,8},{8,9},{9,10},{10,1... | collective-permute-start | bytes 786440 | tf_op jit(solution)/shard_map/ppermute | solution.py:99
  100.5 19.1 %collective-permute-start.16 = (bf16[32,4096]{1,0:T(8,128)(2,1)S(1)}, bf16[32,4096]{1,0:T(8,128)(2,1)S(1)}, u32[]{:S(2)}, u32[]{:S(2)}) collective-permute-start(bf16[32,4096]{1,0:T(8,128)(2,1)S(1)} %get-tuple-element.28), channel_id=1, source_target_pairs={{0,11},{1,0},{2,1},{3,2},{4,3},{5,4},{6,5},{7,6},{8,7},{9,8},{10,9... | collective-permute-start | bytes 786440 | tf_op jit(solution)/shard_map/ppermute | solution.py:104
  117.6 11.2 %collective-permute-start.11 = (bf16[32,4096]{1,0:T(8,128)(2,1)S(1)}, bf16[32,4096]{1,0:T(8,128)(2,1)S(1)}, u32[]{:S(2)}, u32[]{:S(2)}) collective-permute-start(bf16[32,4096]{1,0:T(8,128)(2,1)S(1)} %add_convert_fusion.9), channel_id=1, source_target_pairs={{0,1},{1,2},{2,3},{3,4},{4,5},{5,6},{6,7},{7,8},{8,9},{9,10},{10,1... | collective-permute-start | bytes 786440 | tf_op jit(solution)/shard_map/ppermute | solution.py:99
  130.1 10.4 %collective-permute-start.12 = (bf16[32,4096]{1,0:T(8,128)(2,1)S(1)}, bf16[32,4096]{1,0:T(8,128)(2,1)S(1)}, u32[]{:S(2)}, u32[]{:S(2)}) collective-permute-start(bf16[32,4096]{1,0:T(8,128)(2,1)S(1)} %get-tuple-element.25), channel_id=1, source_target_pairs={{0,1},{1,2},{2,3},{3,4},{4,5},{5,6},{6,7},{7,8},{8,9},{9,10},{10,1... | collective-permute-start | bytes 786440 | tf_op jit(solution)/shard_map/ppermute | solution.py:99
  132.0 9.6 %collective-permute-start.17 = (bf16[32,4096]{1,0:T(8,128)(2,1)S(1)}, bf16[32,4096]{1,0:T(8,128)(2,1)S(1)}, u32[]{:S(2)}, u32[]{:S(2)}) collective-permute-start(bf16[32,4096]{1,0:T(8,128)(2,1)S(1)} %get-tuple-element.26), channel_id=1, source_target_pairs={{0,11},{1,0},{2,1},{3,2},{4,3},{5,4},{6,5},{7,6},{8,7},{9,8},{10,9... | collective-permute-start | bytes 786440 | tf_op jit(solution)/shard_map/ppermute | solution.py:104
  143.0 10.0 %collective-permute-start.13 = (bf16[32,4096]{1,0:T(8,128)(2,1)S(1)}, bf16[32,4096]{1,0:T(8,128)(2,1)S(1)}, u32[]{:S(2)}, u32[]{:S(2)}) collective-permute-start(bf16[32,4096]{1,0:T(8,128)(2,1)S(1)} %get-tuple-element.23), channel_id=1, source_target_pairs={{0,1},{1,2},{2,3},{3,4},{4,5},{5,6},{6,7},{7,8},{8,9},{9,10},{10,1... | collective-permute-start | bytes 786440 | tf_op jit(solution)/shard_map/ppermute | solution.py:99
  144.9 9.5 %collective-permute-start.18 = (bf16[32,4096]{1,0:T(8,128)(2,1)S(1)}, bf16[32,4096]{1,0:T(8,128)(2,1)S(1)}, u32[]{:S(2)}, u32[]{:S(2)}) collective-permute-start(bf16[32,4096]{1,0:T(8,128)(2,1)S(1)} %get-tuple-element.24), channel_id=1, source_target_pairs={{0,11},{1,0},{2,1},{3,2},{4,3},{5,4},{6,5},{7,6},{8,7},{9,8},{10,9... | collective-permute-start | bytes 786440 | tf_op jit(solution)/shard_map/ppermute | solution.py:104
  155.7 9.9 %collective-permute-start.14 = (bf16[32,4096]{1,0:T(8,128)(2,1)S(1)}, bf16[32,4096]{1,0:T(8,128)(2,1)S(1)}, u32[]{:S(2)}, u32[]{:S(2)}) collective-permute-start(bf16[32,4096]{1,0:T(8,128)(2,1)S(1)} %get-tuple-element.21), channel_id=1, source_target_pairs={{0,1},{1,2},{2,3},{3,4},{4,5},{5,6},{6,7},{7,8},{8,9},{9,10},{10,1... | collective-permute-start | bytes 786440 | tf_op jit(solution)/shard_map/ppermute | solution.py:99
  157.6 9.5 %collective-permute-start.19 = (bf16[32,4096]{1,0:T(8,128)(2,1)S(1)}, bf16[32,4096]{1,0:T(8,128)(2,1)S(1)}, u32[]{:S(2)}, u32[]{:S(2)}) collective-permute-start(bf16[32,4096]{1,0:T(8,128)(2,1)S(1)} %get-tuple-element.22), channel_id=1, source_target_pairs={{0,11},{1,0},{2,1},{3,2},{4,3},{5,4},{6,5},{7,6},{8,7},{9,8},{10,9... | collective-permute-start | bytes 786440 | tf_op jit(solution)/shard_map/ppermute | solution.py:104
  168.4 9.5 %collective-permute-start.20 = (bf16[32,4096]{1,0:T(8,128)(2,1)S(1)}, bf16[32,4096]{1,0:T(8,128)(2,1)S(1)}, u32[]{:S(2)}, u32[]{:S(2)}) collective-permute-start(bf16[32,4096]{1,0:T(8,128)(2,1)S(1)} %get-tuple-element.20), channel_id=1, source_target_pairs={{0,11},{1,0},{2,1},{3,2},{4,3},{5,4},{6,5},{7,6},{8,7},{9,8},{10,9... | collective-permute-start | bytes 786440 | tf_op jit(solution)/shard_map/ppermute | solution.py:104
  174.0 9.5 %collective-permute-start.15 = (bf16[32,4096]{1,0:T(8,128)(2,1)S(1)}, bf16[32,4096]{1,0:T(8,128)(2,1)S(1)}, u32[]{:S(2)}, u32[]{:S(2)}) collective-permute-start(bf16[32,4096]{1,0:T(8,128)(2,1)S(1)} %get-tuple-element.19), channel_id=1, source_target_pairs={{0,1},{1,2},{2,3},{3,4},{4,5},{5,6},{6,7},{7,8},{8,9},{9,10},{10,1... | collective-permute-start | bytes 786440 | tf_op jit(solution)/shard_map/ppermute | solution.py:99

commit v9 on v7

--- a/solution.py
+++ b/solution.py
@@ -10,7 +10,7 @@
 SUMMARY = 128
 CTX = ("cx", "cy", "cc")
 CORE = "cc"
-QUERY_CHUNKS = 2
+QUERY_CHUNKS = 1
 
 
 LOW_SCORE = -1e30
@@ -133,7 +133,9 @@
     moved = jnp.asarray(offsets, jnp.int32)[index // row_len]
     source_x = (lax.axis_index("cx") + moved) % x_count
     owner = source_x * (row_len // half_sum) + (index % row_len) // half_sum
-    key_pos = owner * tok_rows + jnp.where(owner % 2 == 0, tok_rows - half_sum, 0) + index % half_sum
+    key_pos = (
+        owner * tok_rows + jnp.where(owner % 2 == 0, tok_rows - half_sum, 0) + index % half_sum
+    )
     sum_mask = own_pos[:, None] - key_pos[None, :] >= BAND
     pieces = []
     for low in range(0, tok_rows, chunk):

time: 184 us -> 178 us (0.967)
  local copies, waits for them, and re-layouts: 18.2 us -> 14.9 us
  waiting for transfers between devices: 39.5 us -> 37 us
  starting transfers between devices: 67.7 us -> 65.8 us
    ppermute x5, starting transfers between devices: 31.9 us -> 27.9 us  [ring_reduce_scatter(): down_sum = lax.ppermute(down, axis, behind).astype(jnp.float32)]
    ppermute x6, waiting for transfers between devices: 28 us -> 24.5 us  [ring_reduce_scatter(): lax.ppermute(up, axis, ahead).astype(jnp.float32)]
    ppermute x6, starting transfers between devices: 11.5 us -> 13.9 us  [ring_reduce_scatter(): lax.ppermute(up, axis, ahead).astype(jnp.float32)]
    dot_general x4 -> x2, matrix products: 3.36 us -> 5.04 us  [attend(): jnp.einsum('hqk,khd->hqd', w.astype(jnp.bfloat16), v, preferred_element_t...]
    dot_general x4 -> x2, matrix products: 6.15 us -> 4.68 us  [attend(): jnp.einsum('qhd,khd->hqk', q, k, preferred_element_type=jnp.float32) * scale]
    unnamed x22 -> x20, local copies, waits for them, and re-layouts: 9.97 us -> 9.11 us
  transfers between devices with their start and end apart: 18 -> 18, of which waited for: 11 -> 12; matrix products, arithmetic and copies ran while one was open for 12% -> 11% of each run, Pallas kernels for 0% -> 0%
where the time goes in v9:
time: 178 us; the launch traced here: 177 us
  starting transfers between devices  65.8 us (37%)
  waiting for transfers between devices  37 us (21%)
  blocking collectives  26.8 us (15%)
  other arithmetic  20.7 us (12%)
  local copies, waits for them, and re-layouts  14.9 us (8%)
  matrix products  10.7 us (6%)
    ppermute x5, starting transfers between devices, ring_reduce_scatter(): down_sum = lax.ppermute(down, axis, behind).astype(jnp.float32)  27.9 us
    all_gather x1, blocking collectives, layer(): gathered = lax.all_gather(my_half, 'cy', axis=0, tiled=True)  24.9 us
    ppermute x6, waiting for transfers between devices, ring_reduce_scatter(): lax.ppermute(up, axis, ahead).astype(jnp.float32)  24.5 us
    ppermute x6, starting transfers between devices, ring_reduce_scatter(): lax.ppermute(up, axis, ahead).astype(jnp.float32)  13.9 us
    unnamed x20, local copies, waits for them, and re-layouts  9.11 us
    ppermute x5, waiting for transfers between devices, ring_reduce_scatter(): down_sum = lax.ppermute(down, axis, behind).astype(jnp.float32)  7.65 us
    ppermute x1, starting transfers between devices, gather_row_blocks(): from_left = lax.ppermute(block, axis, ahead)  6.96 us
    convert_element_type x5, other arithmetic, ring_reduce_scatter(): up = up_sum.astype(jnp.bfloat16)  6.24 us
  transfers between devices with their start and end apart: 18, of which 12 were waited for; matrix products, arithmetic and copies ran while one was open for 11% of the time, Pallas kernels for 0%

profile of v9, /device:TPU:14, one launch (start us, length us, event | category | flops | bytes accessed | tf_op | source)
XLA Modules:
  0.0 176.7 jit_solution(3404880858468927583)
XLA Ops:
  1.7 1.9 %all_gather.6 = bf16[128,512]{1,0:T(8,128)(2,1)S(1)} all-gather(bf16[64,512]{1,0:T(8,128)(2,1)S(1)} %pad_maximum_fusion.2), channel_id=1, replica_groups=mesh['cx'=4,'cy'=8,'cc'=2,'head'=12] {'cc'}, dimensions={0}, use_global_device_ids=true | all-gather | bytes 196608 | tf_op jit(solution)/shard_map/all_gather | solution.py:120
  3.7 24.9 %all_gather.7 = bf16[1024,256]{0,1:T(8,128)(2,1)S(1)} all-gather(bf16[128,256]{0,1:T(8,128)(2,1)S(1)} %copy.37), channel_id=1, replica_groups=mesh['cx'=4,'cy'=8,'cc'=2,'head'=12] {'cy'}, dimensions={0}, use_global_device_ids=true | all-gather | bytes 589824 | tf_op jit(solution)/shard_map/all_gather | solution.py:124
  28.6 7.0 %collective-permute-start.2 = (bf16[1024,256]{0,1:T(8,128)(2,1)S(1)}, bf16[1024,256]{0,1:T(8,128)(2,1)}, u32[]{:S(2)}, u32[]{:S(2)}) collective-permute-start(bf16[1024,256]{0,1:T(8,128)(2,1)S(1)} %all_gather.7), channel_id=1, source_target_pairs={{0,192},{192,384},{384,576},{576,0},{1,193},{193,385},{385,577},{5... | collective-permute-start | bytes 1572872 | tf_op jit(solution)/shard_map/ppermute | solution.py:59
  35.6 1.9 %collective-permute-start.4 = (bf16[1024,256]{0,1:T(8,128)(2,1)S(1)}, bf16[1024,256]{0,1:T(8,128)(2,1)S(1)}, u32[]{:S(2)}, u32[]{:S(2)}) collective-permute-start(bf16[1024,256]{0,1:T(8,128)(2,1)S(1)} %all_gather.7), channel_id=1, source_target_pairs={{0,576},{192,0},{384,192},{576,384},{1,577},{193,1},{385,193},{577... | collective-permute-start | bytes 1572872 | tf_op jit(solution)/shard_map/ppermute | solution.py:60
  37.5 1.1 copy.23
  39.3 1.9 %collective-permute-start = (bf16[256,256]{0,1:T(8,128)(2,1)}, bf16[256,256]{0,1:T(8,128)(2,1)}, u32[]{:S(2)}, u32[]{:S(2)}) collective-permute-start(bf16[256,256]{0,1:T(8,128)(2,1)} %slice.21), channel_id=1, source_target_pairs={{0,12},{12,24},{24,36},{36,48},{48,60},{60,72},{72,84},{84,96},{96... | collective-permute-start | bytes 393224 | tf_op jit(solution)/shard_map/ppermute | solution.py:22
  41.9 4.3 %collective-permute-start.1 = (bf16[256,256]{1,0:T(8,128)(2,1)}, bf16[256,256]{1,0:T(8,128)(2,1)}, u32[]{:S(2)}, u32[]{:S(2)}) collective-permute-start(bf16[256,256]{1,0:T(8,128)(2,1)} %slice.13), channel_id=1, source_target_pairs={{0,12},{12,24},{24,36},{36,48},{48,60},{60,72},{72,84},{84,96},{96... | collective-permute-start | bytes 393224 | tf_op jit(solution)/shard_map/ppermute | solution.py:22
  46.2 1.7 slice.22
  47.9 5.1 %collective-permute-start.3 = (bf16[512,256]{0,1:T(8,128)(2,1)}, bf16[512,256]{0,1:T(8,128)(2,1)}, u32[]{:S(2)}, u32[]{:S(2)}) collective-permute-start(bf16[512,256]{0,1:T(8,128)(2,1)} %slice.22), channel_id=1, source_target_pairs={{0,192},{192,384},{384,576},{576,0},{1,193},{193,385},{385,577},{5... | collective-permute-start | bytes 786440 | tf_op jit(solution)/shard_map/ppermute | solution.py:64
  53.9 1.9 %collective-permute-start.5 = (bf16[512,256]{0,1:T(8,128)(2,1)S(1)}, bf16[512,256]{0,1:T(8,128)(2,1)S(1)}, u32[]{:S(2)}, u32[]{:S(2)}) collective-permute-start(bf16[512,256]{0,1:T(8,128)(2,1)S(1)} %slice.23), channel_id=1, source_target_pairs={{0,576},{192,0},{384,192},{576,384},{1,577},{193,1},{385,193},{577... | collective-permute-start | bytes 786440 | tf_op jit(solution)/shard_map/ppermute | solution.py:65
  56.4 1.9 %constant_dynamic-update-slice_fusion.3 = bf16[4096,256]{0,1:T(8,128)(2,1)} fusion(bf16[4096,256]{0,1:T(8,128)(2,1)} %constant_dynamic-update-slice_fusion.4, bf16[1024,256]{0,1:T(8,128)(2,1)} %collective-permute-done.2), kind=kLoop, calls=%fused_computation.98 | loop fusion | bytes 1048576
  59.1 1.7 constant_dynamic-update-slice_fusion.2
  60.8 4.2 %collective-permute-done.5 = bf16[512,256]{0,1:T(8,128)(2,1)S(1)} collective-permute-done((bf16[512,256]{0,1:T(8,128)(2,1)S(1)}, bf16[512,256]{0,1:T(8,128)(2,1)S(1)}, u32[]{:S(2)}, u32[]{:S(2)}) %collective-permute-start.5) | collective-permute-done | bytes 262176 | tf_op jit(solution)/shard_map/ppermute | solution.py:65
  66.5 1.9 %collective-permute-start.6 = (bf16[4096,256]{0,1:T(8,128)(2,1)}, bf16[4096,256]{0,1:T(8,128)(2,1)}, u32[]{:S(2)}, u32[]{:S(2)}) collective-permute-start(bf16[4096,256]{0,1:T(8,128)(2,1)} %constant_dynamic-update-slice_fusion), channel_id=1, source_target_pairs={{0,12},{12,0},{1,13},{13,1},{2,14},{14,2},{3,15},{15,3},{4,16},{16... | collective-permute-start | bytes 6291464 | tf_op jit(solution)/shard_map/ppermute | solution.py:126
  68.5 2.9 %subtract_compare_fusion = pred[384,4096]{0,1:T(8,128)(4,1)} fusion(s32[4096]{0:T(1024)S(1)} %fusion.40, s32[384]{0:T(512)S(1)} %copy-done.5), kind=kLoop, calls=%fused_computation.5 | loop fusion | flops 3145728 | bytes 1590784 | tf_op jit(solution)/shard_map/ge | solution.py:139
  73.8 1.7 fusion.8
  76.1 2.9 %fusion.7 = (bf16[1,4096,256]{1,2,0:T(8,128)(2,1)S(1)}, bf16[1,4096,256]{1,2,0:T(8,128)(2,1)S(1)}) fusion(s32[]{:T(128)S(6)} %select_n.204, bf16[1,4096,256]{1,2,0:T(8,128)(2,1)S(1)} %bitcast.88, bf16[1,4096,256]{1,2,0:T(8,128)(2,1)} %bitcast.7, s32[]{:T(128)S(6)} %select_n.207), kind=kLoop, calls=%fused_computation.13 | loop fusion | flops 2097152 | bytes 8388616 | tf_op jit(solution)/shard_map/stack | solution.py:127
  79.0 3.0 %fusion = (f32[2,384]{1,0:T(2,128)S(1)}, f32[2,4096,384]{2,1,0:T(8,128)S(1)}) fusion(pred[384,4096]{0,1:T(8,128)(4,1)S(1)} %copy-done.2, bf16[4096,2,128]{0,2,1:T(8,128)(2,1)S(1)} %bitcast.90, bf16[384,256]{1,0:T(8,128)(2,1)S(1)} %copy-done.6), kind=kOutput, calls=%fused_computation.2 | convolution fusion | flops 814742784 | bytes 16452608 | tf_op jit(solution)/shard_map/qhd,khd->hqk/dot_general | solution.py:40
  82.0 3.5 %fusion.1 = f32[2,384]{1,0:T(2,128)S(1)} fusion(f32[2,4096,384]{2,1,0:T(8,128)S(1)} %get-tuple-element.21, f32[2,384]{1,0:T(2,128)S(1)} %get-tuple-element.20, pred[384,4096]{0,1:T(8,128)(4,1)S(1)} %copy-done.2), kind=kLoop, calls=%fused_computation.3 | loop fusion | flops 15727872 | bytes 14161920 | tf_op jit(solution)/shard_map/reduce_sum | solution.py:48
  85.6 4.3 %fusion.17 = f32[384,2,128]{0,2,1:T(8,128)S(1)} fusion(bf16[4096,2,128]{0,2,1:T(8,128)(2,1)S(1)} %bitcast.89, f32[2,4096,384]{2,1,0:T(8,128)S(1)} %get-tuple-element.21, f32[2,384]{1,0:T(2,128)S(1)} %get-tuple-element.20, pred[384,4096]{0,1:T(8,128)(4,1)S(1)} %copy-done.2, f32[384,2]{0,1:T(2,128)S(1)} %get-tuple-element.7), kind=kOutput, calls=%fused_computation.26 | convolution fusion | flops 821133312 | bytes 16652288 | tf_op jit(solution)/shard_map/hqk,khd->hqd/dot_general | solution.py:45
  91.6 2.6 %copy-done.1 = f32[384,4096]{1,0:T(8,128)} copy-done((f32[384,4096]{1,0:T(8,128)}, f32[384,4096]{1,0:T(8,128)S(1)}, u32[]{:S(2)}) %copy-start.1) | copy-done | bytes 6291480
  94.3 1.9 %collective-permute-start.7 = (bf16[32,4096]{1,0:T(8,128)(2,1)S(1)}, bf16[32,4096]{1,0:T(8,128)(2,1)S(1)}, u32[]{:S(2)}, u32[]{:S(2)}) collective-permute-start(bf16[32,4096]{1,0:T(8,128)(2,1)S(1)} %get-tuple-element.16), channel_id=1, source_target_pairs={{0,1},{1,2},{2,3},{3,4},{4,5},{5,6},{6,7},{7,8},{8,9},{9,10},{10,1... | collective-permute-start | bytes 786440 | tf_op jit(solution)/shard_map/ppermute | solution.py:88
  96.3 10.0 %collective-permute-start.13 = (bf16[32,4096]{1,0:T(8,128)(2,1)S(1)}, bf16[32,4096]{1,0:T(8,128)(2,1)S(1)}, u32[]{:S(2)}, u32[]{:S(2)}) collective-permute-start(bf16[32,4096]{1,0:T(8,128)(2,1)S(1)} %get-tuple-element.17), channel_id=1, source_target_pairs={{0,11},{1,0},{2,1},{3,2},{4,3},{5,4},{6,5},{7,6},{8,7},{9,8},{10,9... | collective-permute-start | bytes 786440 | tf_op jit(solution)/shard_map/ppermute | solution.py:93
  106.3 5.0 %collective-permute-done.7 = bf16[32,4096]{1,0:T(8,128)(2,1)S(1)} collective-permute-done((bf16[32,4096]{1,0:T(8,128)(2,1)S(1)}, bf16[32,4096]{1,0:T(8,128)(2,1)S(1)}, u32[]{:S(2)}, u32[]{:S(2)}) %collective-permute-start.7) | collective-permute-done | bytes 262176 | tf_op jit(solution)/shard_map/ppermute | solution.py:88
  111.3 1.1 add_convert_fusion.9
  112.4 1.9 %collective-permute-start.8 = (bf16[32,4096]{1,0:T(8,128)(2,1)S(1)}, bf16[32,4096]{1,0:T(8,128)(2,1)S(1)}, u32[]{:S(2)}, u32[]{:S(2)}) collective-permute-start(bf16[32,4096]{1,0:T(8,128)(2,1)S(1)} %add_convert_fusion.9), channel_id=1, source_target_pairs={{0,1},{1,2},{2,3},{3,4},{4,5},{5,6},{6,7},{7,8},{8,9},{9,10},{10,1... | collective-permute-start | bytes 786440 | tf_op jit(solution)/shard_map/ppermute | solution.py:88
  114.4 9.3 %collective-permute-done.8 = bf16[32,4096]{1,0:T(8,128)(2,1)S(1)} collective-permute-done((bf16[32,4096]{1,0:T(8,128)(2,1)S(1)}, bf16[32,4096]{1,0:T(8,128)(2,1)S(1)}, u32[]{:S(2)}, u32[]{:S(2)}) %collective-permute-start.8) | collective-permute-done | bytes 262176 | tf_op jit(solution)/shard_map/ppermute | solution.py:88
  123.6 1.3 add_convert_fusion.8
  124.9 2.2 %collective-permute-start.14 = (bf16[32,4096]{1,0:T(8,128)(2,1)S(1)}, bf16[32,4096]{1,0:T(8,128)(2,1)S(1)}, u32[]{:S(2)}, u32[]{:S(2)}) collective-permute-start(bf16[32,4096]{1,0:T(8,128)(2,1)S(1)} %get-tuple-element.15), channel_id=1, source_target_pairs={{0,11},{1,0},{2,1},{3,2},{4,3},{5,4},{6,5},{7,6},{8,7},{9,8},{10,9... | collective-permute-start | bytes 786440 | tf_op jit(solution)/shard_map/ppermute | solution.py:93
  127.1 3.7 %collective-permute-start.9 = (bf16[32,4096]{1,0:T(8,128)(2,1)S(1)}, bf16[32,4096]{1,0:T(8,128)(2,1)S(1)}, u32[]{:S(2)}, u32[]{:S(2)}) collective-permute-start(bf16[32,4096]{1,0:T(8,128)(2,1)S(1)} %get-tuple-element.14), channel_id=1, source_target_pairs={{0,1},{1,2},{2,3},{3,4},{4,5},{5,6},{6,7},{7,8},{8,9},{9,10},{10,1... | collective-permute-start | bytes 786440 | tf_op jit(solution)/shard_map/ppermute | solution.py:88
  130.8 3.3 %collective-permute-done.14 = bf16[32,4096]{1,0:T(8,128)(2,1)S(1)} collective-permute-done((bf16[32,4096]{1,0:T(8,128)(2,1)S(1)}, bf16[32,4096]{1,0:T(8,128)(2,1)S(1)}, u32[]{:S(2)}, u32[]{:S(2)}) %collective-permute-start.14) | collective-permute-done | bytes 262176 | tf_op jit(solution)/shard_map/ppermute | solution.py:93
  134.1 3.1 %collective-permute-done.9 = bf16[32,4096]{1,0:T(8,128)(2,1)S(1)} collective-permute-done((bf16[32,4096]{1,0:T(8,128)(2,1)S(1)}, bf16[32,4096]{1,0:T(8,128)(2,1)S(1)}, u32[]{:S(2)}, u32[]{:S(2)}) %collective-permute-start.9) | collective-permute-done | bytes 262176 | tf_op jit(solution)/shard_map/ppermute | solution.py:88
  137.2 1.3 add_convert_fusion.7
  138.5 2.4 %collective-permute-start.10 = (bf16[32,4096]{1,0:T(8,128)(2,1)S(1)}, bf16[32,4096]{1,0:T(8,128)(2,1)S(1)}, u32[]{:S(2)}, u32[]{:S(2)}) collective-permute-start(bf16[32,4096]{1,0:T(8,128)(2,1)S(1)} %get-tuple-element.12), channel_id=1, source_target_pairs={{0,1},{1,2},{2,3},{3,4},{4,5},{5,6},{6,7},{7,8},{8,9},{9,10},{10,1... | collective-permute-start | bytes 786440 | tf_op jit(solution)/shard_map/ppermute | solution.py:88
  141.0 4.6 %collective-permute-start.15 = (bf16[32,4096]{1,0:T(8,128)(2,1)S(1)}, bf16[32,4096]{1,0:T(8,128)(2,1)S(1)}, u32[]{:S(2)}, u32[]{:S(2)}) collective-permute-start(bf16[32,4096]{1,0:T(8,128)(2,1)S(1)} %get-tuple-element.13), channel_id=1, source_target_pairs={{0,11},{1,0},{2,1},{3,2},{4,3},{5,4},{6,5},{7,6},{8,7},{9,8},{10,9... | collective-permute-start | bytes 786440 | tf_op jit(solution)/shard_map/ppermute | solution.py:93
  145.6 2.4 %collective-permute-done.10 = bf16[32,4096]{1,0:T(8,128)(2,1)S(1)} collective-permute-done((bf16[32,4096]{1,0:T(8,128)(2,1)S(1)}, bf16[32,4096]{1,0:T(8,128)(2,1)S(1)}, u32[]{:S(2)}, u32[]{:S(2)}) %collective-permute-start.10) | collective-permute-done | bytes 262176 | tf_op jit(solution)/shard_map/ppermute | solution.py:88
  148.0 1.5 collective-permute-done.15
  149.5 1.3 add_convert_fusion.6
  150.8 2.0 %collective-permute-start.11 = (bf16[32,4096]{1,0:T(8,128)(2,1)S(1)}, bf16[32,4096]{1,0:T(8,128)(2,1)S(1)}, u32[]{:S(2)}, u32[]{:S(2)}) collective-permute-start(bf16[32,4096]{1,0:T(8,128)(2,1)S(1)} %get-tuple-element.10), channel_id=1, source_target_pairs={{0,1},{1,2},{2,3},{3,4},{4,5},{5,6},{6,7},{7,8},{8,9},{9,10},{10,1... | collective-permute-start | bytes 786440 | tf_op jit(solution)/shard_map/ppermute | solution.py:88
  152.7 5.6 %collective-permute-start.16 = (bf16[32,4096]{1,0:T(8,128)(2,1)S(1)}, bf16[32,4096]{1,0:T(8,128)(2,1)S(1)}, u32[]{:S(2)}, u32[]{:S(2)}) collective-permute-start(bf16[32,4096]{1,0:T(8,128)(2,1)S(1)} %get-tuple-element.11), channel_id=1, source_target_pairs={{0,11},{1,0},{2,1},{3,2},{4,3},{5,4},{6,5},{7,6},{8,7},{9,8},{10,9... | collective-permute-start | bytes 786440 | tf_op jit(solution)/shard_map/ppermute | solution.py:93
  158.3 2.4 %collective-permute-done.11 = bf16[32,4096]{1,0:T(8,128)(2,1)S(1)} collective-permute-done((bf16[32,4096]{1,0:T(8,128)(2,1)S(1)}, bf16[32,4096]{1,0:T(8,128)(2,1)S(1)}, u32[]{:S(2)}, u32[]{:S(2)}) %collective-permute-start.11) | collective-permute-done | bytes 262176 | tf_op jit(solution)/shard_map/ppermute | solution.py:88
  160.7 1.5 collective-permute-done.16
  162.2 1.3 add_convert_fusion.5
  163.5 1.9 %collective-permute-start.12 = (bf16[32,4096]{1,0:T(8,128)(2,1)S(1)}, bf16[32,4096]{1,0:T(8,128)(2,1)S(1)}, u32[]{:S(2)}, u32[]{:S(2)}) collective-permute-start(bf16[32,4096]{1,0:T(8,128)(2,1)S(1)} %get-tuple-element.8), channel_id=1, source_target_pairs={{0,1},{1,2},{2,3},{3,4},{4,5},{5,6},{6,7},{7,8},{8,9},{9,10},{10,1... | collective-permute-start | bytes 786440 | tf_op jit(solution)/shard_map/ppermute | solution.py:88
  165.4 5.6 %collective-permute-start.17 = (bf16[32,4096]{1,0:T(8,128)(2,1)S(1)}, bf16[32,4096]{1,0:T(8,128)(2,1)S(1)}, u32[]{:S(2)}, u32[]{:S(2)}) collective-permute-start(bf16[32,4096]{1,0:T(8,128)(2,1)S(1)} %get-tuple-element.9), channel_id=1, source_target_pairs={{0,11},{1,0},{2,1},{3,2},{4,3},{5,4},{6,5},{7,6},{8,7},{9,8},{10,9... | collective-permute-start | bytes 786440 | tf_op jit(solution)/shard_map/ppermute | solution.py:93
  171.0 2.4 %collective-permute-done.12 = bf16[32,4096]{1,0:T(8,128)(2,1)S(1)} collective-permute-done((bf16[32,4096]{1,0:T(8,128)(2,1)S(1)}, bf16[32,4096]{1,0:T(8,128)(2,1)S(1)}, u32[]{:S(2)}, u32[]{:S(2)}) %collective-permute-start.12) | collective-permute-done | bytes 262176 | tf_op jit(solution)/shard_map/ppermute | solution.py:88
  173.4 1.5 collective-permute-done.17
  174.9 1.8 %add_convert_fusion = bf16[32,4096]{1,0:T(8,128)(2,1)} fusion(bf16[32,4096]{1,0:T(8,128)(2,1)S(1)} %collective-permute-done.17, f32[384,4096]{1,0:T(8,128)} %copy-done.1, s32[]{:T(128)S(6)} %select_n.221, bf16[32,4096]{1,0:T(8,128)(2,1)S(1)} %collective-permute-done.12), kind=kLoop, calls=%fused_computation.34 | loop fusion | flops 655360 | bytes 1310724 | tf_op jit(solution)/shard_map/convert_element_type | solution.py:97
  (45 shorter events, 11.8 us)
Async XLA Ops:
  0.0 90.6 %copy-start = (bf16[256,4096]{1,0:T(8,128)(2,1)S(1)}, bf16[256,4096]{1,0:T(8,128)(2,1)}, u32[]{:S(2)}) copy-start(bf16[256,4096]{1,0:T(8,128)(2,1)} %param.8) | copy-start | bytes 6291460
  0.0 41.2 %copy-start.4 = (bf16[384,256]{1,0:T(8,128)(2,1)S(1)}, bf16[384,256]{1,0:T(8,128)(2,1)}, u32[]{:S(2)}) copy-start(bf16[384,256]{1,0:T(8,128)(2,1)} %param.7) | copy-start | bytes 589828
  28.6 17.6 %collective-permute-start.2 = (bf16[1024,256]{0,1:T(8,128)(2,1)S(1)}, bf16[1024,256]{0,1:T(8,128)(2,1)}, u32[]{:S(2)}, u32[]{:S(2)}) collective-permute-start(bf16[1024,256]{0,1:T(8,128)(2,1)S(1)} %all_gather.7), channel_id=1, source_target_pairs={{0,192},{192,384},{384,576},{576,0},{1,193},{193,385},{385,577},{5... | collective-permute-start | bytes 1572872 | tf_op jit(solution)/shard_map/ppermute | solution.py:59
  35.6 18.3 %collective-permute-start.4 = (bf16[1024,256]{0,1:T(8,128)(2,1)S(1)}, bf16[1024,256]{0,1:T(8,128)(2,1)S(1)}, u32[]{:S(2)}, u32[]{:S(2)}) collective-permute-start(bf16[1024,256]{0,1:T(8,128)(2,1)S(1)} %all_gather.7), channel_id=1, source_target_pairs={{0,576},{192,0},{384,192},{576,384},{1,577},{193,1},{385,193},{577... | collective-permute-start | bytes 1572872 | tf_op jit(solution)/shard_map/ppermute | solution.py:60
  39.3 33.6 %collective-permute-start = (bf16[256,256]{0,1:T(8,128)(2,1)}, bf16[256,256]{0,1:T(8,128)(2,1)}, u32[]{:S(2)}, u32[]{:S(2)}) collective-permute-start(bf16[256,256]{0,1:T(8,128)(2,1)} %slice.21), channel_id=1, source_target_pairs={{0,12},{12,24},{24,36},{36,48},{48,60},{60,72},{72,84},{84,96},{96... | collective-permute-start | bytes 393224 | tf_op jit(solution)/shard_map/ppermute | solution.py:22
  41.9 29.9 %collective-permute-start.1 = (bf16[256,256]{1,0:T(8,128)(2,1)}, bf16[256,256]{1,0:T(8,128)(2,1)}, u32[]{:S(2)}, u32[]{:S(2)}) collective-permute-start(bf16[256,256]{1,0:T(8,128)(2,1)} %slice.13), channel_id=1, source_target_pairs={{0,12},{12,24},{24,36},{36,48},{48,60},{60,72},{72,84},{84,96},{96... | collective-permute-start | bytes 393224 | tf_op jit(solution)/shard_map/ppermute | solution.py:22
  47.9 11.2 %collective-permute-start.3 = (bf16[512,256]{0,1:T(8,128)(2,1)}, bf16[512,256]{0,1:T(8,128)(2,1)}, u32[]{:S(2)}, u32[]{:S(2)}) collective-permute-start(bf16[512,256]{0,1:T(8,128)(2,1)} %slice.22), channel_id=1, source_target_pairs={{0,192},{192,384},{384,576},{576,0},{1,193},{193,385},{385,577},{5... | collective-permute-start | bytes 786440 | tf_op jit(solution)/shard_map/ppermute | solution.py:64
  53.9 11.0 %collective-permute-start.5 = (bf16[512,256]{0,1:T(8,128)(2,1)S(1)}, bf16[512,256]{0,1:T(8,128)(2,1)S(1)}, u32[]{:S(2)}, u32[]{:S(2)}) collective-permute-start(bf16[512,256]{0,1:T(8,128)(2,1)S(1)} %slice.23), channel_id=1, source_target_pairs={{0,576},{192,0},{384,192},{576,384},{1,577},{193,1},{385,193},{577... | collective-permute-start | bytes 786440 | tf_op jit(solution)/shard_map/ppermute | solution.py:65
  56.4 12.0 %copy-start.5 = (s32[384]{0:T(512)S(1)}, s32[384]{0:T(512)}, u32[]{:S(2)}) copy-start(s32[384]{0:T(512)} %iota_add_fusion.1) | copy-start | bytes 4612
  66.5 9.5 %collective-permute-start.6 = (bf16[4096,256]{0,1:T(8,128)(2,1)}, bf16[4096,256]{0,1:T(8,128)(2,1)}, u32[]{:S(2)}, u32[]{:S(2)}) collective-permute-start(bf16[4096,256]{0,1:T(8,128)(2,1)} %constant_dynamic-update-slice_fusion), channel_id=1, source_target_pairs={{0,12},{12,0},{1,13},{13,1},{2,14},{14,2},{3,15},{15,3},{4,16},{16... | collective-permute-start | bytes 6291464 | tf_op jit(solution)/shard_map/ppermute | solution.py:126
  73.8 2.2 %copy-start.3 = (bf16[4096,256]{0,1:T(8,128)(2,1)S(1)}, bf16[4096,256]{0,1:T(8,128)(2,1)}, u32[]{:S(2)}) copy-start(bf16[4096,256]{0,1:T(8,128)(2,1)} %constant_dynamic-update-slice_fusion) | copy-start | bytes 6291460
  76.1 2.9 %copy-start.2 = (pred[384,4096]{0,1:T(8,128)(4,1)S(1)}, pred[384,4096]{0,1:T(8,128)(4,1)}, u32[]{:S(2)}) copy-start(pred[384,4096]{0,1:T(8,128)(4,1)} %subtract_compare_fusion) | copy-start | bytes 4718596
  76.1 2.9 %copy-start.6 = (bf16[384,256]{1,0:T(8,128)(2,1)S(1)}, bf16[384,256]{1,0:T(8,128)(2,1)}, u32[]{:S(2)}) copy-start(bf16[384,256]{1,0:T(8,128)(2,1)} %param.5) | copy-start | bytes 589828
  91.6 2.7 %copy-start.1 = (f32[384,4096]{1,0:T(8,128)}, f32[384,4096]{1,0:T(8,128)S(1)}, u32[]{:S(2)}) copy-start(f32[384,4096]{1,0:T(8,128)S(1)} %fusion.62) | copy-start | bytes 18874372
  94.3 17.0 %collective-permute-start.7 = (bf16[32,4096]{1,0:T(8,128)(2,1)S(1)}, bf16[32,4096]{1,0:T(8,128)(2,1)S(1)}, u32[]{:S(2)}, u32[]{:S(2)}) collective-permute-start(bf16[32,4096]{1,0:T(8,128)(2,1)S(1)} %get-tuple-element.16), channel_id=1, source_target_pairs={{0,1},{1,2},{2,3},{3,4},{4,5},{5,6},{6,7},{7,8},{8,9},{9,10},{10,1... | collective-permute-start | bytes 786440 | tf_op jit(solution)/shard_map/ppermute | solution.py:88
  96.3 18.1 %collective-permute-start.13 = (bf16[32,4096]{1,0:T(8,128)(2,1)S(1)}, bf16[32,4096]{1,0:T(8,128)(2,1)S(1)}, u32[]{:S(2)}, u32[]{:S(2)}) collective-permute-start(bf16[32,4096]{1,0:T(8,128)(2,1)S(1)} %get-tuple-element.17), channel_id=1, source_target_pairs={{0,11},{1,0},{2,1},{3,2},{4,3},{5,4},{6,5},{7,6},{8,7},{9,8},{10,9... | collective-permute-start | bytes 786440 | tf_op jit(solution)/shard_map/ppermute | solution.py:93
  112.4 11.2 %collective-permute-start.8 = (bf16[32,4096]{1,0:T(8,128)(2,1)S(1)}, bf16[32,4096]{1,0:T(8,128)(2,1)S(1)}, u32[]{:S(2)}, u32[]{:S(2)}) collective-permute-start(bf16[32,4096]{1,0:T(8,128)(2,1)S(1)} %add_convert_fusion.9), channel_id=1, source_target_pairs={{0,1},{1,2},{2,3},{3,4},{4,5},{5,6},{6,7},{7,8},{8,9},{9,10},{10,1... | collective-permute-start | bytes 786440 | tf_op jit(solution)/shard_map/ppermute | solution.py:88
  124.9 9.2 %collective-permute-start.14 = (bf16[32,4096]{1,0:T(8,128)(2,1)S(1)}, bf16[32,4096]{1,0:T(8,128)(2,1)S(1)}, u32[]{:S(2)}, u32[]{:S(2)}) collective-permute-start(bf16[32,4096]{1,0:T(8,128)(2,1)S(1)} %get-tuple-element.15), channel_id=1, source_target_pairs={{0,11},{1,0},{2,1},{3,2},{4,3},{5,4},{6,5},{7,6},{8,7},{9,8},{10,9... | collective-permute-start | bytes 786440 | tf_op jit(solution)/shard_map/ppermute | solution.py:93
  127.1 10.1 %collective-permute-start.9 = (bf16[32,4096]{1,0:T(8,128)(2,1)S(1)}, bf16[32,4096]{1,0:T(8,128)(2,1)S(1)}, u32[]{:S(2)}, u32[]{:S(2)}) collective-permute-start(bf16[32,4096]{1,0:T(8,128)(2,1)S(1)} %get-tuple-element.14), channel_id=1, source_target_pairs={{0,1},{1,2},{2,3},{3,4},{4,5},{5,6},{6,7},{7,8},{8,9},{9,10},{10,1... | collective-permute-start | bytes 786440 | tf_op jit(solution)/shard_map/ppermute | solution.py:88
  138.5 9.5 %collective-permute-start.10 = (bf16[32,4096]{1,0:T(8,128)(2,1)S(1)}, bf16[32,4096]{1,0:T(8,128)(2,1)S(1)}, u32[]{:S(2)}, u32[]{:S(2)}) collective-permute-start(bf16[32,4096]{1,0:T(8,128)(2,1)S(1)} %get-tuple-element.12), channel_id=1, source_target_pairs={{0,1},{1,2},{2,3},{3,4},{4,5},{5,6},{6,7},{7,8},{8,9},{9,10},{10,1... | collective-permute-start | bytes 786440 | tf_op jit(solution)/shard_map/ppermute | solution.py:88
  141.0 8.5 %collective-permute-start.15 = (bf16[32,4096]{1,0:T(8,128)(2,1)S(1)}, bf16[32,4096]{1,0:T(8,128)(2,1)S(1)}, u32[]{:S(2)}, u32[]{:S(2)}) collective-permute-start(bf16[32,4096]{1,0:T(8,128)(2,1)S(1)} %get-tuple-element.13), channel_id=1, source_target_pairs={{0,11},{1,0},{2,1},{3,2},{4,3},{5,4},{6,5},{7,6},{8,7},{9,8},{10,9... | collective-permute-start | bytes 786440 | tf_op jit(solution)/shard_map/ppermute | solution.py:93
  150.8 9.9 %collective-permute-start.11 = (bf16[32,4096]{1,0:T(8,128)(2,1)S(1)}, bf16[32,4096]{1,0:T(8,128)(2,1)S(1)}, u32[]{:S(2)}, u32[]{:S(2)}) collective-permute-start(bf16[32,4096]{1,0:T(8,128)(2,1)S(1)} %get-tuple-element.10), channel_id=1, source_target_pairs={{0,1},{1,2},{2,3},{3,4},{4,5},{5,6},{6,7},{7,8},{8,9},{9,10},{10,1... | collective-permute-start | bytes 786440 | tf_op jit(solution)/shard_map/ppermute | solution.py:88
  152.7 9.4 %collective-permute-start.16 = (bf16[32,4096]{1,0:T(8,128)(2,1)S(1)}, bf16[32,4096]{1,0:T(8,128)(2,1)S(1)}, u32[]{:S(2)}, u32[]{:S(2)}) collective-permute-start(bf16[32,4096]{1,0:T(8,128)(2,1)S(1)} %get-tuple-element.11), channel_id=1, source_target_pairs={{0,11},{1,0},{2,1},{3,2},{4,3},{5,4},{6,5},{7,6},{8,7},{9,8},{10,9... | collective-permute-start | bytes 786440 | tf_op jit(solution)/shard_map/ppermute | solution.py:93
  163.5 9.9 %collective-permute-start.12 = (bf16[32,4096]{1,0:T(8,128)(2,1)S(1)}, bf16[32,4096]{1,0:T(8,128)(2,1)S(1)}, u32[]{:S(2)}, u32[]{:S(2)}) collective-permute-start(bf16[32,4096]{1,0:T(8,128)(2,1)S(1)} %get-tuple-element.8), channel_id=1, source_target_pairs={{0,1},{1,2},{2,3},{3,4},{4,5},{5,6},{6,7},{7,8},{8,9},{9,10},{10,1... | collective-permute-start | bytes 786440 | tf_op jit(solution)/shard_map/ppermute | solution.py:88
  165.4 9.5 %collective-permute-start.17 = (bf16[32,4096]{1,0:T(8,128)(2,1)S(1)}, bf16[32,4096]{1,0:T(8,128)(2,1)S(1)}, u32[]{:S(2)}, u32[]{:S(2)}) collective-permute-start(bf16[32,4096]{1,0:T(8,128)(2,1)S(1)} %get-tuple-element.9), channel_id=1, source_target_pairs={{0,11},{1,0},{2,1},{3,2},{4,3},{5,4},{6,5},{7,6},{8,7},{9,8},{10,9... | collective-permute-start | bytes 786440 | tf_op jit(solution)/shard_map/ppermute | solution.py:93

commit v10 on v9

--- a/solution.py
+++ b/solution.py
@@ -117,17 +117,27 @@
     sum_start = jnp.where(my_index % 2 == 0, tok_rows - half_sum, 0).astype(jnp.int32)
     own_keys = lax.dynamic_slice_in_dim(keys, sum_start, half_sum, 0)
     own_values = lax.dynamic_slice_in_dim(values, sum_start, half_sum, 0)
-    chip_rows = lax.all_gather(
-        jnp.concatenate([own_keys, own_values], axis=1), CORE, axis=0, tiled=True
+    own_rows = jnp.concatenate([own_keys, own_values], axis=1)
+    packed_q = queries.reshape(-1, own_rows.shape[1])
+    per_core = own_rows.shape[0] + packed_q.shape[0]
+    pair = lax.all_gather(jnp.concatenate([own_rows, packed_q], axis=0), CORE, axis=0, tiled=True)
+    chip_rows = jnp.concatenate(
+        [pair[: own_rows.shape[0]], pair[per_core : per_core + own_rows.shape[0]]], axis=0
     )
-    my_half = lax.dynamic_slice_in_dim(chip_rows, core * width, width, 1)
+    partner_all = lax.dynamic_slice_in_dim(
+        pair, (1 - core) * per_core + own_rows.shape[0], packed_q.shape[0], 0
+    ).reshape(queries.shape)
+    hd = HEAD_DIM
+    swap = [(0, 1), (1, 0)]
+
+    def cols(array, low):
+        return lax.dynamic_slice_in_dim(array, low, hd, 1)
+
+    my_half = jnp.concatenate([cols(chip_rows, core * hd), cols(chip_rows, width + core * hd)], axis=1)
+    partner_q = cols(partner_all, core * hd)
     gathered = lax.all_gather(my_half, "cy", axis=0, tiled=True)
     gathered, offsets = gather_row_blocks(gathered, "cx")
-    other = lax.ppermute(gathered, CORE, [(0, 1), (1, 0)])
-    both = jnp.stack([gathered, other])
-    all_sum_keys = both[core]
-    all_sum_values = both[1 - core]
-    index = jnp.arange(all_sum_keys.shape[0], dtype=jnp.int32)
+    index = jnp.arange(gathered.shape[0], dtype=jnp.int32)
     row_len = index.shape[0] // len(offsets)
     x_count = lax.axis_size("cx")
     moved = jnp.asarray(offsets, jnp.int32)[index // row_len]
@@ -136,14 +146,24 @@
     key_pos = (
         owner * tok_rows + jnp.where(owner % 2 == 0, tok_rows - half_sum, 0) + index % half_sum
     )
-    sum_mask = own_pos[:, None] - key_pos[None, :] >= BAND
-    pieces = []
-    for low in range(0, tok_rows, chunk):
-        rows = slice(low, low + chunk)
-        far = attend(queries[rows], all_sum_keys, all_sum_values, sum_mask[rows])
-        merged = combine_terms(near[low // chunk], far)
-        pieces.append(merged[2] / merged[1][:, :, None])
-    heads_out = jnp.concatenate(pieces, axis=1)
+    partner_pos = (my_index + 1 - 2 * core) * tok_rows + jnp.arange(tok_rows, dtype=jnp.int32)
+    both_pos = jnp.concatenate([own_pos, partner_pos])
+    sum_mask = both_pos[:, None] - key_pos[None, :] >= BAND
+    q_both = jnp.concatenate([cols(queries, core * hd), partner_q], axis=0)
+    top, total, summed = attend(q_both, gathered[:, :hd], gathered[:, hd:], sum_mask)
+    mine = (top[:, :tok_rows], total[:, :tok_rows], summed[:, :tok_rows])
+    packed = jnp.concatenate(
+        [summed[0, tok_rows:], top[0, tok_rows:, None], total[0, tok_rows:, None]], axis=1
+    )
+    got = lax.ppermute(packed, CORE, swap)
+    theirs = (got[None, :, hd], got[None, :, hd + 1], got[None, :, :hd])
+    first = core == 0
+    far = tuple(
+        jnp.concatenate([jnp.where(first, a, b), jnp.where(first, b, a)], axis=0)
+        for a, b in zip(mine, theirs)
+    )
+    merged = combine_terms(near[0], far)
+    heads_out = merged[2] / merged[1][:, :, None]
     attn = jnp.transpose(heads_out, (1, 0, 2)).reshape(tok_rows, width).astype(jnp.bfloat16)
     partial = jnp.dot(attn, out_weight, preferred_element_type=jnp.float32)
     return ring_reduce_scatter(partial, "head")

time: 178 us -> 184 us (1.034)
  the two profiles are of different devices: /device:TPU:14 before, /device:TPU:30 now
where the time goes in v10:
time: 184 us; the launch traced here: 183 us
  starting transfers between devices  66 us (36%)
  waiting for transfers between devices  37.4 us (20%)
  blocking collectives  28 us (15%)
  local copies, waits for them, and re-layouts  19.4 us (11%)
  other arithmetic  18.6 us (10%)
  matrix products  12.9 us (7%)
    ppermute x5, starting transfers between devices, ring_reduce_scatter(): down_sum = lax.ppermute(down, axis, behind).astype(jnp.float32)  28.1 us
    all_gather x1, blocking collectives, layer(): gathered = lax.all_gather(my_half, 'cy', axis=0, tiled=True)  25.8 us
    ppermute x6, waiting for transfers between devices, ring_reduce_scatter(): lax.ppermute(up, axis, ahead).astype(jnp.float32)  23.8 us
    ppermute x6, starting transfers between devices, ring_reduce_scatter(): lax.ppermute(up, axis, ahead).astype(jnp.float32)  13.9 us
    unnamed x15, local copies, waits for them, and re-layouts  8.87 us
    ppermute x5, waiting for transfers between devices, ring_reduce_scatter(): down_sum = lax.ppermute(down, axis, behind).astype(jnp.float32)  7.29 us
    dot_general x2, matrix products, attend(): jnp.einsum('qhd,khd->hqk', q, k, preferred_element_type=jnp.float32) * scale  7.18 us
    ppermute x2, starting transfers between devices, shifted(): lax.ppermute(value, axis, [(source, source + steps) for source in range(l...  7.01 us
  transfers between devices with their start and end apart: 18, of which 12 were waited for; matrix products, arithmetic and copies ran while one was open for 11% of the time, Pallas kernels for 0%

profile of v10, /device:TPU:30, one launch (start us, length us, event | category | flops | bytes accessed | tf_op | source)
XLA Modules:
  0.0 183.0 jit_solution(5461870568110635830)
XLA Ops:
  2.7 2.2 %all_gather.6 = bf16[512,512]{1,0:T(8,128)(2,1)S(1)} all-gather(bf16[256,512]{1,0:T(8,128)(2,1)S(1)} %pad_maximum_fusion.2), channel_id=1, replica_groups=mesh['cx'=4,'cy'=8,'cc'=2,'head'=12] {'cc'}, dimensions={0}, use_global_device_ids=true | all-gather | bytes 786432 | tf_op jit(solution)/shard_map/all_gather | solution.py:123
  5.0 25.8 %all_gather.7 = bf16[1024,256]{1,0:T(8,128)(2,1)S(1)} all-gather(bf16[128,256]{1,0:T(8,128)(2,1)S(1)} %pad_maximum_fusion.4), channel_id=1, replica_groups=mesh['cx'=4,'cy'=8,'cc'=2,'head'=12] {'cy'}, dimensions={0}, use_global_device_ids=true | all-gather | bytes 589824 | tf_op jit(solution)/shard_map/all_gather | solution.py:138
  30.8 5.9 %collective-permute-start.2 = (bf16[1024,256]{1,0:T(8,128)(2,1)S(1)}, bf16[1024,256]{1,0:T(8,128)(2,1)}, u32[]{:S(2)}, u32[]{:S(2)}) collective-permute-start(bf16[1024,256]{1,0:T(8,128)(2,1)S(1)} %all_gather.7), channel_id=1, source_target_pairs={{0,192},{192,384},{384,576},{576,0},{1,193},{193,385},{385,577},{5... | collective-permute-start | bytes 1572872 | tf_op jit(solution)/shard_map/ppermute | solution.py:59
  36.7 1.9 %collective-permute-start.4 = (bf16[1024,256]{1,0:T(8,128)(2,1)S(1)}, bf16[1024,256]{1,0:T(8,128)(2,1)}, u32[]{:S(2)}, u32[]{:S(2)}) collective-permute-start(bf16[1024,256]{1,0:T(8,128)(2,1)S(1)} %all_gather.7), channel_id=1, source_target_pairs={{0,576},{192,0},{384,192},{576,384},{1,577},{193,1},{385,193},{577... | collective-permute-start | bytes 1572872 | tf_op jit(solution)/shard_map/ppermute | solution.py:60
  38.6 1.1 copy.9
  40.4 1.9 %collective-permute-start = (bf16[256,256]{0,1:T(8,128)(2,1)}, bf16[256,256]{0,1:T(8,128)(2,1)}, u32[]{:S(2)}, u32[]{:S(2)}) collective-permute-start(bf16[256,256]{0,1:T(8,128)(2,1)} %slice.73), channel_id=1, source_target_pairs={{0,12},{12,24},{24,36},{36,48},{48,60},{60,72},{72,84},{84,96},{96... | collective-permute-start | bytes 393224 | tf_op jit(solution)/shard_map/ppermute | solution.py:22
  43.0 5.1 %collective-permute-start.1 = (bf16[256,256]{1,0:T(8,128)(2,1)}, bf16[256,256]{1,0:T(8,128)(2,1)}, u32[]{:S(2)}, u32[]{:S(2)}) collective-permute-start(bf16[256,256]{1,0:T(8,128)(2,1)} %slice.52), channel_id=1, source_target_pairs={{0,12},{12,24},{24,36},{36,48},{48,60},{60,72},{72,84},{84,96},{96... | collective-permute-start | bytes 393224 | tf_op jit(solution)/shard_map/ppermute | solution.py:22
  54.5 1.7 slice.76
  56.2 5.1 %collective-permute-start.3 = (bf16[512,256]{1,0:T(8,128)(2,1)}, bf16[512,256]{1,0:T(8,128)(2,1)S(1)}, u32[]{:S(2)}, u32[]{:S(2)}) collective-permute-start(bf16[512,256]{1,0:T(8,128)(2,1)} %slice.76), channel_id=1, source_target_pairs={{0,192},{192,384},{384,576},{576,0},{1,193},{193,385},{385,577},{5... | collective-permute-start | bytes 786440 | tf_op jit(solution)/shard_map/ppermute | solution.py:64
  61.3 2.8 %fusion.3 = (f32[2,384]{1,0:T(2,128)S(1)}, f32[2,640,384]{2,1,0:T(8,128)}) fusion(pred[384,640]{0,1:T(8,128)(4,1)S(1)} %fusion.20, bf16[640,2,128]{0,2,1:T(8,128)(2,1)S(1)} %bitcast.57, bf16[384,256]{1,0:T(8,128)(2,1)} %param.5), kind=kOutput, calls=%fused_computation.8 | convolution fusion | flops 127302912 | bytes 2739200 | tf_op jit(solution)/shard_map/qhd,khd->hqk/dot_general | solution.py:40
  64.1 1.7 slice.77
  65.8 1.9 %collective-permute-start.5 = (bf16[512,256]{1,0:T(8,128)(2,1)}, bf16[512,256]{1,0:T(8,128)(2,1)}, u32[]{:S(2)}, u32[]{:S(2)}) collective-permute-start(bf16[512,256]{1,0:T(8,128)(2,1)} %slice.77), channel_id=1, source_target_pairs={{0,576},{192,0},{384,192},{576,384},{1,577},{193,1},{385,193},{577... | collective-permute-start | bytes 786440 | tf_op jit(solution)/shard_map/ppermute | solution.py:65
  69.0 1.9 %constant_dynamic-update-slice_fusion.3 = bf16[4096,256]{1,0:T(8,128)(2,1)} fusion(bf16[4096,256]{1,0:T(8,128)(2,1)} %constant_dynamic-update-slice_fusion.4, bf16[1024,256]{1,0:T(8,128)(2,1)} %collective-permute-done.2), kind=kLoop, calls=%fused_computation.104 | loop fusion | bytes 1048576
  71.6 5.6 %collective-permute-done.5 = bf16[512,256]{1,0:T(8,128)(2,1)} collective-permute-done((bf16[512,256]{1,0:T(8,128)(2,1)}, bf16[512,256]{1,0:T(8,128)(2,1)}, u32[]{:S(2)}, u32[]{:S(2)}) %collective-permute-start.5) | collective-permute-done | bytes 262176 | tf_op jit(solution)/shard_map/ppermute | solution.py:65
  77.2 1.7 constant_dynamic-update-slice_fusion.1
  78.8 1.9 %constant_dynamic-update-slice_fusion = bf16[4096,256]{1,0:T(8,128)(2,1)} fusion(bf16[4096,256]{1,0:T(8,128)(2,1)} %constant_dynamic-update-slice_fusion.1, bf16[1024,256]{1,0:T(8,128)(2,1)} %collective-permute-done.4), kind=kLoop, calls=%fused_computation.101 | loop fusion | bytes 1048576 | tf_op jit(solution)/shard_map/concatenate | solution.py:69
  80.7 4.4 %fusion = (f32[768]{0:T(1024)S(1)}, f32[768,4096]{1,0:T(8,128)S(1)}) fusion(s32[4096]{0:T(1024)S(1)} %fusion.36, s32[768]{0:T(1024)S(1)} %pad_add_fusion, bf16[4096,256]{1,0:T(8,128)(2,1)} %constant_dynamic-update-slice_fusion, bf16[384,128]{1,0:T(8,128)(2,1)S(1)} %constant_dynamic-slice_fusion, bf16[384,128]{1,0:T(8,128)(2,1)S(1)} %constant_dynamic-slice_fusion.4), kind=kOutput, calls=%fused_computation.3 | convolution fusion | flops 821427456 | bytes 13850624 | tf_op jit(solution)/shard_map/qhd,khd->hqk/dot_general | solution.py:40
  85.1 4.0 %fusion.6 = f32[1,768,128]{1,2,0:T(8,128)S(1)} fusion(bf16[4096,256]{1,0:T(8,128)(2,1)S(1)} %copy-done.4, f32[768,4096]{1,0:T(8,128)S(1)} %get-tuple-element.33, f32[768]{0:T(1024)S(1)} %get-tuple-element.32, s32[4096]{0:T(1024)S(1)} %fusion.36, s32[768]{0:T(1024)S(1)} %pad_add_fusion), kind=kOutput, calls=%fused_computation.13 | convolution fusion | flops 827326464 | bytes 14049280 | tf_op jit(solution)/shard_map/hqk,khd->hqd/dot_general | solution.py:45
  89.1 4.4 %fusion.54 = f32[768]{0:T(1024)S(1)} fusion(f32[768]{0:T(1024)S(1)} %get-tuple-element.32, f32[768,4096]{1,0:T(8,128)S(1)} %get-tuple-element.33, s32[4096]{0:T(1024)S(1)} %fusion.36, s32[768]{0:T(1024)S(1)} %pad_add_fusion), kind=kLoop, calls=%fused_computation.135 | loop fusion | flops 22019328 | bytes 12608512 | tf_op jit(solution)/shard_map/reduce_sum | solution.py:48
  93.6 2.1 %collective-permute-start.6 = (f32[384,130]{0,1:T(8,128)S(1)}, f32[384,130]{0,1:T(8,128)S(1)}, u32[]{:S(2)}, u32[]{:S(2)}) collective-permute-start(f32[384,130]{0,1:T(8,128)S(1)} %pad_maximum_fusion.3), channel_id=1, source_target_pairs={{0,12},{12,0},{1,13},{13,1},{2,14},{14,2},{3,15},{15,3},{4,16},{16... | collective-permute-start | bytes 599048 | tf_op jit(solution)/shard_map/ppermute | solution.py:158
  98.8 2.7 %copy-done.1 = f32[384,4096]{1,0:T(8,128)} copy-done((f32[384,4096]{1,0:T(8,128)}, f32[384,4096]{1,0:T(8,128)S(1)}, u32[]{:S(2)}) %copy-start.1) | copy-done | bytes 6291480
  101.5 1.9 %collective-permute-start.7 = (bf16[32,4096]{1,0:T(8,128)(2,1)S(1)}, bf16[32,4096]{1,0:T(8,128)(2,1)S(1)}, u32[]{:S(2)}, u32[]{:S(2)}) collective-permute-start(bf16[32,4096]{1,0:T(8,128)(2,1)S(1)} %get-tuple-element.16), channel_id=1, source_target_pairs={{0,1},{1,2},{2,3},{3,4},{4,5},{5,6},{6,7},{7,8},{8,9},{9,10},{10,1... | collective-permute-start | bytes 786440 | tf_op jit(solution)/shard_map/ppermute | solution.py:88
  103.5 10.2 %collective-permute-start.13 = (bf16[32,4096]{1,0:T(8,128)(2,1)S(1)}, bf16[32,4096]{1,0:T(8,128)(2,1)S(1)}, u32[]{:S(2)}, u32[]{:S(2)}) collective-permute-start(bf16[32,4096]{1,0:T(8,128)(2,1)S(1)} %get-tuple-element.17), channel_id=1, source_target_pairs={{0,11},{1,0},{2,1},{3,2},{4,3},{5,4},{6,5},{7,6},{8,7},{9,8},{10,9... | collective-permute-start | bytes 786440 | tf_op jit(solution)/shard_map/ppermute | solution.py:93
  113.7 4.6 %collective-permute-done.7 = bf16[32,4096]{1,0:T(8,128)(2,1)S(1)} collective-permute-done((bf16[32,4096]{1,0:T(8,128)(2,1)S(1)}, bf16[32,4096]{1,0:T(8,128)(2,1)S(1)}, u32[]{:S(2)}, u32[]{:S(2)}) %collective-permute-start.7) | collective-permute-done | bytes 262176 | tf_op jit(solution)/shard_map/ppermute | solution.py:88
  118.3 1.1 add_convert_fusion.9
  119.4 1.9 %collective-permute-start.8 = (bf16[32,4096]{1,0:T(8,128)(2,1)S(1)}, bf16[32,4096]{1,0:T(8,128)(2,1)S(1)}, u32[]{:S(2)}, u32[]{:S(2)}) collective-permute-start(bf16[32,4096]{1,0:T(8,128)(2,1)S(1)} %add_convert_fusion.9), channel_id=1, source_target_pairs={{0,1},{1,2},{2,3},{3,4},{4,5},{5,6},{6,7},{7,8},{8,9},{9,10},{10,1... | collective-permute-start | bytes 786440 | tf_op jit(solution)/shard_map/ppermute | solution.py:88
  121.4 8.9 %collective-permute-done.8 = bf16[32,4096]{1,0:T(8,128)(2,1)S(1)} collective-permute-done((bf16[32,4096]{1,0:T(8,128)(2,1)S(1)}, bf16[32,4096]{1,0:T(8,128)(2,1)S(1)}, u32[]{:S(2)}, u32[]{:S(2)}) %collective-permute-start.8) | collective-permute-done | bytes 262176 | tf_op jit(solution)/shard_map/ppermute | solution.py:88
  130.3 1.3 add_convert_fusion.8
  131.6 2.2 %collective-permute-start.14 = (bf16[32,4096]{1,0:T(8,128)(2,1)S(1)}, bf16[32,4096]{1,0:T(8,128)(2,1)S(1)}, u32[]{:S(2)}, u32[]{:S(2)}) collective-permute-start(bf16[32,4096]{1,0:T(8,128)(2,1)S(1)} %get-tuple-element.15), channel_id=1, source_target_pairs={{0,11},{1,0},{2,1},{3,2},{4,3},{5,4},{6,5},{7,6},{8,7},{9,8},{10,9... | collective-permute-start | bytes 786440 | tf_op jit(solution)/shard_map/ppermute | solution.py:93
  133.7 3.7 %collective-permute-start.9 = (bf16[32,4096]{1,0:T(8,128)(2,1)S(1)}, bf16[32,4096]{1,0:T(8,128)(2,1)S(1)}, u32[]{:S(2)}, u32[]{:S(2)}) collective-permute-start(bf16[32,4096]{1,0:T(8,128)(2,1)S(1)} %get-tuple-element.14), channel_id=1, source_target_pairs={{0,1},{1,2},{2,3},{3,4},{4,5},{5,6},{6,7},{7,8},{8,9},{9,10},{10,1... | collective-permute-start | bytes 786440 | tf_op jit(solution)/shard_map/ppermute | solution.py:88
  137.5 2.9 %collective-permute-done.14 = bf16[32,4096]{1,0:T(8,128)(2,1)S(1)} collective-permute-done((bf16[32,4096]{1,0:T(8,128)(2,1)S(1)}, bf16[32,4096]{1,0:T(8,128)(2,1)S(1)}, u32[]{:S(2)}, u32[]{:S(2)}) %collective-permute-start.14) | collective-permute-done | bytes 262176 | tf_op jit(solution)/shard_map/ppermute | solution.py:93
  140.4 3.1 %collective-permute-done.9 = bf16[32,4096]{1,0:T(8,128)(2,1)S(1)} collective-permute-done((bf16[32,4096]{1,0:T(8,128)(2,1)S(1)}, bf16[32,4096]{1,0:T(8,128)(2,1)S(1)}, u32[]{:S(2)}, u32[]{:S(2)}) %collective-permute-start.9) | collective-permute-done | bytes 262176 | tf_op jit(solution)/shard_map/ppermute | solution.py:88
  143.5 1.3 add_convert_fusion.7
  144.8 2.4 %collective-permute-start.10 = (bf16[32,4096]{1,0:T(8,128)(2,1)S(1)}, bf16[32,4096]{1,0:T(8,128)(2,1)S(1)}, u32[]{:S(2)}, u32[]{:S(2)}) collective-permute-start(bf16[32,4096]{1,0:T(8,128)(2,1)S(1)} %get-tuple-element.12), channel_id=1, source_target_pairs={{0,1},{1,2},{2,3},{3,4},{4,5},{5,6},{6,7},{7,8},{8,9},{9,10},{10,1... | collective-permute-start | bytes 786440 | tf_op jit(solution)/shard_map/ppermute | solution.py:88
  147.3 4.6 %collective-permute-start.15 = (bf16[32,4096]{1,0:T(8,128)(2,1)S(1)}, bf16[32,4096]{1,0:T(8,128)(2,1)S(1)}, u32[]{:S(2)}, u32[]{:S(2)}) collective-permute-start(bf16[32,4096]{1,0:T(8,128)(2,1)S(1)} %get-tuple-element.13), channel_id=1, source_target_pairs={{0,11},{1,0},{2,1},{3,2},{4,3},{5,4},{6,5},{7,6},{8,7},{9,8},{10,9... | collective-permute-start | bytes 786440 | tf_op jit(solution)/shard_map/ppermute | solution.py:93
  151.9 2.4 %collective-permute-done.10 = bf16[32,4096]{1,0:T(8,128)(2,1)S(1)} collective-permute-done((bf16[32,4096]{1,0:T(8,128)(2,1)S(1)}, bf16[32,4096]{1,0:T(8,128)(2,1)S(1)}, u32[]{:S(2)}, u32[]{:S(2)}) %collective-permute-start.10) | collective-permute-done | bytes 262176 | tf_op jit(solution)/shard_map/ppermute | solution.py:88
  154.3 1.5 collective-permute-done.15
  155.8 1.3 add_convert_fusion.6
  157.0 2.0 %collective-permute-start.11 = (bf16[32,4096]{1,0:T(8,128)(2,1)S(1)}, bf16[32,4096]{1,0:T(8,128)(2,1)S(1)}, u32[]{:S(2)}, u32[]{:S(2)}) collective-permute-start(bf16[32,4096]{1,0:T(8,128)(2,1)S(1)} %get-tuple-element.10), channel_id=1, source_target_pairs={{0,1},{1,2},{2,3},{3,4},{4,5},{5,6},{6,7},{7,8},{8,9},{9,10},{10,1... | collective-permute-start | bytes 786440 | tf_op jit(solution)/shard_map/ppermute | solution.py:88
  159.0 5.6 %collective-permute-start.16 = (bf16[32,4096]{1,0:T(8,128)(2,1)S(1)}, bf16[32,4096]{1,0:T(8,128)(2,1)S(1)}, u32[]{:S(2)}, u32[]{:S(2)}) collective-permute-start(bf16[32,4096]{1,0:T(8,128)(2,1)S(1)} %get-tuple-element.11), channel_id=1, source_target_pairs={{0,11},{1,0},{2,1},{3,2},{4,3},{5,4},{6,5},{7,6},{8,7},{9,8},{10,9... | collective-permute-start | bytes 786440 | tf_op jit(solution)/shard_map/ppermute | solution.py:93
  164.6 2.4 %collective-permute-done.11 = bf16[32,4096]{1,0:T(8,128)(2,1)S(1)} collective-permute-done((bf16[32,4096]{1,0:T(8,128)(2,1)S(1)}, bf16[32,4096]{1,0:T(8,128)(2,1)S(1)}, u32[]{:S(2)}, u32[]{:S(2)}) %collective-permute-start.11) | collective-permute-done | bytes 262176 | tf_op jit(solution)/shard_map/ppermute | solution.py:88
  167.0 1.5 collective-permute-done.16
  168.5 1.3 add_convert_fusion.5
  169.7 1.9 %collective-permute-start.12 = (bf16[32,4096]{1,0:T(8,128)(2,1)S(1)}, bf16[32,4096]{1,0:T(8,128)(2,1)S(1)}, u32[]{:S(2)}, u32[]{:S(2)}) collective-permute-start(bf16[32,4096]{1,0:T(8,128)(2,1)S(1)} %get-tuple-element.8), channel_id=1, source_target_pairs={{0,1},{1,2},{2,3},{3,4},{4,5},{5,6},{6,7},{7,8},{8,9},{9,10},{10,1... | collective-permute-start | bytes 786440 | tf_op jit(solution)/shard_map/ppermute | solution.py:88
  171.7 5.6 %collective-permute-start.17 = (bf16[32,4096]{1,0:T(8,128)(2,1)S(1)}, bf16[32,4096]{1,0:T(8,128)(2,1)S(1)}, u32[]{:S(2)}, u32[]{:S(2)}) collective-permute-start(bf16[32,4096]{1,0:T(8,128)(2,1)S(1)} %get-tuple-element.9), channel_id=1, source_target_pairs={{0,11},{1,0},{2,1},{3,2},{4,3},{5,4},{6,5},{7,6},{8,7},{9,8},{10,9... | collective-permute-start | bytes 786440 | tf_op jit(solution)/shard_map/ppermute | solution.py:93
  177.3 2.4 %collective-permute-done.12 = bf16[32,4096]{1,0:T(8,128)(2,1)S(1)} collective-permute-done((bf16[32,4096]{1,0:T(8,128)(2,1)S(1)}, bf16[32,4096]{1,0:T(8,128)(2,1)S(1)}, u32[]{:S(2)}, u32[]{:S(2)}) %collective-permute-start.12) | collective-permute-done | bytes 262176 | tf_op jit(solution)/shard_map/ppermute | solution.py:88
  179.7 1.5 collective-permute-done.17
  181.2 1.8 add_convert_fusion
  (54 shorter events, 15.5 us)
Async XLA Ops:
  0.0 97.8 %copy-start = (bf16[256,4096]{1,0:T(8,128)(2,1)S(1)}, bf16[256,4096]{1,0:T(8,128)(2,1)}, u32[]{:S(2)}) copy-start(bf16[256,4096]{1,0:T(8,128)(2,1)} %param.8) | copy-start | bytes 6291460
  0.0 42.3 %copy-start.3 = (bf16[384,256]{1,0:T(8,128)(2,1)S(1)}, bf16[384,256]{1,0:T(8,128)(2,1)}, u32[]{:S(2)}) copy-start(bf16[384,256]{1,0:T(8,128)(2,1)} %param.7) | copy-start | bytes 589828
  30.8 23.8 %collective-permute-start.2 = (bf16[1024,256]{1,0:T(8,128)(2,1)S(1)}, bf16[1024,256]{1,0:T(8,128)(2,1)}, u32[]{:S(2)}, u32[]{:S(2)}) collective-permute-start(bf16[1024,256]{1,0:T(8,128)(2,1)S(1)} %all_gather.7), channel_id=1, source_target_pairs={{0,192},{192,384},{384,576},{576,0},{1,193},{193,385},{385,577},{5... | collective-permute-start | bytes 1572872 | tf_op jit(solution)/shard_map/ppermute | solution.py:59
  36.7 27.4 %collective-permute-start.4 = (bf16[1024,256]{1,0:T(8,128)(2,1)S(1)}, bf16[1024,256]{1,0:T(8,128)(2,1)}, u32[]{:S(2)}, u32[]{:S(2)}) collective-permute-start(bf16[1024,256]{1,0:T(8,128)(2,1)S(1)} %all_gather.7), channel_id=1, source_target_pairs={{0,576},{192,0},{384,192},{576,384},{1,577},{193,1},{385,193},{577... | collective-permute-start | bytes 1572872 | tf_op jit(solution)/shard_map/ppermute | solution.py:60
  40.4 13.2 %collective-permute-start = (bf16[256,256]{0,1:T(8,128)(2,1)}, bf16[256,256]{0,1:T(8,128)(2,1)}, u32[]{:S(2)}, u32[]{:S(2)}) collective-permute-start(bf16[256,256]{0,1:T(8,128)(2,1)} %slice.73), channel_id=1, source_target_pairs={{0,12},{12,24},{24,36},{36,48},{48,60},{60,72},{72,84},{84,96},{96... | collective-permute-start | bytes 393224 | tf_op jit(solution)/shard_map/ppermute | solution.py:22
  43.0 24.8 %collective-permute-start.1 = (bf16[256,256]{1,0:T(8,128)(2,1)}, bf16[256,256]{1,0:T(8,128)(2,1)}, u32[]{:S(2)}, u32[]{:S(2)}) collective-permute-start(bf16[256,256]{1,0:T(8,128)(2,1)} %slice.52), channel_id=1, source_target_pairs={{0,12},{12,24},{24,36},{36,48},{48,60},{60,72},{72,84},{84,96},{96... | collective-permute-start | bytes 393224 | tf_op jit(solution)/shard_map/ppermute | solution.py:22
  56.2 14.7 %collective-permute-start.3 = (bf16[512,256]{1,0:T(8,128)(2,1)}, bf16[512,256]{1,0:T(8,128)(2,1)S(1)}, u32[]{:S(2)}, u32[]{:S(2)}) collective-permute-start(bf16[512,256]{1,0:T(8,128)(2,1)} %slice.76), channel_id=1, source_target_pairs={{0,192},{192,384},{384,576},{576,0},{1,193},{193,385},{385,577},{5... | collective-permute-start | bytes 786440 | tf_op jit(solution)/shard_map/ppermute | solution.py:64
  65.8 11.4 %collective-permute-start.5 = (bf16[512,256]{1,0:T(8,128)(2,1)}, bf16[512,256]{1,0:T(8,128)(2,1)}, u32[]{:S(2)}, u32[]{:S(2)}) collective-permute-start(bf16[512,256]{1,0:T(8,128)(2,1)} %slice.77), channel_id=1, source_target_pairs={{0,576},{192,0},{384,192},{576,384},{1,577},{193,1},{385,193},{577... | collective-permute-start | bytes 786440 | tf_op jit(solution)/shard_map/ppermute | solution.py:65
  80.7 4.4 %copy-start.4 = (bf16[4096,256]{1,0:T(8,128)(2,1)S(1)}, bf16[4096,256]{1,0:T(8,128)(2,1)}, u32[]{:S(2)}) copy-start(bf16[4096,256]{1,0:T(8,128)(2,1)} %constant_dynamic-update-slice_fusion) | copy-start | bytes 6291460
  89.1 6.6 %copy-start.2 = (f32[2,640,384]{2,1,0:T(8,128)S(1)}, f32[2,640,384]{2,1,0:T(8,128)}, u32[]{:S(2)}) copy-start(f32[2,640,384]{2,1,0:T(8,128)} %get-tuple-element.31) | copy-start | bytes 5898244
  93.6 3.4 %collective-permute-start.6 = (f32[384,130]{0,1:T(8,128)S(1)}, f32[384,130]{0,1:T(8,128)S(1)}, u32[]{:S(2)}, u32[]{:S(2)}) collective-permute-start(f32[384,130]{0,1:T(8,128)S(1)} %pad_maximum_fusion.3), channel_id=1, source_target_pairs={{0,12},{12,0},{1,13},{13,1},{2,14},{14,2},{3,15},{15,3},{4,16},{16... | collective-permute-start | bytes 599048 | tf_op jit(solution)/shard_map/ppermute | solution.py:158
  98.8 2.7 %copy-start.1 = (f32[384,4096]{1,0:T(8,128)}, f32[384,4096]{1,0:T(8,128)S(1)}, u32[]{:S(2)}) copy-start(f32[384,4096]{1,0:T(8,128)S(1)} %fusion.58) | copy-start | bytes 18874372
  101.5 16.8 %collective-permute-start.7 = (bf16[32,4096]{1,0:T(8,128)(2,1)S(1)}, bf16[32,4096]{1,0:T(8,128)(2,1)S(1)}, u32[]{:S(2)}, u32[]{:S(2)}) collective-permute-start(bf16[32,4096]{1,0:T(8,128)(2,1)S(1)} %get-tuple-element.16), channel_id=1, source_target_pairs={{0,1},{1,2},{2,3},{3,4},{4,5},{5,6},{6,7},{7,8},{8,9},{9,10},{10,1... | collective-permute-start | bytes 786440 | tf_op jit(solution)/shard_map/ppermute | solution.py:88
  103.5 17.9 %collective-permute-start.13 = (bf16[32,4096]{1,0:T(8,128)(2,1)S(1)}, bf16[32,4096]{1,0:T(8,128)(2,1)S(1)}, u32[]{:S(2)}, u32[]{:S(2)}) collective-permute-start(bf16[32,4096]{1,0:T(8,128)(2,1)S(1)} %get-tuple-element.17), channel_id=1, source_target_pairs={{0,11},{1,0},{2,1},{3,2},{4,3},{5,4},{6,5},{7,6},{8,7},{9,8},{10,9... | collective-permute-start | bytes 786440 | tf_op jit(solution)/shard_map/ppermute | solution.py:93
  119.4 10.9 %collective-permute-start.8 = (bf16[32,4096]{1,0:T(8,128)(2,1)S(1)}, bf16[32,4096]{1,0:T(8,128)(2,1)S(1)}, u32[]{:S(2)}, u32[]{:S(2)}) collective-permute-start(bf16[32,4096]{1,0:T(8,128)(2,1)S(1)} %add_convert_fusion.9), channel_id=1, source_target_pairs={{0,1},{1,2},{2,3},{3,4},{4,5},{5,6},{6,7},{7,8},{8,9},{9,10},{10,1... | collective-permute-start | bytes 786440 | tf_op jit(solution)/shard_map/ppermute | solution.py:88
  131.6 8.8 %collective-permute-start.14 = (bf16[32,4096]{1,0:T(8,128)(2,1)S(1)}, bf16[32,4096]{1,0:T(8,128)(2,1)S(1)}, u32[]{:S(2)}, u32[]{:S(2)}) collective-permute-start(bf16[32,4096]{1,0:T(8,128)(2,1)S(1)} %get-tuple-element.15), channel_id=1, source_target_pairs={{0,11},{1,0},{2,1},{3,2},{4,3},{5,4},{6,5},{7,6},{8,7},{9,8},{10,9... | collective-permute-start | bytes 786440 | tf_op jit(solution)/shard_map/ppermute | solution.py:93
  133.7 9.8 %collective-permute-start.9 = (bf16[32,4096]{1,0:T(8,128)(2,1)S(1)}, bf16[32,4096]{1,0:T(8,128)(2,1)S(1)}, u32[]{:S(2)}, u32[]{:S(2)}) collective-permute-start(bf16[32,4096]{1,0:T(8,128)(2,1)S(1)} %get-tuple-element.14), channel_id=1, source_target_pairs={{0,1},{1,2},{2,3},{3,4},{4,5},{5,6},{6,7},{7,8},{8,9},{9,10},{10,1... | collective-permute-start | bytes 786440 | tf_op jit(solution)/shard_map/ppermute | solution.py:88
  144.8 9.5 %collective-permute-start.10 = (bf16[32,4096]{1,0:T(8,128)(2,1)S(1)}, bf16[32,4096]{1,0:T(8,128)(2,1)S(1)}, u32[]{:S(2)}, u32[]{:S(2)}) collective-permute-start(bf16[32,4096]{1,0:T(8,128)(2,1)S(1)} %get-tuple-element.12), channel_id=1, source_target_pairs={{0,1},{1,2},{2,3},{3,4},{4,5},{5,6},{6,7},{7,8},{8,9},{9,10},{10,1... | collective-permute-start | bytes 786440 | tf_op jit(solution)/shard_map/ppermute | solution.py:88
  147.3 8.5 %collective-permute-start.15 = (bf16[32,4096]{1,0:T(8,128)(2,1)S(1)}, bf16[32,4096]{1,0:T(8,128)(2,1)S(1)}, u32[]{:S(2)}, u32[]{:S(2)}) collective-permute-start(bf16[32,4096]{1,0:T(8,128)(2,1)S(1)} %get-tuple-element.13), channel_id=1, source_target_pairs={{0,11},{1,0},{2,1},{3,2},{4,3},{5,4},{6,5},{7,6},{8,7},{9,8},{10,9... | collective-permute-start | bytes 786440 | tf_op jit(solution)/shard_map/ppermute | solution.py:93
  157.0 9.9 %collective-permute-start.11 = (bf16[32,4096]{1,0:T(8,128)(2,1)S(1)}, bf16[32,4096]{1,0:T(8,128)(2,1)S(1)}, u32[]{:S(2)}, u32[]{:S(2)}) collective-permute-start(bf16[32,4096]{1,0:T(8,128)(2,1)S(1)} %get-tuple-element.10), channel_id=1, source_target_pairs={{0,1},{1,2},{2,3},{3,4},{4,5},{5,6},{6,7},{7,8},{8,9},{9,10},{10,1... | collective-permute-start | bytes 786440 | tf_op jit(solution)/shard_map/ppermute | solution.py:88
  159.0 9.4 %collective-permute-start.16 = (bf16[32,4096]{1,0:T(8,128)(2,1)S(1)}, bf16[32,4096]{1,0:T(8,128)(2,1)S(1)}, u32[]{:S(2)}, u32[]{:S(2)}) collective-permute-start(bf16[32,4096]{1,0:T(8,128)(2,1)S(1)} %get-tuple-element.11), channel_id=1, source_target_pairs={{0,11},{1,0},{2,1},{3,2},{4,3},{5,4},{6,5},{7,6},{8,7},{9,8},{10,9... | collective-permute-start | bytes 786440 | tf_op jit(solution)/shard_map/ppermute | solution.py:93
  169.7 9.9 %collective-permute-start.12 = (bf16[32,4096]{1,0:T(8,128)(2,1)S(1)}, bf16[32,4096]{1,0:T(8,128)(2,1)S(1)}, u32[]{:S(2)}, u32[]{:S(2)}) collective-permute-start(bf16[32,4096]{1,0:T(8,128)(2,1)S(1)} %get-tuple-element.8), channel_id=1, source_target_pairs={{0,1},{1,2},{2,3},{3,4},{4,5},{5,6},{6,7},{7,8},{8,9},{9,10},{10,1... | collective-permute-start | bytes 786440 | tf_op jit(solution)/shard_map/ppermute | solution.py:88
  171.7 9.5 %collective-permute-start.17 = (bf16[32,4096]{1,0:T(8,128)(2,1)S(1)}, bf16[32,4096]{1,0:T(8,128)(2,1)S(1)}, u32[]{:S(2)}, u32[]{:S(2)}) collective-permute-start(bf16[32,4096]{1,0:T(8,128)(2,1)S(1)} %get-tuple-element.9), channel_id=1, source_target_pairs={{0,11},{1,0},{2,1},{3,2},{4,3},{5,4},{6,5},{7,6},{8,7},{9,8},{10,9... | collective-permute-start | bytes 786440 | tf_op jit(solution)/shard_map/ppermute | solution.py:93

commit v11 on v10

--- a/solution.py
+++ b/solution.py
@@ -101,7 +101,10 @@
     tok_rows, width = queries.shape
     half_sum = SUMMARY // 2
     my_index = lax.axis_index(CTX)
-    rim_keys, rim_values = shifted((keys[tok_rows - BAND :], values[tok_rows - BAND :]), CTX, 1)
+    rim = shifted(
+        jnp.concatenate([keys[tok_rows - BAND :], values[tok_rows - BAND :]], axis=1), CTX, 1
+    )
+    rim_keys, rim_values = rim[:, :width], rim[:, width:]
     band_keys = jnp.concatenate([rim_keys, keys], axis=0)
     band_values = jnp.concatenate([rim_values, values], axis=0)
     own_pos = my_index * tok_rows + jnp.arange(tok_rows, dtype=jnp.int32)
@@ -117,16 +120,9 @@
     sum_start = jnp.where(my_index % 2 == 0, tok_rows - half_sum, 0).astype(jnp.int32)
     own_keys = lax.dynamic_slice_in_dim(keys, sum_start, half_sum, 0)
     own_values = lax.dynamic_slice_in_dim(values, sum_start, half_sum, 0)
-    own_rows = jnp.concatenate([own_keys, own_values], axis=1)
-    packed_q = queries.reshape(-1, own_rows.shape[1])
-    per_core = own_rows.shape[0] + packed_q.shape[0]
-    pair = lax.all_gather(jnp.concatenate([own_rows, packed_q], axis=0), CORE, axis=0, tiled=True)
-    chip_rows = jnp.concatenate(
-        [pair[: own_rows.shape[0]], pair[per_core : per_core + own_rows.shape[0]]], axis=0
+    chip_rows = lax.all_gather(
+        jnp.concatenate([own_keys, own_values], axis=1), CORE, axis=0, tiled=True
     )
-    partner_all = lax.dynamic_slice_in_dim(
-        pair, (1 - core) * per_core + own_rows.shape[0], packed_q.shape[0], 0
-    ).reshape(queries.shape)
     hd = HEAD_DIM
     swap = [(0, 1), (1, 0)]
 
@@ -134,7 +130,7 @@
         return lax.dynamic_slice_in_dim(array, low, hd, 1)
 
     my_half = jnp.concatenate([cols(chip_rows, core * hd), cols(chip_rows, width + core * hd)], axis=1)
-    partner_q = cols(partner_all, core * hd)
+    partner_q = lax.ppermute(cols(queries, (1 - core) * hd), CORE, swap)
     gathered = lax.all_gather(my_half, "cy", axis=0, tiled=True)
     gathered, offsets = gather_row_blocks(gathered, "cx")
     index = jnp.arange(gathered.shape[0], dtype=jnp.int32)

time: 184 us -> 185 us (level)
  the two profiles are of different devices: /device:TPU:30 before, /device:TPU:2 now
where the time goes in v11:
time: 185 us; the launch traced here: 184 us
  starting transfers between devices  65.3 us (35%)
  waiting for transfers between devices  38.3 us (21%)
  blocking collectives  29 us (16%)
  local copies, waits for them, and re-layouts  20.9 us (11%)
  other arithmetic  16.5 us (9%)
  matrix products  13.6 us (7%)
    ppermute x5, starting transfers between devices, ring_reduce_scatter(): down_sum = lax.ppermute(down, axis, behind).astype(jnp.float32)  27.6 us
    all_gather x1, blocking collectives, layer(): gathered = lax.all_gather(my_half, 'cy', axis=0, tiled=True)  27.1 us
    ppermute x6, waiting for transfers between devices, ring_reduce_scatter(): lax.ppermute(up, axis, ahead).astype(jnp.float32)  23.8 us
    ppermute x6, starting transfers between devices, ring_reduce_scatter(): lax.ppermute(up, axis, ahead).astype(jnp.float32)  13.9 us
    unnamed x24, local copies, waits for them, and re-layouts  10.6 us
    ppermute x1, starting transfers between devices, gather_row_blocks(): from_right = lax.ppermute(block, axis, behind)  8.22 us
    dot_general x2, matrix products, attend(): jnp.einsum('qhd,khd->hqk', q, k, preferred_element_type=jnp.float32) * scale  7.82 us
    ppermute x5, waiting for transfers between devices, ring_reduce_scatter(): down_sum = lax.ppermute(down, axis, behind).astype(jnp.float32)  7.29 us
  transfers between devices with their start and end apart: 18, of which 13 were waited for; matrix products, arithmetic and copies ran while one was open for 14% of the time, Pallas kernels for 0%

profile of v11, /device:TPU:2, one launch (start us, length us, event | category | flops | bytes accessed | tf_op | source)
XLA Modules:
  0.0 184.2 jit_solution(5893402968012717950)
XLA Ops:
  0.9 1.9 %all_gather.6 = bf16[128,512]{1,0:T(8,128)(2,1)S(1)} all-gather(bf16[64,512]{1,0:T(8,128)(2,1)S(1)} %pad_maximum_fusion.4), channel_id=1, replica_groups=mesh['cx'=4,'cy'=8,'cc'=2,'head'=12] {'cc'}, dimensions={0}, use_global_device_ids=true | all-gather | bytes 196608 | tf_op jit(solution)/shard_map/all_gather | solution.py:123
  2.9 27.1 %all_gather.7 = bf16[1024,256]{1,0:T(8,128)(2,1)S(1)} all-gather(bf16[128,256]{1,0:T(8,128)(2,1)S(1)} %pad_maximum_fusion.5), channel_id=1, replica_groups=mesh['cx'=4,'cy'=8,'cc'=2,'head'=12] {'cy'}, dimensions={0}, use_global_device_ids=true | all-gather | bytes 589824 | tf_op jit(solution)/shard_map/all_gather | solution.py:134
  30.0 3.4 %collective-permute-start.2 = (bf16[1024,256]{1,0:T(8,128)(2,1)S(1)}, bf16[1024,256]{1,0:T(8,128)(2,1)}, u32[]{:S(2)}, u32[]{:S(2)}) collective-permute-start(bf16[1024,256]{1,0:T(8,128)(2,1)S(1)} %all_gather.7), channel_id=1, source_target_pairs={{0,192},{192,384},{384,576},{576,0},{1,193},{193,385},{385,577},{5... | collective-permute-start | bytes 1572872 | tf_op jit(solution)/shard_map/ppermute | solution.py:59
  33.4 8.2 %collective-permute-start.4 = (bf16[1024,256]{1,0:T(8,128)(2,1)S(1)}, bf16[1024,256]{1,0:T(8,128)(2,1)S(1)}, u32[]{:S(2)}, u32[]{:S(2)}) collective-permute-start(bf16[1024,256]{1,0:T(8,128)(2,1)S(1)} %all_gather.7), channel_id=1, source_target_pairs={{0,576},{192,0},{384,192},{576,384},{1,577},{193,1},{385,193},{577... | collective-permute-start | bytes 1572872 | tf_op jit(solution)/shard_map/ppermute | solution.py:60
  41.6 1.7 constant_dynamic-slice_fusion.5
  43.2 1.9 %collective-permute-start.1 = (bf16[384,128]{1,0:T(8,128)(2,1)}, bf16[384,128]{1,0:T(8,128)(2,1)}, u32[]{:S(2)}, u32[]{:S(2)}) collective-permute-start(bf16[384,128]{1,0:T(8,128)(2,1)} %get-tuple-element.29), channel_id=1, source_target_pairs={{0,12},{12,0},{1,13},{13,1},{2,14},{14,2},{3,15},{15,3},{4,16},{16... | collective-permute-start | bytes 294920 | tf_op jit(solution)/shard_map/ppermute | solution.py:133
  48.6 1.7 pad_maximum_fusion.2
  50.3 2.4 %collective-permute-start = (bf16[256,512]{0,1:T(8,128)(2,1)}, bf16[256,512]{0,1:T(8,128)(2,1)}, u32[]{:S(2)}, u32[]{:S(2)}) collective-permute-start(bf16[256,512]{0,1:T(8,128)(2,1)} %pad_maximum_fusion.2), channel_id=1, source_target_pairs={{0,12},{12,24},{24,36},{36,48},{48,60},{60,72},{72,84},{84,96},{96... | collective-permute-start | bytes 786440 | tf_op jit(solution)/shard_map/ppermute | solution.py:22
  55.2 5.1 %collective-permute-done = bf16[256,512]{0,1:T(8,128)(2,1)} collective-permute-done((bf16[256,512]{0,1:T(8,128)(2,1)}, bf16[256,512]{0,1:T(8,128)(2,1)}, u32[]{:S(2)}, u32[]{:S(2)}) %collective-permute-start) | collective-permute-done | bytes 262176 | tf_op jit(solution)/shard_map/ppermute | solution.py:22
  60.4 1.6 fusion.55
  62.0 1.7 slice.76
  63.7 1.9 %collective-permute-start.3 = (bf16[512,256]{1,0:T(8,128)(2,1)}, bf16[512,256]{1,0:T(8,128)(2,1)}, u32[]{:S(2)}, u32[]{:S(2)}) collective-permute-start(bf16[512,256]{1,0:T(8,128)(2,1)} %slice.76), channel_id=1, source_target_pairs={{0,192},{192,384},{384,576},{576,0},{1,193},{193,385},{385,577},{5... | collective-permute-start | bytes 786440 | tf_op jit(solution)/shard_map/ppermute | solution.py:64
  65.6 3.5 %fusion.3 = (f32[2,384]{1,0:T(2,128)}, f32[2,640,384]{2,1,0:T(8,128)}) fusion(pred[384,640]{0,1:T(8,128)(4,1)} %fusion.20, bf16[640,2,128]{0,2,1:T(8,128)(2,1)S(1)} %bitcast.57, bf16[384,256]{1,0:T(8,128)(2,1)} %param.5), kind=kOutput, calls=%fused_computation.8 | convolution fusion | flops 127302912 | bytes 2739200 | tf_op jit(solution)/shard_map/qhd,khd->hqk/dot_general | solution.py:40
  70.8 3.9 %collective-permute-start.5 = (bf16[512,256]{1,0:T(8,128)(2,1)}, bf16[512,256]{1,0:T(8,128)(2,1)}, u32[]{:S(2)}, u32[]{:S(2)}) collective-permute-start(bf16[512,256]{1,0:T(8,128)(2,1)} %slice.77), channel_id=1, source_target_pairs={{0,576},{192,0},{384,192},{576,384},{1,577},{193,1},{385,193},{577... | collective-permute-start | bytes 786440 | tf_op jit(solution)/shard_map/ppermute | solution.py:65
  75.0 1.9 %constant_dynamic-update-slice_fusion.3 = bf16[4096,256]{1,0:T(8,128)(2,1)} fusion(bf16[4096,256]{1,0:T(8,128)(2,1)} %constant_dynamic-update-slice_fusion.4, bf16[1024,256]{1,0:T(8,128)(2,1)} %collective-permute-done.2), kind=kLoop, calls=%fused_computation.99 | loop fusion | bytes 1048576
  76.9 1.7 constant_dynamic-update-slice_fusion.2
  78.6 1.4 collective-permute-done.5
  80.0 1.7 constant_dynamic-update-slice_fusion.1
  82.5 4.4 %fusion = (f32[768]{0:T(1024)S(1)}, f32[768,4096]{1,0:T(8,128)S(1)}) fusion(s32[4096]{0:T(1024)S(1)} %fusion.34, s32[768]{0:T(1024)} %pad_add_fusion, bf16[4096,256]{1,0:T(8,128)(2,1)} %constant_dynamic-update-slice_fusion, bf16[384,128]{1,0:T(8,128)(2,1)} %collective-permute-done.1, bf16[384,128]{1,0:T(8,128)(2,1)S(1)} %copy-done.6), kind=kOutput, calls=%fused_computation.3 | convolution fusion | flops 821427456 | bytes 13851648 | tf_op jit(solution)/shard_map/qhd,khd->hqk/dot_general | solution.py:40
  86.9 4.0 %fusion.6 = f32[1,768,128]{1,2,0:T(8,128)S(1)} fusion(bf16[4096,256]{1,0:T(8,128)(2,1)S(1)} %copy-done.5, f32[768,4096]{1,0:T(8,128)S(1)} %get-tuple-element.35, f32[768]{0:T(1024)S(1)} %get-tuple-element.34, s32[4096]{0:T(1024)S(1)} %fusion.34, s32[768]{0:T(1024)S(1)} %copy-done.7), kind=kOutput, calls=%fused_computation.13 | convolution fusion | flops 827326464 | bytes 14049280 | tf_op jit(solution)/shard_map/hqk,khd->hqd/dot_general | solution.py:45
  90.9 4.4 %fusion.52 = f32[768]{0:T(1024)S(1)} fusion(f32[768]{0:T(1024)S(1)} %get-tuple-element.34, f32[768,4096]{1,0:T(8,128)S(1)} %get-tuple-element.35, s32[4096]{0:T(1024)S(1)} %fusion.34, s32[768]{0:T(1024)S(1)} %copy-done.7), kind=kLoop, calls=%fused_computation.131 | loop fusion | flops 22019328 | bytes 12608512 | tf_op jit(solution)/shard_map/reduce_sum | solution.py:48
  95.4 2.1 %collective-permute-start.6 = (f32[384,130]{0,1:T(8,128)S(1)}, f32[384,130]{0,1:T(8,128)S(1)}, u32[]{:S(2)}, u32[]{:S(2)}) collective-permute-start(f32[384,130]{0,1:T(8,128)S(1)} %pad_maximum_fusion.3), channel_id=1, source_target_pairs={{0,12},{12,0},{1,13},{13,1},{2,14},{14,2},{3,15},{15,3},{4,16},{16... | collective-permute-start | bytes 599048 | tf_op jit(solution)/shard_map/ppermute | solution.py:154
  100.6 2.6 %copy-done.1 = f32[384,4096]{1,0:T(8,128)} copy-done((f32[384,4096]{1,0:T(8,128)}, f32[384,4096]{1,0:T(8,128)S(1)}, u32[]{:S(2)}) %copy-start.1) | copy-done | bytes 6291480
  103.3 1.9 %collective-permute-start.7 = (bf16[32,4096]{1,0:T(8,128)(2,1)S(1)}, bf16[32,4096]{1,0:T(8,128)(2,1)S(1)}, u32[]{:S(2)}, u32[]{:S(2)}) collective-permute-start(bf16[32,4096]{1,0:T(8,128)(2,1)S(1)} %get-tuple-element.16), channel_id=1, source_target_pairs={{0,1},{1,2},{2,3},{3,4},{4,5},{5,6},{6,7},{7,8},{8,9},{9,10},{10,1... | collective-permute-start | bytes 786440 | tf_op jit(solution)/shard_map/ppermute | solution.py:88
  105.3 9.7 %collective-permute-start.13 = (bf16[32,4096]{1,0:T(8,128)(2,1)S(1)}, bf16[32,4096]{1,0:T(8,128)(2,1)S(1)}, u32[]{:S(2)}, u32[]{:S(2)}) collective-permute-start(bf16[32,4096]{1,0:T(8,128)(2,1)S(1)} %get-tuple-element.17), channel_id=1, source_target_pairs={{0,11},{1,0},{2,1},{3,2},{4,3},{5,4},{6,5},{7,6},{8,7},{9,8},{10,9... | collective-permute-start | bytes 786440 | tf_op jit(solution)/shard_map/ppermute | solution.py:93
  115.0 4.6 %collective-permute-done.7 = bf16[32,4096]{1,0:T(8,128)(2,1)S(1)} collective-permute-done((bf16[32,4096]{1,0:T(8,128)(2,1)S(1)}, bf16[32,4096]{1,0:T(8,128)(2,1)S(1)}, u32[]{:S(2)}, u32[]{:S(2)}) %collective-permute-start.7) | collective-permute-done | bytes 262176 | tf_op jit(solution)/shard_map/ppermute | solution.py:88
  120.7 1.9 %collective-permute-start.8 = (bf16[32,4096]{1,0:T(8,128)(2,1)S(1)}, bf16[32,4096]{1,0:T(8,128)(2,1)S(1)}, u32[]{:S(2)}, u32[]{:S(2)}) collective-permute-start(bf16[32,4096]{1,0:T(8,128)(2,1)S(1)} %add_convert_fusion.9), channel_id=1, source_target_pairs={{0,1},{1,2},{2,3},{3,4},{4,5},{5,6},{6,7},{7,8},{8,9},{9,10},{10,1... | collective-permute-start | bytes 786440 | tf_op jit(solution)/shard_map/ppermute | solution.py:88
  122.7 8.9 %collective-permute-done.8 = bf16[32,4096]{1,0:T(8,128)(2,1)S(1)} collective-permute-done((bf16[32,4096]{1,0:T(8,128)(2,1)S(1)}, bf16[32,4096]{1,0:T(8,128)(2,1)S(1)}, u32[]{:S(2)}, u32[]{:S(2)}) %collective-permute-start.8) | collective-permute-done | bytes 262176 | tf_op jit(solution)/shard_map/ppermute | solution.py:88
  131.6 1.3 add_convert_fusion.8
  132.8 2.2 %collective-permute-start.14 = (bf16[32,4096]{1,0:T(8,128)(2,1)S(1)}, bf16[32,4096]{1,0:T(8,128)(2,1)S(1)}, u32[]{:S(2)}, u32[]{:S(2)}) collective-permute-start(bf16[32,4096]{1,0:T(8,128)(2,1)S(1)} %get-tuple-element.15), channel_id=1, source_target_pairs={{0,11},{1,0},{2,1},{3,2},{4,3},{5,4},{6,5},{7,6},{8,7},{9,8},{10,9... | collective-permute-start | bytes 786440 | tf_op jit(solution)/shard_map/ppermute | solution.py:93
  135.0 3.7 %collective-permute-start.9 = (bf16[32,4096]{1,0:T(8,128)(2,1)S(1)}, bf16[32,4096]{1,0:T(8,128)(2,1)S(1)}, u32[]{:S(2)}, u32[]{:S(2)}) collective-permute-start(bf16[32,4096]{1,0:T(8,128)(2,1)S(1)} %get-tuple-element.14), channel_id=1, source_target_pairs={{0,1},{1,2},{2,3},{3,4},{4,5},{5,6},{6,7},{7,8},{8,9},{9,10},{10,1... | collective-permute-start | bytes 786440 | tf_op jit(solution)/shard_map/ppermute | solution.py:88
  138.8 2.9 %collective-permute-done.14 = bf16[32,4096]{1,0:T(8,128)(2,1)S(1)} collective-permute-done((bf16[32,4096]{1,0:T(8,128)(2,1)S(1)}, bf16[32,4096]{1,0:T(8,128)(2,1)S(1)}, u32[]{:S(2)}, u32[]{:S(2)}) %collective-permute-start.14) | collective-permute-done | bytes 262176 | tf_op jit(solution)/shard_map/ppermute | solution.py:93
  141.7 3.1 %collective-permute-done.9 = bf16[32,4096]{1,0:T(8,128)(2,1)S(1)} collective-permute-done((bf16[32,4096]{1,0:T(8,128)(2,1)S(1)}, bf16[32,4096]{1,0:T(8,128)(2,1)S(1)}, u32[]{:S(2)}, u32[]{:S(2)}) %collective-permute-start.9) | collective-permute-done | bytes 262176 | tf_op jit(solution)/shard_map/ppermute | solution.py:88
  144.8 1.3 add_convert_fusion.7
  146.1 2.4 %collective-permute-start.10 = (bf16[32,4096]{1,0:T(8,128)(2,1)S(1)}, bf16[32,4096]{1,0:T(8,128)(2,1)S(1)}, u32[]{:S(2)}, u32[]{:S(2)}) collective-permute-start(bf16[32,4096]{1,0:T(8,128)(2,1)S(1)} %get-tuple-element.12), channel_id=1, source_target_pairs={{0,1},{1,2},{2,3},{3,4},{4,5},{5,6},{6,7},{7,8},{8,9},{9,10},{10,1... | collective-permute-start | bytes 786440 | tf_op jit(solution)/shard_map/ppermute | solution.py:88
  148.5 4.6 %collective-permute-start.15 = (bf16[32,4096]{1,0:T(8,128)(2,1)S(1)}, bf16[32,4096]{1,0:T(8,128)(2,1)S(1)}, u32[]{:S(2)}, u32[]{:S(2)}) collective-permute-start(bf16[32,4096]{1,0:T(8,128)(2,1)S(1)} %get-tuple-element.13), channel_id=1, source_target_pairs={{0,11},{1,0},{2,1},{3,2},{4,3},{5,4},{6,5},{7,6},{8,7},{9,8},{10,9... | collective-permute-start | bytes 786440 | tf_op jit(solution)/shard_map/ppermute | solution.py:93
  153.2 2.4 %collective-permute-done.10 = bf16[32,4096]{1,0:T(8,128)(2,1)S(1)} collective-permute-done((bf16[32,4096]{1,0:T(8,128)(2,1)S(1)}, bf16[32,4096]{1,0:T(8,128)(2,1)S(1)}, u32[]{:S(2)}, u32[]{:S(2)}) %collective-permute-start.10) | collective-permute-done | bytes 262176 | tf_op jit(solution)/shard_map/ppermute | solution.py:88
  155.6 1.5 collective-permute-done.15
  157.0 1.3 add_convert_fusion.6
  158.3 2.0 %collective-permute-start.11 = (bf16[32,4096]{1,0:T(8,128)(2,1)S(1)}, bf16[32,4096]{1,0:T(8,128)(2,1)S(1)}, u32[]{:S(2)}, u32[]{:S(2)}) collective-permute-start(bf16[32,4096]{1,0:T(8,128)(2,1)S(1)} %get-tuple-element.10), channel_id=1, source_target_pairs={{0,1},{1,2},{2,3},{3,4},{4,5},{5,6},{6,7},{7,8},{8,9},{9,10},{10,1... | collective-permute-start | bytes 786440 | tf_op jit(solution)/shard_map/ppermute | solution.py:88
  160.3 5.6 %collective-permute-start.16 = (bf16[32,4096]{1,0:T(8,128)(2,1)S(1)}, bf16[32,4096]{1,0:T(8,128)(2,1)S(1)}, u32[]{:S(2)}, u32[]{:S(2)}) collective-permute-start(bf16[32,4096]{1,0:T(8,128)(2,1)S(1)} %get-tuple-element.11), channel_id=1, source_target_pairs={{0,11},{1,0},{2,1},{3,2},{4,3},{5,4},{6,5},{7,6},{8,7},{9,8},{10,9... | collective-permute-start | bytes 786440 | tf_op jit(solution)/shard_map/ppermute | solution.py:93
  165.9 2.4 %collective-permute-done.11 = bf16[32,4096]{1,0:T(8,128)(2,1)S(1)} collective-permute-done((bf16[32,4096]{1,0:T(8,128)(2,1)S(1)}, bf16[32,4096]{1,0:T(8,128)(2,1)S(1)}, u32[]{:S(2)}, u32[]{:S(2)}) %collective-permute-start.11) | collective-permute-done | bytes 262176 | tf_op jit(solution)/shard_map/ppermute | solution.py:88
  168.3 1.5 collective-permute-done.16
  171.0 1.9 %collective-permute-start.12 = (bf16[32,4096]{1,0:T(8,128)(2,1)S(1)}, bf16[32,4096]{1,0:T(8,128)(2,1)S(1)}, u32[]{:S(2)}, u32[]{:S(2)}) collective-permute-start(bf16[32,4096]{1,0:T(8,128)(2,1)S(1)} %get-tuple-element.8), channel_id=1, source_target_pairs={{0,1},{1,2},{2,3},{3,4},{4,5},{5,6},{6,7},{7,8},{8,9},{9,10},{10,1... | collective-permute-start | bytes 786440 | tf_op jit(solution)/shard_map/ppermute | solution.py:88
  172.9 5.6 %collective-permute-start.17 = (bf16[32,4096]{1,0:T(8,128)(2,1)S(1)}, bf16[32,4096]{1,0:T(8,128)(2,1)S(1)}, u32[]{:S(2)}, u32[]{:S(2)}) collective-permute-start(bf16[32,4096]{1,0:T(8,128)(2,1)S(1)} %get-tuple-element.9), channel_id=1, source_target_pairs={{0,11},{1,0},{2,1},{3,2},{4,3},{5,4},{6,5},{7,6},{8,7},{9,8},{10,9... | collective-permute-start | bytes 786440 | tf_op jit(solution)/shard_map/ppermute | solution.py:93
  178.6 2.4 %collective-permute-done.12 = bf16[32,4096]{1,0:T(8,128)(2,1)S(1)} collective-permute-done((bf16[32,4096]{1,0:T(8,128)(2,1)S(1)}, bf16[32,4096]{1,0:T(8,128)(2,1)S(1)}, u32[]{:S(2)}, u32[]{:S(2)}) %collective-permute-start.12) | collective-permute-done | bytes 262176 | tf_op jit(solution)/shard_map/ppermute | solution.py:88
  181.0 1.5 collective-permute-done.17
  182.4 1.8 add_convert_fusion
  (61 shorter events, 15.3 us)
Async XLA Ops:
  0.0 99.6 %copy-start = (bf16[256,4096]{1,0:T(8,128)(2,1)S(1)}, bf16[256,4096]{1,0:T(8,128)(2,1)}, u32[]{:S(2)}) copy-start(bf16[256,4096]{1,0:T(8,128)(2,1)} %param.8) | copy-start | bytes 6291460
  30.0 32.1 %collective-permute-start.2 = (bf16[1024,256]{1,0:T(8,128)(2,1)S(1)}, bf16[1024,256]{1,0:T(8,128)(2,1)}, u32[]{:S(2)}, u32[]{:S(2)}) collective-permute-start(bf16[1024,256]{1,0:T(8,128)(2,1)S(1)} %all_gather.7), channel_id=1, source_target_pairs={{0,192},{192,384},{384,576},{576,0},{1,193},{193,385},{385,577},{5... | collective-permute-start | bytes 1572872 | tf_op jit(solution)/shard_map/ppermute | solution.py:59
  33.4 36.8 %collective-permute-start.4 = (bf16[1024,256]{1,0:T(8,128)(2,1)S(1)}, bf16[1024,256]{1,0:T(8,128)(2,1)S(1)}, u32[]{:S(2)}, u32[]{:S(2)}) collective-permute-start(bf16[1024,256]{1,0:T(8,128)(2,1)S(1)} %all_gather.7), channel_id=1, source_target_pairs={{0,576},{192,0},{384,192},{576,384},{1,577},{193,1},{385,193},{577... | collective-permute-start | bytes 1572872 | tf_op jit(solution)/shard_map/ppermute | solution.py:60
  43.2 39.3 %collective-permute-start.1 = (bf16[384,128]{1,0:T(8,128)(2,1)}, bf16[384,128]{1,0:T(8,128)(2,1)}, u32[]{:S(2)}, u32[]{:S(2)}) collective-permute-start(bf16[384,128]{1,0:T(8,128)(2,1)} %get-tuple-element.29), channel_id=1, source_target_pairs={{0,12},{12,0},{1,13},{13,1},{2,14},{14,2},{3,15},{15,3},{4,16},{16... | collective-permute-start | bytes 294920 | tf_op jit(solution)/shard_map/ppermute | solution.py:133
  50.3 10.1 %collective-permute-start = (bf16[256,512]{0,1:T(8,128)(2,1)}, bf16[256,512]{0,1:T(8,128)(2,1)}, u32[]{:S(2)}, u32[]{:S(2)}) collective-permute-start(bf16[256,512]{0,1:T(8,128)(2,1)} %pad_maximum_fusion.2), channel_id=1, source_target_pairs={{0,12},{12,24},{24,36},{36,48},{48,60},{60,72},{72,84},{84,96},{96... | collective-permute-start | bytes 786440 | tf_op jit(solution)/shard_map/ppermute | solution.py:22
  54.4 20.4 %copy-start.4 = (bf16[384,256]{1,0:T(8,128)(2,1)S(1)}, bf16[384,256]{1,0:T(8,128)(2,1)}, u32[]{:S(2)}) copy-start(bf16[384,256]{1,0:T(8,128)(2,1)} %param.7) | copy-start | bytes 589828
  63.7 13.2 %collective-permute-start.3 = (bf16[512,256]{1,0:T(8,128)(2,1)}, bf16[512,256]{1,0:T(8,128)(2,1)}, u32[]{:S(2)}, u32[]{:S(2)}) collective-permute-start(bf16[512,256]{1,0:T(8,128)(2,1)} %slice.76), channel_id=1, source_target_pairs={{0,192},{192,384},{384,576},{576,0},{1,193},{193,385},{385,577},{5... | collective-permute-start | bytes 786440 | tf_op jit(solution)/shard_map/ppermute | solution.py:64
  70.8 9.2 %collective-permute-start.5 = (bf16[512,256]{1,0:T(8,128)(2,1)}, bf16[512,256]{1,0:T(8,128)(2,1)}, u32[]{:S(2)}, u32[]{:S(2)}) collective-permute-start(bf16[512,256]{1,0:T(8,128)(2,1)} %slice.77), channel_id=1, source_target_pairs={{0,576},{192,0},{384,192},{576,384},{1,577},{193,1},{385,193},{577... | collective-permute-start | bytes 786440 | tf_op jit(solution)/shard_map/ppermute | solution.py:65
  74.8 7.7 %copy-start.6 = (bf16[384,128]{1,0:T(8,128)(2,1)S(1)}, bf16[384,128]{1,0:T(8,128)(2,1)}, u32[]{:S(2)}) copy-start(bf16[384,128]{1,0:T(8,128)(2,1)} %get-tuple-element.28) | copy-start | bytes 294916
  82.5 4.4 %copy-start.5 = (bf16[4096,256]{1,0:T(8,128)(2,1)S(1)}, bf16[4096,256]{1,0:T(8,128)(2,1)}, u32[]{:S(2)}) copy-start(bf16[4096,256]{1,0:T(8,128)(2,1)} %constant_dynamic-update-slice_fusion) | copy-start | bytes 6291460
  82.5 4.4 %copy-start.7 = (s32[768]{0:T(1024)S(1)}, s32[768]{0:T(1024)}, u32[]{:S(2)}) copy-start(s32[768]{0:T(1024)} %pad_add_fusion) | copy-start | bytes 9220
  90.9 6.6 %copy-start.2 = (f32[2,640,384]{2,1,0:T(8,128)S(1)}, f32[2,640,384]{2,1,0:T(8,128)}, u32[]{:S(2)}) copy-start(f32[2,640,384]{2,1,0:T(8,128)} %get-tuple-element.33) | copy-start | bytes 5898244
  90.9 6.6 %copy-start.3 = (pred[384,640]{0,1:T(8,128)(4,1)S(1)}, pred[384,640]{0,1:T(8,128)(4,1)}, u32[]{:S(2)}) copy-start(pred[384,640]{0,1:T(8,128)(4,1)} %fusion.20) | copy-start | bytes 737284
  90.9 6.6 %copy-start.8 = (f32[2,384]{1,0:T(2,128)S(1)}, f32[2,384]{1,0:T(2,128)}, u32[]{:S(2)}) copy-start(f32[2,384]{1,0:T(2,128)} %get-tuple-element.32) | copy-start | bytes 9220
  95.4 3.4 %collective-permute-start.6 = (f32[384,130]{0,1:T(8,128)S(1)}, f32[384,130]{0,1:T(8,128)S(1)}, u32[]{:S(2)}, u32[]{:S(2)}) collective-permute-start(f32[384,130]{0,1:T(8,128)S(1)} %pad_maximum_fusion.3), channel_id=1, source_target_pairs={{0,12},{12,0},{1,13},{13,1},{2,14},{14,2},{3,15},{15,3},{4,16},{16... | collective-permute-start | bytes 599048 | tf_op jit(solution)/shard_map/ppermute | solution.py:154
  100.6 2.6 %copy-start.1 = (f32[384,4096]{1,0:T(8,128)}, f32[384,4096]{1,0:T(8,128)S(1)}, u32[]{:S(2)}) copy-start(f32[384,4096]{1,0:T(8,128)S(1)} %fusion.56) | copy-start | bytes 18874372
  103.3 16.3 %collective-permute-start.7 = (bf16[32,4096]{1,0:T(8,128)(2,1)S(1)}, bf16[32,4096]{1,0:T(8,128)(2,1)S(1)}, u32[]{:S(2)}, u32[]{:S(2)}) collective-permute-start(bf16[32,4096]{1,0:T(8,128)(2,1)S(1)} %get-tuple-element.16), channel_id=1, source_target_pairs={{0,1},{1,2},{2,3},{3,4},{4,5},{5,6},{6,7},{7,8},{8,9},{9,10},{10,1... | collective-permute-start | bytes 786440 | tf_op jit(solution)/shard_map/ppermute | solution.py:88
  105.3 17.4 %collective-permute-start.13 = (bf16[32,4096]{1,0:T(8,128)(2,1)S(1)}, bf16[32,4096]{1,0:T(8,128)(2,1)S(1)}, u32[]{:S(2)}, u32[]{:S(2)}) collective-permute-start(bf16[32,4096]{1,0:T(8,128)(2,1)S(1)} %get-tuple-element.17), channel_id=1, source_target_pairs={{0,11},{1,0},{2,1},{3,2},{4,3},{5,4},{6,5},{7,6},{8,7},{9,8},{10,9... | collective-permute-start | bytes 786440 | tf_op jit(solution)/shard_map/ppermute | solution.py:93
  120.7 10.9 %collective-permute-start.8 = (bf16[32,4096]{1,0:T(8,128)(2,1)S(1)}, bf16[32,4096]{1,0:T(8,128)(2,1)S(1)}, u32[]{:S(2)}, u32[]{:S(2)}) collective-permute-start(bf16[32,4096]{1,0:T(8,128)(2,1)S(1)} %add_convert_fusion.9), channel_id=1, source_target_pairs={{0,1},{1,2},{2,3},{3,4},{4,5},{5,6},{6,7},{7,8},{8,9},{9,10},{10,1... | collective-permute-start | bytes 786440 | tf_op jit(solution)/shard_map/ppermute | solution.py:88
  132.8 8.8 %collective-permute-start.14 = (bf16[32,4096]{1,0:T(8,128)(2,1)S(1)}, bf16[32,4096]{1,0:T(8,128)(2,1)S(1)}, u32[]{:S(2)}, u32[]{:S(2)}) collective-permute-start(bf16[32,4096]{1,0:T(8,128)(2,1)S(1)} %get-tuple-element.15), channel_id=1, source_target_pairs={{0,11},{1,0},{2,1},{3,2},{4,3},{5,4},{6,5},{7,6},{8,7},{9,8},{10,9... | collective-permute-start | bytes 786440 | tf_op jit(solution)/shard_map/ppermute | solution.py:93
  135.0 9.8 %collective-permute-start.9 = (bf16[32,4096]{1,0:T(8,128)(2,1)S(1)}, bf16[32,4096]{1,0:T(8,128)(2,1)S(1)}, u32[]{:S(2)}, u32[]{:S(2)}) collective-permute-start(bf16[32,4096]{1,0:T(8,128)(2,1)S(1)} %get-tuple-element.14), channel_id=1, source_target_pairs={{0,1},{1,2},{2,3},{3,4},{4,5},{5,6},{6,7},{7,8},{8,9},{9,10},{10,1... | collective-permute-start | bytes 786440 | tf_op jit(solution)/shard_map/ppermute | solution.py:88
  146.1 9.5 %collective-permute-start.10 = (bf16[32,4096]{1,0:T(8,128)(2,1)S(1)}, bf16[32,4096]{1,0:T(8,128)(2,1)S(1)}, u32[]{:S(2)}, u32[]{:S(2)}) collective-permute-start(bf16[32,4096]{1,0:T(8,128)(2,1)S(1)} %get-tuple-element.12), channel_id=1, source_target_pairs={{0,1},{1,2},{2,3},{3,4},{4,5},{5,6},{6,7},{7,8},{8,9},{9,10},{10,1... | collective-permute-start | bytes 786440 | tf_op jit(solution)/shard_map/ppermute | solution.py:88
  148.5 8.5 %collective-permute-start.15 = (bf16[32,4096]{1,0:T(8,128)(2,1)S(1)}, bf16[32,4096]{1,0:T(8,128)(2,1)S(1)}, u32[]{:S(2)}, u32[]{:S(2)}) collective-permute-start(bf16[32,4096]{1,0:T(8,128)(2,1)S(1)} %get-tuple-element.13), channel_id=1, source_target_pairs={{0,11},{1,0},{2,1},{3,2},{4,3},{5,4},{6,5},{7,6},{8,7},{9,8},{10,9... | collective-permute-start | bytes 786440 | tf_op jit(solution)/shard_map/ppermute | solution.py:93
  158.3 9.9 %collective-permute-start.11 = (bf16[32,4096]{1,0:T(8,128)(2,1)S(1)}, bf16[32,4096]{1,0:T(8,128)(2,1)S(1)}, u32[]{:S(2)}, u32[]{:S(2)}) collective-permute-start(bf16[32,4096]{1,0:T(8,128)(2,1)S(1)} %get-tuple-element.10), channel_id=1, source_target_pairs={{0,1},{1,2},{2,3},{3,4},{4,5},{5,6},{6,7},{7,8},{8,9},{9,10},{10,1... | collective-permute-start | bytes 786440 | tf_op jit(solution)/shard_map/ppermute | solution.py:88
  160.3 9.4 %collective-permute-start.16 = (bf16[32,4096]{1,0:T(8,128)(2,1)S(1)}, bf16[32,4096]{1,0:T(8,128)(2,1)S(1)}, u32[]{:S(2)}, u32[]{:S(2)}) collective-permute-start(bf16[32,4096]{1,0:T(8,128)(2,1)S(1)} %get-tuple-element.11), channel_id=1, source_target_pairs={{0,11},{1,0},{2,1},{3,2},{4,3},{5,4},{6,5},{7,6},{8,7},{9,8},{10,9... | collective-permute-start | bytes 786440 | tf_op jit(solution)/shard_map/ppermute | solution.py:93
  171.0 9.9 %collective-permute-start.12 = (bf16[32,4096]{1,0:T(8,128)(2,1)S(1)}, bf16[32,4096]{1,0:T(8,128)(2,1)S(1)}, u32[]{:S(2)}, u32[]{:S(2)}) collective-permute-start(bf16[32,4096]{1,0:T(8,128)(2,1)S(1)} %get-tuple-element.8), channel_id=1, source_target_pairs={{0,1},{1,2},{2,3},{3,4},{4,5},{5,6},{6,7},{7,8},{8,9},{9,10},{10,1... | collective-permute-start | bytes 786440 | tf_op jit(solution)/shard_map/ppermute | solution.py:88
  172.9 9.5 %collective-permute-start.17 = (bf16[32,4096]{1,0:T(8,128)(2,1)S(1)}, bf16[32,4096]{1,0:T(8,128)(2,1)S(1)}, u32[]{:S(2)}, u32[]{:S(2)}) collective-permute-start(bf16[32,4096]{1,0:T(8,128)(2,1)S(1)} %get-tuple-element.9), channel_id=1, source_target_pairs={{0,11},{1,0},{2,1},{3,2},{4,3},{5,4},{6,5},{7,6},{8,7},{9,8},{10,9... | collective-permute-start | bytes 786440 | tf_op jit(solution)/shard_map/ppermute | solution.py:93

commit v12 on v11

--- a/solution.py
+++ b/solution.py
@@ -101,10 +101,7 @@
     tok_rows, width = queries.shape
     half_sum = SUMMARY // 2
     my_index = lax.axis_index(CTX)
-    rim = shifted(
-        jnp.concatenate([keys[tok_rows - BAND :], values[tok_rows - BAND :]], axis=1), CTX, 1
-    )
-    rim_keys, rim_values = rim[:, :width], rim[:, width:]
+    rim_keys, rim_values = shifted((keys[tok_rows - BAND :], values[tok_rows - BAND :]), CTX, 1)
     band_keys = jnp.concatenate([rim_keys, keys], axis=0)
     band_values = jnp.concatenate([rim_values, values], axis=0)
     own_pos = my_index * tok_rows + jnp.arange(tok_rows, dtype=jnp.int32)
@@ -161,7 +158,7 @@
     merged = combine_terms(near[0], far)
     heads_out = merged[2] / merged[1][:, :, None]
     attn = jnp.transpose(heads_out, (1, 0, 2)).reshape(tok_rows, width).astype(jnp.bfloat16)
-    partial = jnp.dot(attn, out_weight, preferred_element_type=jnp.float32)
+    partial = jnp.dot(attn, out_weight, preferred_element_type=jnp.float32).astype(jnp.bfloat16)
     return ring_reduce_scatter(partial, "head")
 
 

time: 185 us -> 184 us (level)
  the two profiles are of different devices: /device:TPU:2 before, /device:TPU:30 now
where the time goes in v12:
time: 184 us; the launch traced here: 182 us
  starting transfers between devices  69.6 us (38%)
  waiting for transfers between devices  35 us (19%)
  blocking collectives  27.7 us (15%)
  other arithmetic  18.5 us (10%)
  local copies, waits for them, and re-layouts  17.9 us (10%)
  matrix products  13.1 us (7%)
    ppermute x5, starting transfers between devices, ring_reduce_scatter(): down_sum = lax.ppermute(down, axis, behind).astype(jnp.float32)  32.2 us
    all_gather x1, blocking collectives, layer(): gathered = lax.all_gather(my_half, 'cy', axis=0, tiled=True)  25.8 us
    ppermute x6, waiting for transfers between devices, ring_reduce_scatter(): lax.ppermute(up, axis, ahead).astype(jnp.float32)  23.5 us
    ppermute x6, starting transfers between devices, ring_reduce_scatter(): lax.ppermute(up, axis, ahead).astype(jnp.float32)  11.5 us
    unnamed x21, local copies, waits for them, and re-layouts  8.84 us
    dot_general x2, matrix products, attend(): jnp.einsum('qhd,khd->hqk', q, k, preferred_element_type=jnp.float32) * scale  7.39 us
    ppermute x2, starting transfers between devices, shifted(): lax.ppermute(value, axis, [(source, source + steps) for source in range(l...  6.98 us
    ppermute x1, starting transfers between devices, gather_row_blocks(): from_left = lax.ppermute(block, axis, ahead)  5.92 us
  transfers between devices with their start and end apart: 19, of which 12 were waited for; matrix products, arithmetic and copies ran while one was open for 14% of the time, Pallas kernels for 0%

profile of v12, /device:TPU:30, one launch (start us, length us, event | category | flops | bytes accessed | tf_op | source)
XLA Modules:
  0.0 182.5 jit_solution(3164987316829490672)
XLA Ops:
  1.7 1.9 %all_gather.6 = bf16[128,512]{1,0:T(8,128)(2,1)S(1)} all-gather(bf16[64,512]{1,0:T(8,128)(2,1)S(1)} %pad_maximum_fusion.3), channel_id=1, replica_groups=mesh['cx'=4,'cy'=8,'cc'=2,'head'=12] {'cc'}, dimensions={0}, use_global_device_ids=true | all-gather | bytes 196608 | tf_op jit(solution)/shard_map/all_gather | solution.py:120
  3.6 25.8 %all_gather.7 = bf16[1024,256]{1,0:T(8,128)(2,1)S(1)} all-gather(bf16[128,256]{1,0:T(8,128)(2,1)S(1)} %pad_maximum_fusion.4), channel_id=1, replica_groups=mesh['cx'=4,'cy'=8,'cc'=2,'head'=12] {'cy'}, dimensions={0}, use_global_device_ids=true | all-gather | bytes 589824 | tf_op jit(solution)/shard_map/all_gather | solution.py:131
  29.4 5.9 %collective-permute-start.3 = (bf16[1024,256]{1,0:T(8,128)(2,1)S(1)}, bf16[1024,256]{1,0:T(8,128)(2,1)}, u32[]{:S(2)}, u32[]{:S(2)}) collective-permute-start(bf16[1024,256]{1,0:T(8,128)(2,1)S(1)} %all_gather.7), channel_id=1, source_target_pairs={{0,192},{192,384},{384,576},{576,0},{1,193},{193,385},{385,577},{5... | collective-permute-start | bytes 1572872 | tf_op jit(solution)/shard_map/ppermute | solution.py:59
  35.4 1.9 %collective-permute-start.5 = (bf16[1024,256]{1,0:T(8,128)(2,1)S(1)}, bf16[1024,256]{1,0:T(8,128)(2,1)S(1)}, u32[]{:S(2)}, u32[]{:S(2)}) collective-permute-start(bf16[1024,256]{1,0:T(8,128)(2,1)S(1)} %all_gather.7), channel_id=1, source_target_pairs={{0,576},{192,0},{384,192},{576,384},{1,577},{193,1},{385,193},{577... | collective-permute-start | bytes 1572872 | tf_op jit(solution)/shard_map/ppermute | solution.py:60
  37.3 1.7 constant_dynamic-slice_fusion.7
  39.0 1.9 %collective-permute-start.2 = (bf16[384,128]{1,0:T(8,128)(2,1)}, bf16[384,128]{1,0:T(8,128)(2,1)}, u32[]{:S(2)}, u32[]{:S(2)}) collective-permute-start(bf16[384,128]{1,0:T(8,128)(2,1)} %get-tuple-element.27), channel_id=1, source_target_pairs={{0,12},{12,0},{1,13},{13,1},{2,14},{14,2},{3,15},{15,3},{4,16},{16... | collective-permute-start | bytes 294920 | tf_op jit(solution)/shard_map/ppermute | solution.py:130
  42.6 2.4 %collective-permute-start = (bf16[256,256]{0,1:T(8,128)(2,1)}, bf16[256,256]{0,1:T(8,128)(2,1)}, u32[]{:S(2)}, u32[]{:S(2)}) collective-permute-start(bf16[256,256]{0,1:T(8,128)(2,1)} %slice.65), channel_id=1, source_target_pairs={{0,12},{12,24},{24,36},{36,48},{48,60},{60,72},{72,84},{84,96},{96... | collective-permute-start | bytes 393224 | tf_op jit(solution)/shard_map/ppermute | solution.py:22
  45.0 1.6 slice.46
  46.6 4.6 %collective-permute-start.1 = (bf16[256,256]{1,0:T(8,128)(2,1)}, bf16[256,256]{1,0:T(8,128)(2,1)}, u32[]{:S(2)}, u32[]{:S(2)}) collective-permute-start(bf16[256,256]{1,0:T(8,128)(2,1)} %slice.46), channel_id=1, source_target_pairs={{0,12},{12,24},{24,36},{36,48},{48,60},{60,72},{72,84},{84,96},{96... | collective-permute-start | bytes 393224 | tf_op jit(solution)/shard_map/ppermute | solution.py:22
  55.1 1.3 pad_add_fusion
  57.3 1.7 slice.66
  59.0 5.1 %collective-permute-start.4 = (bf16[512,256]{1,0:T(8,128)(2,1)}, bf16[512,256]{1,0:T(8,128)(2,1)}, u32[]{:S(2)}, u32[]{:S(2)}) collective-permute-start(bf16[512,256]{1,0:T(8,128)(2,1)} %slice.66), channel_id=1, source_target_pairs={{0,192},{192,384},{384,576},{576,0},{1,193},{193,385},{385,577},{5... | collective-permute-start | bytes 786440 | tf_op jit(solution)/shard_map/ppermute | solution.py:64
  64.1 2.9 %fusion.3 = (f32[2,384]{1,0:T(2,128)S(1)}, f32[2,640,384]{2,1,0:T(8,128)}) fusion(pred[384,640]{0,1:T(8,128)(4,1)} %fusion.20, bf16[640,2,128]{0,2,1:T(8,128)(2,1)S(1)} %bitcast.57, bf16[384,256]{1,0:T(8,128)(2,1)} %param.5), kind=kOutput, calls=%fused_computation.9 | convolution fusion | flops 127302912 | bytes 2739200 | tf_op jit(solution)/shard_map/qhd,khd->hqk/dot_general | solution.py:40
  67.7 1.9 %collective-permute-start.6 = (bf16[512,256]{1,0:T(8,128)(2,1)}, bf16[512,256]{1,0:T(8,128)(2,1)}, u32[]{:S(2)}, u32[]{:S(2)}) collective-permute-start(bf16[512,256]{1,0:T(8,128)(2,1)} %slice.67), channel_id=1, source_target_pairs={{0,576},{192,0},{384,192},{576,384},{1,577},{193,1},{385,193},{577... | collective-permute-start | bytes 786440 | tf_op jit(solution)/shard_map/ppermute | solution.py:65
  70.8 1.9 %constant_dynamic-update-slice_fusion.3 = bf16[4096,256]{1,0:T(8,128)(2,1)} fusion(bf16[4096,256]{1,0:T(8,128)(2,1)} %constant_dynamic-update-slice_fusion.4, bf16[1024,256]{1,0:T(8,128)(2,1)} %collective-permute-done.3), kind=kLoop, calls=%fused_computation.97 | loop fusion | bytes 1048576
  72.7 1.7 constant_dynamic-update-slice_fusion.2
  74.4 5.2 %collective-permute-done.6 = bf16[512,256]{1,0:T(8,128)(2,1)} collective-permute-done((bf16[512,256]{1,0:T(8,128)(2,1)}, bf16[512,256]{1,0:T(8,128)(2,1)}, u32[]{:S(2)}, u32[]{:S(2)}) %collective-permute-start.6) | collective-permute-done | bytes 262176 | tf_op jit(solution)/shard_map/ppermute | solution.py:65
  79.6 1.7 constant_dynamic-update-slice_fusion.1
  82.1 4.5 %fusion = (f32[768]{0:T(1024)S(1)}, f32[768,4096]{1,0:T(8,128)S(1)}) fusion(s32[4096]{0:T(1024)S(1)} %fusion.34, s32[768]{0:T(1024)S(1)} %copy-done.7, bf16[4096,256]{1,0:T(8,128)(2,1)} %constant_dynamic-update-slice_fusion, bf16[384,128]{1,0:T(8,128)(2,1)} %collective-permute-done.2, bf16[384,128]{1,0:T(8,128)(2,1)} %get-tuple-element.26), kind=kOutput, calls=%fused_computation.3 | convolution fusion | flops 821427456 | bytes 13850624 | tf_op jit(solution)/shard_map/qhd,khd->hqk/dot_general | solution.py:40
  86.6 4.0 %fusion.6 = f32[1,768,128]{1,2,0:T(8,128)S(1)} fusion(bf16[4096,256]{1,0:T(8,128)(2,1)S(1)} %copy-done.5, f32[768,4096]{1,0:T(8,128)S(1)} %get-tuple-element.33, f32[768]{0:T(1024)S(1)} %get-tuple-element.32, s32[4096]{0:T(1024)S(1)} %fusion.34, s32[768]{0:T(1024)S(1)} %copy-done.7), kind=kOutput, calls=%fused_computation.14 | convolution fusion | flops 827326464 | bytes 14049280 | tf_op jit(solution)/shard_map/hqk,khd->hqd/dot_general | solution.py:45
  90.6 4.4 %fusion.52 = f32[768]{0:T(1024)S(1)} fusion(f32[768]{0:T(1024)S(1)} %get-tuple-element.32, f32[768,4096]{1,0:T(8,128)S(1)} %get-tuple-element.33, s32[4096]{0:T(1024)S(1)} %fusion.34, s32[768]{0:T(1024)S(1)} %copy-done.7), kind=kLoop, calls=%fused_computation.131 | loop fusion | flops 22019328 | bytes 12608512 | tf_op jit(solution)/shard_map/reduce_sum | solution.py:48
  95.0 2.1 %collective-permute-start.7 = (f32[384,130]{0,1:T(8,128)S(1)}, f32[384,130]{0,1:T(8,128)S(1)}, u32[]{:S(2)}, u32[]{:S(2)}) collective-permute-start(f32[384,130]{0,1:T(8,128)S(1)} %pad_maximum_fusion.2), channel_id=1, source_target_pairs={{0,12},{12,0},{1,13},{13,1},{2,14},{14,2},{3,15},{15,3},{4,16},{16... | collective-permute-start | bytes 599048 | tf_op jit(solution)/shard_map/ppermute | solution.py:151
  100.3 1.6 copy-done.1
  101.9 1.9 %collective-permute-start.8 = (bf16[32,4096]{1,0:T(8,128)(2,1)S(1)}, bf16[32,4096]{1,0:T(8,128)(2,1)S(1)}, u32[]{:S(2)}, u32[]{:S(2)}) collective-permute-start(bf16[32,4096]{1,0:T(8,128)(2,1)S(1)} %get-tuple-element.16), channel_id=1, source_target_pairs={{0,1},{1,2},{2,3},{3,4},{4,5},{5,6},{6,7},{7,8},{8,9},{9,10},{10,1... | collective-permute-start | bytes 786440 | tf_op jit(solution)/shard_map/ppermute | solution.py:88
  103.9 10.3 %collective-permute-start.14 = (bf16[32,4096]{1,0:T(8,128)(2,1)S(1)}, bf16[32,4096]{1,0:T(8,128)(2,1)S(1)}, u32[]{:S(2)}, u32[]{:S(2)}) collective-permute-start(bf16[32,4096]{1,0:T(8,128)(2,1)S(1)} %get-tuple-element.17), channel_id=1, source_target_pairs={{0,11},{1,0},{2,1},{3,2},{4,3},{5,4},{6,5},{7,6},{8,7},{9,8},{10,9... | collective-permute-start | bytes 786440 | tf_op jit(solution)/shard_map/ppermute | solution.py:93
  114.2 4.6 %collective-permute-done.8 = bf16[32,4096]{1,0:T(8,128)(2,1)S(1)} collective-permute-done((bf16[32,4096]{1,0:T(8,128)(2,1)S(1)}, bf16[32,4096]{1,0:T(8,128)(2,1)S(1)}, u32[]{:S(2)}, u32[]{:S(2)}) %collective-permute-start.8) | collective-permute-done | bytes 262176 | tf_op jit(solution)/shard_map/ppermute | solution.py:88
  119.8 1.9 %collective-permute-start.9 = (bf16[32,4096]{1,0:T(8,128)(2,1)S(1)}, bf16[32,4096]{1,0:T(8,128)(2,1)S(1)}, u32[]{:S(2)}, u32[]{:S(2)}) collective-permute-start(bf16[32,4096]{1,0:T(8,128)(2,1)S(1)} %add_convert_fusion.9), channel_id=1, source_target_pairs={{0,1},{1,2},{2,3},{3,4},{4,5},{5,6},{6,7},{7,8},{8,9},{9,10},{10,1... | collective-permute-start | bytes 786440 | tf_op jit(solution)/shard_map/ppermute | solution.py:88
  121.8 8.9 %collective-permute-done.9 = bf16[32,4096]{1,0:T(8,128)(2,1)S(1)} collective-permute-done((bf16[32,4096]{1,0:T(8,128)(2,1)S(1)}, bf16[32,4096]{1,0:T(8,128)(2,1)S(1)}, u32[]{:S(2)}, u32[]{:S(2)}) %collective-permute-start.9) | collective-permute-done | bytes 262176 | tf_op jit(solution)/shard_map/ppermute | solution.py:88
  130.7 1.2 add_convert_fusion.8
  131.8 1.9 %collective-permute-start.10 = (bf16[32,4096]{1,0:T(8,128)(2,1)S(1)}, bf16[32,4096]{1,0:T(8,128)(2,1)S(1)}, u32[]{:S(2)}, u32[]{:S(2)}) collective-permute-start(bf16[32,4096]{1,0:T(8,128)(2,1)S(1)} %get-tuple-element.14), channel_id=1, source_target_pairs={{0,1},{1,2},{2,3},{3,4},{4,5},{5,6},{6,7},{7,8},{8,9},{9,10},{10,1... | collective-permute-start | bytes 786440 | tf_op jit(solution)/shard_map/ppermute | solution.py:88
  133.8 5.1 %collective-permute-start.15 = (bf16[32,4096]{1,0:T(8,128)(2,1)S(1)}, bf16[32,4096]{1,0:T(8,128)(2,1)S(1)}, u32[]{:S(2)}, u32[]{:S(2)}) collective-permute-start(bf16[32,4096]{1,0:T(8,128)(2,1)S(1)} %get-tuple-element.15), channel_id=1, source_target_pairs={{0,11},{1,0},{2,1},{3,2},{4,3},{5,4},{6,5},{7,6},{8,7},{9,8},{10,9... | collective-permute-start | bytes 786440 | tf_op jit(solution)/shard_map/ppermute | solution.py:93
  138.9 2.9 %collective-permute-done.10 = bf16[32,4096]{1,0:T(8,128)(2,1)S(1)} collective-permute-done((bf16[32,4096]{1,0:T(8,128)(2,1)S(1)}, bf16[32,4096]{1,0:T(8,128)(2,1)S(1)}, u32[]{:S(2)}, u32[]{:S(2)}) %collective-permute-start.10) | collective-permute-done | bytes 262176 | tf_op jit(solution)/shard_map/ppermute | solution.py:88
  141.9 1.2 collective-permute-done.15
  144.2 1.9 %collective-permute-start.11 = (bf16[32,4096]{1,0:T(8,128)(2,1)S(1)}, bf16[32,4096]{1,0:T(8,128)(2,1)S(1)}, u32[]{:S(2)}, u32[]{:S(2)}) collective-permute-start(bf16[32,4096]{1,0:T(8,128)(2,1)S(1)} %get-tuple-element.12), channel_id=1, source_target_pairs={{0,1},{1,2},{2,3},{3,4},{4,5},{5,6},{6,7},{7,8},{8,9},{9,10},{10,1... | collective-permute-start | bytes 786440 | tf_op jit(solution)/shard_map/ppermute | solution.py:88
  146.1 5.6 %collective-permute-start.16 = (bf16[32,4096]{1,0:T(8,128)(2,1)S(1)}, bf16[32,4096]{1,0:T(8,128)(2,1)S(1)}, u32[]{:S(2)}, u32[]{:S(2)}) collective-permute-start(bf16[32,4096]{1,0:T(8,128)(2,1)S(1)} %get-tuple-element.13), channel_id=1, source_target_pairs={{0,11},{1,0},{2,1},{3,2},{4,3},{5,4},{6,5},{7,6},{8,7},{9,8},{10,9... | collective-permute-start | bytes 786440 | tf_op jit(solution)/shard_map/ppermute | solution.py:93
  151.8 2.4 %collective-permute-done.11 = bf16[32,4096]{1,0:T(8,128)(2,1)S(1)} collective-permute-done((bf16[32,4096]{1,0:T(8,128)(2,1)S(1)}, bf16[32,4096]{1,0:T(8,128)(2,1)S(1)}, u32[]{:S(2)}, u32[]{:S(2)}) %collective-permute-start.11) | collective-permute-done | bytes 262176 | tf_op jit(solution)/shard_map/ppermute | solution.py:88
  154.1 1.5 collective-permute-done.16
  155.6 1.2 add_convert_fusion.6
  156.7 1.9 %collective-permute-start.12 = (bf16[32,4096]{1,0:T(8,128)(2,1)S(1)}, bf16[32,4096]{1,0:T(8,128)(2,1)S(1)}, u32[]{:S(2)}, u32[]{:S(2)}) collective-permute-start(bf16[32,4096]{1,0:T(8,128)(2,1)S(1)} %get-tuple-element.10), channel_id=1, source_target_pairs={{0,1},{1,2},{2,3},{3,4},{4,5},{5,6},{6,7},{7,8},{8,9},{9,10},{10,1... | collective-permute-start | bytes 786440 | tf_op jit(solution)/shard_map/ppermute | solution.py:88
  158.7 5.6 %collective-permute-start.17 = (bf16[32,4096]{1,0:T(8,128)(2,1)S(1)}, bf16[32,4096]{1,0:T(8,128)(2,1)S(1)}, u32[]{:S(2)}, u32[]{:S(2)}) collective-permute-start(bf16[32,4096]{1,0:T(8,128)(2,1)S(1)} %get-tuple-element.11), channel_id=1, source_target_pairs={{0,11},{1,0},{2,1},{3,2},{4,3},{5,4},{6,5},{7,6},{8,7},{9,8},{10,9... | collective-permute-start | bytes 786440 | tf_op jit(solution)/shard_map/ppermute | solution.py:93
  164.3 2.4 %collective-permute-done.12 = bf16[32,4096]{1,0:T(8,128)(2,1)S(1)} collective-permute-done((bf16[32,4096]{1,0:T(8,128)(2,1)S(1)}, bf16[32,4096]{1,0:T(8,128)(2,1)S(1)}, u32[]{:S(2)}, u32[]{:S(2)}) %collective-permute-start.12) | collective-permute-done | bytes 262176 | tf_op jit(solution)/shard_map/ppermute | solution.py:88
  166.7 1.5 collective-permute-done.17
  168.2 1.2 add_convert_fusion.5
  169.3 1.9 %collective-permute-start.13 = (bf16[32,4096]{1,0:T(8,128)(2,1)S(1)}, bf16[32,4096]{1,0:T(8,128)(2,1)S(1)}, u32[]{:S(2)}, u32[]{:S(2)}) collective-permute-start(bf16[32,4096]{1,0:T(8,128)(2,1)S(1)} %get-tuple-element.8), channel_id=1, source_target_pairs={{0,1},{1,2},{2,3},{3,4},{4,5},{5,6},{6,7},{7,8},{8,9},{9,10},{10,1... | collective-permute-start | bytes 786440 | tf_op jit(solution)/shard_map/ppermute | solution.py:88
  171.2 5.6 %collective-permute-start.18 = (bf16[32,4096]{1,0:T(8,128)(2,1)S(1)}, bf16[32,4096]{1,0:T(8,128)(2,1)S(1)}, u32[]{:S(2)}, u32[]{:S(2)}) collective-permute-start(bf16[32,4096]{1,0:T(8,128)(2,1)S(1)} %get-tuple-element.9), channel_id=1, source_target_pairs={{0,11},{1,0},{2,1},{3,2},{4,3},{5,4},{6,5},{7,6},{8,7},{9,8},{10,9... | collective-permute-start | bytes 786440 | tf_op jit(solution)/shard_map/ppermute | solution.py:93
  176.9 2.4 %collective-permute-done.13 = bf16[32,4096]{1,0:T(8,128)(2,1)S(1)} collective-permute-done((bf16[32,4096]{1,0:T(8,128)(2,1)S(1)}, bf16[32,4096]{1,0:T(8,128)(2,1)S(1)}, u32[]{:S(2)}, u32[]{:S(2)}) %collective-permute-start.13) | collective-permute-done | bytes 262176 | tf_op jit(solution)/shard_map/ppermute | solution.py:88
  179.3 1.5 collective-permute-done.18
  180.7 1.7 add_convert_fusion
  (57 shorter events, 16.3 us)
Async XLA Ops:
  0.0 99.2 %copy-start = (bf16[256,4096]{1,0:T(8,128)(2,1)S(1)}, bf16[256,4096]{1,0:T(8,128)(2,1)}, u32[]{:S(2)}) copy-start(bf16[256,4096]{1,0:T(8,128)(2,1)} %param.8) | copy-start | bytes 6291460
  29.4 27.8 %collective-permute-start.3 = (bf16[1024,256]{1,0:T(8,128)(2,1)S(1)}, bf16[1024,256]{1,0:T(8,128)(2,1)}, u32[]{:S(2)}, u32[]{:S(2)}) collective-permute-start(bf16[1024,256]{1,0:T(8,128)(2,1)S(1)} %all_gather.7), channel_id=1, source_target_pairs={{0,192},{192,384},{384,576},{576,0},{1,193},{193,385},{385,577},{5... | collective-permute-start | bytes 1572872 | tf_op jit(solution)/shard_map/ppermute | solution.py:59
  35.4 31.6 %collective-permute-start.5 = (bf16[1024,256]{1,0:T(8,128)(2,1)S(1)}, bf16[1024,256]{1,0:T(8,128)(2,1)S(1)}, u32[]{:S(2)}, u32[]{:S(2)}) collective-permute-start(bf16[1024,256]{1,0:T(8,128)(2,1)S(1)} %all_gather.7), channel_id=1, source_target_pairs={{0,576},{192,0},{384,192},{576,384},{1,577},{193,1},{385,193},{577... | collective-permute-start | bytes 1572872 | tf_op jit(solution)/shard_map/ppermute | solution.py:60
  39.0 43.1 %collective-permute-start.2 = (bf16[384,128]{1,0:T(8,128)(2,1)}, bf16[384,128]{1,0:T(8,128)(2,1)}, u32[]{:S(2)}, u32[]{:S(2)}) collective-permute-start(bf16[384,128]{1,0:T(8,128)(2,1)} %get-tuple-element.27), channel_id=1, source_target_pairs={{0,12},{12,0},{1,13},{13,1},{2,14},{14,2},{3,15},{15,3},{4,16},{16... | collective-permute-start | bytes 294920 | tf_op jit(solution)/shard_map/ppermute | solution.py:130
  42.0 27.7 %copy-start.4 = (bf16[384,256]{1,0:T(8,128)(2,1)S(1)}, bf16[384,256]{1,0:T(8,128)(2,1)}, u32[]{:S(2)}) copy-start(bf16[384,256]{1,0:T(8,128)(2,1)} %param.7) | copy-start | bytes 589828
  42.6 13.7 %collective-permute-start = (bf16[256,256]{0,1:T(8,128)(2,1)}, bf16[256,256]{0,1:T(8,128)(2,1)}, u32[]{:S(2)}, u32[]{:S(2)}) collective-permute-start(bf16[256,256]{0,1:T(8,128)(2,1)} %slice.65), channel_id=1, source_target_pairs={{0,12},{12,24},{24,36},{36,48},{48,60},{60,72},{72,84},{84,96},{96... | collective-permute-start | bytes 393224 | tf_op jit(solution)/shard_map/ppermute | solution.py:22
  46.6 23.0 %collective-permute-start.1 = (bf16[256,256]{1,0:T(8,128)(2,1)}, bf16[256,256]{1,0:T(8,128)(2,1)}, u32[]{:S(2)}, u32[]{:S(2)}) collective-permute-start(bf16[256,256]{1,0:T(8,128)(2,1)} %slice.46), channel_id=1, source_target_pairs={{0,12},{12,24},{24,36},{36,48},{48,60},{60,72},{72,84},{84,96},{96... | collective-permute-start | bytes 393224 | tf_op jit(solution)/shard_map/ppermute | solution.py:22
  52.7 1.1 copy-start.6
  59.0 13.7 %collective-permute-start.4 = (bf16[512,256]{1,0:T(8,128)(2,1)}, bf16[512,256]{1,0:T(8,128)(2,1)}, u32[]{:S(2)}, u32[]{:S(2)}) collective-permute-start(bf16[512,256]{1,0:T(8,128)(2,1)} %slice.66), channel_id=1, source_target_pairs={{0,192},{192,384},{384,576},{576,0},{1,193},{193,385},{385,577},{5... | collective-permute-start | bytes 786440 | tf_op jit(solution)/shard_map/ppermute | solution.py:64
  67.0 15.1 %copy-start.7 = (s32[768]{0:T(1024)S(1)}, s32[768]{0:T(1024)}, u32[]{:S(2)}) copy-start(s32[768]{0:T(1024)} %pad_add_fusion) | copy-start | bytes 9220
  67.7 11.8 %collective-permute-start.6 = (bf16[512,256]{1,0:T(8,128)(2,1)}, bf16[512,256]{1,0:T(8,128)(2,1)}, u32[]{:S(2)}, u32[]{:S(2)}) collective-permute-start(bf16[512,256]{1,0:T(8,128)(2,1)} %slice.67), channel_id=1, source_target_pairs={{0,576},{192,0},{384,192},{576,384},{1,577},{193,1},{385,193},{577... | collective-permute-start | bytes 786440 | tf_op jit(solution)/shard_map/ppermute | solution.py:65
  82.1 4.5 %copy-start.5 = (bf16[4096,256]{1,0:T(8,128)(2,1)S(1)}, bf16[4096,256]{1,0:T(8,128)(2,1)}, u32[]{:S(2)}) copy-start(bf16[4096,256]{1,0:T(8,128)(2,1)} %constant_dynamic-update-slice_fusion) | copy-start | bytes 6291460
  90.6 6.6 %copy-start.2 = (f32[2,640,384]{2,1,0:T(8,128)S(1)}, f32[2,640,384]{2,1,0:T(8,128)}, u32[]{:S(2)}) copy-start(f32[2,640,384]{2,1,0:T(8,128)} %get-tuple-element.31) | copy-start | bytes 5898244
  90.6 6.6 %copy-start.3 = (pred[384,640]{0,1:T(8,128)(4,1)S(1)}, pred[384,640]{0,1:T(8,128)(4,1)}, u32[]{:S(2)}) copy-start(pred[384,640]{0,1:T(8,128)(4,1)} %fusion.20) | copy-start | bytes 737284
  95.0 3.4 %collective-permute-start.7 = (f32[384,130]{0,1:T(8,128)S(1)}, f32[384,130]{0,1:T(8,128)S(1)}, u32[]{:S(2)}, u32[]{:S(2)}) collective-permute-start(f32[384,130]{0,1:T(8,128)S(1)} %pad_maximum_fusion.2), channel_id=1, source_target_pairs={{0,12},{12,0},{1,13},{13,1},{2,14},{14,2},{3,15},{15,3},{4,16},{16... | collective-permute-start | bytes 599048 | tf_op jit(solution)/shard_map/ppermute | solution.py:151
  100.3 1.6 copy-start.1
  101.9 16.9 %collective-permute-start.8 = (bf16[32,4096]{1,0:T(8,128)(2,1)S(1)}, bf16[32,4096]{1,0:T(8,128)(2,1)S(1)}, u32[]{:S(2)}, u32[]{:S(2)}) collective-permute-start(bf16[32,4096]{1,0:T(8,128)(2,1)S(1)} %get-tuple-element.16), channel_id=1, source_target_pairs={{0,1},{1,2},{2,3},{3,4},{4,5},{5,6},{6,7},{7,8},{8,9},{9,10},{10,1... | collective-permute-start | bytes 786440 | tf_op jit(solution)/shard_map/ppermute | solution.py:88
  103.9 17.9 %collective-permute-start.14 = (bf16[32,4096]{1,0:T(8,128)(2,1)S(1)}, bf16[32,4096]{1,0:T(8,128)(2,1)S(1)}, u32[]{:S(2)}, u32[]{:S(2)}) collective-permute-start(bf16[32,4096]{1,0:T(8,128)(2,1)S(1)} %get-tuple-element.17), channel_id=1, source_target_pairs={{0,11},{1,0},{2,1},{3,2},{4,3},{5,4},{6,5},{7,6},{8,7},{9,8},{10,9... | collective-permute-start | bytes 786440 | tf_op jit(solution)/shard_map/ppermute | solution.py:93
  119.8 10.9 %collective-permute-start.9 = (bf16[32,4096]{1,0:T(8,128)(2,1)S(1)}, bf16[32,4096]{1,0:T(8,128)(2,1)S(1)}, u32[]{:S(2)}, u32[]{:S(2)}) collective-permute-start(bf16[32,4096]{1,0:T(8,128)(2,1)S(1)} %add_convert_fusion.9), channel_id=1, source_target_pairs={{0,1},{1,2},{2,3},{3,4},{4,5},{5,6},{6,7},{7,8},{8,9},{9,10},{10,1... | collective-permute-start | bytes 786440 | tf_op jit(solution)/shard_map/ppermute | solution.py:88
  131.8 10.0 %collective-permute-start.10 = (bf16[32,4096]{1,0:T(8,128)(2,1)S(1)}, bf16[32,4096]{1,0:T(8,128)(2,1)S(1)}, u32[]{:S(2)}, u32[]{:S(2)}) collective-permute-start(bf16[32,4096]{1,0:T(8,128)(2,1)S(1)} %get-tuple-element.14), channel_id=1, source_target_pairs={{0,1},{1,2},{2,3},{3,4},{4,5},{5,6},{6,7},{7,8},{8,9},{9,10},{10,1... | collective-permute-start | bytes 786440 | tf_op jit(solution)/shard_map/ppermute | solution.py:88
  133.8 9.3 %collective-permute-start.15 = (bf16[32,4096]{1,0:T(8,128)(2,1)S(1)}, bf16[32,4096]{1,0:T(8,128)(2,1)S(1)}, u32[]{:S(2)}, u32[]{:S(2)}) collective-permute-start(bf16[32,4096]{1,0:T(8,128)(2,1)S(1)} %get-tuple-element.15), channel_id=1, source_target_pairs={{0,11},{1,0},{2,1},{3,2},{4,3},{5,4},{6,5},{7,6},{8,7},{9,8},{10,9... | collective-permute-start | bytes 786440 | tf_op jit(solution)/shard_map/ppermute | solution.py:93
  144.2 9.9 %collective-permute-start.11 = (bf16[32,4096]{1,0:T(8,128)(2,1)S(1)}, bf16[32,4096]{1,0:T(8,128)(2,1)S(1)}, u32[]{:S(2)}, u32[]{:S(2)}) collective-permute-start(bf16[32,4096]{1,0:T(8,128)(2,1)S(1)} %get-tuple-element.12), channel_id=1, source_target_pairs={{0,1},{1,2},{2,3},{3,4},{4,5},{5,6},{6,7},{7,8},{8,9},{9,10},{10,1... | collective-permute-start | bytes 786440 | tf_op jit(solution)/shard_map/ppermute | solution.py:88
  146.1 9.5 %collective-permute-start.16 = (bf16[32,4096]{1,0:T(8,128)(2,1)S(1)}, bf16[32,4096]{1,0:T(8,128)(2,1)S(1)}, u32[]{:S(2)}, u32[]{:S(2)}) collective-permute-start(bf16[32,4096]{1,0:T(8,128)(2,1)S(1)} %get-tuple-element.13), channel_id=1, source_target_pairs={{0,11},{1,0},{2,1},{3,2},{4,3},{5,4},{6,5},{7,6},{8,7},{9,8},{10,9... | collective-permute-start | bytes 786440 | tf_op jit(solution)/shard_map/ppermute | solution.py:93
  156.7 9.9 %collective-permute-start.12 = (bf16[32,4096]{1,0:T(8,128)(2,1)S(1)}, bf16[32,4096]{1,0:T(8,128)(2,1)S(1)}, u32[]{:S(2)}, u32[]{:S(2)}) collective-permute-start(bf16[32,4096]{1,0:T(8,128)(2,1)S(1)} %get-tuple-element.10), channel_id=1, source_target_pairs={{0,1},{1,2},{2,3},{3,4},{4,5},{5,6},{6,7},{7,8},{8,9},{9,10},{10,1... | collective-permute-start | bytes 786440 | tf_op jit(solution)/shard_map/ppermute | solution.py:88
  158.7 9.5 %collective-permute-start.17 = (bf16[32,4096]{1,0:T(8,128)(2,1)S(1)}, bf16[32,4096]{1,0:T(8,128)(2,1)S(1)}, u32[]{:S(2)}, u32[]{:S(2)}) collective-permute-start(bf16[32,4096]{1,0:T(8,128)(2,1)S(1)} %get-tuple-element.11), channel_id=1, source_target_pairs={{0,11},{1,0},{2,1},{3,2},{4,3},{5,4},{6,5},{7,6},{8,7},{9,8},{10,9... | collective-permute-start | bytes 786440 | tf_op jit(solution)/shard_map/ppermute | solution.py:93
  169.3 9.9 %collective-permute-start.13 = (bf16[32,4096]{1,0:T(8,128)(2,1)S(1)}, bf16[32,4096]{1,0:T(8,128)(2,1)S(1)}, u32[]{:S(2)}, u32[]{:S(2)}) collective-permute-start(bf16[32,4096]{1,0:T(8,128)(2,1)S(1)} %get-tuple-element.8), channel_id=1, source_target_pairs={{0,1},{1,2},{2,3},{3,4},{4,5},{5,6},{6,7},{7,8},{8,9},{9,10},{10,1... | collective-permute-start | bytes 786440 | tf_op jit(solution)/shard_map/ppermute | solution.py:88
  171.2 9.5 %collective-permute-start.18 = (bf16[32,4096]{1,0:T(8,128)(2,1)S(1)}, bf16[32,4096]{1,0:T(8,128)(2,1)S(1)}, u32[]{:S(2)}, u32[]{:S(2)}) collective-permute-start(bf16[32,4096]{1,0:T(8,128)(2,1)S(1)} %get-tuple-element.9), channel_id=1, source_target_pairs={{0,11},{1,0},{2,1},{3,2},{4,3},{5,4},{6,5},{7,6},{8,7},{9,8},{10,9... | collective-permute-start | bytes 786440 | tf_op jit(solution)/shard_map/ppermute | solution.py:93
